TPU v7x, 256 devices: a whole 4x4x8 slice. The times are simulated.
256 devices in a mesh: req: 32 (over y, x, core), tp: 8 (over z).
Axes of the slice: x: 4, y: 4, z: 8, core: 2. Of those that a mesh axis runs over, the one named last changes fastest.
Arguments:
- tokens: bfloat16 [256, 4, 1536], P('req'), may hold values from -6 to 6
- lengths: int32 [256], P('req'), may hold values from 16 to 32768, as said below
- page_table: int32 [256, 9], P('req'), may hold values from 0 to 2303, as said below
- kv_pages: bfloat16 [2304, 2, 128, 128], P('req'), may hold values from -480 to 480
- norm_gain: float32 [1536], replicated, may hold values from 0.1 to 1.9
- query_weight: bfloat16 [1536, 1024], P(None, 'tp'), may hold values from -0.15625 to 0.15625
- key_weight: bfloat16 [1536, 128], replicated, may hold values from -0.15625 to 0.15625
- value_weight: bfloat16 [1536, 128], replicated, may hold values from -0.15625 to 0.15625
- out_weight: bfloat16 [1024, 1536], P('tp'), may hold values from -0.1875 to 0.1875
- mlp_gain: float32 [1536], replicated, may hold values from 0.1 to 1.9
- gate_weight: bfloat16 [1536, 4608], P(None, 'tp'), may hold values from -0.15625 to 0.15625
- up_weight: bfloat16 [1536, 4608], P(None, 'tp'), may hold values from -0.15625 to 0.15625
- down_weight: bfloat16 [4608, 1536], P('tp'), may hold values from -0.09375 to 0.09375
Outputs:
- layer_out: bfloat16 [256, 4, 1536], P('req')
Inputs may be any that keep to these rules, and one draw needn't show every extreme that they name: `lengths`: one request has exactly 32768 cached positions in every draw. `page_table`: all entries together are a permutation of the 2304 pool pages. Entry (r, j) is pool page r * 9 + j, in the part of the pool held with request r, except for spilled entries chosen from the seed (about a fifth of all); the spilled entries hold one another's pool pages in an order drawn from the seed, mostly on other devices of req.
All inputs are finite; a program needn't handle non-finite values.
Results may differ from a plain program's by a relative error of at most 0.0095.
The roundings to bfloat16 on the way count: a program that leaves them out, or rounds other values in their place, can miss the bound.
Values may be sent and summed in bfloat16 or wider, within the bound.
No kernel may reach another device: no remote copies, remote signals or barrier semaphores. Data moves between devices by JAX's collectives and lax.ppermute only.
A program may use at most 128 MiB of HBM per device.

v0:
```python
import jax
import jax.numpy as jnp
from jax import lax
from jax.sharding import PartitionSpec as P

WINDOW = 1024


negative = -1e30
epsilon = 1e-06


def rms_norm(values, gain):
    return values * lax.rsqrt(jnp.mean(values * values, axis=-1, keepdims=True) + epsilon) * gain


def body(
    tokens,
    lengths,
    page_table,
    kv_pages,
    norm_gain,
    query_weight,
    key_weight,
    value_weight,
    out_weight,
    mlp_gain,
    gate_weight,
    up_weight,
    down_weight,
):
    req_dev, steps, width = tokens.shape
    head_dim = key_weight.shape[1]
    heads_dev = query_weight.shape[1] // head_dim
    pool_size = kv_pages.shape[0]
    page_size = kv_pages.shape[2]
    window_pages = page_table.shape[1]
    token_rows = tokens.reshape(req_dev * steps, width)
    normed = rms_norm(token_rows.astype(jnp.float32), norm_gain).astype(jnp.bfloat16)
    queries = (
        jnp.dot(normed, query_weight, preferred_element_type=jnp.float32) * head_dim ** (-0.5)
    ).astype(jnp.bfloat16)
    key_new = jnp.dot(normed, key_weight, preferred_element_type=jnp.float32).astype(jnp.bfloat16)
    value_new = jnp.dot(normed, value_weight, preferred_element_type=jnp.float32).astype(
        jnp.bfloat16
    )
    all_lengths, all_table = (
        lax.all_gather(lengths, "req", axis=0, tiled=True),
        lax.all_gather(page_table, "req", axis=0, tiled=True),
    )
    all_queries = lax.all_gather(
        queries.reshape(req_dev, steps, heads_dev * head_dim), "req", axis=0, tiled=True
    )
    requests = all_lengths.shape[0]
    flat_table = all_table.reshape(-1)
    local_slot = flat_table - lax.axis_index("req") * pool_size
    inside = (local_slot >= 0) & (local_slot < pool_size)
    owner_entry = (
        jnp.zeros((pool_size,), jnp.int32)
        .at[jnp.where(inside, local_slot, pool_size)]
        .set(jnp.arange(flat_table.shape[0], dtype=jnp.int32), mode="drop")
    )
    page_request = owner_entry // window_pages
    page_number = owner_entry % window_pages
    page_length = all_lengths[page_request]
    first_page = jnp.maximum(page_length - (WINDOW - 1), 0) // page_size
    position = (first_page + page_number)[:, None] * page_size + jnp.arange(
        page_size, dtype=jnp.int32
    )[None, :]
    current = page_length[:, None] + jnp.arange(steps, dtype=jnp.int32)[None, :]
    visible = (position[:, None, :] < page_length[:, None, None]) & (
        position[:, None, :] > current[:, :, None] - WINDOW
    )
    visible = visible[:, :, None, :]
    page_queries = all_queries[page_request]
    scores = jnp.einsum(
        "pqd,pkd->pqk", page_queries, kv_pages[:, 0], preferred_element_type=jnp.float32
    )
    scores = jnp.where(visible, scores.reshape(pool_size, steps, heads_dev, page_size), negative)
    block_max = jnp.max(scores, axis=-1)
    weights = jnp.where(visible, jnp.exp(scores - block_max[..., None]), 0.0)
    block_total = jnp.sum(weights, axis=-1)
    block_out = jnp.einsum(
        "pqk,pkd->pqd",
        weights.astype(jnp.bfloat16).reshape(pool_size, steps * heads_dev, page_size),
        kv_pages[:, 1],
        preferred_element_type=jnp.float32,
    )
    block_out = block_out.reshape(pool_size, steps, heads_dev, head_dim)
    request_max = jnp.maximum(
        jax.ops.segment_max(block_max, page_request, num_segments=requests), negative
    )
    start_row = lax.axis_index("req") * req_dev
    cache_max = lax.pmax(request_max, "req")
    scale = jnp.exp(block_max - cache_max[page_request])
    sent_out = jax.ops.segment_sum(
        block_out * scale[..., None], page_request, num_segments=requests
    )
    sent_total = jax.ops.segment_sum(block_total * scale, page_request, num_segments=requests)
    cache_out, cache_total = (
        lax.psum_scatter(sent_out, "req", scatter_dimension=0, tiled=True),
        lax.psum_scatter(sent_total, "req", scatter_dimension=0, tiled=True),
    )
    mine_max = lax.dynamic_slice_in_dim(cache_max, start_row, req_dev, 0)
    local_queries = queries.reshape(req_dev, steps, heads_dev, head_dim)
    new_scores = jnp.einsum(
        "rshd,rtd->rsht",
        local_queries,
        key_new.reshape(req_dev, steps, head_dim),
        preferred_element_type=jnp.float32,
    )
    causal = (jnp.arange(steps)[None, :] <= jnp.arange(steps)[:, None])[None, :, None, :]
    new_scores = jnp.where(causal, new_scores, negative)
    new_max = jnp.max(new_scores, axis=-1)
    new_weights = jnp.where(causal, jnp.exp(new_scores - new_max[..., None]), 0.0)
    new_total = jnp.sum(new_weights, axis=-1)
    new_out = jnp.einsum(
        "rsht,rtd->rshd",
        new_weights.astype(jnp.bfloat16),
        value_new.reshape(req_dev, steps, head_dim),
        preferred_element_type=jnp.float32,
    )
    overall = jnp.maximum(mine_max, new_max)
    cache_scale = jnp.exp(mine_max - overall)
    new_scale = jnp.exp(new_max - overall)
    total = cache_total * cache_scale + new_total * new_scale
    summed = cache_out * cache_scale[..., None] + new_out * new_scale[..., None]
    attended = (
        (summed / total[..., None])
        .astype(jnp.bfloat16)
        .reshape(req_dev * steps, heads_dev * head_dim)
    )
    projected = jnp.dot(attended, out_weight, preferred_element_type=jnp.float32)
    attn_total = lax.psum(projected, "tp")
    residual = (token_rows.astype(jnp.float32) + attn_total).astype(jnp.bfloat16)
    mlp_in = rms_norm(residual.astype(jnp.float32), mlp_gain).astype(jnp.bfloat16)
    gate = jnp.dot(mlp_in, gate_weight, preferred_element_type=jnp.float32)
    upward = jnp.dot(mlp_in, up_weight, preferred_element_type=jnp.float32)
    hidden = (jax.nn.gelu(gate, approximate=True) * upward).astype(jnp.bfloat16)
    mlp_total = lax.psum(
        jnp.dot(hidden, down_weight, preferred_element_type=jnp.float32).astype(jnp.bfloat16), "tp"
    ).astype(jnp.float32)
    layer_out = (residual.astype(jnp.float32) + mlp_total).astype(jnp.bfloat16)
    return layer_out.reshape(req_dev, steps, width)


def solution(mesh):
    return jax.shard_map(
        body,
        mesh=mesh,
        in_specs=(
            P("req", None, None),
            P("req"),
            P("req", None),
            P("req", None, None, None),
            P(),
            P(None, "tp"),
            P(),
            P(),
            P("tp", None),
            P(),
            P(None, "tp"),
            P(None, "tp"),
            P("tp", None),
        ),
        out_specs=P("req", None, None),
        check_vma=False,
    )
```

profile of v0, /device:TPU:2, one launch (start us, length us, event | category | flops | bytes accessed | tf_op | source)
XLA Modules:
  0.0 512.9 jit_solution(16299514413610461038)
XLA Ops:
  6.5 1.4 fusion.63
  8.6 0.9 dynamic-update-slice
  9.5 15.7 %all-reduce = s32[256]{0:T(256)S(1)} all-reduce(s32[256]{0:T(256)S(1)} %dynamic-update-slice), channel_id=1, replica_groups=mesh['req'=32,'tp'=8] {'req'}, use_global_device_ids=true, to_apply=%add | all-reduce | flops 256 | bytes 2048
  25.2 23.4 %all_gather.9 = s32[256,9]{1,0:T(8,128)S(1)} all-gather(s32[8,9]{1,0:T(8,128)} %param.15), channel_id=1, replica_groups=mesh['req'=32,'tp'=8] {'req'}, dimensions={0}, use_global_device_ids=true | all-gather | bytes 9504 | tf_op jit(solution)/shard_map/all_gather | solution.py:49
  48.5 0.2 sub.78
  48.8 9.0 %scatter_custom_fusion = s32[72]{0:T(128)S(1)} fusion(s32[2304]{0:T(1024)S(1)} %fusion.44, s32[2304]{0:T(1024)S(1)} %iota.34, s32[]{:T(128)} %constant.27.clone.1), kind=kCustom, calls=%fused_computation.93 | custom fusion | bytes 292 | tf_op jit(solution)/shard_map/scatter | solution.py:61
  57.8 1.3 gather_fusion
  59.4 1.0 multiply_reduce_fusion
  60.4 0.9 reshape.246
  61.4 0.8 multiply_convert_fusion
  62.4 22.6 %all_gather.11 = bf16[256,4,128]{2,1,0:T(4,128)(2,1)S(1)} all-gather(bf16[8,4,128]{2,1,0:T(4,128)(2,1)S(1)} %bitcast.89), channel_id=1, replica_groups=mesh['req'=32,'tp'=8] {'req'}, dimensions={0}, use_global_device_ids=true | all-gather | bytes 270336 | tf_op jit(solution)/shard_map/all_gather | solution.py:51
  85.0 0.7 gather_fusion.1
  85.7 3.1 fusion.64
  88.8 1.0 scatter_custom_fusion.1
  89.8 123.3 %pmax.7 = f32[256,4,1]{1,0,2:T(8,128)S(1)} all-reduce(f32[256,4,1]{1,0,2:T(8,128)S(1)} %maximum_bitcast_fusion), channel_id=1, replica_groups=mesh['req'=32,'tp'=8] {'req'}, use_global_device_ids=true, to_apply=%region_4.5 | all-reduce | flops 1024 | bytes 8192 | tf_op jit(solution)/shard_map/pmax | solution.py:94
  213.1 0.6 gather_fusion.2
  213.8 2.5 fusion.9
  216.3 3.4 scatter_fusion
  219.8 0.8 copy.86
  221.7 1.3 fusion.57
  222.9 1.2 scatter_custom_fusion.3
  224.7 123.8 %all-reduce.1 = f32[256,4,1]{1,0,2:T(8,128)S(1)} all-reduce(f32[256,4,1]{1,0,2:T(8,128)S(1)} %bitcast.88), channel_id=3, replica_groups=mesh['req'=32,'tp'=8] {'req'}, use_global_device_ids=true, to_apply=%region_10.11.clone | all-reduce | flops 1024 | bytes 8192
  348.5 1.2 convolution_convert_fusion.1
  349.8 0.7 reshape.332
  350.6 0.9 fusion.66
  351.6 75.8 %all-reduce.5.cloned.1.call-done = f32[32,1536]{1,0:T(8,128)} async-done(((f32[32,1536]{1,0:T(8,128)}), f32[32,1536]{1,0:T(8,128)}) %all-reduce.5.cloned.1.call-update) | async-done | bytes 196624 | tf_op jit(solution)/shard_map/psum | solution.py:134
  427.4 1.1 fusion.18
  428.4 2.1 fusion.42
  430.5 3.2 convolution_convert_fusion
  433.8 71.0 %all-reduce.7.cloned.1.call-done = bf16[32,1536]{1,0:T(8,128)(2,1)} async-done(((bf16[32,1536]{1,0:T(8,128)(2,1)}), bf16[32,1536]{1,0:T(8,128)(2,1)}) %all-reduce.7.cloned.1.call-update) | async-done | bytes 98320 | tf_op jit(solution)/shard_map/psum | solution.py:140
  504.8 0.9 fusion.21
  505.7 0.7 reshape.245
  (55 shorter events, 1.9 us)
Async XLA Ops:
  6.5 424.0 %copy-start = (bf16[576,1536]{1,0:T(8,128)(2,1)S(1)}, bf16[576,1536]{1,0:T(8,128)(2,1)}, u32[]{:S(2)}) copy-start(bf16[576,1536]{1,0:T(8,128)(2,1)} %param.25) | copy-start | bytes 5308420
  6.5 55.7 %copy-start.2 = (bf16[1536,128]{1,0:T(8,128)(2,1)S(1)}, bf16[1536,128]{1,0:T(8,128)(2,1)}, u32[]{:S(2)}) copy-start(bf16[1536,128]{1,0:T(8,128)(2,1)} %param.18) | copy-start | bytes 1179652
  6.5 343.2 %reduce-scatter.6.cloned.1.call-start = ((), (), s32[]{:S(2)}) async-start(), calls=%async_computation.3 | async-start | bytes 540672
  59.2 154.5 %copy-start.8 = (pred[72,128]{1,0:T(8,128)(4,1)}, pred[72,128]{1,0:T(8,128)(4,1)S(1)}, u32[]{:S(2)}) copy-start(pred[72,128]{1,0:T(8,128)(4,1)S(1)} %broadcast_compare_fusion) | copy-start | bytes 27652
  59.3 154.5 %copy-start.4 = (s32[72,128]{1,0:T(8,128)}, s32[72,128]{1,0:T(8,128)S(1)}, u32[]{:S(2)}) copy-start(s32[72,128]{1,0:T(8,128)S(1)} %iota_add_fusion) | copy-start | bytes 110596
  59.4 154.4 %copy-start.5 = (s32[72,4]{1,0:T(8,128)}, s32[72,4]{1,0:T(8,128)S(1)}, u32[]{:S(2)}) copy-start(s32[72,4]{1,0:T(8,128)S(1)} %add_add_fusion) | copy-start | bytes 3460
  88.8 125.0 %copy-start.7 = (f32[72,4,128]{2,1,0:T(4,128)}, f32[72,4,128]{2,1,0:T(4,128)S(1)}, u32[]{:S(2)}) copy-start(f32[72,4,128]{2,1,0:T(4,128)S(1)} %get-tuple-element.17) | copy-start | bytes 442372
  213.7 2.6 copy-start.6
  216.3 4.5 copy-start.3
  219.8 130.8 %copy-start.1 = (bf16[128,1536]{1,0:T(8,128)(2,1)S(1)}, bf16[128,1536]{1,0:T(8,128)(2,1)}, u32[]{:S(2)}) copy-start(bf16[128,1536]{1,0:T(8,128)(2,1)} %param.21) | copy-start | bytes 1179652
  220.7 207.8 %copy-start.9 = (f32[1536]{0:T(1024)S(1)}, f32[1536]{0:T(1024)}, u32[]{:S(2)}) copy-start(f32[1536]{0:T(1024)} %param.22) | copy-start | bytes 18436
  220.7 206.7 %all-reduce.5.cloned.1.call-start = ((), (), s32[]{:S(2)}) async-start(), calls=%async_computation.1 | async-start | bytes 393216 | tf_op jit(solution)/shard_map/psum | solution.py:134
  351.5 153.3 %all-reduce.7.cloned.1.call-start = ((), (), s32[]{:S(2)}) async-start(), calls=%async_computation.2 | async-start | bytes 196608 | tf_op jit(solution)/shard_map/psum | solution.py:140
Sparse Core Ops, SparseCore 0:
  220.8 87.7 reduce-scatter.5
  351.6 75.6 all-reduce.4
  433.9 70.8 all-reduce.6
where the time goes:
time: 514 us; the launch traced here: 513 us
  blocking collectives  309 us (60%)
  waiting for transfers between devices  147 us (29%)
  local copies, waits for them, and re-layouts  17.7 us (3%)
  between operations  14.6 us (3%)
  matrix products  13.5 us (3%)
  other arithmetic  11.3 us (2%)
    unnamed x2, blocking collectives  140 us
    pmax x1, blocking collectives, body(): cache_max = lax.pmax(request_max, 'req')  123 us
    psum x1, waiting for transfers between devices, body(): attn_total = lax.psum(projected, 'tp')  75.8 us
    psum x1, waiting for transfers between devices, body(): lax.psum(jnp.dot(hidden, down_weight, preferred_element_type=jnp.float32)...  71 us
    all_gather x1, blocking collectives, body(): lax.all_gather(page_table, 'req', axis=0, tiled=True)  23.4 us
    all_gather x1, blocking collectives, body(): lax.all_gather(queries.reshape(req_dev, steps, heads_dev * head_dim), 're...  22.6 us
  transfers between devices with their start and end apart: 3, of which 2 were waited for; matrix products, arithmetic and copies ran while one was open for 1% of the time, Pallas kernels for 0%

commit v1 on v0

v1 whole, which is shorter than its diff:
```python
import jax
import jax.numpy as jnp
from jax import lax
from jax.sharding import PartitionSpec as P

WINDOW = 1024


negative = -1e30
epsilon = 1e-06


def rms_norm(values, gain):
    return values * lax.rsqrt(jnp.mean(values * values, axis=-1, keepdims=True) + epsilon) * gain


def tree_sum(values, axis, size):
    step = 1
    while step < size:
        values = values + lax.ppermute(values, axis, [(i, i ^ step) for i in range(size)])
        step *= 2
    return values


def make_body(req_size, tp_size):
    def body(
        tokens,
        lengths,
        page_table,
        kv_pages,
        norm_gain,
        query_weight,
        key_weight,
        value_weight,
        out_weight,
        mlp_gain,
        gate_weight,
        up_weight,
        down_weight,
    ):
        req_dev, steps, width = tokens.shape
        head_dim = key_weight.shape[1]
        heads_dev = query_weight.shape[1] // head_dim
        pool_size = kv_pages.shape[0]
        page_size = kv_pages.shape[2]
        window_pages = page_table.shape[1]
        requests = req_dev * req_size
        qwidth = steps * heads_dev * head_dim
        token_rows = tokens.reshape(req_dev * steps, width)
        normed = rms_norm(token_rows.astype(jnp.float32), norm_gain).astype(jnp.bfloat16)
        queries = (
            jnp.dot(normed, query_weight, preferred_element_type=jnp.float32) * head_dim ** (-0.5)
        ).astype(jnp.bfloat16)
        key_new = jnp.dot(normed, key_weight, preferred_element_type=jnp.float32).astype(jnp.bfloat16)
        value_new = jnp.dot(normed, value_weight, preferred_element_type=jnp.float32).astype(
            jnp.bfloat16
        )
        packed = jnp.concatenate(
            [
                queries.reshape(req_dev, qwidth).astype(jnp.float32),
                page_table.astype(jnp.float32),
                lengths.reshape(req_dev, 1).astype(jnp.float32),
            ],
            axis=1,
        )
        gathered = lax.all_gather(packed, "req", axis=0, tiled=True)
        all_queries = gathered[:, :qwidth].astype(jnp.bfloat16).reshape(
            requests, steps * heads_dev, head_dim
        )
        all_table = gathered[:, qwidth : qwidth + window_pages].astype(jnp.int32)
        all_lengths = gathered[:, qwidth + window_pages].astype(jnp.int32)
        flat_table = all_table.reshape(-1)
        entries = flat_table.shape[0]
        my_slots = lax.axis_index("req") * pool_size + jnp.arange(pool_size, dtype=jnp.int32)
        match = flat_table[None, :] == my_slots[:, None]
        owner_entry = jnp.sum(
            jnp.where(match, jnp.arange(entries, dtype=jnp.int32)[None, :], 0), axis=1
        )
        page_request = owner_entry // window_pages
        page_number = owner_entry % window_pages
        page_length = all_lengths[page_request]
        first_page = jnp.maximum(page_length - (WINDOW - 1), 0) // page_size
        position = (first_page + page_number)[:, None] * page_size + jnp.arange(
            page_size, dtype=jnp.int32
        )[None, :]
        current = page_length[:, None] + jnp.arange(steps, dtype=jnp.int32)[None, :]
        visible = (position[:, None, :] < page_length[:, None, None]) & (
            position[:, None, :] > current[:, :, None] - WINDOW
        )
        visible = visible[:, :, None, :]
        page_queries = all_queries[page_request]
        scores = jnp.einsum(
            "pqd,pkd->pqk", page_queries, kv_pages[:, 0], preferred_element_type=jnp.float32
        )
        scores = jnp.where(visible, scores.reshape(pool_size, steps, heads_dev, page_size), negative)
        block_max = jnp.max(scores, axis=-1)
        weights = jnp.where(visible, jnp.exp(scores - block_max[..., None]), 0.0)
        block_total = jnp.sum(weights, axis=-1)
        block_out = jnp.einsum(
            "pqk,pkd->pqd",
            weights.astype(jnp.bfloat16).reshape(pool_size, steps * heads_dev, page_size),
            kv_pages[:, 1],
            preferred_element_type=jnp.float32,
        )
        block_out = block_out.reshape(pool_size, steps, heads_dev, head_dim)
        member = page_request[None, :] == jnp.arange(requests, dtype=jnp.int32)[:, None]
        local_max = jnp.max(
            jnp.where(member[:, :, None, None], block_max[None], negative), axis=1
        )
        scale = jnp.exp(block_max - local_max[page_request])
        sent_out = jax.ops.segment_sum(
            block_out * scale[..., None], page_request, num_segments=requests
        )
        sent_total = jax.ops.segment_sum(block_total * scale, page_request, num_segments=requests)
        nsh = steps * heads_dev
        send = jnp.concatenate(
            [
                sent_out.reshape(requests, nsh * head_dim),
                sent_total.reshape(requests, nsh),
                local_max.reshape(requests, nsh),
            ],
            axis=1,
        )
        recv = lax.all_to_all(send, "req", 0, 0, tiled=True).reshape(req_size, req_dev, -1)
        got_out = recv[:, :, : nsh * head_dim].reshape(req_size, req_dev, steps, heads_dev, head_dim)
        got_total = recv[:, :, nsh * head_dim : nsh * (head_dim + 1)].reshape(
            req_size, req_dev, steps, heads_dev
        )
        got_max = recv[:, :, nsh * (head_dim + 1) :].reshape(req_size, req_dev, steps, heads_dev)
        cache_max = jnp.max(got_max, axis=0)
        local_queries = queries.reshape(req_dev, steps, heads_dev, head_dim)
        new_scores = jnp.einsum(
            "rshd,rtd->rsht",
            local_queries,
            key_new.reshape(req_dev, steps, head_dim),
            preferred_element_type=jnp.float32,
        )
        causal = (jnp.arange(steps)[None, :] <= jnp.arange(steps)[:, None])[None, :, None, :]
        new_scores = jnp.where(causal, new_scores, negative)
        new_max = jnp.max(new_scores, axis=-1)
        new_weights = jnp.where(causal, jnp.exp(new_scores - new_max[..., None]), 0.0)
        new_total = jnp.sum(new_weights, axis=-1)
        new_out = jnp.einsum(
            "rsht,rtd->rshd",
            new_weights.astype(jnp.bfloat16),
            value_new.reshape(req_dev, steps, head_dim),
            preferred_element_type=jnp.float32,
        )
        overall = jnp.maximum(cache_max, new_max)
        src_scale = jnp.exp(got_max - overall[None])
        new_scale = jnp.exp(new_max - overall)
        total = jnp.sum(got_total * src_scale, axis=0) + new_total * new_scale
        summed = jnp.sum(got_out * src_scale[..., None], axis=0) + new_out * new_scale[..., None]
        attended = (
            (summed / total[..., None])
            .astype(jnp.bfloat16)
            .reshape(req_dev * steps, heads_dev * head_dim)
        )
        projected = jnp.dot(attended, out_weight, preferred_element_type=jnp.float32)
        attn_total = tree_sum(projected, "tp", tp_size)
        residual = (token_rows.astype(jnp.float32) + attn_total).astype(jnp.bfloat16)
        mlp_in = rms_norm(residual.astype(jnp.float32), mlp_gain).astype(jnp.bfloat16)
        gate = jnp.dot(mlp_in, gate_weight, preferred_element_type=jnp.float32)
        upward = jnp.dot(mlp_in, up_weight, preferred_element_type=jnp.float32)
        hidden = (jax.nn.gelu(gate, approximate=True) * upward).astype(jnp.bfloat16)
        mlp_part = jnp.dot(hidden, down_weight, preferred_element_type=jnp.float32).astype(
            jnp.bfloat16
        )
        mlp_total = tree_sum(mlp_part, "tp", tp_size).astype(jnp.float32)
        layer_out = (residual.astype(jnp.float32) + mlp_total).astype(jnp.bfloat16)
        return layer_out.reshape(req_dev, steps, width)

    return body


def solution(mesh):
    return jax.shard_map(
        make_body(mesh.shape["req"], mesh.shape["tp"]),
        mesh=mesh,
        in_specs=(
            P("req", None, None),
            P("req"),
            P("req", None),
            P("req", None, None, None),
            P(),
            P(None, "tp"),
            P(),
            P(),
            P("tp", None),
            P(),
            P(None, "tp"),
            P(None, "tp"),
            P("tp", None),
        ),
        out_specs=P("req", None, None),
        check_vma=False,
    )
```

time: 514 us -> 129 us (0.25)
  blocking collectives: 309 us -> 24.8 us
  waiting for transfers between devices: 147 us -> 42.6 us
  starting transfers between devices: 0.09 us -> 26.1 us
  between operations: 14.6 us -> 0.35 us
  local copies, waits for them, and re-layouts: 17.7 us -> 8.5 us
    psum x2 -> x0, waiting for transfers between devices: 147 us -> none  [the longest x1 75.8 us: body(): attn_total = lax.psum(projected, 'tp')]
    unnamed x2 -> x0, blocking collectives: 140 us -> none
    pmax x1 -> x0, blocking collectives: 123 us -> none  [body(): cache_max = lax.pmax(request_max, 'req')]
    ppermute x0 -> x6, waiting for transfers between devices: none -> 33.5 us  [tree_sum(): lax.ppermute(values, axis, [(i, i ^ step) for i in range(size)])]
    all_gather x2 -> x1, blocking collectives: 46 us -> 24.8 us  [body(): gathered = lax.all_gather(packed, 'req', axis=0, tiled=True)]
    ppermute x0 -> x6, starting transfers between devices: none -> 20.3 us  [tree_sum(): lax.ppermute(values, axis, [(i, i ^ step) for i in range(size)])]
    all_to_all x0 -> x1, waiting for transfers between devices: none -> 9.05 us  [body(): lax.all_to_all(send, 'req', 0, 0, tiled=True).reshape(req_size, req_dev, -1)]
    scatter x1 -> x0, local copies, waits for them, and re-layouts: 8.97 us -> none  [body(): owner_entry = jnp.zeros((pool_size,), jnp.int32).at[jnp.where(inside, loc...]
  transfers between devices with their start and end apart: 3 -> 7, of which waited for: 2 -> 7; matrix products, arithmetic and copies ran while one was open for 1% -> 2% of each run, Pallas kernels for 0% -> 0%
where the time goes in v1:
time: 129 us
  waiting for transfers between devices  42.6 us (33%)
  starting transfers between devices  26.1 us (20%)
  blocking collectives  24.8 us (19%)
  matrix products  13.7 us (11%)
  other arithmetic  12.9 us (10%)
  local copies, waits for them, and re-layouts  8.5 us (7%)
    ppermute x6, waiting for transfers between devices, tree_sum(): lax.ppermute(values, axis, [(i, i ^ step) for i in range(size)])  33.5 us
    all_gather x1, blocking collectives, body(): gathered = lax.all_gather(packed, 'req', axis=0, tiled=True)  24.8 us
    ppermute x6, starting transfers between devices, tree_sum(): lax.ppermute(values, axis, [(i, i ^ step) for i in range(size)])  20.3 us
    all_to_all x1, waiting for transfers between devices, body(): lax.all_to_all(send, 'req', 0, 0, tiled=True).reshape(req_size, req_dev, -1)  9.05 us
    all_to_all x1, starting transfers between devices, body(): lax.all_to_all(send, 'req', 0, 0, tiled=True).reshape(req_size, req_dev, -1)  5.79 us
    scatter-add x1, other arithmetic, body(): jax.ops.segment_sum(block_out * scale[..., None], page_request, num_segme...  3.47 us
    dot_general x1, matrix products, body(): jnp.einsum('pqd,pkd->pqk', page_queries, kv_pages[:, 0], preferred_elemen...  3.08 us
  transfers between devices with their start and end apart: 7, of which 7 were waited for; matrix products, arithmetic and copies ran while one was open for 2% of the time, Pallas kernels for 0%

profile of v1, /device:TPU:2, one launch (start us, length us, event | category | flops | bytes accessed | tf_op | source)
XLA Modules:
  0.0 128.9 jit_solution(3212656176788903538)
XLA Ops:
  0.0 1.0 reshape.413
  1.1 1.1 multiply_reduce_fusion
  3.7 0.8 multiply_convert_fusion
  4.5 1.2 fusion.16
  5.8 24.8 %all_gather.3 = f32[256,522]{1,0:T(8,128)S(1)} all-gather(f32[8,522]{1,0:T(8,128)S(1)} %pad_maximum_fusion.1), channel_id=1, replica_groups=mesh['req'=32,'tp'=8] {'req'}, dimensions={0}, use_global_device_ids=true | all-gather | bytes 551232 | tf_op jit(solution)/shard_map/all_gather | solution.py:66
  31.3 1.3 gather_fusion
  33.6 3.1 %fusion.55 = (f32[72,4]{1,0:T(8,128)S(1)}, f32[72,4,128]{2,1,0:T(4,128)S(1)}) fusion(bf16[72,4,128]{2,1,0:T(4,128)(2,1)S(1)} %gather_fusion.1, bf16[72,2,128,128]{3,2,1,0:T(8,128)(2,1)} %param.16, s32[72,4]{1,0:T(8,128)S(1)} %add_add_fusion, s32[72,128]{1,0:T(8,128)S(1)} %iota_add_fusion, pred[72,128]{1,0:T(8,128)(4,1)S(1)} %broadcast_compare_fusion), kind=kOutput, calls=%fused_computation.100 | convolution fusion | flops 9584352 | bytes 2628864 | tf_op jit(solution)/shard_map/pqd,pkd->pqk/dot_general | solution.py:92
  38.1 2.5 %fusion.9 = f32[72,4,128]{2,1,0:T(4,128)S(1)} fusion(bf16[72,2,128,128]{3,2,1,0:T(8,128)(2,1)} %param.16, f32[72,4]{1,0:T(8,128)S(1)} %subtract_exponential_fusion, f32[72,4,128]{2,1,0:T(4,128)S(1)} %get-tuple-element.21, f32[72,4]{1,0:T(8,128)S(1)} %get-tuple-element.20, s32[72,4]{1,0:T(8,128)S(1)} %add_add_fusion, s32[72,128]{1,0:T(8,128)S(1)} %iota_add_fusion, ...), kind=kOutput, calls=%fused_computation.13 | convolution fusion | flops 9658368 | bytes 2703744 | tf_op jit(solution)/shard_map/pqk,pkd->pqd/dot_general | solution.py:99
  40.6 1.0 scatter_custom_fusion.1
  41.7 3.5 %scatter_fusion = f32[256,4,128]{2,1,0:T(4,128)S(1)} fusion(f32[256,4,128]{2,1,0:T(4,128)S(1)} %broadcast.329, s32[72]{0:T(128)S(1)} %get-tuple-element.11, f32[72,4,128]{2,1,0:T(4,128)S(1)} %fusion.9), kind=kCustom, calls=%fused_computation.3 | custom fusion | flops 36864 | bytes 442656 | tf_op jit(solution)/shard_map/scatter-add | solution.py:111
  45.4 0.9 pad_maximum_fusion
  46.3 5.8 %all-to-all-start = ((f32[32,8,520]{2,1,0:T(8,128)}), f32[32,8,520]{2,1,0:T(8,128)S(1)}, u32[]{:S(2)}, u32[]{:S(2)}) async-start(f32[32,8,520]{2,1,0:T(8,128)} %pad_maximum_fusion), calls=%async_computation | async-start | bytes 1310720 | tf_op jit(solution)/shard_map/all_to_all | solution.py:124
  53.4 0.7 copy.133
  54.1 0.8 convolution_convert_fusion.1
  54.9 9.1 %all-to-all-done = f32[32,8,520]{2,1,0:T(8,128)S(1)} async-done(((f32[32,8,520]{2,1,0:T(8,128)}), f32[32,8,520]{2,1,0:T(8,128)S(1)}, u32[]{:S(2)}, u32[]{:S(2)}) %all-to-all-start) | async-done | bytes 532512 | tf_op jit(solution)/shard_map/all_to_all | solution.py:124
  64.4 0.8 multiply_reduce_fusion.1
  66.1 0.7 multiply_add_fusion
  67.6 0.9 fusion.15
  68.5 1.2 fusion.57
  69.7 2.0 %collective-permute-start = (f32[32,1536]{1,0:T(8,128)S(1)}, f32[32,1536]{1,0:T(8,128)S(1)}, u32[]{:S(2)}, u32[]{:S(2)}) collective-permute-start(f32[32,1536]{1,0:T(8,128)S(1)} %fusion.57), channel_id=1, source_target_pairs={{0,1},{1,0},{2,3},{3,2},{4,5},{5,4},{6,7},{7,6},{8,9},{9,8},{10,11... | collective-permute-start | bytes 589832 | tf_op jit(solution)/shard_map/ppermute | solution.py:20
  71.7 5.5 %collective-permute-done = f32[32,1536]{1,0:T(8,128)S(1)} collective-permute-done((f32[32,1536]{1,0:T(8,128)S(1)}, f32[32,1536]{1,0:T(8,128)S(1)}, u32[]{:S(2)}, u32[]{:S(2)}) %collective-permute-start) | collective-permute-done | bytes 196640 | tf_op jit(solution)/shard_map/ppermute | solution.py:20
  77.2 3.4 %collective-permute-start.1 = (f32[32,1536]{1,0:T(8,128)S(1)}, f32[32,1536]{1,0:T(8,128)S(1)}, u32[]{:S(2)}, u32[]{:S(2)}) collective-permute-start(f32[32,1536]{1,0:T(8,128)S(1)} %add.189), channel_id=1, source_target_pairs={{0,2},{1,3},{2,0},{3,1},{4,6},{5,7},{6,4},{7,5},{8,10},{9,11},{10,... | collective-permute-start | bytes 589832 | tf_op jit(solution)/shard_map/ppermute | solution.py:20
  80.5 9.0 %collective-permute-done.1 = f32[32,1536]{1,0:T(8,128)S(1)} collective-permute-done((f32[32,1536]{1,0:T(8,128)S(1)}, f32[32,1536]{1,0:T(8,128)S(1)}, u32[]{:S(2)}, u32[]{:S(2)}) %collective-permute-start.1) | collective-permute-done | bytes 196640 | tf_op jit(solution)/shard_map/ppermute | solution.py:20
  89.6 6.3 %collective-permute-start.2 = (f32[32,1536]{1,0:T(8,128)S(1)}, f32[32,1536]{1,0:T(8,128)S(1)}, u32[]{:S(2)}, u32[]{:S(2)}) collective-permute-start(f32[32,1536]{1,0:T(8,128)S(1)} %add.190), channel_id=1, source_target_pairs={{0,4},{1,5},{2,6},{3,7},{4,0},{5,1},{6,2},{7,3},{8,12},{9,13},{10,... | collective-permute-start | bytes 589832 | tf_op jit(solution)/shard_map/ppermute | solution.py:20
  95.8 7.6 %collective-permute-done.2 = f32[32,1536]{1,0:T(8,128)S(1)} collective-permute-done((f32[32,1536]{1,0:T(8,128)S(1)}, f32[32,1536]{1,0:T(8,128)S(1)}, u32[]{:S(2)}, u32[]{:S(2)}) %collective-permute-start.2) | collective-permute-done | bytes 196640 | tf_op jit(solution)/shard_map/ppermute | solution.py:20
  104.2 1.3 fusion.41
  105.5 2.5 %convolution_convert_fusion = bf16[32,1536]{1,0:T(8,128)(2,1)S(1)} fusion(bf16[576,1536]{1,0:T(8,128)(2,1)S(1)} %copy-done, bf16[1536,576]{0,1:T(8,128)(2,1)} %param.24, f32[32,576]{1,0:T(8,128)} %fusion.41, bf16[32,1536]{1,0:T(8,128)(2,1)} %copy-done.4, f32[1536]{0:T(1024)S(1)} %copy-done.8, f32[32]{0:T(128)S(1)} %add_rsqrt_fusion.1), kind=kOutput, calls=%fused_computation.11 | convolution fusion | flops 113676288 | bytes 3815552 | tf_op jit(solution)/shard_map/dot_general | solution.py:166
  108.1 4.6 %collective-permute-done.3 = bf16[32,1536]{1,0:T(8,128)(2,1)S(1)} collective-permute-done((bf16[32,1536]{1,0:T(8,128)(2,1)S(1)}, bf16[32,1536]{1,0:T(8,128)(2,1)S(1)}, u32[]{:S(2)}, u32[]{:S(2)}) %collective-permute-start.3) | collective-permute-done | bytes 98336 | tf_op jit(solution)/shard_map/ppermute | solution.py:20
  112.7 3.3 %collective-permute-start.4 = (bf16[32,1536]{1,0:T(8,128)(2,1)S(1)}, bf16[32,1536]{1,0:T(8,128)(2,1)S(1)}, u32[]{:S(2)}, u32[]{:S(2)}) collective-permute-start(bf16[32,1536]{1,0:T(8,128)(2,1)S(1)} %add.197), channel_id=1, source_target_pairs={{0,2},{1,3},{2,0},{3,1},{4,6},{5,7},{6,4},{7,5},{8,10},{9,11},{10,... | collective-permute-start | bytes 294920 | tf_op jit(solution)/shard_map/ppermute | solution.py:20
  116.0 2.6 %collective-permute-done.4 = bf16[32,1536]{1,0:T(8,128)(2,1)S(1)} collective-permute-done((bf16[32,1536]{1,0:T(8,128)(2,1)S(1)}, bf16[32,1536]{1,0:T(8,128)(2,1)S(1)}, u32[]{:S(2)}, u32[]{:S(2)}) %collective-permute-start.4) | collective-permute-done | bytes 98336 | tf_op jit(solution)/shard_map/ppermute | solution.py:20
  118.7 5.2 %collective-permute-start.5 = (bf16[32,1536]{1,0:T(8,128)(2,1)S(1)}, bf16[32,1536]{1,0:T(8,128)(2,1)S(1)}, u32[]{:S(2)}, u32[]{:S(2)}) collective-permute-start(bf16[32,1536]{1,0:T(8,128)(2,1)S(1)} %add.198), channel_id=1, source_target_pairs={{0,4},{1,5},{2,6},{3,7},{4,0},{5,1},{6,2},{7,3},{8,12},{9,13},{10,... | collective-permute-start | bytes 294920 | tf_op jit(solution)/shard_map/ppermute | solution.py:20
  123.9 4.2 %collective-permute-done.5 = bf16[32,1536]{1,0:T(8,128)(2,1)S(1)} collective-permute-done((bf16[32,1536]{1,0:T(8,128)(2,1)S(1)}, bf16[32,1536]{1,0:T(8,128)(2,1)S(1)}, u32[]{:S(2)}, u32[]{:S(2)}) %collective-permute-start.5) | collective-permute-done | bytes 98336 | tf_op jit(solution)/shard_map/ppermute | solution.py:20
  (78 shorter events, 9.9 us)
Async XLA Ops:
  0.0 105.5 %copy-start = (bf16[576,1536]{1,0:T(8,128)(2,1)S(1)}, bf16[576,1536]{1,0:T(8,128)(2,1)}, u32[]{:S(2)}) copy-start(bf16[576,1536]{1,0:T(8,128)(2,1)} %param.25) | copy-start | bytes 5308420
  1.0 29.6 %copy-start.2 = (f32[32,1536]{1,0:T(8,128)}, f32[32,1536]{1,0:T(8,128)S(1)}, u32[]{:S(2)}) copy-start(f32[32,1536]{1,0:T(8,128)S(1)} %reshape.413) | copy-start | bytes 589828
  45.4 6.8 %copy-start.6 = (bf16[1536,128]{1,0:T(8,128)(2,1)S(1)}, bf16[1536,128]{1,0:T(8,128)(2,1)}, u32[]{:S(2)}) copy-start(bf16[1536,128]{1,0:T(8,128)(2,1)} %param.19) | copy-start | bytes 1179652
  45.4 8.7 %copy-start.7 = (bf16[1536,128]{1,0:T(8,128)(2,1)S(1)}, bf16[1536,128]{1,0:T(8,128)(2,1)}, u32[]{:S(2)}) copy-start(bf16[1536,128]{1,0:T(8,128)(2,1)} %param.20) | copy-start | bytes 1179652
  46.3 17.6 %all-to-all-start = ((f32[32,8,520]{2,1,0:T(8,128)}), f32[32,8,520]{2,1,0:T(8,128)S(1)}, u32[]{:S(2)}, u32[]{:S(2)}) async-start(f32[32,8,520]{2,1,0:T(8,128)} %pad_maximum_fusion), calls=%async_computation | async-start | bytes 1310720 | tf_op jit(solution)/shard_map/all_to_all | solution.py:124
  52.7 12.6 %copy-start.9 = (f32[8,4]{0,1:T(4,128)}, f32[8,4]{0,1:T(4,128)S(1)}, u32[]{:S(2)}) copy-start(f32[8,4]{0,1:T(4,128)S(1)} %select_reduce_fusion.2) | copy-start | bytes 388
  64.4 0.9 copy-start.10
  65.5 38.8 %copy-start.1 = (bf16[1536,576]{0,1:T(8,128)(2,1)S(1)}, bf16[1536,576]{0,1:T(8,128)(2,1)}, u32[]{:S(2)}) copy-start(bf16[1536,576]{0,1:T(8,128)(2,1)} %param.23) | copy-start | bytes 5308420
  66.1 38.1 %copy-start.8 = (f32[1536]{0:T(1024)S(1)}, f32[1536]{0:T(1024)}, u32[]{:S(2)}) copy-start(f32[1536]{0:T(1024)} %param.22) | copy-start | bytes 18436
  67.6 35.9 %copy-start.3 = (f32[32,1536]{1,0:T(8,128)S(1)}, f32[32,1536]{1,0:T(8,128)}, u32[]{:S(2)}) copy-start(f32[32,1536]{1,0:T(8,128)} %copy-done.2) | copy-start | bytes 589828
  69.7 7.5 %collective-permute-start = (f32[32,1536]{1,0:T(8,128)S(1)}, f32[32,1536]{1,0:T(8,128)S(1)}, u32[]{:S(2)}, u32[]{:S(2)}) collective-permute-start(f32[32,1536]{1,0:T(8,128)S(1)} %fusion.57), channel_id=1, source_target_pairs={{0,1},{1,0},{2,3},{3,2},{4,5},{5,4},{6,7},{7,6},{8,9},{9,8},{10,11... | collective-permute-start | bytes 589832 | tf_op jit(solution)/shard_map/ppermute | solution.py:20
  77.2 12.4 %collective-permute-start.1 = (f32[32,1536]{1,0:T(8,128)S(1)}, f32[32,1536]{1,0:T(8,128)S(1)}, u32[]{:S(2)}, u32[]{:S(2)}) collective-permute-start(f32[32,1536]{1,0:T(8,128)S(1)} %add.189), channel_id=1, source_target_pairs={{0,2},{1,3},{2,0},{3,1},{4,6},{5,7},{6,4},{7,5},{8,10},{9,11},{10,... | collective-permute-start | bytes 589832 | tf_op jit(solution)/shard_map/ppermute | solution.py:20
  89.6 13.9 %collective-permute-start.2 = (f32[32,1536]{1,0:T(8,128)S(1)}, f32[32,1536]{1,0:T(8,128)S(1)}, u32[]{:S(2)}, u32[]{:S(2)}) collective-permute-start(f32[32,1536]{1,0:T(8,128)S(1)} %add.190), channel_id=1, source_target_pairs={{0,4},{1,5},{2,6},{3,7},{4,0},{5,1},{6,2},{7,3},{8,12},{9,13},{10,... | collective-permute-start | bytes 589832 | tf_op jit(solution)/shard_map/ppermute | solution.py:20
  103.6 0.6 copy-start.4
  105.5 22.7 %copy-start.5 = (bf16[32,1536]{1,0:T(8,128)(2,1)S(1)}, bf16[32,1536]{1,0:T(8,128)(2,1)}, u32[]{:S(2)}) copy-start(bf16[32,1536]{1,0:T(8,128)(2,1)} %copy-done.4) | copy-start | bytes 294916
  108.0 4.7 %collective-permute-start.3 = (bf16[32,1536]{1,0:T(8,128)(2,1)S(1)}, bf16[32,1536]{1,0:T(8,128)(2,1)S(1)}, u32[]{:S(2)}, u32[]{:S(2)}) collective-permute-start(bf16[32,1536]{1,0:T(8,128)(2,1)S(1)} %convolution_convert_fusion), channel_id=1, source_target_pairs={{0,1},{1,0},{2,3},{3,2},{4,5},{5,4},{6,7},{7,6},{8,9},{9,8},{10,11... | collective-permute-start | bytes 294920 | tf_op jit(solution)/shard_map/ppermute | solution.py:20
  112.7 5.9 %collective-permute-start.4 = (bf16[32,1536]{1,0:T(8,128)(2,1)S(1)}, bf16[32,1536]{1,0:T(8,128)(2,1)S(1)}, u32[]{:S(2)}, u32[]{:S(2)}) collective-permute-start(bf16[32,1536]{1,0:T(8,128)(2,1)S(1)} %add.197), channel_id=1, source_target_pairs={{0,2},{1,3},{2,0},{3,1},{4,6},{5,7},{6,4},{7,5},{8,10},{9,11},{10,... | collective-permute-start | bytes 294920 | tf_op jit(solution)/shard_map/ppermute | solution.py:20
  118.7 9.5 %collective-permute-start.5 = (bf16[32,1536]{1,0:T(8,128)(2,1)S(1)}, bf16[32,1536]{1,0:T(8,128)(2,1)S(1)}, u32[]{:S(2)}, u32[]{:S(2)}) collective-permute-start(bf16[32,1536]{1,0:T(8,128)(2,1)S(1)} %add.198), channel_id=1, source_target_pairs={{0,4},{1,5},{2,6},{3,7},{4,0},{5,1},{6,2},{7,3},{8,12},{9,13},{10,... | collective-permute-start | bytes 294920 | tf_op jit(solution)/shard_map/ppermute | solution.py:20

commit v2 on v1

--- a/solution.py
+++ b/solution.py
@@ -20,6 +20,20 @@
         values = values + lax.ppermute(values, axis, [(i, i ^ step) for i in range(size)])
         step *= 2
     return values
+
+
+def tree_gather(values, axis, size):
+    index = lax.axis_index(axis)
+    parts = values[None]
+    step = 1
+    while step < size:
+        other = lax.ppermute(parts, axis, [(i, i ^ step) for i in range(size)])
+        upper = (index // step) % 2 == 1
+        parts = jnp.concatenate(
+            [jnp.where(upper, other, parts), jnp.where(upper, parts, other)], axis=0
+        )
+        step *= 2
+    return parts
 
 
 def make_body(req_size, tp_size):
@@ -47,6 +61,7 @@
         requests = req_dev * req_size
         qwidth = steps * heads_dev * head_dim
         token_rows = tokens.reshape(req_dev * steps, width)
+        full_out_weight = lax.all_gather(out_weight, "tp", axis=0, tiled=True)
         normed = rms_norm(token_rows.astype(jnp.float32), norm_gain).astype(jnp.bfloat16)
         queries = (
             jnp.dot(normed, query_weight, preferred_element_type=jnp.float32) * head_dim ** (-0.5)
@@ -63,7 +78,9 @@
             ],
             axis=1,
         )
-        gathered = lax.all_gather(packed, "req", axis=0, tiled=True)
+        gathered = lax.all_to_all(
+            jnp.broadcast_to(packed[None], (req_size,) + packed.shape), "req", 0, 0, tiled=False
+        ).reshape(requests, packed.shape[1])
         all_queries = gathered[:, :qwidth].astype(jnp.bfloat16).reshape(
             requests, steps * heads_dev, head_dim
         )
@@ -156,8 +173,9 @@
             .astype(jnp.bfloat16)
             .reshape(req_dev * steps, heads_dev * head_dim)
         )
-        projected = jnp.dot(attended, out_weight, preferred_element_type=jnp.float32)
-        attn_total = tree_sum(projected, "tp", tp_size)
+        all_heads = tree_gather(attended, "tp", tp_size)
+        all_heads = jnp.moveaxis(all_heads, 0, 1).reshape(req_dev * steps, -1)
+        attn_total = jnp.dot(all_heads, full_out_weight, preferred_element_type=jnp.float32)
         residual = (token_rows.astype(jnp.float32) + attn_total).astype(jnp.bfloat16)
         mlp_in = rms_norm(residual.astype(jnp.float32), mlp_gain).astype(jnp.bfloat16)
         gate = jnp.dot(mlp_in, gate_weight, preferred_element_type=jnp.float32)

time: 129 us -> 123 us (0.953)
  blocking collectives: 24.8 us -> 0 us
  between operations: 0.35 us -> 13.7 us
  starting transfers between devices: 26.1 us -> 35.6 us
  waiting for transfers between devices: 42.6 us -> 39.3 us
  local copies, waits for them, and re-layouts: 8.5 us -> 6.99 us
    all_gather x1 -> x0, blocking collectives: 24.8 us -> none  [body(): gathered = lax.all_gather(packed, 'req', axis=0, tiled=True)]
    ppermute x6 -> x3, waiting for transfers between devices: 33.5 us -> 11 us  [tree_sum(): lax.ppermute(values, axis, [(i, i ^ step) for i in range(size)])]
    ppermute x0 -> x3, starting transfers between devices: none -> 12.1 us  [tree_gather(): other = lax.ppermute(parts, axis, [(i, i ^ step) for i in range(size)])]
    all_to_all x0 -> x1, waiting for transfers between devices: none -> 10.6 us  [body(): lax.all_to_all(jnp.broadcast_to(packed[None], (req_size,) + packed.shape)...]
    ppermute x6 -> x3, starting transfers between devices: 20.3 us -> 10.6 us  [tree_sum(): lax.ppermute(values, axis, [(i, i ^ step) for i in range(size)])]
    all_to_all x0 -> x1, starting transfers between devices: none -> 7.62 us  [body(): lax.all_to_all(jnp.broadcast_to(packed[None], (req_size,) + packed.shape)...]
    ppermute x0 -> x3, waiting for transfers between devices: none -> 5.55 us  [tree_gather(): other = lax.ppermute(parts, axis, [(i, i ^ step) for i in range(size)])]
    all_to_all x1, waiting for transfers between devices: 9.05 us -> 11.4 us  [body(): lax.all_to_all(send, 'req', 0, 0, tiled=True).reshape(req_size, req_dev, -1)]
  transfers between devices with their start and end apart: 7 -> 9, of which waited for: 7 -> 8; matrix products, arithmetic and copies ran while one was open for 2% -> 15% of each run, Pallas kernels for 0% -> 0%
where the time goes in v2:
time: 123 us; the launch traced here: 122 us
  waiting for transfers between devices  39.3 us (32%)
  starting transfers between devices  35.6 us (29%)
  matrix products  14.6 us (12%)
  between operations  13.7 us (11%)
  other arithmetic  11.9 us (10%)
  local copies, waits for them, and re-layouts  6.99 us (6%)
    ppermute x3, starting transfers between devices, tree_gather(): other = lax.ppermute(parts, axis, [(i, i ^ step) for i in range(size)])  12.1 us
    all_to_all x1, waiting for transfers between devices, body(): lax.all_to_all(send, 'req', 0, 0, tiled=True).reshape(req_size, req_dev, -1)  11.4 us
    ppermute x3, waiting for transfers between devices, tree_sum(): lax.ppermute(values, axis, [(i, i ^ step) for i in range(size)])  11 us
    ppermute x3, starting transfers between devices, tree_sum(): lax.ppermute(values, axis, [(i, i ^ step) for i in range(size)])  10.6 us
    all_to_all x1, waiting for transfers between devices, body(): lax.all_to_all(jnp.broadcast_to(packed[None], (req_size,) + packed.shape)...  10.6 us
    all_to_all x1, starting transfers between devices, body(): lax.all_to_all(jnp.broadcast_to(packed[None], (req_size,) + packed.shape)...  7.62 us
    ppermute x3, waiting for transfers between devices, tree_gather(): other = lax.ppermute(parts, axis, [(i, i ^ step) for i in range(size)])  5.55 us
    all_to_all x1, starting transfers between devices, body(): lax.all_to_all(send, 'req', 0, 0, tiled=True).reshape(req_size, req_dev, -1)  5.22 us
  transfers between devices with their start and end apart: 9, of which 8 were waited for; matrix products, arithmetic and copies ran while one was open for 15% of the time, Pallas kernels for 0%

profile of v2, /device:TPU:2, one launch (start us, length us, event | category | flops | bytes accessed | tf_op | source)
XLA Modules:
  0.0 122.1 jit_solution(5123481206820797892)
XLA Ops:
  6.5 1.1 reshape.418
  7.6 1.0 multiply_reduce_fusion.1
  8.7 0.8 multiply_convert_fusion.1
  9.5 1.2 fusion.18
  11.5 0.7 convert_element_type.88
  12.2 0.9 broadcast_in_dim.66
  13.1 7.6 %all-to-all-start = ((f32[32,8,522]{2,1,0:T(8,128)}), f32[32,8,522]{2,1,0:T(8,128)S(1)}, u32[]{:S(2)}, u32[]{:S(2)}) async-start(f32[32,8,522]{2,1,0:T(8,128)} %broadcast_in_dim.66), calls=%async_computation | async-start | bytes 1310720 | tf_op jit(solution)/shard_map/all_to_all | solution.py:81
  21.9 10.6 %all-to-all-done = f32[32,8,522]{2,1,0:T(8,128)S(1)} async-done(((f32[32,8,522]{2,1,0:T(8,128)}), f32[32,8,522]{2,1,0:T(8,128)S(1)}, u32[]{:S(2)}, u32[]{:S(2)}) %all-to-all-start) | async-done | bytes 534560 | tf_op jit(solution)/shard_map/all_to_all | solution.py:81
  33.3 1.3 %gather_fusion = s32[72]{0:T(128)S(1)} fusion(s32[256]{0:T(256)S(1)} %fusion.20, s32[1024]{0:T(1024)S(1)} %pad_clamp_fusion), kind=kCustom, calls=%fused_computation | custom fusion | bytes 864 | tf_op jit(solution)/shard_map/gather | solution.py:98
  35.5 3.1 %fusion.52 = (f32[72,4]{1,0:T(8,128)S(1)}, f32[72,4,128]{2,1,0:T(4,128)S(1)}) fusion(bf16[72,4,128]{2,1,0:T(4,128)(2,1)S(1)} %gather_fusion.1, bf16[72,2,128,128]{3,2,1,0:T(8,128)(2,1)} %param.16, s32[72,4]{1,0:T(8,128)S(1)} %add_add_fusion, s32[72,128]{1,0:T(8,128)S(1)} %iota_add_fusion, pred[72,128]{1,0:T(8,128)(4,1)S(1)} %broadcast_compare_fusion), kind=kOutput, calls=%fused_computation.109 | convolution fusion | flops 9584352 | bytes 2628864 | tf_op jit(solution)/shard_map/pqd,pkd->pqk/dot_general | solution.py:109
  39.7 2.5 %fusion.11 = f32[72,4,128]{2,1,0:T(4,128)S(1)} fusion(bf16[72,2,128,128]{3,2,1,0:T(8,128)(2,1)} %param.16, f32[72,4]{1,0:T(8,128)S(1)} %subtract_exponential_fusion, f32[72,4,128]{2,1,0:T(4,128)S(1)} %get-tuple-element.25, f32[72,4]{1,0:T(8,128)S(1)} %get-tuple-element.24, s32[72,4]{1,0:T(8,128)S(1)} %add_add_fusion, s32[72,128]{1,0:T(8,128)S(1)} %iota_add_fusion, ...), kind=kOutput, calls=%fused_computation.16 | convolution fusion | flops 9658368 | bytes 2703744 | tf_op jit(solution)/shard_map/pqk,pkd->pqd/dot_general | solution.py:116
  42.2 3.4 %scatter_fusion = f32[256,4,128]{2,1,0:T(4,128)S(1)} fusion(f32[256,4,128]{2,1,0:T(4,128)S(1)} %broadcast.342, s32[72]{0:T(128)S(1)} %get-tuple-element.9, f32[72,4,128]{2,1,0:T(4,128)S(1)} %fusion.11), kind=kCustom, calls=%fused_computation.3 | custom fusion | flops 36864 | bytes 442656 | tf_op jit(solution)/shard_map/scatter-add | solution.py:128
  45.9 1.3 %fusion.44 = f32[72,4]{1,0:T(8,128)S(1)} fusion(f32[72,4,128]{2,1,0:T(4,128)} %copy-done.3, f32[72,4]{1,0:T(8,128)S(1)} %get-tuple-element.24, s32[72,4]{1,0:T(8,128)S(1)} %add_add_fusion, s32[72,128]{1,0:T(8,128)S(1)} %iota_add_fusion, pred[72,128]{1,0:T(8,128)(4,1)S(1)} %broadcast_compare_fusion), kind=kLoop, calls=%fused_computation.100 | loop fusion | flops 184032 | bytes 196992 | tf_op jit(solution)/shard_map/reduce_sum | solution.py:115
  47.2 1.0 scatter_custom_fusion.1
  48.2 0.9 pad_maximum_fusion
  49.1 5.2 %all-to-all-start.1 = ((f32[32,8,520]{2,1,0:T(8,128)}), f32[32,8,520]{2,1,0:T(8,128)S(1)}, u32[]{:S(2)}, u32[]{:S(2)}) async-start(f32[32,8,520]{2,1,0:T(8,128)} %pad_maximum_fusion), calls=%async_computation.1 | async-start | bytes 1310720 | tf_op jit(solution)/shard_map/all_to_all | solution.py:141
  54.9 11.4 %all-to-all-done.1 = f32[32,8,520]{2,1,0:T(8,128)S(1)} async-done(((f32[32,8,520]{2,1,0:T(8,128)}), f32[32,8,520]{2,1,0:T(8,128)S(1)}, u32[]{:S(2)}, u32[]{:S(2)}) %all-to-all-start.1) | async-done | bytes 532512 | tf_op jit(solution)/shard_map/all_to_all | solution.py:141
  67.6 2.0 %collective-permute-start = (bf16[1,32,128]{2,0,1:T(2,128)(2,1)S(1)}, bf16[1,32,128]{2,0,1:T(2,128)(2,1)S(1)}, u32[]{:S(2)}, u32[]{:S(2)}) collective-permute-start(bf16[1,32,128]{2,0,1:T(2,128)(2,1)S(1)} %copy.153), channel_id=1, source_target_pairs={{0,1},{1,0},{2,3},{3,2},{4,5},{5,4},{6,7},{7,6},{8,9},{9,8},{10,11... | collective-permute-start | bytes 24584 | tf_op jit(solution)/shard_map/ppermute | solution.py:30
  69.5 1.8 %collective-permute-done = bf16[1,32,128]{2,0,1:T(2,128)(2,1)S(1)} collective-permute-done((bf16[1,32,128]{2,0,1:T(2,128)(2,1)S(1)}, bf16[1,32,128]{2,0,1:T(2,128)(2,1)S(1)}, u32[]{:S(2)}, u32[]{:S(2)}) %collective-permute-start) | collective-permute-done | bytes 8224 | tf_op jit(solution)/shard_map/ppermute | solution.py:30
  71.5 3.3 %collective-permute-start.1 = (bf16[2,32,128]{2,0,1:T(2,128)(2,1)S(1)}, bf16[2,32,128]{2,0,1:T(2,128)(2,1)S(1)}, u32[]{:S(2)}, u32[]{:S(2)}) collective-permute-start(bf16[2,32,128]{2,0,1:T(2,128)(2,1)S(1)} %pad_maximum_fusion.4), channel_id=1, source_target_pairs={{0,2},{1,3},{2,0},{3,1},{4,6},{5,7},{6,4},{7,5},{8,10},{9,11},{10,... | collective-permute-start | bytes 49160 | tf_op jit(solution)/shard_map/ppermute | solution.py:30
  74.7 1.8 %collective-permute-done.1 = bf16[2,32,128]{2,0,1:T(2,128)(2,1)S(1)} collective-permute-done((bf16[2,32,128]{2,0,1:T(2,128)(2,1)S(1)}, bf16[2,32,128]{2,0,1:T(2,128)(2,1)S(1)}, u32[]{:S(2)}, u32[]{:S(2)}) %collective-permute-start.1) | collective-permute-done | bytes 16416 | tf_op jit(solution)/shard_map/ppermute | solution.py:30
  76.7 6.8 %collective-permute-start.2 = (bf16[4,32,128]{2,0,1:T(4,128)(2,1)S(1)}, bf16[4,32,128]{2,0,1:T(4,128)(2,1)S(1)}, u32[]{:S(2)}, u32[]{:S(2)}) collective-permute-start(bf16[4,32,128]{2,0,1:T(4,128)(2,1)S(1)} %pad_maximum_fusion.2), channel_id=1, source_target_pairs={{0,4},{1,5},{2,6},{3,7},{4,0},{5,1},{6,2},{7,3},{8,12},{9,13},{10,... | collective-permute-start | bytes 98312 | tf_op jit(solution)/shard_map/ppermute | solution.py:30
  83.5 1.9 %collective-permute-done.2 = bf16[4,32,128]{2,0,1:T(4,128)(2,1)S(1)} collective-permute-done((bf16[4,32,128]{2,0,1:T(4,128)(2,1)S(1)}, bf16[4,32,128]{2,0,1:T(4,128)(2,1)S(1)}, u32[]{:S(2)}, u32[]{:S(2)}) %collective-permute-start.2) | collective-permute-done | bytes 32800 | tf_op jit(solution)/shard_map/ppermute | solution.py:30
  85.5 2.6 %multiply_reduce_fusion = (f32[32]{0:T(128)S(1)}, f32[32,1536]{1,0:T(8,128)S(1)}) fusion(f32[32,1536]{1,0:T(8,128)S(1)} %reshape.418, bf16[1024,1536]{1,0:T(8,128)(2,1)} %all-gather.2.cloned.1.call-done, bf16[4,8,8,128]{3,2,1,0:T(8,128)(2,1)S(1)} %bitcast.70), kind=kOutput, calls=%fused_computation.35 | convolution fusion | flops 100909024 | bytes 3604608 | tf_op jit(solution)/shard_map/dot_general | solution.py:178
  88.2 2.1 %fusion.51 = f32[32,576]{1,0:T(8,128)S(1)} fusion(bf16[1536,576]{0,1:T(8,128)(2,1)} %param.23, f32[32,1536]{1,0:T(8,128)S(1)} %get-tuple-element.27, f32[1536]{0:T(1024)S(1)} %copy-done.4, f32[32]{0:T(128)S(1)} %add_rsqrt_fusion.1), kind=kOutput, calls=%fused_computation.108 | convolution fusion | flops 56770560 | bytes 2046080 | tf_op jit(solution)/shard_map/dot_general | solution.py:181
  90.3 2.5 %convolution_convert_fusion = bf16[32,1536]{1,0:T(8,128)(2,1)S(1)} fusion(bf16[576,1536]{1,0:T(8,128)(2,1)S(1)} %copy-done, bf16[1536,576]{0,1:T(8,128)(2,1)} %param.24, f32[32,576]{1,0:T(8,128)S(1)} %fusion.51, f32[32,1536]{1,0:T(8,128)S(1)} %get-tuple-element.27, f32[1536]{0:T(1024)S(1)} %copy-done.4, f32[32]{0:T(128)S(1)} %add_rsqrt_fusion.1), kind=kOutput, calls=%fused_computation.14 | convolution fusion | flops 113627136 | bytes 3913856 | tf_op jit(solution)/shard_map/dot_general | solution.py:184
  92.8 1.0 collective-permute-start.3
  93.9 4.2 %collective-permute-done.3 = bf16[32,1536]{1,0:T(8,128)(2,1)S(1)} collective-permute-done((bf16[32,1536]{1,0:T(8,128)(2,1)S(1)}, bf16[32,1536]{1,0:T(8,128)(2,1)S(1)}, u32[]{:S(2)}, u32[]{:S(2)}) %collective-permute-start.3) | collective-permute-done | bytes 98336 | tf_op jit(solution)/shard_map/ppermute | solution.py:20
  98.0 2.4 %collective-permute-start.4 = (bf16[32,1536]{1,0:T(8,128)(2,1)S(1)}, bf16[32,1536]{1,0:T(8,128)(2,1)S(1)}, u32[]{:S(2)}, u32[]{:S(2)}) collective-permute-start(bf16[32,1536]{1,0:T(8,128)(2,1)S(1)} %add.201), channel_id=1, source_target_pairs={{0,2},{1,3},{2,0},{3,1},{4,6},{5,7},{6,4},{7,5},{8,10},{9,11},{10,... | collective-permute-start | bytes 294920 | tf_op jit(solution)/shard_map/ppermute | solution.py:20
  100.4 4.3 %collective-permute-done.4 = bf16[32,1536]{1,0:T(8,128)(2,1)S(1)} collective-permute-done((bf16[32,1536]{1,0:T(8,128)(2,1)S(1)}, bf16[32,1536]{1,0:T(8,128)(2,1)S(1)}, u32[]{:S(2)}, u32[]{:S(2)}) %collective-permute-start.4) | collective-permute-done | bytes 98336 | tf_op jit(solution)/shard_map/ppermute | solution.py:20
  104.7 7.2 %collective-permute-start.5 = (bf16[32,1536]{1,0:T(8,128)(2,1)S(1)}, bf16[32,1536]{1,0:T(8,128)(2,1)S(1)}, u32[]{:S(2)}, u32[]{:S(2)}) collective-permute-start(bf16[32,1536]{1,0:T(8,128)(2,1)S(1)} %add.202), channel_id=1, source_target_pairs={{0,4},{1,5},{2,6},{3,7},{4,0},{5,1},{6,2},{7,3},{8,12},{9,13},{10,... | collective-permute-start | bytes 294920 | tf_op jit(solution)/shard_map/ppermute | solution.py:20
  112.0 2.6 %collective-permute-done.5 = bf16[32,1536]{1,0:T(8,128)(2,1)S(1)} collective-permute-done((bf16[32,1536]{1,0:T(8,128)(2,1)S(1)}, bf16[32,1536]{1,0:T(8,128)(2,1)S(1)}, u32[]{:S(2)}, u32[]{:S(2)}) %collective-permute-start.5) | collective-permute-done | bytes 98336 | tf_op jit(solution)/shard_map/ppermute | solution.py:20
  (75 shorter events, 7.9 us)
Async XLA Ops:
  6.5 83.8 %copy-start = (bf16[576,1536]{1,0:T(8,128)(2,1)S(1)}, bf16[576,1536]{1,0:T(8,128)(2,1)}, u32[]{:S(2)}) copy-start(bf16[576,1536]{1,0:T(8,128)(2,1)} %param.25) | copy-start | bytes 5308420
  6.5 14.9 %copy-start.1 = (bf16[1536,128]{1,0:T(8,128)(2,1)S(1)}, bf16[1536,128]{1,0:T(8,128)(2,1)}, u32[]{:S(2)}) copy-start(bf16[1536,128]{1,0:T(8,128)(2,1)} %param.19) | copy-start | bytes 1179652
  13.1 19.4 %all-to-all-start = ((f32[32,8,522]{2,1,0:T(8,128)}), f32[32,8,522]{2,1,0:T(8,128)S(1)}, u32[]{:S(2)}, u32[]{:S(2)}) async-start(f32[32,8,522]{2,1,0:T(8,128)} %broadcast_in_dim.66), calls=%async_computation | async-start | bytes 1310720 | tf_op jit(solution)/shard_map/all_to_all | solution.py:81
  20.7 64.8 %all-gather.2.cloned.1.call-start = ((), (), s32[]{:S(2)}) async-start(), calls=%async_computation.2 | async-start | bytes 3538944 | tf_op jit(solution)/shard_map/all_gather | solution.py:64
  38.6 3.6 %copy-start.3 = (f32[72,4,128]{2,1,0:T(4,128)}, f32[72,4,128]{2,1,0:T(4,128)S(1)}, u32[]{:S(2)}) copy-start(f32[72,4,128]{2,1,0:T(4,128)S(1)} %get-tuple-element.25) | copy-start | bytes 442372
  45.9 8.8 %copy-start.2 = (bf16[1536,128]{1,0:T(8,128)(2,1)S(1)}, bf16[1536,128]{1,0:T(8,128)(2,1)}, u32[]{:S(2)}) copy-start(bf16[1536,128]{1,0:T(8,128)(2,1)} %param.20) | copy-start | bytes 1179652
  49.1 17.1 %all-to-all-start.1 = ((f32[32,8,520]{2,1,0:T(8,128)}), f32[32,8,520]{2,1,0:T(8,128)S(1)}, u32[]{:S(2)}, u32[]{:S(2)}) async-start(f32[32,8,520]{2,1,0:T(8,128)} %pad_maximum_fusion), calls=%async_computation.1 | async-start | bytes 1310720 | tf_op jit(solution)/shard_map/all_to_all | solution.py:141
  67.4 20.8 %copy-start.4 = (f32[1536]{0:T(1024)S(1)}, f32[1536]{0:T(1024)}, u32[]{:S(2)}) copy-start(f32[1536]{0:T(1024)} %param.22) | copy-start | bytes 18436
  67.6 3.8 %collective-permute-start = (bf16[1,32,128]{2,0,1:T(2,128)(2,1)S(1)}, bf16[1,32,128]{2,0,1:T(2,128)(2,1)S(1)}, u32[]{:S(2)}, u32[]{:S(2)}) collective-permute-start(bf16[1,32,128]{2,0,1:T(2,128)(2,1)S(1)} %copy.153), channel_id=1, source_target_pairs={{0,1},{1,0},{2,3},{3,2},{4,5},{5,4},{6,7},{7,6},{8,9},{9,8},{10,11... | collective-permute-start | bytes 24584 | tf_op jit(solution)/shard_map/ppermute | solution.py:30
  71.5 5.1 %collective-permute-start.1 = (bf16[2,32,128]{2,0,1:T(2,128)(2,1)S(1)}, bf16[2,32,128]{2,0,1:T(2,128)(2,1)S(1)}, u32[]{:S(2)}, u32[]{:S(2)}) collective-permute-start(bf16[2,32,128]{2,0,1:T(2,128)(2,1)S(1)} %pad_maximum_fusion.4), channel_id=1, source_target_pairs={{0,2},{1,3},{2,0},{3,1},{4,6},{5,7},{6,4},{7,5},{8,10},{9,11},{10,... | collective-permute-start | bytes 49160 | tf_op jit(solution)/shard_map/ppermute | solution.py:30
  76.7 8.7 %collective-permute-start.2 = (bf16[4,32,128]{2,0,1:T(4,128)(2,1)S(1)}, bf16[4,32,128]{2,0,1:T(4,128)(2,1)S(1)}, u32[]{:S(2)}, u32[]{:S(2)}) collective-permute-start(bf16[4,32,128]{2,0,1:T(4,128)(2,1)S(1)} %pad_maximum_fusion.2), channel_id=1, source_target_pairs={{0,4},{1,5},{2,6},{3,7},{4,0},{5,1},{6,2},{7,3},{8,12},{9,13},{10,... | collective-permute-start | bytes 98312 | tf_op jit(solution)/shard_map/ppermute | solution.py:30
  92.8 5.2 %collective-permute-start.3 = (bf16[32,1536]{1,0:T(8,128)(2,1)S(1)}, bf16[32,1536]{1,0:T(8,128)(2,1)S(1)}, u32[]{:S(2)}, u32[]{:S(2)}) collective-permute-start(bf16[32,1536]{1,0:T(8,128)(2,1)S(1)} %convolution_convert_fusion), channel_id=1, source_target_pairs={{0,1},{1,0},{2,3},{3,2},{4,5},{5,4},{6,7},{7,6},{8,9},{9,8},{10,11... | collective-permute-start | bytes 294920 | tf_op jit(solution)/shard_map/ppermute | solution.py:20
  98.0 6.7 %collective-permute-start.4 = (bf16[32,1536]{1,0:T(8,128)(2,1)S(1)}, bf16[32,1536]{1,0:T(8,128)(2,1)S(1)}, u32[]{:S(2)}, u32[]{:S(2)}) collective-permute-start(bf16[32,1536]{1,0:T(8,128)(2,1)S(1)} %add.201), channel_id=1, source_target_pairs={{0,2},{1,3},{2,0},{3,1},{4,6},{5,7},{6,4},{7,5},{8,10},{9,11},{10,... | collective-permute-start | bytes 294920 | tf_op jit(solution)/shard_map/ppermute | solution.py:20
  104.7 9.8 %collective-permute-start.5 = (bf16[32,1536]{1,0:T(8,128)(2,1)S(1)}, bf16[32,1536]{1,0:T(8,128)(2,1)S(1)}, u32[]{:S(2)}, u32[]{:S(2)}) collective-permute-start(bf16[32,1536]{1,0:T(8,128)(2,1)S(1)} %add.202), channel_id=1, source_target_pairs={{0,4},{1,5},{2,6},{3,7},{4,0},{5,1},{6,2},{7,3},{8,12},{9,13},{10,... | collective-permute-start | bytes 294920 | tf_op jit(solution)/shard_map/ppermute | solution.py:20
Sparse Core Ops, SparseCore 0:
  23.3 47.7 all-gather.1

commit v3 on v2

--- a/solution.py
+++ b/solution.py
@@ -70,22 +70,24 @@
         value_new = jnp.dot(normed, value_weight, preferred_element_type=jnp.float32).astype(
             jnp.bfloat16
         )
+        ints = jnp.concatenate([page_table, lengths.reshape(req_dev, 1)], axis=1)
         packed = jnp.concatenate(
             [
-                queries.reshape(req_dev, qwidth).astype(jnp.float32),
-                page_table.astype(jnp.float32),
-                lengths.reshape(req_dev, 1).astype(jnp.float32),
+                queries.reshape(req_dev, qwidth),
+                (ints // 256).astype(jnp.bfloat16),
+                (ints % 256).astype(jnp.bfloat16),
             ],
             axis=1,
         )
         gathered = lax.all_to_all(
             jnp.broadcast_to(packed[None], (req_size,) + packed.shape), "req", 0, 0, tiled=False
         ).reshape(requests, packed.shape[1])
-        all_queries = gathered[:, :qwidth].astype(jnp.bfloat16).reshape(
-            requests, steps * heads_dev, head_dim
-        )
-        all_table = gathered[:, qwidth : qwidth + window_pages].astype(jnp.int32)
-        all_lengths = gathered[:, qwidth + window_pages].astype(jnp.int32)
+        all_queries = gathered[:, :qwidth].reshape(requests, steps * heads_dev, head_dim)
+        nints = window_pages + 1
+        digits = gathered[:, qwidth:].astype(jnp.int32)
+        all_ints = digits[:, :nints] * 256 + digits[:, nints:]
+        all_table = all_ints[:, :window_pages]
+        all_lengths = all_ints[:, window_pages]
         flat_table = all_table.reshape(-1)
         entries = flat_table.shape[0]
         my_slots = lax.axis_index("req") * pool_size + jnp.arange(pool_size, dtype=jnp.int32)
@@ -125,19 +127,21 @@
             jnp.where(member[:, :, None, None], block_max[None], negative), axis=1
         )
         scale = jnp.exp(block_max - local_max[page_request])
-        sent_out = jax.ops.segment_sum(
-            block_out * scale[..., None], page_request, num_segments=requests
-        )
-        sent_total = jax.ops.segment_sum(block_total * scale, page_request, num_segments=requests)
         nsh = steps * heads_dev
-        send = jnp.concatenate(
+        scaled = jnp.concatenate(
             [
-                sent_out.reshape(requests, nsh * head_dim),
-                sent_total.reshape(requests, nsh),
-                local_max.reshape(requests, nsh),
+                (block_out * scale[..., None]).reshape(pool_size, nsh * head_dim),
+                (block_total * scale).reshape(pool_size, nsh),
             ],
             axis=1,
         )
+        sent = jnp.dot(
+            member.astype(jnp.float32),
+            scaled,
+            precision=lax.Precision.HIGHEST,
+            preferred_element_type=jnp.float32,
+        )
+        send = jnp.concatenate([sent, local_max.reshape(requests, nsh)], axis=1)
         recv = lax.all_to_all(send, "req", 0, 0, tiled=True).reshape(req_size, req_dev, -1)
         got_out = recv[:, :, : nsh * head_dim].reshape(req_size, req_dev, steps, heads_dev, head_dim)
         got_total = recv[:, :, nsh * head_dim : nsh * (head_dim + 1)].reshape(

time: 123 us -> 115 us (0.935); the launches traced: 122 us -> 113 us
  other arithmetic: 11.9 us -> 5.81 us
  waiting for transfers between devices: 39.3 us -> 34 us
    scatter-add x2 -> x0, other arithmetic: 4.43 us -> none  [the longest x1 3.45 us: body(): jax.ops.segment_sum(block_out * scale[..., None], page_request, num_segme...]
    all_to_all x1, waiting for transfers between devices: 10.6 us -> 7.09 us  [body(): lax.all_to_all(jnp.broadcast_to(packed[None], (req_size,) + packed.shape)...]
    ppermute x3, waiting for transfers between devices: 11 us -> 9.22 us  [tree_sum(): lax.ppermute(values, axis, [(i, i ^ step) for i in range(size)])]
    ppermute x3, starting transfers between devices: 10.6 us -> 11.9 us  [tree_sum(): lax.ppermute(values, axis, [(i, i ^ step) for i in range(size)])]
  transfers between devices with their start and end apart: 9 -> 9, of which waited for: 8 -> 8; matrix products, arithmetic and copies ran while one was open for 15% -> 12% of each run, Pallas kernels for 0% -> 0%
where the time goes in v3:
time: 115 us; the launch traced here: 113 us
  starting transfers between devices  36.8 us (32%)
  waiting for transfers between devices  34 us (30%)
  matrix products  15.3 us (13%)
  between operations  13.7 us (12%)
  local copies, waits for them, and re-layouts  7.23 us (6%)
  other arithmetic  5.81 us (5%)
    ppermute x3, starting transfers between devices, tree_gather(): other = lax.ppermute(parts, axis, [(i, i ^ step) for i in range(size)])  12.4 us
    ppermute x3, starting transfers between devices, tree_sum(): lax.ppermute(values, axis, [(i, i ^ step) for i in range(size)])  11.9 us
    all_to_all x1, waiting for transfers between devices, body(): lax.all_to_all(send, 'req', 0, 0, tiled=True).reshape(req_size, req_dev, -1)  11.2 us
    ppermute x3, waiting for transfers between devices, tree_sum(): lax.ppermute(values, axis, [(i, i ^ step) for i in range(size)])  9.22 us
    all_to_all x1, starting transfers between devices, body(): lax.all_to_all(jnp.broadcast_to(packed[None], (req_size,) + packed.shape)...  7.62 us
    all_to_all x1, waiting for transfers between devices, body(): lax.all_to_all(jnp.broadcast_to(packed[None], (req_size,) + packed.shape)...  7.09 us
    ppermute x3, waiting for transfers between devices, tree_gather(): other = lax.ppermute(parts, axis, [(i, i ^ step) for i in range(size)])  5.82 us
    all_to_all x1, starting transfers between devices, body(): lax.all_to_all(send, 'req', 0, 0, tiled=True).reshape(req_size, req_dev, -1)  4.88 us
  transfers between devices with their start and end apart: 9, of which 8 were waited for; matrix products, arithmetic and copies ran while one was open for 12% of the time, Pallas kernels for 0%

profile of v3, /device:TPU:2, one launch (start us, length us, event | category | flops | bytes accessed | tf_op | source)
XLA Modules:
  0.0 112.9 jit_solution(12169526944096546375)
XLA Ops:
  6.5 1.1 reshape.404
  7.6 1.0 multiply_reduce_fusion.1
  8.7 0.8 multiply_convert_fusion.1
  9.5 1.2 %fusion.18 = bf16[32,128]{1,0:T(8,128)(2,1)S(1)} fusion(bf16[32,1536]{1,0:T(8,128)(2,1)S(1)} %multiply_convert_fusion.1, bf16[1536,128]{1,0:T(8,128)(2,1)} %param.18), kind=kOutput, calls=%fused_computation.23 | convolution fusion | flops 12591104 | bytes 499712 | tf_op jit(solution)/shard_map/dot_general | solution.py:67
  10.7 0.7 copy.94
  11.5 0.8 fusion.41
  12.3 0.8 broadcast_in_dim.61
  13.1 7.6 %all-to-all-start = ((bf16[32,8,532]{2,1,0:T(8,128)(2,1)}), bf16[32,8,532]{2,1,0:T(8,128)(2,1)S(1)}, u32[]{:S(2)}, u32[]{:S(2)}) async-start(bf16[32,8,532]{2,1,0:T(8,128)(2,1)} %broadcast_in_dim.61), calls=%async_computation | async-start | bytes 655360 | tf_op jit(solution)/shard_map/all_to_all | solution.py:82
  20.7 0.7 all-gather.2.cloned.1.call-update
  21.9 7.1 %all-to-all-done = bf16[32,8,532]{2,1,0:T(8,128)(2,1)S(1)} async-done(((bf16[32,8,532]{2,1,0:T(8,128)(2,1)}), bf16[32,8,532]{2,1,0:T(8,128)(2,1)S(1)}, u32[]{:S(2)}, u32[]{:S(2)}) %all-to-all-start) | async-done | bytes 272416 | tf_op jit(solution)/shard_map/all_to_all | solution.py:82
  29.8 1.3 %gather_fusion = s32[72]{0:T(128)S(1)} fusion(s32[256]{0:T(256)S(1)} %slice_reduce_fusion, s32[1024]{0:T(1024)S(1)} %pad_clamp_fusion), kind=kCustom, calls=%fused_computation | custom fusion | bytes 864 | tf_op jit(solution)/shard_map/gather | solution.py:100
  32.1 3.1 %fusion.57 = (f32[72,4]{1,0:T(8,128)S(1)}, f32[72,4,128]{2,1,0:T(4,128)S(1)}) fusion(bf16[72,4,128]{2,1,0:T(4,128)(2,1)S(1)} %gather_fusion.1, bf16[72,2,128,128]{3,2,1,0:T(8,128)(2,1)} %param.16, s32[72,4]{1,0:T(8,128)S(1)} %add_add_fusion, s32[72,128]{1,0:T(8,128)S(1)} %iota_add_fusion, pred[72,128]{1,0:T(8,128)(4,1)S(1)} %broadcast_compare_fusion), kind=kOutput, calls=%fused_computation.121 | convolution fusion | flops 9584352 | bytes 2628864 | tf_op jit(solution)/shard_map/pqd,pkd->pqk/dot_general | solution.py:111
  36.6 2.6 %fusion.11 = f32[72,4,128]{2,1,0:T(4,128)S(1)} fusion(bf16[72,2,128,128]{3,2,1,0:T(8,128)(2,1)} %param.16, f32[72,4]{1,0:T(8,128)S(1)} %get-tuple-element.10, f32[72,4,128]{2,1,0:T(4,128)S(1)} %get-tuple-element.24, f32[72,4]{1,0:T(8,128)S(1)} %get-tuple-element.23, s32[72,4]{1,0:T(8,128)S(1)} %add_add_fusion, s32[72,128]{1,0:T(8,128)S(1)} %iota_add_fusion, ...), kind=kOutput, calls=%fused_computation.15 | convolution fusion | flops 9658368 | bytes 2703744 | tf_op jit(solution)/shard_map/pqk,pkd->pqd/dot_general | solution.py:118
  39.7 0.9 pad_maximum_fusion
  40.6 4.9 %all-to-all-start.1 = ((f32[32,8,520]{2,1,0:T(8,128)}), f32[32,8,520]{2,1,0:T(8,128)S(1)}, u32[]{:S(2)}, u32[]{:S(2)}) async-start(f32[32,8,520]{2,1,0:T(8,128)} %pad_maximum_fusion), calls=%async_computation.1 | async-start | bytes 1310720 | tf_op jit(solution)/shard_map/all_to_all | solution.py:145
  46.2 11.2 %all-to-all-done.1 = f32[32,8,520]{2,1,0:T(8,128)S(1)} async-done(((f32[32,8,520]{2,1,0:T(8,128)}), f32[32,8,520]{2,1,0:T(8,128)S(1)}, u32[]{:S(2)}, u32[]{:S(2)}) %all-to-all-start.1) | async-done | bytes 532512 | tf_op jit(solution)/shard_map/all_to_all | solution.py:145
  58.3 2.0 %collective-permute-start = (bf16[1,32,128]{2,0,1:T(2,128)(2,1)S(1)}, bf16[1,32,128]{2,0,1:T(2,128)(2,1)S(1)}, u32[]{:S(2)}, u32[]{:S(2)}) collective-permute-start(bf16[1,32,128]{2,0,1:T(2,128)(2,1)S(1)} %copy.107), channel_id=1, source_target_pairs={{0,1},{1,0},{2,3},{3,2},{4,5},{5,4},{6,7},{7,6},{8,9},{9,8},{10,11... | collective-permute-start | bytes 24584 | tf_op jit(solution)/shard_map/ppermute | solution.py:30
  60.3 2.0 %collective-permute-done = bf16[1,32,128]{2,0,1:T(2,128)(2,1)S(1)} collective-permute-done((bf16[1,32,128]{2,0,1:T(2,128)(2,1)S(1)}, bf16[1,32,128]{2,0,1:T(2,128)(2,1)S(1)}, u32[]{:S(2)}, u32[]{:S(2)}) %collective-permute-start) | collective-permute-done | bytes 8224 | tf_op jit(solution)/shard_map/ppermute | solution.py:30
  62.4 3.4 %collective-permute-start.1 = (bf16[2,32,128]{2,0,1:T(2,128)(2,1)S(1)}, bf16[2,32,128]{2,0,1:T(2,128)(2,1)S(1)}, u32[]{:S(2)}, u32[]{:S(2)}) collective-permute-start(bf16[2,32,128]{2,0,1:T(2,128)(2,1)S(1)} %pad_maximum_fusion.3), channel_id=1, source_target_pairs={{0,2},{1,3},{2,0},{3,1},{4,6},{5,7},{6,4},{7,5},{8,10},{9,11},{10,... | collective-permute-start | bytes 49160 | tf_op jit(solution)/shard_map/ppermute | solution.py:30
  65.9 1.8 %collective-permute-done.1 = bf16[2,32,128]{2,0,1:T(2,128)(2,1)S(1)} collective-permute-done((bf16[2,32,128]{2,0,1:T(2,128)(2,1)S(1)}, bf16[2,32,128]{2,0,1:T(2,128)(2,1)S(1)}, u32[]{:S(2)}, u32[]{:S(2)}) %collective-permute-start.1) | collective-permute-done | bytes 16416 | tf_op jit(solution)/shard_map/ppermute | solution.py:30
  67.8 6.9 %collective-permute-start.2 = (bf16[4,32,128]{2,0,1:T(4,128)(2,1)S(1)}, bf16[4,32,128]{2,0,1:T(4,128)(2,1)S(1)}, u32[]{:S(2)}, u32[]{:S(2)}) collective-permute-start(bf16[4,32,128]{2,0,1:T(4,128)(2,1)S(1)} %pad_maximum_fusion.2), channel_id=1, source_target_pairs={{0,4},{1,5},{2,6},{3,7},{4,0},{5,1},{6,2},{7,3},{8,12},{9,13},{10,... | collective-permute-start | bytes 98312 | tf_op jit(solution)/shard_map/ppermute | solution.py:30
  74.7 2.0 %collective-permute-done.2 = bf16[4,32,128]{2,0,1:T(4,128)(2,1)S(1)} collective-permute-done((bf16[4,32,128]{2,0,1:T(4,128)(2,1)S(1)}, bf16[4,32,128]{2,0,1:T(4,128)(2,1)S(1)}, u32[]{:S(2)}, u32[]{:S(2)}) %collective-permute-start.2) | collective-permute-done | bytes 32800 | tf_op jit(solution)/shard_map/ppermute | solution.py:30
  76.9 2.6 %multiply_reduce_fusion = (f32[32]{0:T(128)S(1)}, f32[32,1536]{1,0:T(8,128)S(1)}) fusion(f32[32,1536]{1,0:T(8,128)S(1)} %reshape.404, bf16[1024,1536]{1,0:T(8,128)(2,1)} %all-gather.2.cloned.1.call-done, bf16[4,8,8,128]{3,2,1,0:T(8,128)(2,1)S(1)} %bitcast.71), kind=kOutput, calls=%fused_computation.33 | convolution fusion | flops 100909024 | bytes 3604608 | tf_op jit(solution)/shard_map/dot_general | solution.py:182
  79.5 2.1 %fusion.55 = f32[32,576]{1,0:T(8,128)S(1)} fusion(bf16[1536,576]{0,1:T(8,128)(2,1)} %param.23, f32[32,1536]{1,0:T(8,128)S(1)} %get-tuple-element.26, f32[1536]{0:T(1024)S(1)} %copy-done.3, f32[32]{0:T(128)S(1)} %add_rsqrt_fusion.1), kind=kOutput, calls=%fused_computation.119 | convolution fusion | flops 56770560 | bytes 2046080 | tf_op jit(solution)/shard_map/dot_general | solution.py:185
  81.6 2.5 %convolution_convert_fusion = bf16[32,1536]{1,0:T(8,128)(2,1)S(1)} fusion(bf16[576,1536]{1,0:T(8,128)(2,1)S(1)} %copy-done, bf16[1536,576]{0,1:T(8,128)(2,1)} %param.24, f32[32,576]{1,0:T(8,128)S(1)} %fusion.55, f32[32,1536]{1,0:T(8,128)S(1)} %get-tuple-element.26, f32[1536]{0:T(1024)S(1)} %copy-done.3, f32[32]{0:T(128)S(1)} %add_rsqrt_fusion.1), kind=kOutput, calls=%fused_computation.12 | convolution fusion | flops 113627136 | bytes 3913856 | tf_op jit(solution)/shard_map/dot_general | solution.py:188
  84.2 1.8 %collective-permute-start.3 = (bf16[32,1536]{1,0:T(8,128)(2,1)S(1)}, bf16[32,1536]{1,0:T(8,128)(2,1)S(1)}, u32[]{:S(2)}, u32[]{:S(2)}) collective-permute-start(bf16[32,1536]{1,0:T(8,128)(2,1)S(1)} %convolution_convert_fusion), channel_id=1, source_target_pairs={{0,1},{1,0},{2,3},{3,2},{4,5},{5,4},{6,7},{7,6},{8,9},{9,8},{10,11... | collective-permute-start | bytes 294920 | tf_op jit(solution)/shard_map/ppermute | solution.py:20
  85.9 2.9 %collective-permute-done.3 = bf16[32,1536]{1,0:T(8,128)(2,1)S(1)} collective-permute-done((bf16[32,1536]{1,0:T(8,128)(2,1)S(1)}, bf16[32,1536]{1,0:T(8,128)(2,1)S(1)}, u32[]{:S(2)}, u32[]{:S(2)}) %collective-permute-start.3) | collective-permute-done | bytes 98336 | tf_op jit(solution)/shard_map/ppermute | solution.py:20
  88.8 3.6 %collective-permute-start.4 = (bf16[32,1536]{1,0:T(8,128)(2,1)S(1)}, bf16[32,1536]{1,0:T(8,128)(2,1)S(1)}, u32[]{:S(2)}, u32[]{:S(2)}) collective-permute-start(bf16[32,1536]{1,0:T(8,128)(2,1)S(1)} %add.205), channel_id=1, source_target_pairs={{0,2},{1,3},{2,0},{3,1},{4,6},{5,7},{6,4},{7,5},{8,10},{9,11},{10,... | collective-permute-start | bytes 294920 | tf_op jit(solution)/shard_map/ppermute | solution.py:20
  92.5 3.6 %collective-permute-done.4 = bf16[32,1536]{1,0:T(8,128)(2,1)S(1)} collective-permute-done((bf16[32,1536]{1,0:T(8,128)(2,1)S(1)}, bf16[32,1536]{1,0:T(8,128)(2,1)S(1)}, u32[]{:S(2)}, u32[]{:S(2)}) %collective-permute-start.4) | collective-permute-done | bytes 98336 | tf_op jit(solution)/shard_map/ppermute | solution.py:20
  96.2 6.5 %collective-permute-start.5 = (bf16[32,1536]{1,0:T(8,128)(2,1)S(1)}, bf16[32,1536]{1,0:T(8,128)(2,1)S(1)}, u32[]{:S(2)}, u32[]{:S(2)}) collective-permute-start(bf16[32,1536]{1,0:T(8,128)(2,1)S(1)} %add.206), channel_id=1, source_target_pairs={{0,4},{1,5},{2,6},{3,7},{4,0},{5,1},{6,2},{7,3},{8,12},{9,13},{10,... | collective-permute-start | bytes 294920 | tf_op jit(solution)/shard_map/ppermute | solution.py:20
  102.6 2.7 %collective-permute-done.5 = bf16[32,1536]{1,0:T(8,128)(2,1)S(1)} collective-permute-done((bf16[32,1536]{1,0:T(8,128)(2,1)S(1)}, bf16[32,1536]{1,0:T(8,128)(2,1)S(1)}, u32[]{:S(2)}, u32[]{:S(2)}) %collective-permute-start.5) | collective-permute-done | bytes 98336 | tf_op jit(solution)/shard_map/ppermute | solution.py:20
  105.4 0.7 reshape.403
  (68 shorter events, 6.2 us)
Async XLA Ops:
  6.5 75.1 %copy-start = (bf16[576,1536]{1,0:T(8,128)(2,1)S(1)}, bf16[576,1536]{1,0:T(8,128)(2,1)}, u32[]{:S(2)}) copy-start(bf16[576,1536]{1,0:T(8,128)(2,1)} %param.25) | copy-start | bytes 5308420
  6.5 14.9 %copy-start.1 = (bf16[1536,128]{1,0:T(8,128)(2,1)S(1)}, bf16[1536,128]{1,0:T(8,128)(2,1)}, u32[]{:S(2)}) copy-start(bf16[1536,128]{1,0:T(8,128)(2,1)} %param.19) | copy-start | bytes 1179652
  13.1 15.9 %all-to-all-start = ((bf16[32,8,532]{2,1,0:T(8,128)(2,1)}), bf16[32,8,532]{2,1,0:T(8,128)(2,1)S(1)}, u32[]{:S(2)}, u32[]{:S(2)}) async-start(bf16[32,8,532]{2,1,0:T(8,128)(2,1)} %broadcast_in_dim.61), calls=%async_computation | async-start | bytes 655360 | tf_op jit(solution)/shard_map/all_to_all | solution.py:82
  20.7 56.2 %all-gather.2.cloned.1.call-start = ((), (), s32[]{:S(2)}) async-start(), calls=%async_computation.2 | async-start | bytes 3538944 | tf_op jit(solution)/shard_map/all_gather | solution.py:64
  39.1 6.9 %copy-start.2 = (bf16[1536,128]{1,0:T(8,128)(2,1)S(1)}, bf16[1536,128]{1,0:T(8,128)(2,1)}, u32[]{:S(2)}) copy-start(bf16[1536,128]{1,0:T(8,128)(2,1)} %param.20) | copy-start | bytes 1179652
  40.6 16.8 %all-to-all-start.1 = ((f32[32,8,520]{2,1,0:T(8,128)}), f32[32,8,520]{2,1,0:T(8,128)S(1)}, u32[]{:S(2)}, u32[]{:S(2)}) async-start(f32[32,8,520]{2,1,0:T(8,128)} %pad_maximum_fusion), calls=%async_computation.1 | async-start | bytes 1310720 | tf_op jit(solution)/shard_map/all_to_all | solution.py:145
  58.1 21.4 %copy-start.3 = (f32[1536]{0:T(1024)S(1)}, f32[1536]{0:T(1024)}, u32[]{:S(2)}) copy-start(f32[1536]{0:T(1024)} %param.22) | copy-start | bytes 18436
  58.3 4.0 %collective-permute-start = (bf16[1,32,128]{2,0,1:T(2,128)(2,1)S(1)}, bf16[1,32,128]{2,0,1:T(2,128)(2,1)S(1)}, u32[]{:S(2)}, u32[]{:S(2)}) collective-permute-start(bf16[1,32,128]{2,0,1:T(2,128)(2,1)S(1)} %copy.107), channel_id=1, source_target_pairs={{0,1},{1,0},{2,3},{3,2},{4,5},{5,4},{6,7},{7,6},{8,9},{9,8},{10,11... | collective-permute-start | bytes 24584 | tf_op jit(solution)/shard_map/ppermute | solution.py:30
  62.4 5.3 %collective-permute-start.1 = (bf16[2,32,128]{2,0,1:T(2,128)(2,1)S(1)}, bf16[2,32,128]{2,0,1:T(2,128)(2,1)S(1)}, u32[]{:S(2)}, u32[]{:S(2)}) collective-permute-start(bf16[2,32,128]{2,0,1:T(2,128)(2,1)S(1)} %pad_maximum_fusion.3), channel_id=1, source_target_pairs={{0,2},{1,3},{2,0},{3,1},{4,6},{5,7},{6,4},{7,5},{8,10},{9,11},{10,... | collective-permute-start | bytes 49160 | tf_op jit(solution)/shard_map/ppermute | solution.py:30
  67.8 8.9 %collective-permute-start.2 = (bf16[4,32,128]{2,0,1:T(4,128)(2,1)S(1)}, bf16[4,32,128]{2,0,1:T(4,128)(2,1)S(1)}, u32[]{:S(2)}, u32[]{:S(2)}) collective-permute-start(bf16[4,32,128]{2,0,1:T(4,128)(2,1)S(1)} %pad_maximum_fusion.2), channel_id=1, source_target_pairs={{0,4},{1,5},{2,6},{3,7},{4,0},{5,1},{6,2},{7,3},{8,12},{9,13},{10,... | collective-permute-start | bytes 98312 | tf_op jit(solution)/shard_map/ppermute | solution.py:30
  84.2 4.7 %collective-permute-start.3 = (bf16[32,1536]{1,0:T(8,128)(2,1)S(1)}, bf16[32,1536]{1,0:T(8,128)(2,1)S(1)}, u32[]{:S(2)}, u32[]{:S(2)}) collective-permute-start(bf16[32,1536]{1,0:T(8,128)(2,1)S(1)} %convolution_convert_fusion), channel_id=1, source_target_pairs={{0,1},{1,0},{2,3},{3,2},{4,5},{5,4},{6,7},{7,6},{8,9},{9,8},{10,11... | collective-permute-start | bytes 294920 | tf_op jit(solution)/shard_map/ppermute | solution.py:20
  88.8 7.3 %collective-permute-start.4 = (bf16[32,1536]{1,0:T(8,128)(2,1)S(1)}, bf16[32,1536]{1,0:T(8,128)(2,1)S(1)}, u32[]{:S(2)}, u32[]{:S(2)}) collective-permute-start(bf16[32,1536]{1,0:T(8,128)(2,1)S(1)} %add.205), channel_id=1, source_target_pairs={{0,2},{1,3},{2,0},{3,1},{4,6},{5,7},{6,4},{7,5},{8,10},{9,11},{10,... | collective-permute-start | bytes 294920 | tf_op jit(solution)/shard_map/ppermute | solution.py:20
  96.2 9.2 %collective-permute-start.5 = (bf16[32,1536]{1,0:T(8,128)(2,1)S(1)}, bf16[32,1536]{1,0:T(8,128)(2,1)S(1)}, u32[]{:S(2)}, u32[]{:S(2)}) collective-permute-start(bf16[32,1536]{1,0:T(8,128)(2,1)S(1)} %add.206), channel_id=1, source_target_pairs={{0,4},{1,5},{2,6},{3,7},{4,0},{5,1},{6,2},{7,3},{8,12},{9,13},{10,... | collective-permute-start | bytes 294920 | tf_op jit(solution)/shard_map/ppermute | solution.py:20
Sparse Core Ops, SparseCore 0:
  23.3 48.0 all-gather.1

commit v4 on v3

--- a/solution.py
+++ b/solution.py
@@ -61,7 +61,6 @@
         requests = req_dev * req_size
         qwidth = steps * heads_dev * head_dim
         token_rows = tokens.reshape(req_dev * steps, width)
-        full_out_weight = lax.all_gather(out_weight, "tp", axis=0, tiled=True)
         normed = rms_norm(token_rows.astype(jnp.float32), norm_gain).astype(jnp.bfloat16)
         queries = (
             jnp.dot(normed, query_weight, preferred_element_type=jnp.float32) * head_dim ** (-0.5)
@@ -177,9 +176,8 @@
             .astype(jnp.bfloat16)
             .reshape(req_dev * steps, heads_dev * head_dim)
         )
-        all_heads = tree_gather(attended, "tp", tp_size)
-        all_heads = jnp.moveaxis(all_heads, 0, 1).reshape(req_dev * steps, -1)
-        attn_total = jnp.dot(all_heads, full_out_weight, preferred_element_type=jnp.float32)
+        projected = jnp.dot(attended, out_weight, preferred_element_type=jnp.float32)
+        attn_total = tree_sum(projected.astype(jnp.bfloat16), "tp", tp_size).astype(jnp.float32)
         residual = (token_rows.astype(jnp.float32) + attn_total).astype(jnp.bfloat16)
         mlp_in = rms_norm(residual.astype(jnp.float32), mlp_gain).astype(jnp.bfloat16)
         gate = jnp.dot(mlp_in, gate_weight, preferred_element_type=jnp.float32)

time: 115 us -> 102 us (0.89)
  the two profiles are of different devices: /device:TPU:2 before, /device:TPU:8 now
where the time goes in v4:
time: 102 us; the launch traced here: 101 us
  waiting for transfers between devices  43 us (42%)
  starting transfers between devices  33.8 us (33%)
  matrix products  11.2 us (11%)
  local copies, waits for them, and re-layouts  7.07 us (7%)
  other arithmetic  5.89 us (6%)
    ppermute x6, waiting for transfers between devices, tree_sum(): lax.ppermute(values, axis, [(i, i ^ step) for i in range(size)])  25.3 us
    ppermute x6, starting transfers between devices, tree_sum(): lax.ppermute(values, axis, [(i, i ^ step) for i in range(size)])  20.8 us
    all_to_all x1, waiting for transfers between devices, body(): lax.all_to_all(send, 'req', 0, 0, tiled=True).reshape(req_size, req_dev, -1)  10.2 us
    all_to_all x1, waiting for transfers between devices, body(): lax.all_to_all(jnp.broadcast_to(packed[None], (req_size,) + packed.shape)...  7.54 us
    all_to_all x1, starting transfers between devices, body(): lax.all_to_all(jnp.broadcast_to(packed[None], (req_size,) + packed.shape)...  7.53 us
    all_to_all x1, starting transfers between devices, body(): lax.all_to_all(send, 'req', 0, 0, tiled=True).reshape(req_size, req_dev, -1)  5.46 us
    dot_general x1, matrix products, body(): jnp.einsum('pqd,pkd->pqk', page_queries, kv_pages[:, 0], preferred_elemen...  3.08 us
    dot_general x1, matrix products, body(): jnp.dot(hidden, down_weight, preferred_element_type=jnp.float32)  2.52 us
  transfers between devices with their start and end apart: 8, of which 8 were waited for; matrix products, arithmetic and copies ran while one was open for 1% of the time, Pallas kernels for 0%

profile of v4, /device:TPU:8, one launch (start us, length us, event | category | flops | bytes accessed | tf_op | source)
XLA Modules:
  0.0 101.3 jit_solution(16873597148335284390)
XLA Ops:
  0.0 1.2 %multiply_reduce_fusion = f32[8,4]{1,0:T(8,128)S(1)} fusion(bf16[8,4,1536]{2,1,0:T(4,128)(2,1)} %param.13), kind=kLoop, calls=%fused_computation.38 | loop fusion | flops 147424 | bytes 98432 | tf_op jit(solution)/shard_map/reduce_sum | solution.py:14
  1.2 0.9 reshape.404
  2.1 0.7 copy.76
  2.9 0.8 multiply_convert_fusion
  3.7 1.2 %fusion.16 = bf16[32,128]{1,0:T(8,128)(2,1)S(1)} fusion(bf16[32,1536]{1,0:T(8,128)(2,1)S(1)} %multiply_convert_fusion, bf16[1536,128]{1,0:T(8,128)(2,1)} %param.18), kind=kOutput, calls=%fused_computation.21 | convolution fusion | flops 12591104 | bytes 499712 | tf_op jit(solution)/shard_map/dot_general | solution.py:66
  4.9 0.8 fusion.45
  5.8 0.7 broadcast_in_dim.61
  6.5 7.5 %all-to-all-start = ((bf16[32,8,532]{2,1,0:T(8,128)(2,1)}), bf16[32,8,532]{2,1,0:T(8,128)(2,1)S(1)}, u32[]{:S(2)}, u32[]{:S(2)}) async-start(bf16[32,8,532]{2,1,0:T(8,128)(2,1)} %broadcast_in_dim.61), calls=%async_computation | async-start | bytes 655360 | tf_op jit(solution)/shard_map/all_to_all | solution.py:81
  14.5 7.5 %all-to-all-done = bf16[32,8,532]{2,1,0:T(8,128)(2,1)S(1)} async-done(((bf16[32,8,532]{2,1,0:T(8,128)(2,1)}), bf16[32,8,532]{2,1,0:T(8,128)(2,1)S(1)}, u32[]{:S(2)}, u32[]{:S(2)}) %all-to-all-start) | async-done | bytes 272416 | tf_op jit(solution)/shard_map/all_to_all | solution.py:81
  22.9 1.3 %gather_fusion = s32[72]{0:T(128)S(1)} fusion(s32[256]{0:T(256)S(1)} %slice_reduce_fusion, s32[1024]{0:T(1024)S(1)} %pad_clamp_fusion), kind=kCustom, calls=%fused_computation | custom fusion | bytes 864 | tf_op jit(solution)/shard_map/gather | solution.py:99
  24.5 0.7 gather_fusion.1
  25.2 3.1 %fusion.60 = (f32[72,4]{1,0:T(8,128)S(1)}, f32[72,4,128]{2,1,0:T(4,128)S(1)}) fusion(bf16[72,4,128]{2,1,0:T(4,128)(2,1)S(1)} %gather_fusion.1, bf16[72,2,128,128]{3,2,1,0:T(8,128)(2,1)} %param.16, s32[72,4]{1,0:T(8,128)S(1)} %add_add_fusion, s32[72,128]{1,0:T(8,128)S(1)} %iota_add_fusion, pred[72,128]{1,0:T(8,128)(4,1)S(1)} %broadcast_compare_fusion), kind=kOutput, calls=%fused_computation.113 | convolution fusion | flops 9584352 | bytes 2628864 | tf_op jit(solution)/shard_map/pqd,pkd->pqk/dot_general | solution.py:110
  29.0 0.6 gather_fusion.2
  29.6 2.5 %fusion.9 = f32[72,4,128]{2,1,0:T(4,128)S(1)} fusion(bf16[72,2,128,128]{3,2,1,0:T(8,128)(2,1)} %param.16, f32[72,4]{1,0:T(8,128)S(1)} %get-tuple-element.12, f32[72,4,128]{2,1,0:T(4,128)S(1)} %get-tuple-element.20, f32[72,4]{1,0:T(8,128)S(1)} %get-tuple-element.19, s32[72,4]{1,0:T(8,128)S(1)} %add_add_fusion, s32[72,128]{1,0:T(8,128)S(1)} %iota_add_fusion, ...), kind=kOutput, calls=%fused_computation.13 | convolution fusion | flops 9658368 | bytes 2703744 | tf_op jit(solution)/shard_map/pqk,pkd->pqd/dot_general | solution.py:117
  32.1 0.5 convolution_bitcast_fusion
  32.7 0.9 pad_maximum_fusion
  33.6 5.5 %all-to-all-start.1 = ((f32[32,8,520]{2,1,0:T(8,128)}), f32[32,8,520]{2,1,0:T(8,128)S(1)}, u32[]{:S(2)}, u32[]{:S(2)}) async-start(f32[32,8,520]{2,1,0:T(8,128)} %pad_maximum_fusion), calls=%async_computation.1 | async-start | bytes 1310720 | tf_op jit(solution)/shard_map/all_to_all | solution.py:144
  39.8 10.2 %all-to-all-done.1 = f32[32,8,520]{2,1,0:T(8,128)S(1)} async-done(((f32[32,8,520]{2,1,0:T(8,128)}), f32[32,8,520]{2,1,0:T(8,128)S(1)}, u32[]{:S(2)}, u32[]{:S(2)}) %all-to-all-start.1) | async-done | bytes 532512 | tf_op jit(solution)/shard_map/all_to_all | solution.py:144
  51.0 2.0 %collective-permute-start = (bf16[32,1536]{1,0:T(8,128)(2,1)S(1)}, bf16[32,1536]{1,0:T(8,128)(2,1)S(1)}, u32[]{:S(2)}, u32[]{:S(2)}) collective-permute-start(bf16[32,1536]{1,0:T(8,128)(2,1)S(1)} %convolution_convert_fusion.1), channel_id=1, source_target_pairs={{0,1},{1,0},{2,3},{3,2},{4,5},{5,4},{6,7},{7,6},{8,9},{9,8},{10,11... | collective-permute-start | bytes 294920 | tf_op jit(solution)/shard_map/ppermute | solution.py:20
  53.0 3.6 %collective-permute-done = bf16[32,1536]{1,0:T(8,128)(2,1)S(1)} collective-permute-done((bf16[32,1536]{1,0:T(8,128)(2,1)S(1)}, bf16[32,1536]{1,0:T(8,128)(2,1)S(1)}, u32[]{:S(2)}, u32[]{:S(2)}) %collective-permute-start) | collective-permute-done | bytes 98336 | tf_op jit(solution)/shard_map/ppermute | solution.py:20
  56.6 3.4 %collective-permute-start.1 = (bf16[32,1536]{1,0:T(8,128)(2,1)S(1)}, bf16[32,1536]{1,0:T(8,128)(2,1)S(1)}, u32[]{:S(2)}, u32[]{:S(2)}) collective-permute-start(bf16[32,1536]{1,0:T(8,128)(2,1)S(1)} %add.193), channel_id=1, source_target_pairs={{0,2},{1,3},{2,0},{3,1},{4,6},{5,7},{6,4},{7,5},{8,10},{9,11},{10,... | collective-permute-start | bytes 294920 | tf_op jit(solution)/shard_map/ppermute | solution.py:20
  60.0 5.2 %collective-permute-done.1 = bf16[32,1536]{1,0:T(8,128)(2,1)S(1)} collective-permute-done((bf16[32,1536]{1,0:T(8,128)(2,1)S(1)}, bf16[32,1536]{1,0:T(8,128)(2,1)S(1)}, u32[]{:S(2)}, u32[]{:S(2)}) %collective-permute-start.1) | collective-permute-done | bytes 98336 | tf_op jit(solution)/shard_map/ppermute | solution.py:20
  65.2 6.8 %collective-permute-start.2 = (bf16[32,1536]{1,0:T(8,128)(2,1)S(1)}, bf16[32,1536]{1,0:T(8,128)(2,1)S(1)}, u32[]{:S(2)}, u32[]{:S(2)}) collective-permute-start(bf16[32,1536]{1,0:T(8,128)(2,1)S(1)} %add.194), channel_id=1, source_target_pairs={{0,4},{1,5},{2,6},{3,7},{4,0},{5,1},{6,2},{7,3},{8,12},{9,13},{10,... | collective-permute-start | bytes 294920 | tf_op jit(solution)/shard_map/ppermute | solution.py:20
  72.0 2.6 %collective-permute-done.2 = bf16[32,1536]{1,0:T(8,128)(2,1)S(1)} collective-permute-done((bf16[32,1536]{1,0:T(8,128)(2,1)S(1)}, bf16[32,1536]{1,0:T(8,128)(2,1)S(1)}, u32[]{:S(2)}, u32[]{:S(2)}) %collective-permute-start.2) | collective-permute-done | bytes 98336 | tf_op jit(solution)/shard_map/ppermute | solution.py:20
  74.8 0.6 fusion.41
  75.4 2.5 %convolution_convert_fusion = bf16[32,1536]{1,0:T(8,128)(2,1)S(1)} fusion(bf16[576,1536]{1,0:T(8,128)(2,1)S(1)} %copy-done, bf16[1536,576]{0,1:T(8,128)(2,1)} %param.24, f32[32,576]{1,0:T(8,128)S(1)} %fusion.41, bf16[32,1536]{1,0:T(8,128)(2,1)S(1)} %get-tuple-element.6, f32[1536]{0:T(1024)S(1)} %copy-done.5, f32[32]{0:T(128)S(1)} %add_rsqrt_fusion.1), kind=kOutput, calls=%fused_computation.9 | convolution fusion | flops 113676288 | bytes 3815552 | tf_op jit(solution)/shard_map/dot_general | solution.py:186
  78.0 4.6 %collective-permute-done.3 = bf16[32,1536]{1,0:T(8,128)(2,1)S(1)} collective-permute-done((bf16[32,1536]{1,0:T(8,128)(2,1)S(1)}, bf16[32,1536]{1,0:T(8,128)(2,1)S(1)}, u32[]{:S(2)}, u32[]{:S(2)}) %collective-permute-start.3) | collective-permute-done | bytes 98336 | tf_op jit(solution)/shard_map/ppermute | solution.py:20
  82.6 4.6 %collective-permute-start.4 = (bf16[32,1536]{1,0:T(8,128)(2,1)S(1)}, bf16[32,1536]{1,0:T(8,128)(2,1)S(1)}, u32[]{:S(2)}, u32[]{:S(2)}) collective-permute-start(bf16[32,1536]{1,0:T(8,128)(2,1)S(1)} %add.201), channel_id=1, source_target_pairs={{0,2},{1,3},{2,0},{3,1},{4,6},{5,7},{6,4},{7,5},{8,10},{9,11},{10,... | collective-permute-start | bytes 294920 | tf_op jit(solution)/shard_map/ppermute | solution.py:20
  87.2 3.6 %collective-permute-done.4 = bf16[32,1536]{1,0:T(8,128)(2,1)S(1)} collective-permute-done((bf16[32,1536]{1,0:T(8,128)(2,1)S(1)}, bf16[32,1536]{1,0:T(8,128)(2,1)S(1)}, u32[]{:S(2)}, u32[]{:S(2)}) %collective-permute-start.4) | collective-permute-done | bytes 98336 | tf_op jit(solution)/shard_map/ppermute | solution.py:20
  90.9 4.0 %collective-permute-start.5 = (bf16[32,1536]{1,0:T(8,128)(2,1)S(1)}, bf16[32,1536]{1,0:T(8,128)(2,1)S(1)}, u32[]{:S(2)}, u32[]{:S(2)}) collective-permute-start(bf16[32,1536]{1,0:T(8,128)(2,1)S(1)} %add.202), channel_id=1, source_target_pairs={{0,4},{1,5},{2,6},{3,7},{4,0},{5,1},{6,2},{7,3},{8,12},{9,13},{10,... | collective-permute-start | bytes 294920 | tf_op jit(solution)/shard_map/ppermute | solution.py:20
  94.9 5.7 %collective-permute-done.5 = bf16[32,1536]{1,0:T(8,128)(2,1)S(1)} collective-permute-done((bf16[32,1536]{1,0:T(8,128)(2,1)S(1)}, bf16[32,1536]{1,0:T(8,128)(2,1)S(1)}, u32[]{:S(2)}, u32[]{:S(2)}) %collective-permute-start.5) | collective-permute-done | bytes 98336 | tf_op jit(solution)/shard_map/ppermute | solution.py:20
  100.6 0.7 reshape.403
  (65 shorter events, 4.5 us)
Async XLA Ops:
  0.0 75.4 %copy-start = (bf16[576,1536]{1,0:T(8,128)(2,1)S(1)}, bf16[576,1536]{1,0:T(8,128)(2,1)}, u32[]{:S(2)}) copy-start(bf16[576,1536]{1,0:T(8,128)(2,1)} %param.25) | copy-start | bytes 5308420
  0.0 14.1 %copy-start.2 = (bf16[1536,128]{1,0:T(8,128)(2,1)S(1)}, bf16[1536,128]{1,0:T(8,128)(2,1)}, u32[]{:S(2)}) copy-start(bf16[1536,128]{1,0:T(8,128)(2,1)} %param.19) | copy-start | bytes 1179652
  6.5 15.5 %all-to-all-start = ((bf16[32,8,532]{2,1,0:T(8,128)(2,1)}), bf16[32,8,532]{2,1,0:T(8,128)(2,1)S(1)}, u32[]{:S(2)}, u32[]{:S(2)}) async-start(bf16[32,8,532]{2,1,0:T(8,128)(2,1)} %broadcast_in_dim.61), calls=%async_computation | async-start | bytes 655360 | tf_op jit(solution)/shard_map/all_to_all | solution.py:81
  32.1 7.4 %copy-start.3 = (bf16[1536,128]{1,0:T(8,128)(2,1)S(1)}, bf16[1536,128]{1,0:T(8,128)(2,1)}, u32[]{:S(2)}) copy-start(bf16[1536,128]{1,0:T(8,128)(2,1)} %param.20) | copy-start | bytes 1179652
  33.6 17.2 %copy-start.4 = (bf16[128,1536]{1,0:T(8,128)(2,1)S(1)}, bf16[128,1536]{1,0:T(8,128)(2,1)}, u32[]{:S(2)}) copy-start(bf16[128,1536]{1,0:T(8,128)(2,1)} %param.21) | copy-start | bytes 1179652
  33.6 16.3 %all-to-all-start.1 = ((f32[32,8,520]{2,1,0:T(8,128)}), f32[32,8,520]{2,1,0:T(8,128)S(1)}, u32[]{:S(2)}, u32[]{:S(2)}) async-start(f32[32,8,520]{2,1,0:T(8,128)} %pad_maximum_fusion), calls=%async_computation.1 | async-start | bytes 1310720 | tf_op jit(solution)/shard_map/all_to_all | solution.py:144
  39.6 35.2 %copy-start.5 = (f32[1536]{0:T(1024)S(1)}, f32[1536]{0:T(1024)}, u32[]{:S(2)}) copy-start(f32[1536]{0:T(1024)} %param.22) | copy-start | bytes 18436
  50.7 24.1 %copy-start.1 = (bf16[1536,576]{0,1:T(8,128)(2,1)S(1)}, bf16[1536,576]{0,1:T(8,128)(2,1)}, u32[]{:S(2)}) copy-start(bf16[1536,576]{0,1:T(8,128)(2,1)} %param.23) | copy-start | bytes 5308420
  51.0 5.6 %collective-permute-start = (bf16[32,1536]{1,0:T(8,128)(2,1)S(1)}, bf16[32,1536]{1,0:T(8,128)(2,1)S(1)}, u32[]{:S(2)}, u32[]{:S(2)}) collective-permute-start(bf16[32,1536]{1,0:T(8,128)(2,1)S(1)} %convolution_convert_fusion.1), channel_id=1, source_target_pairs={{0,1},{1,0},{2,3},{3,2},{4,5},{5,4},{6,7},{7,6},{8,9},{9,8},{10,11... | collective-permute-start | bytes 294920 | tf_op jit(solution)/shard_map/ppermute | solution.py:20
  56.6 8.5 %collective-permute-start.1 = (bf16[32,1536]{1,0:T(8,128)(2,1)S(1)}, bf16[32,1536]{1,0:T(8,128)(2,1)S(1)}, u32[]{:S(2)}, u32[]{:S(2)}) collective-permute-start(bf16[32,1536]{1,0:T(8,128)(2,1)S(1)} %add.193), channel_id=1, source_target_pairs={{0,2},{1,3},{2,0},{3,1},{4,6},{5,7},{6,4},{7,5},{8,10},{9,11},{10,... | collective-permute-start | bytes 294920 | tf_op jit(solution)/shard_map/ppermute | solution.py:20
  65.2 9.4 %collective-permute-start.2 = (bf16[32,1536]{1,0:T(8,128)(2,1)S(1)}, bf16[32,1536]{1,0:T(8,128)(2,1)S(1)}, u32[]{:S(2)}, u32[]{:S(2)}) collective-permute-start(bf16[32,1536]{1,0:T(8,128)(2,1)S(1)} %add.194), channel_id=1, source_target_pairs={{0,4},{1,5},{2,6},{3,7},{4,0},{5,1},{6,2},{7,3},{8,12},{9,13},{10,... | collective-permute-start | bytes 294920 | tf_op jit(solution)/shard_map/ppermute | solution.py:20
  77.9 4.7 %collective-permute-start.3 = (bf16[32,1536]{1,0:T(8,128)(2,1)S(1)}, bf16[32,1536]{1,0:T(8,128)(2,1)S(1)}, u32[]{:S(2)}, u32[]{:S(2)}) collective-permute-start(bf16[32,1536]{1,0:T(8,128)(2,1)S(1)} %convolution_convert_fusion), channel_id=1, source_target_pairs={{0,1},{1,0},{2,3},{3,2},{4,5},{5,4},{6,7},{7,6},{8,9},{9,8},{10,11... | collective-permute-start | bytes 294920 | tf_op jit(solution)/shard_map/ppermute | solution.py:20
  82.6 8.2 %collective-permute-start.4 = (bf16[32,1536]{1,0:T(8,128)(2,1)S(1)}, bf16[32,1536]{1,0:T(8,128)(2,1)S(1)}, u32[]{:S(2)}, u32[]{:S(2)}) collective-permute-start(bf16[32,1536]{1,0:T(8,128)(2,1)S(1)} %add.201), channel_id=1, source_target_pairs={{0,2},{1,3},{2,0},{3,1},{4,6},{5,7},{6,4},{7,5},{8,10},{9,11},{10,... | collective-permute-start | bytes 294920 | tf_op jit(solution)/shard_map/ppermute | solution.py:20
  90.9 9.7 %collective-permute-start.5 = (bf16[32,1536]{1,0:T(8,128)(2,1)S(1)}, bf16[32,1536]{1,0:T(8,128)(2,1)S(1)}, u32[]{:S(2)}, u32[]{:S(2)}) collective-permute-start(bf16[32,1536]{1,0:T(8,128)(2,1)S(1)} %add.202), channel_id=1, source_target_pairs={{0,4},{1,5},{2,6},{3,7},{4,0},{5,1},{6,2},{7,3},{8,12},{9,13},{10,... | collective-permute-start | bytes 294920 | tf_op jit(solution)/shard_map/ppermute | solution.py:20

commit v5 on v4

--- a/solution.py
+++ b/solution.py
@@ -140,13 +140,29 @@
             precision=lax.Precision.HIGHEST,
             preferred_element_type=jnp.float32,
         )
-        send = jnp.concatenate([sent, local_max.reshape(requests, nsh)], axis=1)
+        flat_max = local_max.reshape(requests, nsh)
+        max_hi = lax.reduce_precision(flat_max, exponent_bits=8, mantissa_bits=7)
+        rest = flat_max - max_hi
+        max_mid = lax.reduce_precision(rest, exponent_bits=8, mantissa_bits=7)
+        max_lo = rest - max_mid
+        send = jnp.concatenate(
+            [sent, max_hi, max_mid, max_lo], axis=1
+        ).astype(jnp.bfloat16)
         recv = lax.all_to_all(send, "req", 0, 0, tiled=True).reshape(req_size, req_dev, -1)
-        got_out = recv[:, :, : nsh * head_dim].reshape(req_size, req_dev, steps, heads_dev, head_dim)
-        got_total = recv[:, :, nsh * head_dim : nsh * (head_dim + 1)].reshape(
-            req_size, req_dev, steps, heads_dev
-        )
-        got_max = recv[:, :, nsh * (head_dim + 1) :].reshape(req_size, req_dev, steps, heads_dev)
+        got_out = (
+            recv[:, :, : nsh * head_dim]
+            .astype(jnp.float32)
+            .reshape(req_size, req_dev, steps, heads_dev, head_dim)
+        )
+        got_total = (
+            recv[:, :, nsh * head_dim : nsh * (head_dim + 1)]
+            .astype(jnp.float32)
+            .reshape(req_size, req_dev, steps, heads_dev)
+        )
+        pieces = recv[:, :, nsh * (head_dim + 1) :].astype(jnp.float32)
+        got_max = (
+            (pieces[:, :, :nsh] + pieces[:, :, nsh : 2 * nsh]) + pieces[:, :, 2 * nsh :]
+        ).reshape(req_size, req_dev, steps, heads_dev)
         cache_max = jnp.max(got_max, axis=0)
         local_queries = queries.reshape(req_dev, steps, heads_dev, head_dim)
         new_scores = jnp.einsum(

time: 102 us -> 98.5 us (0.966)
  the two profiles are of different devices: /device:TPU:8 before, /device:TPU:10 now
where the time goes in v5:
time: 98.5 us; the launch traced here: 98 us
  waiting for transfers between devices  37.8 us (38%)
  starting transfers between devices  35 us (36%)
  matrix products  11.1 us (11%)
  local copies, waits for them, and re-layouts  7.89 us (8%)
  other arithmetic  5.97 us (6%)
    ppermute x6, waiting for transfers between devices, tree_sum(): lax.ppermute(values, axis, [(i, i ^ step) for i in range(size)])  25.2 us
    ppermute x6, starting transfers between devices, tree_sum(): lax.ppermute(values, axis, [(i, i ^ step) for i in range(size)])  20.8 us
    all_to_all x1, starting transfers between devices, body(): lax.all_to_all(jnp.broadcast_to(packed[None], (req_size,) + packed.shape)...  7.51 us
    all_to_all x1, starting transfers between devices, body(): lax.all_to_all(send, 'req', 0, 0, tiled=True).reshape(req_size, req_dev, -1)  6.61 us
    all_to_all x1, waiting for transfers between devices, body(): lax.all_to_all(jnp.broadcast_to(packed[None], (req_size,) + packed.shape)...  6.29 us
    all_to_all x1, waiting for transfers between devices, body(): lax.all_to_all(send, 'req', 0, 0, tiled=True).reshape(req_size, req_dev, -1)  6.29 us
    dot_general x1, matrix products, body(): jnp.einsum('pqd,pkd->pqk', page_queries, kv_pages[:, 0], preferred_elemen...  3.08 us
    dot_general x1, matrix products, body(): jnp.dot(hidden, down_weight, preferred_element_type=jnp.float32)  2.52 us
  transfers between devices with their start and end apart: 8, of which 8 were waited for; matrix products, arithmetic and copies ran while one was open for 1% of the time, Pallas kernels for 0%

profile of v5, /device:TPU:10, one launch (start us, length us, event | category | flops | bytes accessed | tf_op | source)
XLA Modules:
  0.0 98.0 jit_solution(6539092265332269053)
XLA Ops:
  0.0 1.2 %multiply_reduce_fusion = f32[8,4]{1,0:T(8,128)S(1)} fusion(bf16[8,4,1536]{2,1,0:T(4,128)(2,1)} %param.13), kind=kLoop, calls=%fused_computation.38 | loop fusion | flops 147424 | bytes 98432 | tf_op jit(solution)/shard_map/reduce_sum | solution.py:14
  1.2 0.9 reshape.409
  2.1 0.7 copy.87
  2.9 0.8 multiply_convert_fusion
  3.7 1.2 %fusion.16 = bf16[32,128]{1,0:T(8,128)(2,1)S(1)} fusion(bf16[32,1536]{1,0:T(8,128)(2,1)S(1)} %multiply_convert_fusion, bf16[1536,128]{1,0:T(8,128)(2,1)} %param.18), kind=kOutput, calls=%fused_computation.21 | convolution fusion | flops 12591104 | bytes 499712 | tf_op jit(solution)/shard_map/dot_general | solution.py:66
  4.9 0.8 fusion.45
  5.8 0.7 broadcast_in_dim.61
  6.5 7.5 %all-to-all-start = ((bf16[32,8,532]{2,1,0:T(8,128)(2,1)}), bf16[32,8,532]{2,1,0:T(8,128)(2,1)S(1)}, u32[]{:S(2)}, u32[]{:S(2)}) async-start(bf16[32,8,532]{2,1,0:T(8,128)(2,1)} %broadcast_in_dim.61), calls=%async_computation | async-start | bytes 655360 | tf_op jit(solution)/shard_map/all_to_all | solution.py:81
  14.6 6.3 %all-to-all-done = bf16[32,8,532]{2,1,0:T(8,128)(2,1)S(1)} async-done(((bf16[32,8,532]{2,1,0:T(8,128)(2,1)}), bf16[32,8,532]{2,1,0:T(8,128)(2,1)S(1)}, u32[]{:S(2)}, u32[]{:S(2)}) %all-to-all-start) | async-done | bytes 272416 | tf_op jit(solution)/shard_map/all_to_all | solution.py:81
  21.7 1.3 %gather_fusion = s32[72]{0:T(128)S(1)} fusion(s32[256]{0:T(256)S(1)} %slice_reduce_fusion, s32[1024]{0:T(1024)S(1)} %pad_clamp_fusion), kind=kCustom, calls=%fused_computation | custom fusion | bytes 864 | tf_op jit(solution)/shard_map/gather | solution.py:99
  23.3 0.7 gather_fusion.1
  24.0 3.1 %fusion.61 = (f32[72,4]{1,0:T(8,128)S(1)}, f32[72,4,128]{2,1,0:T(4,128)S(1)}) fusion(bf16[72,4,128]{2,1,0:T(4,128)(2,1)S(1)} %gather_fusion.1, bf16[72,2,128,128]{3,2,1,0:T(8,128)(2,1)} %param.16, s32[72,4]{1,0:T(8,128)S(1)} %add_add_fusion, s32[72,128]{1,0:T(8,128)S(1)} %iota_add_fusion, pred[72,128]{1,0:T(8,128)(4,1)S(1)} %broadcast_compare_fusion), kind=kOutput, calls=%fused_computation.120 | convolution fusion | flops 9584352 | bytes 2628864 | tf_op jit(solution)/shard_map/pqd,pkd->pqk/dot_general | solution.py:110
  28.5 0.6 gather_fusion.2
  29.1 2.5 %fusion.9 = f32[72,4,128]{2,1,0:T(4,128)S(1)} fusion(bf16[72,2,128,128]{3,2,1,0:T(8,128)(2,1)} %param.16, f32[72,4]{1,0:T(8,128)S(1)} %get-tuple-element.12, f32[72,4,128]{2,1,0:T(4,128)S(1)} %get-tuple-element.23, f32[72,4]{1,0:T(8,128)S(1)} %get-tuple-element.22, s32[72,4]{1,0:T(8,128)S(1)} %add_add_fusion, s32[72,128]{1,0:T(8,128)S(1)} %iota_add_fusion, ...), kind=kOutput, calls=%fused_computation.13 | convolution fusion | flops 9658368 | bytes 2703744 | tf_op jit(solution)/shard_map/pqk,pkd->pqd/dot_general | solution.py:117
  31.6 0.5 convolution_convert_fusion.2
  32.3 0.8 pad_maximum_fusion
  33.1 6.6 %all-to-all-start.1 = ((bf16[32,8,528]{2,1,0:T(8,128)(2,1)}), bf16[32,8,528]{2,1,0:T(8,128)(2,1)S(1)}, u32[]{:S(2)}, u32[]{:S(2)}) async-start(bf16[32,8,528]{2,1,0:T(8,128)(2,1)} %pad_maximum_fusion), calls=%async_computation.1 | async-start | bytes 655360 | tf_op jit(solution)/shard_map/all_to_all | solution.py:151
  40.3 6.3 %all-to-all-done.1 = bf16[32,8,528]{2,1,0:T(8,128)(2,1)S(1)} async-done(((bf16[32,8,528]{2,1,0:T(8,128)(2,1)}), bf16[32,8,528]{2,1,0:T(8,128)(2,1)S(1)}, u32[]{:S(2)}, u32[]{:S(2)}) %all-to-all-start.1) | async-done | bytes 270368 | tf_op jit(solution)/shard_map/all_to_all | solution.py:151
  47.8 2.0 %collective-permute-start = (bf16[32,1536]{1,0:T(8,128)(2,1)S(1)}, bf16[32,1536]{1,0:T(8,128)(2,1)S(1)}, u32[]{:S(2)}, u32[]{:S(2)}) collective-permute-start(bf16[32,1536]{1,0:T(8,128)(2,1)S(1)} %convolution_convert_fusion.1), channel_id=1, source_target_pairs={{0,1},{1,0},{2,3},{3,2},{4,5},{5,4},{6,7},{7,6},{8,9},{9,8},{10,11... | collective-permute-start | bytes 294920 | tf_op jit(solution)/shard_map/ppermute | solution.py:20
  49.8 3.4 %collective-permute-done = bf16[32,1536]{1,0:T(8,128)(2,1)S(1)} collective-permute-done((bf16[32,1536]{1,0:T(8,128)(2,1)S(1)}, bf16[32,1536]{1,0:T(8,128)(2,1)S(1)}, u32[]{:S(2)}, u32[]{:S(2)}) %collective-permute-start) | collective-permute-done | bytes 98336 | tf_op jit(solution)/shard_map/ppermute | solution.py:20
  53.3 3.4 %collective-permute-start.1 = (bf16[32,1536]{1,0:T(8,128)(2,1)S(1)}, bf16[32,1536]{1,0:T(8,128)(2,1)S(1)}, u32[]{:S(2)}, u32[]{:S(2)}) collective-permute-start(bf16[32,1536]{1,0:T(8,128)(2,1)S(1)} %add.201), channel_id=1, source_target_pairs={{0,2},{1,3},{2,0},{3,1},{4,6},{5,7},{6,4},{7,5},{8,10},{9,11},{10,... | collective-permute-start | bytes 294920 | tf_op jit(solution)/shard_map/ppermute | solution.py:20
  56.7 5.2 %collective-permute-done.1 = bf16[32,1536]{1,0:T(8,128)(2,1)S(1)} collective-permute-done((bf16[32,1536]{1,0:T(8,128)(2,1)S(1)}, bf16[32,1536]{1,0:T(8,128)(2,1)S(1)}, u32[]{:S(2)}, u32[]{:S(2)}) %collective-permute-start.1) | collective-permute-done | bytes 98336 | tf_op jit(solution)/shard_map/ppermute | solution.py:20
  61.9 6.8 %collective-permute-start.2 = (bf16[32,1536]{1,0:T(8,128)(2,1)S(1)}, bf16[32,1536]{1,0:T(8,128)(2,1)S(1)}, u32[]{:S(2)}, u32[]{:S(2)}) collective-permute-start(bf16[32,1536]{1,0:T(8,128)(2,1)S(1)} %add.202), channel_id=1, source_target_pairs={{0,4},{1,5},{2,6},{3,7},{4,0},{5,1},{6,2},{7,3},{8,12},{9,13},{10,... | collective-permute-start | bytes 294920 | tf_op jit(solution)/shard_map/ppermute | solution.py:20
  68.7 2.6 %collective-permute-done.2 = bf16[32,1536]{1,0:T(8,128)(2,1)S(1)} collective-permute-done((bf16[32,1536]{1,0:T(8,128)(2,1)S(1)}, bf16[32,1536]{1,0:T(8,128)(2,1)S(1)}, u32[]{:S(2)}, u32[]{:S(2)}) %collective-permute-start.2) | collective-permute-done | bytes 98336 | tf_op jit(solution)/shard_map/ppermute | solution.py:20
  71.5 0.6 fusion.40
  72.1 2.5 %convolution_convert_fusion = bf16[32,1536]{1,0:T(8,128)(2,1)S(1)} fusion(bf16[576,1536]{1,0:T(8,128)(2,1)S(1)} %copy-done, bf16[1536,576]{0,1:T(8,128)(2,1)} %param.24, f32[32,576]{1,0:T(8,128)S(1)} %fusion.40, bf16[32,1536]{1,0:T(8,128)(2,1)S(1)} %get-tuple-element.6, f32[1536]{0:T(1024)S(1)} %copy-done.5, f32[32]{0:T(128)S(1)} %add_rsqrt_fusion.1), kind=kOutput, calls=%fused_computation.9 | convolution fusion | flops 113676288 | bytes 3815552 | tf_op jit(solution)/shard_map/dot_general | solution.py:202
  74.7 4.6 %collective-permute-done.3 = bf16[32,1536]{1,0:T(8,128)(2,1)S(1)} collective-permute-done((bf16[32,1536]{1,0:T(8,128)(2,1)S(1)}, bf16[32,1536]{1,0:T(8,128)(2,1)S(1)}, u32[]{:S(2)}, u32[]{:S(2)}) %collective-permute-start.3) | collective-permute-done | bytes 98336 | tf_op jit(solution)/shard_map/ppermute | solution.py:20
  79.3 4.6 %collective-permute-start.4 = (bf16[32,1536]{1,0:T(8,128)(2,1)S(1)}, bf16[32,1536]{1,0:T(8,128)(2,1)S(1)}, u32[]{:S(2)}, u32[]{:S(2)}) collective-permute-start(bf16[32,1536]{1,0:T(8,128)(2,1)S(1)} %add.209), channel_id=1, source_target_pairs={{0,2},{1,3},{2,0},{3,1},{4,6},{5,7},{6,4},{7,5},{8,10},{9,11},{10,... | collective-permute-start | bytes 294920 | tf_op jit(solution)/shard_map/ppermute | solution.py:20
  83.9 3.6 %collective-permute-done.4 = bf16[32,1536]{1,0:T(8,128)(2,1)S(1)} collective-permute-done((bf16[32,1536]{1,0:T(8,128)(2,1)S(1)}, bf16[32,1536]{1,0:T(8,128)(2,1)S(1)}, u32[]{:S(2)}, u32[]{:S(2)}) %collective-permute-start.4) | collective-permute-done | bytes 98336 | tf_op jit(solution)/shard_map/ppermute | solution.py:20
  87.6 3.9 %collective-permute-start.5 = (bf16[32,1536]{1,0:T(8,128)(2,1)S(1)}, bf16[32,1536]{1,0:T(8,128)(2,1)S(1)}, u32[]{:S(2)}, u32[]{:S(2)}) collective-permute-start(bf16[32,1536]{1,0:T(8,128)(2,1)S(1)} %add.210), channel_id=1, source_target_pairs={{0,4},{1,5},{2,6},{3,7},{4,0},{5,1},{6,2},{7,3},{8,12},{9,13},{10,... | collective-permute-start | bytes 294920 | tf_op jit(solution)/shard_map/ppermute | solution.py:20
  91.6 5.7 %collective-permute-done.5 = bf16[32,1536]{1,0:T(8,128)(2,1)S(1)} collective-permute-done((bf16[32,1536]{1,0:T(8,128)(2,1)S(1)}, bf16[32,1536]{1,0:T(8,128)(2,1)S(1)}, u32[]{:S(2)}, u32[]{:S(2)}) %collective-permute-start.5) | collective-permute-done | bytes 98336 | tf_op jit(solution)/shard_map/ppermute | solution.py:20
  97.3 0.7 reshape.408
  (73 shorter events, 5.6 us)
Async XLA Ops:
  0.0 72.1 %copy-start = (bf16[576,1536]{1,0:T(8,128)(2,1)S(1)}, bf16[576,1536]{1,0:T(8,128)(2,1)}, u32[]{:S(2)}) copy-start(bf16[576,1536]{1,0:T(8,128)(2,1)} %param.25) | copy-start | bytes 5308420
  0.0 14.0 %copy-start.2 = (bf16[1536,128]{1,0:T(8,128)(2,1)S(1)}, bf16[1536,128]{1,0:T(8,128)(2,1)}, u32[]{:S(2)}) copy-start(bf16[1536,128]{1,0:T(8,128)(2,1)} %param.19) | copy-start | bytes 1179652
  6.5 14.3 %all-to-all-start = ((bf16[32,8,532]{2,1,0:T(8,128)(2,1)}), bf16[32,8,532]{2,1,0:T(8,128)(2,1)S(1)}, u32[]{:S(2)}, u32[]{:S(2)}) async-start(bf16[32,8,532]{2,1,0:T(8,128)(2,1)} %broadcast_in_dim.61), calls=%async_computation | async-start | bytes 655360 | tf_op jit(solution)/shard_map/all_to_all | solution.py:81
  31.6 8.5 %copy-start.3 = (bf16[1536,128]{1,0:T(8,128)(2,1)S(1)}, bf16[1536,128]{1,0:T(8,128)(2,1)}, u32[]{:S(2)}) copy-start(bf16[1536,128]{1,0:T(8,128)(2,1)} %param.20) | copy-start | bytes 1179652
  33.1 14.5 %copy-start.4 = (bf16[128,1536]{1,0:T(8,128)(2,1)S(1)}, bf16[128,1536]{1,0:T(8,128)(2,1)}, u32[]{:S(2)}) copy-start(bf16[128,1536]{1,0:T(8,128)(2,1)} %param.21) | copy-start | bytes 1179652
  33.1 13.5 %all-to-all-start.1 = ((bf16[32,8,528]{2,1,0:T(8,128)(2,1)}), bf16[32,8,528]{2,1,0:T(8,128)(2,1)S(1)}, u32[]{:S(2)}, u32[]{:S(2)}) async-start(bf16[32,8,528]{2,1,0:T(8,128)(2,1)} %pad_maximum_fusion), calls=%async_computation.1 | async-start | bytes 655360 | tf_op jit(solution)/shard_map/all_to_all | solution.py:151
  40.3 31.2 %copy-start.5 = (f32[1536]{0:T(1024)S(1)}, f32[1536]{0:T(1024)}, u32[]{:S(2)}) copy-start(f32[1536]{0:T(1024)} %param.22) | copy-start | bytes 18436
  47.5 24.0 %copy-start.1 = (bf16[1536,576]{0,1:T(8,128)(2,1)S(1)}, bf16[1536,576]{0,1:T(8,128)(2,1)}, u32[]{:S(2)}) copy-start(bf16[1536,576]{0,1:T(8,128)(2,1)} %param.23) | copy-start | bytes 5308420
  47.8 5.4 %collective-permute-start = (bf16[32,1536]{1,0:T(8,128)(2,1)S(1)}, bf16[32,1536]{1,0:T(8,128)(2,1)S(1)}, u32[]{:S(2)}, u32[]{:S(2)}) collective-permute-start(bf16[32,1536]{1,0:T(8,128)(2,1)S(1)} %convolution_convert_fusion.1), channel_id=1, source_target_pairs={{0,1},{1,0},{2,3},{3,2},{4,5},{5,4},{6,7},{7,6},{8,9},{9,8},{10,11... | collective-permute-start | bytes 294920 | tf_op jit(solution)/shard_map/ppermute | solution.py:20
  53.3 8.6 %collective-permute-start.1 = (bf16[32,1536]{1,0:T(8,128)(2,1)S(1)}, bf16[32,1536]{1,0:T(8,128)(2,1)S(1)}, u32[]{:S(2)}, u32[]{:S(2)}) collective-permute-start(bf16[32,1536]{1,0:T(8,128)(2,1)S(1)} %add.201), channel_id=1, source_target_pairs={{0,2},{1,3},{2,0},{3,1},{4,6},{5,7},{6,4},{7,5},{8,10},{9,11},{10,... | collective-permute-start | bytes 294920 | tf_op jit(solution)/shard_map/ppermute | solution.py:20
  61.9 9.4 %collective-permute-start.2 = (bf16[32,1536]{1,0:T(8,128)(2,1)S(1)}, bf16[32,1536]{1,0:T(8,128)(2,1)S(1)}, u32[]{:S(2)}, u32[]{:S(2)}) collective-permute-start(bf16[32,1536]{1,0:T(8,128)(2,1)S(1)} %add.202), channel_id=1, source_target_pairs={{0,4},{1,5},{2,6},{3,7},{4,0},{5,1},{6,2},{7,3},{8,12},{9,13},{10,... | collective-permute-start | bytes 294920 | tf_op jit(solution)/shard_map/ppermute | solution.py:20
  74.6 4.7 %collective-permute-start.3 = (bf16[32,1536]{1,0:T(8,128)(2,1)S(1)}, bf16[32,1536]{1,0:T(8,128)(2,1)S(1)}, u32[]{:S(2)}, u32[]{:S(2)}) collective-permute-start(bf16[32,1536]{1,0:T(8,128)(2,1)S(1)} %convolution_convert_fusion), channel_id=1, source_target_pairs={{0,1},{1,0},{2,3},{3,2},{4,5},{5,4},{6,7},{7,6},{8,9},{9,8},{10,11... | collective-permute-start | bytes 294920 | tf_op jit(solution)/shard_map/ppermute | solution.py:20
  79.3 8.3 %collective-permute-start.4 = (bf16[32,1536]{1,0:T(8,128)(2,1)S(1)}, bf16[32,1536]{1,0:T(8,128)(2,1)S(1)}, u32[]{:S(2)}, u32[]{:S(2)}) collective-permute-start(bf16[32,1536]{1,0:T(8,128)(2,1)S(1)} %add.209), channel_id=1, source_target_pairs={{0,2},{1,3},{2,0},{3,1},{4,6},{5,7},{6,4},{7,5},{8,10},{9,11},{10,... | collective-permute-start | bytes 294920 | tf_op jit(solution)/shard_map/ppermute | solution.py:20
  87.6 9.7 %collective-permute-start.5 = (bf16[32,1536]{1,0:T(8,128)(2,1)S(1)}, bf16[32,1536]{1,0:T(8,128)(2,1)S(1)}, u32[]{:S(2)}, u32[]{:S(2)}) collective-permute-start(bf16[32,1536]{1,0:T(8,128)(2,1)S(1)} %add.210), channel_id=1, source_target_pairs={{0,4},{1,5},{2,6},{3,7},{4,0},{5,1},{6,2},{7,3},{8,12},{9,13},{10,... | collective-permute-start | bytes 294920 | tf_op jit(solution)/shard_map/ppermute | solution.py:20

commit v6 on v5

--- a/solution.py
+++ b/solution.py
@@ -14,26 +14,20 @@
     return values * lax.rsqrt(jnp.mean(values * values, axis=-1, keepdims=True) + epsilon) * gain
 
 
-def tree_sum(values, axis, size):
+def staggered_sum(values, req_size, tp_size):
+    steps = []
     step = 1
-    while step < size:
-        values = values + lax.ppermute(values, axis, [(i, i ^ step) for i in range(size)])
+    while step < tp_size:
+        steps.append(step)
         step *= 2
+    for round_index in range(len(steps)):
+        pairs = []
+        for q in range(req_size):
+            order = steps if q % 2 == 0 else steps[::-1]
+            for t in range(tp_size):
+                pairs.append((q * tp_size + t, q * tp_size + (t ^ order[round_index])))
+        values = values + lax.ppermute(values, ("req", "tp"), pairs)
     return values
-
-
-def tree_gather(values, axis, size):
-    index = lax.axis_index(axis)
-    parts = values[None]
-    step = 1
-    while step < size:
-        other = lax.ppermute(parts, axis, [(i, i ^ step) for i in range(size)])
-        upper = (index // step) % 2 == 1
-        parts = jnp.concatenate(
-            [jnp.where(upper, other, parts), jnp.where(upper, parts, other)], axis=0
-        )
-        step *= 2
-    return parts
 
 
 def make_body(req_size, tp_size):
@@ -193,7 +187,7 @@
             .reshape(req_dev * steps, heads_dev * head_dim)
         )
         projected = jnp.dot(attended, out_weight, preferred_element_type=jnp.float32)
-        attn_total = tree_sum(projected.astype(jnp.bfloat16), "tp", tp_size).astype(jnp.float32)
+        attn_total = staggered_sum(projected.astype(jnp.bfloat16), req_size, tp_size).astype(jnp.float32)
         residual = (token_rows.astype(jnp.float32) + attn_total).astype(jnp.bfloat16)
         mlp_in = rms_norm(residual.astype(jnp.float32), mlp_gain).astype(jnp.bfloat16)
         gate = jnp.dot(mlp_in, gate_weight, preferred_element_type=jnp.float32)
@@ -202,7 +196,7 @@
         mlp_part = jnp.dot(hidden, down_weight, preferred_element_type=jnp.float32).astype(
             jnp.bfloat16
         )
-        mlp_total = tree_sum(mlp_part, "tp", tp_size).astype(jnp.float32)
+        mlp_total = staggered_sum(mlp_part, req_size, tp_size).astype(jnp.float32)
         layer_out = (residual.astype(jnp.float32) + mlp_total).astype(jnp.bfloat16)
         return layer_out.reshape(req_dev, steps, width)
 

time: 98.5 us -> 98.4 us (level)
  the two profiles are of different devices: /device:TPU:10 before, /device:TPU:2 now
where the time goes in v6:
time: 98.4 us; the launch traced here: 96.9 us
  waiting for transfers between devices  37.5 us (38%)
  starting transfers between devices  34.1 us (35%)
  matrix products  11.1 us (11%)
  local copies, waits for them, and re-layouts  7.89 us (8%)
  other arithmetic  5.97 us (6%)
    ppermute x6, waiting for transfers between devices, staggered_sum(): values = values + lax.ppermute(values, ('req', 'tp'), pairs)  22 us
    ppermute x6, starting transfers between devices, staggered_sum(): values = values + lax.ppermute(values, ('req', 'tp'), pairs)  21.4 us
    all_to_all x1, waiting for transfers between devices, body(): lax.all_to_all(send, 'req', 0, 0, tiled=True).reshape(req_size, req_dev, -1)  7.79 us
    all_to_all x1, waiting for transfers between devices, body(): lax.all_to_all(jnp.broadcast_to(packed[None], (req_size,) + packed.shape)...  7.74 us
    all_to_all x1, starting transfers between devices, body(): lax.all_to_all(jnp.broadcast_to(packed[None], (req_size,) + packed.shape)...  7.62 us
    all_to_all x1, starting transfers between devices, body(): lax.all_to_all(send, 'req', 0, 0, tiled=True).reshape(req_size, req_dev, -1)  5.11 us
    dot_general x1, matrix products, body(): jnp.einsum('pqd,pkd->pqk', page_queries, kv_pages[:, 0], preferred_elemen...  3.08 us
    dot_general x1, matrix products, body(): jnp.dot(hidden, down_weight, preferred_element_type=jnp.float32)  2.52 us
  transfers between devices with their start and end apart: 8, of which 8 were waited for; matrix products, arithmetic and copies ran while one was open for 1% of the time, Pallas kernels for 0%

profile of v6, /device:TPU:2, one launch (start us, length us, event | category | flops | bytes accessed | tf_op | source)
XLA Modules:
  0.0 96.9 jit_solution(16884897534245886626)
XLA Ops:
  0.0 1.2 %multiply_reduce_fusion = f32[8,4]{1,0:T(8,128)S(1)} fusion(bf16[8,4,1536]{2,1,0:T(4,128)(2,1)} %param.13), kind=kLoop, calls=%fused_computation.38 | loop fusion | flops 147424 | bytes 98432 | tf_op jit(solution)/shard_map/reduce_sum | solution.py:14
  1.2 0.9 reshape.409
  2.1 0.7 copy.87
  2.9 0.8 multiply_convert_fusion
  3.7 1.2 %fusion.16 = bf16[32,128]{1,0:T(8,128)(2,1)S(1)} fusion(bf16[32,1536]{1,0:T(8,128)(2,1)S(1)} %multiply_convert_fusion, bf16[1536,128]{1,0:T(8,128)(2,1)} %param.18), kind=kOutput, calls=%fused_computation.21 | convolution fusion | flops 12591104 | bytes 499712 | tf_op jit(solution)/shard_map/dot_general | solution.py:60
  4.9 0.8 fusion.45
  5.8 0.7 broadcast_in_dim.61
  6.5 7.6 %all-to-all-start = ((bf16[32,8,532]{2,1,0:T(8,128)(2,1)}), bf16[32,8,532]{2,1,0:T(8,128)(2,1)S(1)}, u32[]{:S(2)}, u32[]{:S(2)}) async-start(bf16[32,8,532]{2,1,0:T(8,128)(2,1)} %broadcast_in_dim.61), calls=%async_computation | async-start | bytes 655360 | tf_op jit(solution)/shard_map/all_to_all | solution.py:75
  14.7 7.7 %all-to-all-done = bf16[32,8,532]{2,1,0:T(8,128)(2,1)S(1)} async-done(((bf16[32,8,532]{2,1,0:T(8,128)(2,1)}), bf16[32,8,532]{2,1,0:T(8,128)(2,1)S(1)}, u32[]{:S(2)}, u32[]{:S(2)}) %all-to-all-start) | async-done | bytes 272416 | tf_op jit(solution)/shard_map/all_to_all | solution.py:75
  23.2 1.3 %gather_fusion = s32[72]{0:T(128)S(1)} fusion(s32[256]{0:T(256)S(1)} %slice_reduce_fusion, s32[1024]{0:T(1024)S(1)} %pad_clamp_fusion), kind=kCustom, calls=%fused_computation | custom fusion | bytes 864 | tf_op jit(solution)/shard_map/gather | solution.py:93
  24.8 0.7 gather_fusion.1
  25.6 3.1 %fusion.61 = (f32[72,4]{1,0:T(8,128)S(1)}, f32[72,4,128]{2,1,0:T(4,128)S(1)}) fusion(bf16[72,4,128]{2,1,0:T(4,128)(2,1)S(1)} %gather_fusion.1, bf16[72,2,128,128]{3,2,1,0:T(8,128)(2,1)} %param.16, s32[72,4]{1,0:T(8,128)S(1)} %add_add_fusion, s32[72,128]{1,0:T(8,128)S(1)} %iota_add_fusion, pred[72,128]{1,0:T(8,128)(4,1)S(1)} %broadcast_compare_fusion), kind=kOutput, calls=%fused_computation.120 | convolution fusion | flops 9584352 | bytes 2628864 | tf_op jit(solution)/shard_map/pqd,pkd->pqk/dot_general | solution.py:104
  30.0 0.6 gather_fusion.2
  30.7 2.5 %fusion.9 = f32[72,4,128]{2,1,0:T(4,128)S(1)} fusion(bf16[72,2,128,128]{3,2,1,0:T(8,128)(2,1)} %param.16, f32[72,4]{1,0:T(8,128)S(1)} %get-tuple-element.12, f32[72,4,128]{2,1,0:T(4,128)S(1)} %get-tuple-element.23, f32[72,4]{1,0:T(8,128)S(1)} %get-tuple-element.22, s32[72,4]{1,0:T(8,128)S(1)} %add_add_fusion, s32[72,128]{1,0:T(8,128)S(1)} %iota_add_fusion, ...), kind=kOutput, calls=%fused_computation.13 | convolution fusion | flops 9658368 | bytes 2703744 | tf_op jit(solution)/shard_map/pqk,pkd->pqd/dot_general | solution.py:111
  33.2 0.5 convolution_convert_fusion.2
  33.8 0.8 pad_maximum_fusion
  34.7 5.1 %all-to-all-start.1 = ((bf16[32,8,528]{2,1,0:T(8,128)(2,1)}), bf16[32,8,528]{2,1,0:T(8,128)(2,1)S(1)}, u32[]{:S(2)}, u32[]{:S(2)}) async-start(bf16[32,8,528]{2,1,0:T(8,128)(2,1)} %pad_maximum_fusion), calls=%async_computation.1 | async-start | bytes 655360 | tf_op jit(solution)/shard_map/all_to_all | solution.py:145
  40.4 7.8 %all-to-all-done.1 = bf16[32,8,528]{2,1,0:T(8,128)(2,1)S(1)} async-done(((bf16[32,8,528]{2,1,0:T(8,128)(2,1)}), bf16[32,8,528]{2,1,0:T(8,128)(2,1)S(1)}, u32[]{:S(2)}, u32[]{:S(2)}) %all-to-all-start.1) | async-done | bytes 270368 | tf_op jit(solution)/shard_map/all_to_all | solution.py:145
  49.4 2.0 %collective-permute-start = (bf16[32,1536]{1,0:T(8,128)(2,1)S(1)}, bf16[32,1536]{1,0:T(8,128)(2,1)S(1)}, u32[]{:S(2)}, u32[]{:S(2)}) collective-permute-start(bf16[32,1536]{1,0:T(8,128)(2,1)S(1)} %convolution_convert_fusion.1), channel_id=1, source_target_pairs={{0,1},{1,0},{2,3},{3,2},{4,5},{5,4},{6,7},{7,6},{8,12},{9,13},{10,... | collective-permute-start | bytes 294920 | tf_op jit(solution)/shard_map/ppermute | solution.py:29
  51.4 2.7 %collective-permute-done = bf16[32,1536]{1,0:T(8,128)(2,1)S(1)} collective-permute-done((bf16[32,1536]{1,0:T(8,128)(2,1)S(1)}, bf16[32,1536]{1,0:T(8,128)(2,1)S(1)}, u32[]{:S(2)}, u32[]{:S(2)}) %collective-permute-start) | collective-permute-done | bytes 98336 | tf_op jit(solution)/shard_map/ppermute | solution.py:29
  54.1 3.4 %collective-permute-start.1 = (bf16[32,1536]{1,0:T(8,128)(2,1)S(1)}, bf16[32,1536]{1,0:T(8,128)(2,1)S(1)}, u32[]{:S(2)}, u32[]{:S(2)}) collective-permute-start(bf16[32,1536]{1,0:T(8,128)(2,1)S(1)} %add.201), channel_id=1, source_target_pairs={{0,2},{1,3},{2,0},{3,1},{4,6},{5,7},{6,4},{7,5},{8,10},{9,11},{10,... | collective-permute-start | bytes 294920 | tf_op jit(solution)/shard_map/ppermute | solution.py:29
  57.5 5.2 %collective-permute-done.1 = bf16[32,1536]{1,0:T(8,128)(2,1)S(1)} collective-permute-done((bf16[32,1536]{1,0:T(8,128)(2,1)S(1)}, bf16[32,1536]{1,0:T(8,128)(2,1)S(1)}, u32[]{:S(2)}, u32[]{:S(2)}) %collective-permute-start.1) | collective-permute-done | bytes 98336 | tf_op jit(solution)/shard_map/ppermute | solution.py:29
  62.7 5.7 %collective-permute-start.2 = (bf16[32,1536]{1,0:T(8,128)(2,1)S(1)}, bf16[32,1536]{1,0:T(8,128)(2,1)S(1)}, u32[]{:S(2)}, u32[]{:S(2)}) collective-permute-start(bf16[32,1536]{1,0:T(8,128)(2,1)S(1)} %add.202), channel_id=1, source_target_pairs={{0,4},{1,5},{2,6},{3,7},{4,0},{5,1},{6,2},{7,3},{8,9},{9,8},{10,11... | collective-permute-start | bytes 294920 | tf_op jit(solution)/shard_map/ppermute | solution.py:29
  68.4 3.0 %collective-permute-done.2 = bf16[32,1536]{1,0:T(8,128)(2,1)S(1)} collective-permute-done((bf16[32,1536]{1,0:T(8,128)(2,1)S(1)}, bf16[32,1536]{1,0:T(8,128)(2,1)S(1)}, u32[]{:S(2)}, u32[]{:S(2)}) %collective-permute-start.2) | collective-permute-done | bytes 98336 | tf_op jit(solution)/shard_map/ppermute | solution.py:29
  71.6 0.6 fusion.40
  72.2 2.5 %convolution_convert_fusion = bf16[32,1536]{1,0:T(8,128)(2,1)S(1)} fusion(bf16[576,1536]{1,0:T(8,128)(2,1)S(1)} %copy-done, bf16[1536,576]{0,1:T(8,128)(2,1)} %param.24, f32[32,576]{1,0:T(8,128)S(1)} %fusion.40, bf16[32,1536]{1,0:T(8,128)(2,1)S(1)} %get-tuple-element.6, f32[1536]{0:T(1024)S(1)} %copy-done.5, f32[32]{0:T(128)S(1)} %add_rsqrt_fusion.1), kind=kOutput, calls=%fused_computation.9 | convolution fusion | flops 113676288 | bytes 3815552 | tf_op jit(solution)/shard_map/dot_general | solution.py:196
  75.2 4.9 %collective-permute-done.3 = bf16[32,1536]{1,0:T(8,128)(2,1)S(1)} collective-permute-done((bf16[32,1536]{1,0:T(8,128)(2,1)S(1)}, bf16[32,1536]{1,0:T(8,128)(2,1)S(1)}, u32[]{:S(2)}, u32[]{:S(2)}) %collective-permute-start.3) | collective-permute-done | bytes 98336 | tf_op jit(solution)/shard_map/ppermute | solution.py:29
  80.1 3.8 %collective-permute-start.4 = (bf16[32,1536]{1,0:T(8,128)(2,1)S(1)}, bf16[32,1536]{1,0:T(8,128)(2,1)S(1)}, u32[]{:S(2)}, u32[]{:S(2)}) collective-permute-start(bf16[32,1536]{1,0:T(8,128)(2,1)S(1)} %add.209), channel_id=1, source_target_pairs={{0,2},{1,3},{2,0},{3,1},{4,6},{5,7},{6,4},{7,5},{8,10},{9,11},{10,... | collective-permute-start | bytes 294920 | tf_op jit(solution)/shard_map/ppermute | solution.py:29
  83.9 3.0 %collective-permute-done.4 = bf16[32,1536]{1,0:T(8,128)(2,1)S(1)} collective-permute-done((bf16[32,1536]{1,0:T(8,128)(2,1)S(1)}, bf16[32,1536]{1,0:T(8,128)(2,1)S(1)}, u32[]{:S(2)}, u32[]{:S(2)}) %collective-permute-start.4) | collective-permute-done | bytes 98336 | tf_op jit(solution)/shard_map/ppermute | solution.py:29
  87.0 6.1 %collective-permute-start.5 = (bf16[32,1536]{1,0:T(8,128)(2,1)S(1)}, bf16[32,1536]{1,0:T(8,128)(2,1)S(1)}, u32[]{:S(2)}, u32[]{:S(2)}) collective-permute-start(bf16[32,1536]{1,0:T(8,128)(2,1)S(1)} %add.210), channel_id=1, source_target_pairs={{0,4},{1,5},{2,6},{3,7},{4,0},{5,1},{6,2},{7,3},{8,9},{9,8},{10,11... | collective-permute-start | bytes 294920 | tf_op jit(solution)/shard_map/ppermute | solution.py:29
  93.0 3.2 %collective-permute-done.5 = bf16[32,1536]{1,0:T(8,128)(2,1)S(1)} collective-permute-done((bf16[32,1536]{1,0:T(8,128)(2,1)S(1)}, bf16[32,1536]{1,0:T(8,128)(2,1)S(1)}, u32[]{:S(2)}, u32[]{:S(2)}) %collective-permute-start.5) | collective-permute-done | bytes 98336 | tf_op jit(solution)/shard_map/ppermute | solution.py:29
  96.3 0.7 reshape.408
  (73 shorter events, 5.9 us)
Async XLA Ops:
  0.0 72.2 %copy-start = (bf16[576,1536]{1,0:T(8,128)(2,1)S(1)}, bf16[576,1536]{1,0:T(8,128)(2,1)}, u32[]{:S(2)}) copy-start(bf16[576,1536]{1,0:T(8,128)(2,1)} %param.25) | copy-start | bytes 5308420
  0.0 14.1 %copy-start.2 = (bf16[1536,128]{1,0:T(8,128)(2,1)S(1)}, bf16[1536,128]{1,0:T(8,128)(2,1)}, u32[]{:S(2)}) copy-start(bf16[1536,128]{1,0:T(8,128)(2,1)} %param.19) | copy-start | bytes 1179652
  6.5 15.9 %all-to-all-start = ((bf16[32,8,532]{2,1,0:T(8,128)(2,1)}), bf16[32,8,532]{2,1,0:T(8,128)(2,1)S(1)}, u32[]{:S(2)}, u32[]{:S(2)}) async-start(bf16[32,8,532]{2,1,0:T(8,128)(2,1)} %broadcast_in_dim.61), calls=%async_computation | async-start | bytes 655360 | tf_op jit(solution)/shard_map/all_to_all | solution.py:75
  33.1 7.0 %copy-start.3 = (bf16[1536,128]{1,0:T(8,128)(2,1)S(1)}, bf16[1536,128]{1,0:T(8,128)(2,1)}, u32[]{:S(2)}) copy-start(bf16[1536,128]{1,0:T(8,128)(2,1)} %param.20) | copy-start | bytes 1179652
  34.7 14.5 %copy-start.4 = (bf16[128,1536]{1,0:T(8,128)(2,1)S(1)}, bf16[128,1536]{1,0:T(8,128)(2,1)}, u32[]{:S(2)}) copy-start(bf16[128,1536]{1,0:T(8,128)(2,1)} %param.21) | copy-start | bytes 1179652
  34.7 13.5 %all-to-all-start.1 = ((bf16[32,8,528]{2,1,0:T(8,128)(2,1)}), bf16[32,8,528]{2,1,0:T(8,128)(2,1)S(1)}, u32[]{:S(2)}, u32[]{:S(2)}) async-start(bf16[32,8,528]{2,1,0:T(8,128)(2,1)} %pad_maximum_fusion), calls=%async_computation.1 | async-start | bytes 655360 | tf_op jit(solution)/shard_map/all_to_all | solution.py:145
  40.4 31.2 %copy-start.5 = (f32[1536]{0:T(1024)S(1)}, f32[1536]{0:T(1024)}, u32[]{:S(2)}) copy-start(f32[1536]{0:T(1024)} %param.22) | copy-start | bytes 18436
  49.0 22.5 %copy-start.1 = (bf16[1536,576]{0,1:T(8,128)(2,1)S(1)}, bf16[1536,576]{0,1:T(8,128)(2,1)}, u32[]{:S(2)}) copy-start(bf16[1536,576]{0,1:T(8,128)(2,1)} %param.23) | copy-start | bytes 5308420
  49.4 4.7 %collective-permute-start = (bf16[32,1536]{1,0:T(8,128)(2,1)S(1)}, bf16[32,1536]{1,0:T(8,128)(2,1)S(1)}, u32[]{:S(2)}, u32[]{:S(2)}) collective-permute-start(bf16[32,1536]{1,0:T(8,128)(2,1)S(1)} %convolution_convert_fusion.1), channel_id=1, source_target_pairs={{0,1},{1,0},{2,3},{3,2},{4,5},{5,4},{6,7},{7,6},{8,12},{9,13},{10,... | collective-permute-start | bytes 294920 | tf_op jit(solution)/shard_map/ppermute | solution.py:29
  54.1 8.6 %collective-permute-start.1 = (bf16[32,1536]{1,0:T(8,128)(2,1)S(1)}, bf16[32,1536]{1,0:T(8,128)(2,1)S(1)}, u32[]{:S(2)}, u32[]{:S(2)}) collective-permute-start(bf16[32,1536]{1,0:T(8,128)(2,1)S(1)} %add.201), channel_id=1, source_target_pairs={{0,2},{1,3},{2,0},{3,1},{4,6},{5,7},{6,4},{7,5},{8,10},{9,11},{10,... | collective-permute-start | bytes 294920 | tf_op jit(solution)/shard_map/ppermute | solution.py:29
  62.7 8.6 %collective-permute-start.2 = (bf16[32,1536]{1,0:T(8,128)(2,1)S(1)}, bf16[32,1536]{1,0:T(8,128)(2,1)S(1)}, u32[]{:S(2)}, u32[]{:S(2)}) collective-permute-start(bf16[32,1536]{1,0:T(8,128)(2,1)S(1)} %add.202), channel_id=1, source_target_pairs={{0,4},{1,5},{2,6},{3,7},{4,0},{5,1},{6,2},{7,3},{8,9},{9,8},{10,11... | collective-permute-start | bytes 294920 | tf_op jit(solution)/shard_map/ppermute | solution.py:29
  74.7 5.3 %collective-permute-start.3 = (bf16[32,1536]{1,0:T(8,128)(2,1)S(1)}, bf16[32,1536]{1,0:T(8,128)(2,1)S(1)}, u32[]{:S(2)}, u32[]{:S(2)}) collective-permute-start(bf16[32,1536]{1,0:T(8,128)(2,1)S(1)} %convolution_convert_fusion), channel_id=1, source_target_pairs={{0,1},{1,0},{2,3},{3,2},{4,5},{5,4},{6,7},{7,6},{8,12},{9,13},{10,... | collective-permute-start | bytes 294920 | tf_op jit(solution)/shard_map/ppermute | solution.py:29
  80.1 6.9 %collective-permute-start.4 = (bf16[32,1536]{1,0:T(8,128)(2,1)S(1)}, bf16[32,1536]{1,0:T(8,128)(2,1)S(1)}, u32[]{:S(2)}, u32[]{:S(2)}) collective-permute-start(bf16[32,1536]{1,0:T(8,128)(2,1)S(1)} %add.209), channel_id=1, source_target_pairs={{0,2},{1,3},{2,0},{3,1},{4,6},{5,7},{6,4},{7,5},{8,10},{9,11},{10,... | collective-permute-start | bytes 294920 | tf_op jit(solution)/shard_map/ppermute | solution.py:29
  87.0 9.3 %collective-permute-start.5 = (bf16[32,1536]{1,0:T(8,128)(2,1)S(1)}, bf16[32,1536]{1,0:T(8,128)(2,1)S(1)}, u32[]{:S(2)}, u32[]{:S(2)}) collective-permute-start(bf16[32,1536]{1,0:T(8,128)(2,1)S(1)} %add.210), channel_id=1, source_target_pairs={{0,4},{1,5},{2,6},{3,7},{4,0},{5,1},{6,2},{7,3},{8,9},{9,8},{10,11... | collective-permute-start | bytes 294920 | tf_op jit(solution)/shard_map/ppermute | solution.py:29

commit v7 on v6

--- a/solution.py
+++ b/solution.py
@@ -28,6 +28,20 @@
                 pairs.append((q * tp_size + t, q * tp_size + (t ^ order[round_index])))
         values = values + lax.ppermute(values, ("req", "tp"), pairs)
     return values
+
+
+def tree_gather(values, axis, size):
+    index = lax.axis_index(axis)
+    parts = values[None]
+    step = 1
+    while step < size:
+        other = lax.ppermute(parts, axis, [(i, i ^ step) for i in range(size)])
+        upper = (index // step) % 2 == 1
+        parts = jnp.concatenate(
+            [jnp.where(upper, other, parts), jnp.where(upper, parts, other)], axis=0
+        )
+        step *= 2
+    return parts
 
 
 def make_body(req_size, tp_size):
@@ -55,6 +69,9 @@
         requests = req_dev * req_size
         qwidth = steps * heads_dev * head_dim
         token_rows = tokens.reshape(req_dev * steps, width)
+        full_out_weight = lax.all_to_all(
+            jnp.broadcast_to(out_weight[None], (tp_size,) + out_weight.shape), "tp", 0, 0, tiled=False
+        ).reshape(tp_size * out_weight.shape[0], width)
         normed = rms_norm(token_rows.astype(jnp.float32), norm_gain).astype(jnp.bfloat16)
         queries = (
             jnp.dot(normed, query_weight, preferred_element_type=jnp.float32) * head_dim ** (-0.5)
@@ -186,8 +203,9 @@
             .astype(jnp.bfloat16)
             .reshape(req_dev * steps, heads_dev * head_dim)
         )
-        projected = jnp.dot(attended, out_weight, preferred_element_type=jnp.float32)
-        attn_total = staggered_sum(projected.astype(jnp.bfloat16), req_size, tp_size).astype(jnp.float32)
+        all_heads = tree_gather(attended, "tp", tp_size)
+        all_heads = jnp.moveaxis(all_heads, 0, 1).reshape(req_dev * steps, -1)
+        attn_total = jnp.dot(all_heads, full_out_weight, preferred_element_type=jnp.float32)
         residual = (token_rows.astype(jnp.float32) + attn_total).astype(jnp.bfloat16)
         mlp_in = rms_norm(residual.astype(jnp.float32), mlp_gain).astype(jnp.bfloat16)
         gate = jnp.dot(mlp_in, gate_weight, preferred_element_type=jnp.float32)

time: 98.4 us -> 172 us (1.75)
  waiting for transfers between devices: 37.5 us -> 101 us
  blocking collectives: 0 us -> 13 us
  starting transfers between devices: 34.1 us -> 27 us
  matrix products: 11.1 us -> 15.1 us
  local copies, waits for them, and re-layouts: 7.89 us -> 9.98 us
    ppermute x0 -> x3, waiting for transfers between devices: none -> 74.1 us  [tree_gather(): other = lax.ppermute(parts, axis, [(i, i ^ step) for i in range(size)])]
    ppermute x6 -> x3, starting transfers between devices: 21.4 us -> 3.77 us  [staggered_sum(): values = values + lax.ppermute(values, ('req', 'tp'), pairs)]
    all_to_all x0 -> x1, blocking collectives: none -> 13 us  [body(): lax.all_to_all(send, 'req', 0, 0, tiled=True).reshape(req_size, req_dev, -1)]
    all_to_all x1, waiting for transfers between devices: 7.79 us -> 0.01 us  [body(): lax.all_to_all(jnp.broadcast_to(out_weight[None], (tp_size,) + out_weight...]
    ppermute x0 -> x3, starting transfers between devices: none -> 7.02 us  [tree_gather(): other = lax.ppermute(parts, axis, [(i, i ^ step) for i in range(size)])]
    all_to_all x1, starting transfers between devices: 5.11 us -> 8.6 us  [body(): lax.all_to_all(jnp.broadcast_to(out_weight[None], (tp_size,) + out_weight...]
    ppermute x6 -> x3, waiting for transfers between devices: 22 us -> 18.7 us  [staggered_sum(): values = values + lax.ppermute(values, ('req', 'tp'), pairs)]
    dot_general x1, matrix products: 0.17 us -> 2.64 us  [body(): jnp.dot(all_heads, full_out_weight, preferred_element_type=jnp.float32)]
  transfers between devices with their start and end apart: 8 -> 8, of which waited for: 8 -> 7; matrix products, arithmetic and copies ran while one was open for 1% -> 1% of each run, Pallas kernels for 0% -> 0%
where the time goes in v7:
time: 172 us; the launch traced here: 171 us
  waiting for transfers between devices  101 us (59%)
  starting transfers between devices  27 us (16%)
  matrix products  15.1 us (9%)
  blocking collectives  13 us (8%)
  local copies, waits for them, and re-layouts  9.98 us (6%)
  other arithmetic  4.95 us (3%)
    ppermute x3, waiting for transfers between devices, tree_gather(): other = lax.ppermute(parts, axis, [(i, i ^ step) for i in range(size)])  74.1 us
    ppermute x3, waiting for transfers between devices, staggered_sum(): values = values + lax.ppermute(values, ('req', 'tp'), pairs)  18.7 us
    all_to_all x1, blocking collectives, body(): lax.all_to_all(send, 'req', 0, 0, tiled=True).reshape(req_size, req_dev, -1)  13 us
    all_to_all x1, starting transfers between devices, body(): lax.all_to_all(jnp.broadcast_to(out_weight[None], (tp_size,) + out_weight...  8.6 us
    all_to_all x1, waiting for transfers between devices, body(): lax.all_to_all(jnp.broadcast_to(packed[None], (req_size,) + packed.shape)...  8.25 us
    all_to_all x1, starting transfers between devices, body(): lax.all_to_all(jnp.broadcast_to(packed[None], (req_size,) + packed.shape)...  7.62 us
    ppermute x3, starting transfers between devices, tree_gather(): other = lax.ppermute(parts, axis, [(i, i ^ step) for i in range(size)])  7.02 us
    ppermute x3, starting transfers between devices, staggered_sum(): values = values + lax.ppermute(values, ('req', 'tp'), pairs)  3.77 us
  transfers between devices with their start and end apart: 8, of which 7 were waited for; matrix products, arithmetic and copies ran while one was open for 1% of the time, Pallas kernels for 0%

profile of v7, /device:TPU:2, one launch (start us, length us, event | category | flops | bytes accessed | tf_op | source)
XLA Modules:
  0.0 171.5 jit_solution(9783443676375568998)
XLA Ops:
  0.0 1.0 reshape.408
  1.0 1.0 multiply_reduce_fusion.1
  2.1 0.7 copy.87
  2.9 0.8 multiply_convert_fusion.1
  3.7 1.2 fusion.19
  4.9 0.8 fusion.42
  5.8 0.7 broadcast_in_dim.59
  6.5 7.6 %all-to-all-start = ((bf16[32,8,532]{2,1,0:T(8,128)(2,1)}), bf16[32,8,532]{2,1,0:T(8,128)(2,1)S(1)}, u32[]{:S(2)}, u32[]{:S(2)}) async-start(bf16[32,8,532]{2,1,0:T(8,128)(2,1)} %broadcast_in_dim.59), calls=%async_computation | async-start | bytes 655360 | tf_op jit(solution)/shard_map/all_to_all | solution.py:92
  14.1 8.3 %all-to-all-done = bf16[32,8,532]{2,1,0:T(8,128)(2,1)S(1)} async-done(((bf16[32,8,532]{2,1,0:T(8,128)(2,1)}), bf16[32,8,532]{2,1,0:T(8,128)(2,1)S(1)}, u32[]{:S(2)}, u32[]{:S(2)}) %all-to-all-start) | async-done | bytes 272416 | tf_op jit(solution)/shard_map/all_to_all | solution.py:92
  23.2 1.3 gather_fusion
  24.8 0.7 gather_fusion.1
  25.5 3.1 %fusion.60 = (f32[72,4]{1,0:T(8,128)S(1)}, f32[72,4,128]{2,1,0:T(4,128)S(1)}) fusion(bf16[72,4,128]{2,1,0:T(4,128)(2,1)S(1)} %gather_fusion.1, bf16[72,2,128,128]{3,2,1,0:T(8,128)(2,1)} %param.16, s32[72,4]{1,0:T(8,128)S(1)} %add_add_fusion, s32[72,128]{1,0:T(8,128)S(1)} %iota_add_fusion, pred[72,128]{1,0:T(8,128)(4,1)S(1)} %broadcast_compare_fusion), kind=kOutput, calls=%fused_computation.130 | convolution fusion | flops 9584352 | bytes 2628864 | tf_op jit(solution)/shard_map/pqd,pkd->pqk/dot_general | solution.py:121
  30.0 0.6 gather_fusion.2
  30.7 2.5 %fusion.12 = f32[72,4,128]{2,1,0:T(4,128)S(1)} fusion(bf16[72,2,128,128]{3,2,1,0:T(8,128)(2,1)} %param.16, f32[72,4]{1,0:T(8,128)S(1)} %get-tuple-element.10, f32[72,4,128]{2,1,0:T(4,128)S(1)} %get-tuple-element.27, f32[72,4]{1,0:T(8,128)S(1)} %get-tuple-element.26, s32[72,4]{1,0:T(8,128)S(1)} %add_add_fusion, s32[72,128]{1,0:T(8,128)S(1)} %iota_add_fusion, ...), kind=kOutput, calls=%fused_computation.16 | convolution fusion | flops 9658368 | bytes 2703744 | tf_op jit(solution)/shard_map/pqk,pkd->pqd/dot_general | solution.py:128
  34.0 13.0 %all_to_all.16 = bf16[32,8,528]{2,1,0:T(8,128)(2,1)S(1)} all-to-all(bf16[32,8,528]{2,1,0:T(8,128)(2,1)S(1)} %pad_maximum_fusion), channel_id=1, replica_groups=mesh['req'=32,'tp'=8] {'req'}, dimensions={0} | all-to-all | bytes 540672 | tf_op jit(solution)/shard_map/all_to_all | solution.py:162
  47.0 2.0 %broadcast_in_dim.114 = bf16[8,128,1536]{2,1,0:T(8,128)(2,1)} broadcast(bf16[128,1536]{1,0:T(8,128)(2,1)S(1)} %copy-done.1), dimensions={1,2} | broadcast | bytes 3538944 | tf_op jit(solution)/shard_map/broadcast_in_dim | solution.py:73
  49.0 8.6 %all-to-all-start.2 = ((bf16[8,128,1536]{2,1,0:T(8,128)(2,1)}), bf16[8,128,1536]{2,1,0:T(8,128)(2,1)}, u32[]{:S(2)}, u32[]{:S(2)}) async-start(bf16[8,128,1536]{2,1,0:T(8,128)(2,1)} %broadcast_in_dim.114), calls=%async_computation.2 | async-start | bytes 6291456 | tf_op jit(solution)/shard_map/all_to_all | solution.py:72
  59.7 2.1 %collective-permute-start = (bf16[1,32,128]{2,1,0:T(8,128)(2,1)S(1)}, bf16[1,32,128]{2,1,0:T(8,128)(2,1)S(1)}, u32[]{:S(2)}, u32[]{:S(2)}) collective-permute-start(bf16[1,32,128]{2,1,0:T(8,128)(2,1)S(1)} %bitcast.86), channel_id=1, source_target_pairs={{0,1},{1,0},{2,3},{3,2},{4,5},{5,4},{6,7},{7,6},{8,9},{9,8},{10,11... | collective-permute-start | bytes 24584 | tf_op jit(solution)/shard_map/ppermute | solution.py:38
  61.9 66.4 %collective-permute-done = bf16[1,32,128]{2,1,0:T(8,128)(2,1)S(1)} collective-permute-done((bf16[1,32,128]{2,1,0:T(8,128)(2,1)S(1)}, bf16[1,32,128]{2,1,0:T(8,128)(2,1)S(1)}, u32[]{:S(2)}, u32[]{:S(2)}) %collective-permute-start) | collective-permute-done | bytes 8224 | tf_op jit(solution)/shard_map/ppermute | solution.py:38
  128.6 4.4 %collective-permute-done.1 = bf16[2,32,128]{2,1,0:T(8,128)(2,1)S(1)} collective-permute-done((bf16[2,32,128]{2,1,0:T(8,128)(2,1)S(1)}, bf16[2,32,128]{2,1,0:T(8,128)(2,1)S(1)}, u32[]{:S(2)}, u32[]{:S(2)}) %collective-permute-start.1) | collective-permute-done | bytes 16416 | tf_op jit(solution)/shard_map/ppermute | solution.py:38
  133.0 4.6 %collective-permute-start.2 = (bf16[4,32,128]{2,1,0:T(8,128)(2,1)S(1)}, bf16[4,32,128]{2,1,0:T(8,128)(2,1)S(1)}, u32[]{:S(2)}, u32[]{:S(2)}) collective-permute-start(bf16[4,32,128]{2,1,0:T(8,128)(2,1)S(1)} %pad_maximum_fusion.1), channel_id=1, source_target_pairs={{0,4},{1,5},{2,6},{3,7},{4,0},{5,1},{6,2},{7,3},{8,12},{9,13},{10,... | collective-permute-start | bytes 98312 | tf_op jit(solution)/shard_map/ppermute | solution.py:38
  137.5 3.3 %collective-permute-done.2 = bf16[4,32,128]{2,1,0:T(8,128)(2,1)S(1)} collective-permute-done((bf16[4,32,128]{2,1,0:T(8,128)(2,1)S(1)}, bf16[4,32,128]{2,1,0:T(8,128)(2,1)S(1)}, u32[]{:S(2)}, u32[]{:S(2)}) %collective-permute-start.2) | collective-permute-done | bytes 32800 | tf_op jit(solution)/shard_map/ppermute | solution.py:38
  140.9 2.6 %multiply_reduce_fusion = (f32[32]{0:T(128)S(1)}, f32[32,1536]{1,0:T(8,128)S(1)}) fusion(f32[32,1536]{1,0:T(8,128)S(1)} %reshape.408, bf16[8,128,1536]{2,1,0:T(8,128)(2,1)} %all-to-all-done.2, bf16[4,32,128]{2,1,0:T(8,128)(2,1)S(1)} %get-tuple-element.14, bf16[4,32,128]{2,1,0:T(8,128)(2,1)S(1)} %get-tuple-element.13), kind=kOutput, calls=%fused_computation.34 | convolution fusion | flops 100941792 | bytes 3604608 | tf_op jit(solution)/shard_map/dot_general | solution.py:208
  143.6 2.1 %fusion.57 = f32[32,576]{1,0:T(8,128)S(1)} fusion(bf16[1536,576]{0,1:T(8,128)(2,1)} %param.23, f32[32,1536]{1,0:T(8,128)S(1)} %get-tuple-element.29, f32[1536]{0:T(1024)S(1)} %copy-done.4, f32[32]{0:T(128)S(1)} %add_rsqrt_fusion.1), kind=kOutput, calls=%fused_computation.127 | convolution fusion | flops 56770560 | bytes 2046080 | tf_op jit(solution)/shard_map/dot_general | solution.py:211
  145.7 2.5 %convolution_convert_fusion = bf16[32,1536]{1,0:T(8,128)(2,1)S(1)} fusion(bf16[576,1536]{1,0:T(8,128)(2,1)S(1)} %copy-done, bf16[1536,576]{0,1:T(8,128)(2,1)} %param.24, f32[32,576]{1,0:T(8,128)S(1)} %fusion.57, f32[32,1536]{1,0:T(8,128)S(1)} %get-tuple-element.29, f32[1536]{0:T(1024)S(1)} %copy-done.4, f32[32]{0:T(128)S(1)} %add_rsqrt_fusion.1), kind=kOutput, calls=%fused_computation.13 | convolution fusion | flops 113627136 | bytes 3913856 | tf_op jit(solution)/shard_map/dot_general | solution.py:214
  148.2 0.6 collective-permute-start.3
  148.8 4.8 %collective-permute-done.3 = bf16[32,1536]{1,0:T(8,128)(2,1)S(1)} collective-permute-done((bf16[32,1536]{1,0:T(8,128)(2,1)S(1)}, bf16[32,1536]{1,0:T(8,128)(2,1)S(1)}, u32[]{:S(2)}, u32[]{:S(2)}) %collective-permute-start.3) | collective-permute-done | bytes 98336 | tf_op jit(solution)/shard_map/ppermute | solution.py:29
  153.6 1.8 %collective-permute-start.4 = (bf16[32,1536]{1,0:T(8,128)(2,1)S(1)}, bf16[32,1536]{1,0:T(8,128)(2,1)S(1)}, u32[]{:S(2)}, u32[]{:S(2)}) collective-permute-start(bf16[32,1536]{1,0:T(8,128)(2,1)S(1)} %add.213), channel_id=1, source_target_pairs={{0,2},{1,3},{2,0},{3,1},{4,6},{5,7},{6,4},{7,5},{8,10},{9,11},{10,... | collective-permute-start | bytes 294920 | tf_op jit(solution)/shard_map/ppermute | solution.py:29
  155.4 6.4 %collective-permute-done.4 = bf16[32,1536]{1,0:T(8,128)(2,1)S(1)} collective-permute-done((bf16[32,1536]{1,0:T(8,128)(2,1)S(1)}, bf16[32,1536]{1,0:T(8,128)(2,1)S(1)}, u32[]{:S(2)}, u32[]{:S(2)}) %collective-permute-start.4) | collective-permute-done | bytes 98336 | tf_op jit(solution)/shard_map/ppermute | solution.py:29
  161.8 1.4 collective-permute-start.5
  163.2 7.6 %collective-permute-done.5 = bf16[32,1536]{1,0:T(8,128)(2,1)S(1)} collective-permute-done((bf16[32,1536]{1,0:T(8,128)(2,1)S(1)}, bf16[32,1536]{1,0:T(8,128)(2,1)S(1)}, u32[]{:S(2)}, u32[]{:S(2)}) %collective-permute-start.5) | collective-permute-done | bytes 98336 | tf_op jit(solution)/shard_map/ppermute | solution.py:29
  170.8 0.7 reshape.407
  (75 shorter events, 6.1 us)
Async XLA Ops:
  0.0 145.7 %copy-start = (bf16[576,1536]{1,0:T(8,128)(2,1)S(1)}, bf16[576,1536]{1,0:T(8,128)(2,1)}, u32[]{:S(2)}) copy-start(bf16[576,1536]{1,0:T(8,128)(2,1)} %param.25) | copy-start | bytes 5308420
  6.5 15.9 %all-to-all-start = ((bf16[32,8,532]{2,1,0:T(8,128)(2,1)}), bf16[32,8,532]{2,1,0:T(8,128)(2,1)S(1)}, u32[]{:S(2)}, u32[]{:S(2)}) async-start(bf16[32,8,532]{2,1,0:T(8,128)(2,1)} %broadcast_in_dim.59), calls=%async_computation | async-start | bytes 655360 | tf_op jit(solution)/shard_map/all_to_all | solution.py:92
  30.6 16.4 %copy-start.1 = (bf16[128,1536]{1,0:T(8,128)(2,1)S(1)}, bf16[128,1536]{1,0:T(8,128)(2,1)}, u32[]{:S(2)}) copy-start(bf16[128,1536]{1,0:T(8,128)(2,1)} %param.21) | copy-start | bytes 1179652
  49.0 8.6 %copy-start.2 = (bf16[1536,128]{1,0:T(8,128)(2,1)S(1)}, bf16[1536,128]{1,0:T(8,128)(2,1)}, u32[]{:S(2)}) copy-start(bf16[1536,128]{1,0:T(8,128)(2,1)} %param.19) | copy-start | bytes 1179652
  49.0 9.5 %copy-start.3 = (bf16[1536,128]{1,0:T(8,128)(2,1)S(1)}, bf16[1536,128]{1,0:T(8,128)(2,1)}, u32[]{:S(2)}) copy-start(bf16[1536,128]{1,0:T(8,128)(2,1)} %param.20) | copy-start | bytes 1179652
  49.0 91.9 %all-to-all-start.2 = ((bf16[8,128,1536]{2,1,0:T(8,128)(2,1)}), bf16[8,128,1536]{2,1,0:T(8,128)(2,1)}, u32[]{:S(2)}, u32[]{:S(2)}) async-start(bf16[8,128,1536]{2,1,0:T(8,128)(2,1)} %broadcast_in_dim.114), calls=%async_computation.2 | async-start | bytes 6291456 | tf_op jit(solution)/shard_map/all_to_all | solution.py:72
  59.4 84.2 %copy-start.4 = (f32[1536]{0:T(1024)S(1)}, f32[1536]{0:T(1024)}, u32[]{:S(2)}) copy-start(f32[1536]{0:T(1024)} %param.22) | copy-start | bytes 18436
  59.7 68.5 %collective-permute-start = (bf16[1,32,128]{2,1,0:T(8,128)(2,1)S(1)}, bf16[1,32,128]{2,1,0:T(8,128)(2,1)S(1)}, u32[]{:S(2)}, u32[]{:S(2)}) collective-permute-start(bf16[1,32,128]{2,1,0:T(8,128)(2,1)S(1)} %bitcast.86), channel_id=1, source_target_pairs={{0,1},{1,0},{2,3},{3,2},{4,5},{5,4},{6,7},{7,6},{8,9},{9,8},{10,11... | collective-permute-start | bytes 24584 | tf_op jit(solution)/shard_map/ppermute | solution.py:38
  128.2 4.7 %collective-permute-start.1 = (bf16[2,32,128]{2,1,0:T(8,128)(2,1)S(1)}, bf16[2,32,128]{2,1,0:T(8,128)(2,1)S(1)}, u32[]{:S(2)}, u32[]{:S(2)}) collective-permute-start(bf16[2,32,128]{2,1,0:T(8,128)(2,1)S(1)} %pad_maximum_fusion.2), channel_id=1, source_target_pairs={{0,2},{1,3},{2,0},{3,1},{4,6},{5,7},{6,4},{7,5},{8,10},{9,11},{10,... | collective-permute-start | bytes 49160 | tf_op jit(solution)/shard_map/ppermute | solution.py:38
  133.0 7.9 %collective-permute-start.2 = (bf16[4,32,128]{2,1,0:T(8,128)(2,1)S(1)}, bf16[4,32,128]{2,1,0:T(8,128)(2,1)S(1)}, u32[]{:S(2)}, u32[]{:S(2)}) collective-permute-start(bf16[4,32,128]{2,1,0:T(8,128)(2,1)S(1)} %pad_maximum_fusion.1), channel_id=1, source_target_pairs={{0,4},{1,5},{2,6},{3,7},{4,0},{5,1},{6,2},{7,3},{8,12},{9,13},{10,... | collective-permute-start | bytes 98312 | tf_op jit(solution)/shard_map/ppermute | solution.py:38
  148.2 5.4 %collective-permute-start.3 = (bf16[32,1536]{1,0:T(8,128)(2,1)S(1)}, bf16[32,1536]{1,0:T(8,128)(2,1)S(1)}, u32[]{:S(2)}, u32[]{:S(2)}) collective-permute-start(bf16[32,1536]{1,0:T(8,128)(2,1)S(1)} %convolution_convert_fusion), channel_id=1, source_target_pairs={{0,1},{1,0},{2,3},{3,2},{4,5},{5,4},{6,7},{7,6},{8,12},{9,13},{10,... | collective-permute-start | bytes 294920 | tf_op jit(solution)/shard_map/ppermute | solution.py:29
  153.6 8.2 %collective-permute-start.4 = (bf16[32,1536]{1,0:T(8,128)(2,1)S(1)}, bf16[32,1536]{1,0:T(8,128)(2,1)S(1)}, u32[]{:S(2)}, u32[]{:S(2)}) collective-permute-start(bf16[32,1536]{1,0:T(8,128)(2,1)S(1)} %add.213), channel_id=1, source_target_pairs={{0,2},{1,3},{2,0},{3,1},{4,6},{5,7},{6,4},{7,5},{8,10},{9,11},{10,... | collective-permute-start | bytes 294920 | tf_op jit(solution)/shard_map/ppermute | solution.py:29
  161.8 8.9 %collective-permute-start.5 = (bf16[32,1536]{1,0:T(8,128)(2,1)S(1)}, bf16[32,1536]{1,0:T(8,128)(2,1)S(1)}, u32[]{:S(2)}, u32[]{:S(2)}) collective-permute-start(bf16[32,1536]{1,0:T(8,128)(2,1)S(1)} %add.214), channel_id=1, source_target_pairs={{0,4},{1,5},{2,6},{3,7},{4,0},{5,1},{6,2},{7,3},{8,9},{9,8},{10,11... | collective-permute-start | bytes 294920 | tf_op jit(solution)/shard_map/ppermute | solution.py:29

commit v8 on v6

--- a/solution.py
+++ b/solution.py
@@ -55,20 +55,24 @@
         requests = req_dev * req_size
         qwidth = steps * heads_dev * head_dim
         token_rows = tokens.reshape(req_dev * steps, width)
-        normed = rms_norm(token_rows.astype(jnp.float32), norm_gain).astype(jnp.bfloat16)
+        normed3 = rms_norm(tokens.astype(jnp.float32), norm_gain).astype(jnp.bfloat16)
+        normed = normed3.reshape(req_dev * steps, width)
         queries = (
-            jnp.dot(normed, query_weight, preferred_element_type=jnp.float32) * head_dim ** (-0.5)
-        ).astype(jnp.bfloat16)
+            jnp.einsum("rsd,dh->rsh", normed3, query_weight, preferred_element_type=jnp.float32)
+            * head_dim ** (-0.5)
+        ).astype(jnp.bfloat16).reshape(req_dev * steps, heads_dev * head_dim)
         key_new = jnp.dot(normed, key_weight, preferred_element_type=jnp.float32).astype(jnp.bfloat16)
         value_new = jnp.dot(normed, value_weight, preferred_element_type=jnp.float32).astype(
             jnp.bfloat16
         )
-        ints = jnp.concatenate([page_table, lengths.reshape(req_dev, 1)], axis=1)
+        length_col = jnp.broadcast_to(lengths[:, None], (req_dev, 1))
         packed = jnp.concatenate(
             [
                 queries.reshape(req_dev, qwidth),
-                (ints // 256).astype(jnp.bfloat16),
-                (ints % 256).astype(jnp.bfloat16),
+                (page_table // 256).astype(jnp.bfloat16),
+                (length_col // 256).astype(jnp.bfloat16),
+                (page_table % 256).astype(jnp.bfloat16),
+                (length_col % 256).astype(jnp.bfloat16),
             ],
             axis=1,
         )

time: 98.4 us -> 109 us (1.11)
  other arithmetic: 5.97 us -> 12.2 us
  local copies, waits for them, and re-layouts: 7.89 us -> 12.7 us
  matrix products: 11.1 us -> 14.1 us
  starting transfers between devices: 34.1 us -> 31.9 us
    reduce_sum x1, other arithmetic: 0.15 us -> 2.32 us  [body(): total = jnp.sum(got_total * src_scale, axis=0) + new_total * new_scale]
    ppermute x6, starting transfers between devices: 21.4 us -> 19.2 us  [staggered_sum(): values = values + lax.ppermute(values, ('req', 'tp'), pairs)]
    all_to_all x1, waiting for transfers between devices: 7.79 us -> 6.03 us  [body(): lax.all_to_all(send, 'req', 0, 0, tiled=True).reshape(req_size, req_dev, -1)]
    exp x1, local copies, waits for them, and re-layouts: 0.25 us -> 1.79 us  [body(): src_scale = jnp.exp(got_max - overall[None])]
    unnamed x13 -> x22, local copies, waits for them, and re-layouts: 0.04 us -> 1.39 us
    ppermute x6, waiting for transfers between devices: 22 us -> 23.2 us  [staggered_sum(): values = values + lax.ppermute(values, ('req', 'tp'), pairs)]
    convert_element_type x2 -> x3, other arithmetic: 1.56 us -> 2.38 us  [the longest x1 1.02 us: body(): rms_norm(tokens.astype(jnp.float32), norm_gain).astype(jnp.bfloat16)]
  transfers between devices with their start and end apart: 8 -> 8, of which waited for: 8 -> 8; matrix products, arithmetic and copies ran while one was open for 1% -> 4% of each run, Pallas kernels for 0% -> 0%
where the time goes in v8:
time: 109 us; the launch traced here: 108 us
  waiting for transfers between devices  36.9 us (34%)
  starting transfers between devices  31.9 us (29%)
  matrix products  14.1 us (13%)
  local copies, waits for them, and re-layouts  12.7 us (12%)
  other arithmetic  12.2 us (11%)
    ppermute x6, waiting for transfers between devices, staggered_sum(): values = values + lax.ppermute(values, ('req', 'tp'), pairs)  23.2 us
    ppermute x6, starting transfers between devices, staggered_sum(): values = values + lax.ppermute(values, ('req', 'tp'), pairs)  19.2 us
    all_to_all x1, waiting for transfers between devices, body(): lax.all_to_all(jnp.broadcast_to(packed[None], (req_size,) + packed.shape)...  7.71 us
    all_to_all x1, starting transfers between devices, body(): lax.all_to_all(jnp.broadcast_to(packed[None], (req_size,) + packed.shape)...  7.62 us
    all_to_all x1, waiting for transfers between devices, body(): lax.all_to_all(send, 'req', 0, 0, tiled=True).reshape(req_size, req_dev, -1)  6.03 us
    all_to_all x1, starting transfers between devices, body(): lax.all_to_all(send, 'req', 0, 0, tiled=True).reshape(req_size, req_dev, -1)  4.98 us
    dot_general x1, matrix products, body(): jnp.einsum('pqd,pkd->pqk', page_queries, kv_pages[:, 0], preferred_elemen...  3.08 us
    dot_general x1, matrix products, body(): jnp.dot(hidden, down_weight, preferred_element_type=jnp.float32)  2.53 us
  transfers between devices with their start and end apart: 8, of which 8 were waited for; matrix products, arithmetic and copies ran while one was open for 4% of the time, Pallas kernels for 0%

profile of v8, /device:TPU:2, one launch (start us, length us, event | category | flops | bytes accessed | tf_op | source)
XLA Modules:
  0.0 108.1 jit_solution(8437040566656791994)
XLA Ops:
  0.0 1.2 %multiply_reduce_fusion = f32[8,4]{1,0:T(8,128)S(1)} fusion(bf16[8,4,1536]{2,1,0:T(4,128)(2,1)} %param.13), kind=kLoop, calls=%fused_computation.39 | loop fusion | flops 147424 | bytes 98432 | tf_op jit(solution)/shard_map/reduce_sum | solution.py:14
  1.2 1.0 multiply_convert_fusion
  2.2 1.2 %fusion.16 = bf16[8,4,128]{2,1,0:T(4,128)(2,1)S(1)} fusion(bf16[8,4,1536]{2,1,0:T(4,128)(2,1)S(1)} %multiply_convert_fusion, bf16[1536,128]{1,0:T(8,128)(2,1)} %param.18), kind=kOutput, calls=%fused_computation.21 | convolution fusion | flops 12591104 | bytes 499712 | tf_op jit(solution)/shard_map/rsd,dh->rsh/dot_general | solution.py:61
  5.8 7.6 %all-to-all-start = ((bf16[32,8,532]{2,1,0:T(8,128)(2,1)}), bf16[32,8,532]{2,1,0:T(8,128)(2,1)S(1)}, u32[]{:S(2)}, u32[]{:S(2)}) async-start(bf16[32,8,532]{2,1,0:T(8,128)(2,1)} %broadcast_in_dim.57), calls=%async_computation | async-start | bytes 655360 | tf_op jit(solution)/shard_map/all_to_all | solution.py:79
  14.0 7.7 %all-to-all-done = bf16[32,8,532]{2,1,0:T(8,128)(2,1)S(1)} async-done(((bf16[32,8,532]{2,1,0:T(8,128)(2,1)}), bf16[32,8,532]{2,1,0:T(8,128)(2,1)S(1)}, u32[]{:S(2)}, u32[]{:S(2)}) %all-to-all-start) | async-done | bytes 272416 | tf_op jit(solution)/shard_map/all_to_all | solution.py:79
  22.5 1.3 %gather_fusion = s32[72]{0:T(128)S(1)} fusion(s32[256]{0:T(256)S(1)} %slice_reduce_fusion, s32[1024]{0:T(1024)S(1)} %pad_clamp_fusion), kind=kCustom, calls=%fused_computation | custom fusion | bytes 864 | tf_op jit(solution)/shard_map/gather | solution.py:97
  24.8 3.1 %fusion.64 = (f32[72,4]{1,0:T(8,128)S(1)}, f32[72,4,128]{2,1,0:T(4,128)S(1)}) fusion(bf16[72,4,128]{2,1,0:T(4,128)(2,1)S(1)} %gather_fusion.1, bf16[72,2,128,128]{3,2,1,0:T(8,128)(2,1)} %param.16, s32[72,4]{1,0:T(8,128)S(1)} %add_add_fusion, s32[72,128]{1,0:T(8,128)S(1)} %iota_add_fusion, pred[72,128]{1,0:T(8,128)(4,1)S(1)} %broadcast_compare_fusion), kind=kOutput, calls=%fused_computation.128 | convolution fusion | flops 9584352 | bytes 2628864 | tf_op jit(solution)/shard_map/pqd,pkd->pqk/dot_general | solution.py:108
  29.4 2.5 %fusion.9 = f32[72,4,128]{2,1,0:T(4,128)S(1)} fusion(bf16[72,2,128,128]{3,2,1,0:T(8,128)(2,1)} %param.16, f32[72,4]{1,0:T(8,128)S(1)} %get-tuple-element.12, f32[72,4,128]{2,1,0:T(4,128)S(1)} %get-tuple-element.25, f32[72,4]{1,0:T(8,128)S(1)} %get-tuple-element.24, s32[72,4]{1,0:T(8,128)S(1)} %add_add_fusion, s32[72,128]{1,0:T(8,128)S(1)} %iota_add_fusion, ...), kind=kOutput, calls=%fused_computation.13 | convolution fusion | flops 9658368 | bytes 2703744 | tf_op jit(solution)/shard_map/pqk,pkd->pqd/dot_general | solution.py:115
  33.1 0.8 pad_maximum_fusion
  34.0 5.0 %all-to-all-start.1 = ((bf16[32,8,528]{2,1,0:T(8,128)(2,1)}), bf16[32,8,528]{2,1,0:T(8,128)(2,1)S(1)}, u32[]{:S(2)}, u32[]{:S(2)}) async-start(bf16[32,8,528]{2,1,0:T(8,128)(2,1)} %pad_maximum_fusion), calls=%async_computation.1 | async-start | bytes 655360 | tf_op jit(solution)/shard_map/all_to_all | solution.py:149
  40.5 0.8 convolution_convert_fusion.3
  41.3 6.0 %all-to-all-done.1 = bf16[32,8,528]{2,1,0:T(8,128)(2,1)S(1)} async-done(((bf16[32,8,528]{2,1,0:T(8,128)(2,1)}), bf16[32,8,528]{2,1,0:T(8,128)(2,1)S(1)}, u32[]{:S(2)}, u32[]{:S(2)}) %all-to-all-start.1) | async-done | bytes 270368 | tf_op jit(solution)/shard_map/all_to_all | solution.py:149
  48.3 2.3 %multiply_reduce_fusion.1 = (f32[8,4]{1,0:T(8,128)}, f32[32,8,4]{2,1,0:T(8,128)}) fusion(bf16[32,8,528]{2,1,0:T(8,128)(2,1)} %copy-done.2, f32[8,4]{1,0:T(8,128)S(1)} %max.26, f32[32,8,12]{2,1,0:T(8,128)S(1)} %slice_convert_fusion), kind=kLoop, calls=%fused_computation.51 | loop fusion | flops 6112 | bytes 18688 | tf_op jit(solution)/shard_map/reduce_sum | solution.py:186
  50.6 1.8 %copy.111 = f32[32,8,4]{1,2,0:T(4,128)} copy(f32[32,8,4]{2,1,0:T(8,128)} %get-tuple-element.10) | data formatting | bytes 8192 | tf_op jit(solution)/shard_map/exp | solution.py:184
  52.4 1.2 %fusion.17 = f32[8,512]{1,0:T(8,128)S(1)} fusion(bf16[32,8,528]{2,1,0:T(8,128)(2,1)} %copy-done.2, f32[32,8,4]{1,2,0:T(4,128)} %copy.111), kind=kLoop, calls=%fused_computation.26 | loop fusion | flops 389120 | bytes 282624 | tf_op jit(solution)/shard_map/reduce_sum | solution.py:187
  54.9 0.9 fusion.15
  55.8 1.2 %convolution_convert_fusion.1 = bf16[32,1536]{1,0:T(8,128)(2,1)S(1)} fusion(bf16[32,128]{1,0:T(8,128)(2,1)S(1)} %bitcast.80, bf16[128,1536]{1,0:T(8,128)(2,1)} %param.21), kind=kOutput, calls=%fused_computation.10 | convolution fusion | flops 12632064 | bytes 499712 | tf_op jit(solution)/shard_map/dot_general | solution.py:193
  57.0 2.0 %collective-permute-start = (bf16[32,1536]{1,0:T(8,128)(2,1)S(1)}, bf16[32,1536]{1,0:T(8,128)(2,1)S(1)}, u32[]{:S(2)}, u32[]{:S(2)}) collective-permute-start(bf16[32,1536]{1,0:T(8,128)(2,1)S(1)} %convolution_convert_fusion.1), channel_id=1, source_target_pairs={{0,1},{1,0},{2,3},{3,2},{4,5},{5,4},{6,7},{7,6},{8,12},{9,13},{10,... | collective-permute-start | bytes 294920 | tf_op jit(solution)/shard_map/ppermute | solution.py:29
  59.0 2.7 %collective-permute-done = bf16[32,1536]{1,0:T(8,128)(2,1)S(1)} collective-permute-done((bf16[32,1536]{1,0:T(8,128)(2,1)S(1)}, bf16[32,1536]{1,0:T(8,128)(2,1)S(1)}, u32[]{:S(2)}, u32[]{:S(2)}) %collective-permute-start) | collective-permute-done | bytes 98336 | tf_op jit(solution)/shard_map/ppermute | solution.py:29
  61.7 3.4 %collective-permute-start.1 = (bf16[32,1536]{1,0:T(8,128)(2,1)S(1)}, bf16[32,1536]{1,0:T(8,128)(2,1)S(1)}, u32[]{:S(2)}, u32[]{:S(2)}) collective-permute-start(bf16[32,1536]{1,0:T(8,128)(2,1)S(1)} %add.217), channel_id=1, source_target_pairs={{0,2},{1,3},{2,0},{3,1},{4,6},{5,7},{6,4},{7,5},{8,10},{9,11},{10,... | collective-permute-start | bytes 294920 | tf_op jit(solution)/shard_map/ppermute | solution.py:29
  65.1 5.2 %collective-permute-done.1 = bf16[32,1536]{1,0:T(8,128)(2,1)S(1)} collective-permute-done((bf16[32,1536]{1,0:T(8,128)(2,1)S(1)}, bf16[32,1536]{1,0:T(8,128)(2,1)S(1)}, u32[]{:S(2)}, u32[]{:S(2)}) %collective-permute-start.1) | collective-permute-done | bytes 98336 | tf_op jit(solution)/shard_map/ppermute | solution.py:29
  71.0 5.6 %collective-permute-start.2 = (bf16[32,1536]{1,0:T(8,128)(2,1)}, bf16[32,1536]{1,0:T(8,128)(2,1)}, u32[]{:S(2)}, u32[]{:S(2)}) collective-permute-start(bf16[32,1536]{1,0:T(8,128)(2,1)} %add.218), channel_id=1, source_target_pairs={{0,4},{1,5},{2,6},{3,7},{4,0},{5,1},{6,2},{7,3},{8,9},{9,8},{10,11... | collective-permute-start | bytes 294920 | tf_op jit(solution)/shard_map/ppermute | solution.py:29
  76.5 1.6 %reshape.418 = f32[32,1536]{1,0:T(8,128)} reshape(bf16[8,4,1536]{2,1,0:T(4,128)(2,1)} %param.13) | data formatting | bytes 294912 | tf_op jit(solution)/shard_map/convert_element_type | solution.py:195
  78.1 1.7 %collective-permute-done.2 = bf16[32,1536]{1,0:T(8,128)(2,1)} collective-permute-done((bf16[32,1536]{1,0:T(8,128)(2,1)}, bf16[32,1536]{1,0:T(8,128)(2,1)}, u32[]{:S(2)}, u32[]{:S(2)}) %collective-permute-start.2) | collective-permute-done | bytes 98336 | tf_op jit(solution)/shard_map/ppermute | solution.py:29
  79.8 1.2 %fusion.19 = (f32[32]{0:T(128)S(1)}, bf16[32,1536]{1,0:T(8,128)(2,1)S(1)}) fusion(f32[32,1536]{1,0:T(8,128)} %reshape.418, bf16[32,1536]{1,0:T(8,128)(2,1)} %add.218, bf16[32,1536]{1,0:T(8,128)(2,1)} %collective-permute-done.2), kind=kLoop, calls=%fused_computation.33 | loop fusion | flops 344032 | bytes 491648 | tf_op jit(solution)/shard_map/reduce_sum | solution.py:14
  81.6 1.3 %fusion.41 = f32[32,576]{1,0:T(8,128)} fusion(bf16[1536,576]{0,1:T(8,128)(2,1)S(1)} %copy-done.1, bf16[32,1536]{1,0:T(8,128)(2,1)S(1)} %get-tuple-element.6, f32[1536]{0:T(1024)S(1)} %copy-done.9, f32[32]{0:T(128)S(1)} %add_rsqrt_fusion.1), kind=kOutput, calls=%fused_computation.72 | convolution fusion | flops 56819712 | bytes 1947776 | tf_op jit(solution)/shard_map/dot_general | solution.py:197
  82.9 2.5 %convolution_convert_fusion = bf16[32,1536]{1,0:T(8,128)(2,1)S(1)} fusion(bf16[576,1536]{1,0:T(8,128)(2,1)S(1)} %copy-done, bf16[1536,576]{0,1:T(8,128)(2,1)} %param.24, f32[32,576]{1,0:T(8,128)} %fusion.41, bf16[32,1536]{1,0:T(8,128)(2,1)} %copy-done.3, f32[1536]{0:T(1024)S(1)} %copy-done.9, f32[32]{0:T(128)S(1)} %add_rsqrt_fusion.1), kind=kOutput, calls=%fused_computation.9 | convolution fusion | flops 113676288 | bytes 3815552 | tf_op jit(solution)/shard_map/dot_general | solution.py:200
  85.9 4.8 %collective-permute-done.3 = bf16[32,1536]{1,0:T(8,128)(2,1)S(1)} collective-permute-done((bf16[32,1536]{1,0:T(8,128)(2,1)S(1)}, bf16[32,1536]{1,0:T(8,128)(2,1)S(1)}, u32[]{:S(2)}, u32[]{:S(2)}) %collective-permute-start.3) | collective-permute-done | bytes 98336 | tf_op jit(solution)/shard_map/ppermute | solution.py:29
  90.8 2.4 %collective-permute-start.4 = (bf16[32,1536]{1,0:T(8,128)(2,1)S(1)}, bf16[32,1536]{1,0:T(8,128)(2,1)S(1)}, u32[]{:S(2)}, u32[]{:S(2)}) collective-permute-start(bf16[32,1536]{1,0:T(8,128)(2,1)S(1)} %add.226), channel_id=1, source_target_pairs={{0,2},{1,3},{2,0},{3,1},{4,6},{5,7},{6,4},{7,5},{8,10},{9,11},{10,... | collective-permute-start | bytes 294920 | tf_op jit(solution)/shard_map/ppermute | solution.py:29
  93.1 5.6 %collective-permute-done.4 = bf16[32,1536]{1,0:T(8,128)(2,1)S(1)} collective-permute-done((bf16[32,1536]{1,0:T(8,128)(2,1)S(1)}, bf16[32,1536]{1,0:T(8,128)(2,1)S(1)}, u32[]{:S(2)}, u32[]{:S(2)}) %collective-permute-start.4) | collective-permute-done | bytes 98336 | tf_op jit(solution)/shard_map/ppermute | solution.py:29
  98.7 5.5 %collective-permute-start.5 = (bf16[32,1536]{1,0:T(8,128)(2,1)S(1)}, bf16[32,1536]{1,0:T(8,128)(2,1)S(1)}, u32[]{:S(2)}, u32[]{:S(2)}) collective-permute-start(bf16[32,1536]{1,0:T(8,128)(2,1)S(1)} %add.227), channel_id=1, source_target_pairs={{0,4},{1,5},{2,6},{3,7},{4,0},{5,1},{6,2},{7,3},{8,9},{9,8},{10,11... | collective-permute-start | bytes 294920 | tf_op jit(solution)/shard_map/ppermute | solution.py:29
  104.2 3.1 %collective-permute-done.5 = bf16[32,1536]{1,0:T(8,128)(2,1)S(1)} collective-permute-done((bf16[32,1536]{1,0:T(8,128)(2,1)S(1)}, bf16[32,1536]{1,0:T(8,128)(2,1)S(1)}, u32[]{:S(2)}, u32[]{:S(2)}) %collective-permute-start.5) | collective-permute-done | bytes 98336 | tf_op jit(solution)/shard_map/ppermute | solution.py:29
  (83 shorter events, 13.8 us)
Async XLA Ops:
  0.0 82.9 %copy-start = (bf16[576,1536]{1,0:T(8,128)(2,1)S(1)}, bf16[576,1536]{1,0:T(8,128)(2,1)}, u32[]{:S(2)}) copy-start(bf16[576,1536]{1,0:T(8,128)(2,1)} %param.25) | copy-start | bytes 5308420
  0.0 13.5 %copy-start.5 = (bf16[1536,128]{1,0:T(8,128)(2,1)S(1)}, bf16[1536,128]{1,0:T(8,128)(2,1)}, u32[]{:S(2)}) copy-start(bf16[1536,128]{1,0:T(8,128)(2,1)} %param.19) | copy-start | bytes 1179652
  5.8 15.9 %all-to-all-start = ((bf16[32,8,532]{2,1,0:T(8,128)(2,1)}), bf16[32,8,532]{2,1,0:T(8,128)(2,1)S(1)}, u32[]{:S(2)}, u32[]{:S(2)}) async-start(bf16[32,8,532]{2,1,0:T(8,128)(2,1)} %broadcast_in_dim.57), calls=%async_computation | async-start | bytes 655360 | tf_op jit(solution)/shard_map/all_to_all | solution.py:79
  31.9 8.6 %copy-start.6 = (bf16[1536,128]{1,0:T(8,128)(2,1)S(1)}, bf16[1536,128]{1,0:T(8,128)(2,1)}, u32[]{:S(2)}) copy-start(bf16[1536,128]{1,0:T(8,128)(2,1)} %param.20) | copy-start | bytes 1179652
  34.0 13.4 %all-to-all-start.1 = ((bf16[32,8,528]{2,1,0:T(8,128)(2,1)}), bf16[32,8,528]{2,1,0:T(8,128)(2,1)S(1)}, u32[]{:S(2)}, u32[]{:S(2)}) async-start(bf16[32,8,528]{2,1,0:T(8,128)(2,1)} %pad_maximum_fusion), calls=%async_computation.1 | async-start | bytes 655360 | tf_op jit(solution)/shard_map/all_to_all | solution.py:149
  39.1 11.5 %copy-start.8 = (f32[8,4]{1,0:T(8,128)}, f32[8,4]{1,0:T(8,128)S(1)}, u32[]{:S(2)}) copy-start(f32[8,4]{1,0:T(8,128)S(1)} %copy.110) | copy-start | bytes 388
  47.3 0.7 copy-start.2
  48.1 33.5 %copy-start.1 = (bf16[1536,576]{0,1:T(8,128)(2,1)S(1)}, bf16[1536,576]{0,1:T(8,128)(2,1)}, u32[]{:S(2)}) copy-start(bf16[1536,576]{0,1:T(8,128)(2,1)} %param.23) | copy-start | bytes 5308420
  48.3 2.3 %copy-start.7 = (f32[8,4]{1,0:T(8,128)}, f32[8,4]{1,0:T(8,128)S(1)}, u32[]{:S(2)}) copy-start(f32[8,4]{1,0:T(8,128)S(1)} %max.26) | copy-start | bytes 388
  54.2 27.4 %copy-start.9 = (f32[1536]{0:T(1024)S(1)}, f32[1536]{0:T(1024)}, u32[]{:S(2)}) copy-start(f32[1536]{0:T(1024)} %param.22) | copy-start | bytes 18436
  57.0 4.7 %collective-permute-start = (bf16[32,1536]{1,0:T(8,128)(2,1)S(1)}, bf16[32,1536]{1,0:T(8,128)(2,1)S(1)}, u32[]{:S(2)}, u32[]{:S(2)}) collective-permute-start(bf16[32,1536]{1,0:T(8,128)(2,1)S(1)} %convolution_convert_fusion.1), channel_id=1, source_target_pairs={{0,1},{1,0},{2,3},{3,2},{4,5},{5,4},{6,7},{7,6},{8,12},{9,13},{10,... | collective-permute-start | bytes 294920 | tf_op jit(solution)/shard_map/ppermute | solution.py:29
  61.7 8.6 %collective-permute-start.1 = (bf16[32,1536]{1,0:T(8,128)(2,1)S(1)}, bf16[32,1536]{1,0:T(8,128)(2,1)S(1)}, u32[]{:S(2)}, u32[]{:S(2)}) collective-permute-start(bf16[32,1536]{1,0:T(8,128)(2,1)S(1)} %add.217), channel_id=1, source_target_pairs={{0,2},{1,3},{2,0},{3,1},{4,6},{5,7},{6,4},{7,5},{8,10},{9,11},{10,... | collective-permute-start | bytes 294920 | tf_op jit(solution)/shard_map/ppermute | solution.py:29
  71.0 8.8 %collective-permute-start.2 = (bf16[32,1536]{1,0:T(8,128)(2,1)}, bf16[32,1536]{1,0:T(8,128)(2,1)}, u32[]{:S(2)}, u32[]{:S(2)}) collective-permute-start(bf16[32,1536]{1,0:T(8,128)(2,1)} %add.218), channel_id=1, source_target_pairs={{0,4},{1,5},{2,6},{3,7},{4,0},{5,1},{6,2},{7,3},{8,9},{9,8},{10,11... | collective-permute-start | bytes 294920 | tf_op jit(solution)/shard_map/ppermute | solution.py:29
  81.0 0.6 copy-start.3
  82.9 24.5 %copy-start.4 = (bf16[32,1536]{1,0:T(8,128)(2,1)S(1)}, bf16[32,1536]{1,0:T(8,128)(2,1)}, u32[]{:S(2)}) copy-start(bf16[32,1536]{1,0:T(8,128)(2,1)} %copy-done.3) | copy-start | bytes 294916
  85.4 5.3 %collective-permute-start.3 = (bf16[32,1536]{1,0:T(8,128)(2,1)S(1)}, bf16[32,1536]{1,0:T(8,128)(2,1)S(1)}, u32[]{:S(2)}, u32[]{:S(2)}) collective-permute-start(bf16[32,1536]{1,0:T(8,128)(2,1)S(1)} %convolution_convert_fusion), channel_id=1, source_target_pairs={{0,1},{1,0},{2,3},{3,2},{4,5},{5,4},{6,7},{7,6},{8,12},{9,13},{10,... | collective-permute-start | bytes 294920 | tf_op jit(solution)/shard_map/ppermute | solution.py:29
  90.8 8.0 %collective-permute-start.4 = (bf16[32,1536]{1,0:T(8,128)(2,1)S(1)}, bf16[32,1536]{1,0:T(8,128)(2,1)S(1)}, u32[]{:S(2)}, u32[]{:S(2)}) collective-permute-start(bf16[32,1536]{1,0:T(8,128)(2,1)S(1)} %add.226), channel_id=1, source_target_pairs={{0,2},{1,3},{2,0},{3,1},{4,6},{5,7},{6,4},{7,5},{8,10},{9,11},{10,... | collective-permute-start | bytes 294920 | tf_op jit(solution)/shard_map/ppermute | solution.py:29
  98.7 8.6 %collective-permute-start.5 = (bf16[32,1536]{1,0:T(8,128)(2,1)S(1)}, bf16[32,1536]{1,0:T(8,128)(2,1)S(1)}, u32[]{:S(2)}, u32[]{:S(2)}) collective-permute-start(bf16[32,1536]{1,0:T(8,128)(2,1)S(1)} %add.227), channel_id=1, source_target_pairs={{0,4},{1,5},{2,6},{3,7},{4,0},{5,1},{6,2},{7,3},{8,9},{9,8},{10,11... | collective-permute-start | bytes 294920 | tf_op jit(solution)/shard_map/ppermute | solution.py:29

commit v9 on v8

--- a/solution.py
+++ b/solution.py
@@ -55,12 +55,10 @@
         requests = req_dev * req_size
         qwidth = steps * heads_dev * head_dim
         token_rows = tokens.reshape(req_dev * steps, width)
-        normed3 = rms_norm(tokens.astype(jnp.float32), norm_gain).astype(jnp.bfloat16)
-        normed = normed3.reshape(req_dev * steps, width)
+        normed = rms_norm(token_rows.astype(jnp.float32), norm_gain).astype(jnp.bfloat16)
         queries = (
-            jnp.einsum("rsd,dh->rsh", normed3, query_weight, preferred_element_type=jnp.float32)
-            * head_dim ** (-0.5)
-        ).astype(jnp.bfloat16).reshape(req_dev * steps, heads_dev * head_dim)
+            jnp.dot(normed, query_weight, preferred_element_type=jnp.float32) * head_dim ** (-0.5)
+        ).astype(jnp.bfloat16)
         key_new = jnp.dot(normed, key_weight, preferred_element_type=jnp.float32).astype(jnp.bfloat16)
         value_new = jnp.dot(normed, value_weight, preferred_element_type=jnp.float32).astype(
             jnp.bfloat16
@@ -94,7 +92,8 @@
         )
         page_request = owner_entry // window_pages
         page_number = owner_entry % window_pages
-        page_length = all_lengths[page_request]
+        entry_length = jnp.repeat(all_lengths, window_pages)
+        page_length = jnp.sum(jnp.where(match, entry_length[None, :], 0), axis=1)
         first_page = jnp.maximum(page_length - (WINDOW - 1), 0) // page_size
         position = (first_page + page_number)[:, None] * page_size + jnp.arange(
             page_size, dtype=jnp.int32
@@ -123,7 +122,11 @@
         local_max = jnp.max(
             jnp.where(member[:, :, None, None], block_max[None], negative), axis=1
         )
-        scale = jnp.exp(block_max - local_max[page_request])
+        same_request = page_request[:, None] == page_request[None, :]
+        page_ref_max = jnp.max(
+            jnp.where(same_request[:, :, None, None], block_max[None], negative), axis=1
+        )
+        scale = jnp.exp(block_max - page_ref_max)
         nsh = steps * heads_dev
         scaled = jnp.concatenate(
             [

time: 109 us -> 97.2 us (0.89)
  local copies, waits for them, and re-layouts: 12.7 us -> 5.84 us
  other arithmetic: 12.2 us -> 6.76 us
  matrix products: 14.1 us -> 11.1 us
  starting transfers between devices: 31.9 us -> 34.1 us
    reduce_sum x1, other arithmetic: 2.32 us -> 0.15 us  [body(): total = jnp.sum(got_total * src_scale, axis=0) + new_total * new_scale]
    ppermute x6, starting transfers between devices: 19.2 us -> 21.3 us  [staggered_sum(): values = values + lax.ppermute(values, ('req', 'tp'), pairs)]
    gather x2 -> x0, local copies, waits for them, and re-layouts: 1.87 us -> none  [the longest x1 1.27 us: body(): page_length = all_lengths[page_request]]
    all_to_all x1, waiting for transfers between devices: 6.03 us -> 7.79 us  [body(): lax.all_to_all(send, 'req', 0, 0, tiled=True).reshape(req_size, req_dev, -1)]
    exp x1, local copies, waits for them, and re-layouts: 1.79 us -> 0.25 us  [body(): src_scale = jnp.exp(got_max - overall[None])]
    unnamed x22 -> x13, local copies, waits for them, and re-layouts: 1.39 us -> 0.04 us
    ppermute x6, waiting for transfers between devices: 23.2 us -> 22 us  [staggered_sum(): values = values + lax.ppermute(values, ('req', 'tp'), pairs)]
  transfers between devices with their start and end apart: 8 -> 8, of which waited for: 8 -> 8; matrix products, arithmetic and copies ran while one was open for 4% -> 1% of each run, Pallas kernels for 0% -> 0%
where the time goes in v9:
time: 97.2 us; the launch traced here: 95.7 us
  waiting for transfers between devices  37.6 us (39%)
  starting transfers between devices  34.1 us (35%)
  matrix products  11.1 us (11%)
  other arithmetic  6.76 us (7%)
  local copies, waits for them, and re-layouts  5.84 us (6%)
    ppermute x6, waiting for transfers between devices, staggered_sum(): values = values + lax.ppermute(values, ('req', 'tp'), pairs)  22 us
    ppermute x6, starting transfers between devices, staggered_sum(): values = values + lax.ppermute(values, ('req', 'tp'), pairs)  21.3 us
    all_to_all x1, waiting for transfers between devices, body(): lax.all_to_all(send, 'req', 0, 0, tiled=True).reshape(req_size, req_dev, -1)  7.79 us
    all_to_all x1, waiting for transfers between devices, body(): lax.all_to_all(jnp.broadcast_to(packed[None], (req_size,) + packed.shape)...  7.74 us
    all_to_all x1, starting transfers between devices, body(): lax.all_to_all(jnp.broadcast_to(packed[None], (req_size,) + packed.shape)...  7.62 us
    all_to_all x1, starting transfers between devices, body(): lax.all_to_all(send, 'req', 0, 0, tiled=True).reshape(req_size, req_dev, -1)  5.11 us
    dot_general x1, matrix products, body(): jnp.einsum('pqd,pkd->pqk', page_queries, kv_pages[:, 0], preferred_elemen...  3.08 us
    dot_general x1, matrix products, body(): jnp.dot(hidden, down_weight, preferred_element_type=jnp.float32)  2.52 us
  transfers between devices with their start and end apart: 8, of which 8 were waited for; matrix products, arithmetic and copies ran while one was open for 1% of the time, Pallas kernels for 0%

profile of v9, /device:TPU:2, one launch (start us, length us, event | category | flops | bytes accessed | tf_op | source)
XLA Modules:
  0.0 95.7 jit_solution(1329257037065867290)
XLA Ops:
  0.0 1.2 %multiply_reduce_fusion = f32[8,4]{1,0:T(8,128)S(1)} fusion(bf16[8,4,1536]{2,1,0:T(4,128)(2,1)} %param.13), kind=kLoop, calls=%fused_computation.39 | loop fusion | flops 147424 | bytes 98432 | tf_op jit(solution)/shard_map/reduce_sum | solution.py:14
  1.2 0.9 reshape.470
  2.1 0.7 fusion.53
  3.0 0.7 fusion.48
  3.7 0.8 multiply_convert_fusion
  4.5 1.2 %fusion.16 = bf16[32,128]{1,0:T(8,128)(2,1)S(1)} fusion(bf16[32,1536]{1,0:T(8,128)(2,1)S(1)} %multiply_convert_fusion, bf16[1536,128]{1,0:T(8,128)(2,1)} %param.18), kind=kOutput, calls=%fused_computation.19 | convolution fusion | flops 12591104 | bytes 499712 | tf_op jit(solution)/shard_map/dot_general | solution.py:60
  5.8 0.7 broadcast_in_dim.131
  6.6 7.6 %all-to-all-start = ((bf16[32,8,532]{2,1,0:T(8,128)(2,1)}), bf16[32,8,532]{2,1,0:T(8,128)(2,1)S(1)}, u32[]{:S(2)}, u32[]{:S(2)}) async-start(bf16[32,8,532]{2,1,0:T(8,128)(2,1)} %broadcast_in_dim.131), calls=%async_computation | async-start | bytes 655360 | tf_op jit(solution)/shard_map/all_to_all | solution.py:77
  14.7 7.7 %all-to-all-done = bf16[32,8,532]{2,1,0:T(8,128)(2,1)S(1)} async-done(((bf16[32,8,532]{2,1,0:T(8,128)(2,1)}), bf16[32,8,532]{2,1,0:T(8,128)(2,1)S(1)}, u32[]{:S(2)}, u32[]{:S(2)}) %all-to-all-start) | async-done | bytes 272416 | tf_op jit(solution)/shard_map/all_to_all | solution.py:77
  24.2 0.7 gather_fusion
  24.8 3.1 %fusion.65 = (f32[72,4]{1,0:T(8,128)S(1)}, f32[72,4,128]{2,1,0:T(4,128)S(1)}) fusion(bf16[72,4,128]{2,1,0:T(4,128)(2,1)S(1)} %gather_fusion, bf16[72,2,128,128]{3,2,1,0:T(8,128)(2,1)} %param.16, s32[72,4]{1,0:T(8,128)S(1)} %add_add_fusion, s32[72,128]{1,0:T(8,128)S(1)} %iota_add_fusion, pred[72,128]{1,0:T(8,128)(4,1)S(1)} %broadcast_compare_fusion.1), kind=kOutput, calls=%fused_computation.129 | convolution fusion | flops 9584352 | bytes 2628864 | tf_op jit(solution)/shard_map/pqd,pkd->pqk/dot_general | solution.py:107
  28.4 0.3 fusion.56
  28.7 2.5 %fusion.9 = f32[72,4,128]{2,1,0:T(4,128)S(1)} fusion(bf16[72,2,128,128]{3,2,1,0:T(8,128)(2,1)} %param.16, f32[72,4]{1,0:T(8,128)S(1)} %get-tuple-element.14, f32[72,4,128]{2,1,0:T(4,128)S(1)} %get-tuple-element.28, f32[72,4]{1,0:T(8,128)S(1)} %get-tuple-element.27, s32[72,4]{1,0:T(8,128)S(1)} %add_add_fusion, s32[72,128]{1,0:T(8,128)S(1)} %iota_add_fusion, ...), kind=kOutput, calls=%fused_computation.11 | convolution fusion | flops 9658368 | bytes 2703744 | tf_op jit(solution)/shard_map/pqk,pkd->pqd/dot_general | solution.py:114
  31.9 0.5 convolution_convert_fusion.2
  32.6 0.8 pad_maximum_fusion
  33.4 5.1 %all-to-all-start.1 = ((bf16[32,8,528]{2,1,0:T(8,128)(2,1)}), bf16[32,8,528]{2,1,0:T(8,128)(2,1)S(1)}, u32[]{:S(2)}, u32[]{:S(2)}) async-start(bf16[32,8,528]{2,1,0:T(8,128)(2,1)} %pad_maximum_fusion), calls=%async_computation.1 | async-start | bytes 655360 | tf_op jit(solution)/shard_map/all_to_all | solution.py:152
  39.1 7.8 %all-to-all-done.1 = bf16[32,8,528]{2,1,0:T(8,128)(2,1)S(1)} async-done(((bf16[32,8,528]{2,1,0:T(8,128)(2,1)}), bf16[32,8,528]{2,1,0:T(8,128)(2,1)S(1)}, u32[]{:S(2)}, u32[]{:S(2)}) %all-to-all-start.1) | async-done | bytes 270368 | tf_op jit(solution)/shard_map/all_to_all | solution.py:152
  48.2 2.0 %collective-permute-start = (bf16[32,1536]{1,0:T(8,128)(2,1)S(1)}, bf16[32,1536]{1,0:T(8,128)(2,1)S(1)}, u32[]{:S(2)}, u32[]{:S(2)}) collective-permute-start(bf16[32,1536]{1,0:T(8,128)(2,1)S(1)} %convolution_convert_fusion.1), channel_id=1, source_target_pairs={{0,1},{1,0},{2,3},{3,2},{4,5},{5,4},{6,7},{7,6},{8,12},{9,13},{10,... | collective-permute-start | bytes 294920 | tf_op jit(solution)/shard_map/ppermute | solution.py:29
  50.2 2.7 %collective-permute-done = bf16[32,1536]{1,0:T(8,128)(2,1)S(1)} collective-permute-done((bf16[32,1536]{1,0:T(8,128)(2,1)S(1)}, bf16[32,1536]{1,0:T(8,128)(2,1)S(1)}, u32[]{:S(2)}, u32[]{:S(2)}) %collective-permute-start) | collective-permute-done | bytes 98336 | tf_op jit(solution)/shard_map/ppermute | solution.py:29
  52.9 3.4 %collective-permute-start.1 = (bf16[32,1536]{1,0:T(8,128)(2,1)S(1)}, bf16[32,1536]{1,0:T(8,128)(2,1)S(1)}, u32[]{:S(2)}, u32[]{:S(2)}) collective-permute-start(bf16[32,1536]{1,0:T(8,128)(2,1)S(1)} %add.216), channel_id=1, source_target_pairs={{0,2},{1,3},{2,0},{3,1},{4,6},{5,7},{6,4},{7,5},{8,10},{9,11},{10,... | collective-permute-start | bytes 294920 | tf_op jit(solution)/shard_map/ppermute | solution.py:29
  56.2 5.2 %collective-permute-done.1 = bf16[32,1536]{1,0:T(8,128)(2,1)S(1)} collective-permute-done((bf16[32,1536]{1,0:T(8,128)(2,1)S(1)}, bf16[32,1536]{1,0:T(8,128)(2,1)S(1)}, u32[]{:S(2)}, u32[]{:S(2)}) %collective-permute-start.1) | collective-permute-done | bytes 98336 | tf_op jit(solution)/shard_map/ppermute | solution.py:29
  61.5 5.7 %collective-permute-start.2 = (bf16[32,1536]{1,0:T(8,128)(2,1)S(1)}, bf16[32,1536]{1,0:T(8,128)(2,1)S(1)}, u32[]{:S(2)}, u32[]{:S(2)}) collective-permute-start(bf16[32,1536]{1,0:T(8,128)(2,1)S(1)} %add.217), channel_id=1, source_target_pairs={{0,4},{1,5},{2,6},{3,7},{4,0},{5,1},{6,2},{7,3},{8,9},{9,8},{10,11... | collective-permute-start | bytes 294920 | tf_op jit(solution)/shard_map/ppermute | solution.py:29
  67.2 3.0 %collective-permute-done.2 = bf16[32,1536]{1,0:T(8,128)(2,1)S(1)} collective-permute-done((bf16[32,1536]{1,0:T(8,128)(2,1)S(1)}, bf16[32,1536]{1,0:T(8,128)(2,1)S(1)}, u32[]{:S(2)}, u32[]{:S(2)}) %collective-permute-start.2) | collective-permute-done | bytes 98336 | tf_op jit(solution)/shard_map/ppermute | solution.py:29
  70.3 0.6 fusion.42
  71.0 2.5 %convolution_convert_fusion = bf16[32,1536]{1,0:T(8,128)(2,1)S(1)} fusion(bf16[576,1536]{1,0:T(8,128)(2,1)S(1)} %copy-done, bf16[1536,576]{0,1:T(8,128)(2,1)} %param.24, f32[32,576]{1,0:T(8,128)S(1)} %fusion.42, bf16[32,1536]{1,0:T(8,128)(2,1)S(1)} %get-tuple-element.8, f32[1536]{0:T(1024)S(1)} %copy-done.5, f32[32]{0:T(128)S(1)} %add_rsqrt_fusion.1), kind=kOutput, calls=%fused_computation.7 | convolution fusion | flops 113676288 | bytes 3815552 | tf_op jit(solution)/shard_map/dot_general | solution.py:203
  73.5 0.4 collective-permute-start.3
  73.9 4.9 %collective-permute-done.3 = bf16[32,1536]{1,0:T(8,128)(2,1)S(1)} collective-permute-done((bf16[32,1536]{1,0:T(8,128)(2,1)S(1)}, bf16[32,1536]{1,0:T(8,128)(2,1)S(1)}, u32[]{:S(2)}, u32[]{:S(2)}) %collective-permute-start.3) | collective-permute-done | bytes 98336 | tf_op jit(solution)/shard_map/ppermute | solution.py:29
  78.8 3.8 %collective-permute-start.4 = (bf16[32,1536]{1,0:T(8,128)(2,1)S(1)}, bf16[32,1536]{1,0:T(8,128)(2,1)S(1)}, u32[]{:S(2)}, u32[]{:S(2)}) collective-permute-start(bf16[32,1536]{1,0:T(8,128)(2,1)S(1)} %add.224), channel_id=1, source_target_pairs={{0,2},{1,3},{2,0},{3,1},{4,6},{5,7},{6,4},{7,5},{8,10},{9,11},{10,... | collective-permute-start | bytes 294920 | tf_op jit(solution)/shard_map/ppermute | solution.py:29
  82.6 3.0 %collective-permute-done.4 = bf16[32,1536]{1,0:T(8,128)(2,1)S(1)} collective-permute-done((bf16[32,1536]{1,0:T(8,128)(2,1)S(1)}, bf16[32,1536]{1,0:T(8,128)(2,1)S(1)}, u32[]{:S(2)}, u32[]{:S(2)}) %collective-permute-start.4) | collective-permute-done | bytes 98336 | tf_op jit(solution)/shard_map/ppermute | solution.py:29
  85.7 6.1 %collective-permute-start.5 = (bf16[32,1536]{1,0:T(8,128)(2,1)S(1)}, bf16[32,1536]{1,0:T(8,128)(2,1)S(1)}, u32[]{:S(2)}, u32[]{:S(2)}) collective-permute-start(bf16[32,1536]{1,0:T(8,128)(2,1)S(1)} %add.225), channel_id=1, source_target_pairs={{0,4},{1,5},{2,6},{3,7},{4,0},{5,1},{6,2},{7,3},{8,9},{9,8},{10,11... | collective-permute-start | bytes 294920 | tf_op jit(solution)/shard_map/ppermute | solution.py:29
  91.8 3.2 %collective-permute-done.5 = bf16[32,1536]{1,0:T(8,128)(2,1)S(1)} collective-permute-done((bf16[32,1536]{1,0:T(8,128)(2,1)S(1)}, bf16[32,1536]{1,0:T(8,128)(2,1)S(1)}, u32[]{:S(2)}, u32[]{:S(2)}) %collective-permute-start.5) | collective-permute-done | bytes 98336 | tf_op jit(solution)/shard_map/ppermute | solution.py:29
  95.0 0.7 reshape.469
  (76 shorter events, 5.9 us)
Async XLA Ops:
  0.0 70.9 %copy-start = (bf16[576,1536]{1,0:T(8,128)(2,1)S(1)}, bf16[576,1536]{1,0:T(8,128)(2,1)}, u32[]{:S(2)}) copy-start(bf16[576,1536]{1,0:T(8,128)(2,1)} %param.25) | copy-start | bytes 5308420
  0.0 14.2 %copy-start.2 = (bf16[1536,128]{1,0:T(8,128)(2,1)S(1)}, bf16[1536,128]{1,0:T(8,128)(2,1)}, u32[]{:S(2)}) copy-start(bf16[1536,128]{1,0:T(8,128)(2,1)} %param.19) | copy-start | bytes 1179652
  6.6 15.9 %all-to-all-start = ((bf16[32,8,532]{2,1,0:T(8,128)(2,1)}), bf16[32,8,532]{2,1,0:T(8,128)(2,1)S(1)}, u32[]{:S(2)}, u32[]{:S(2)}) async-start(bf16[32,8,532]{2,1,0:T(8,128)(2,1)} %broadcast_in_dim.131), calls=%async_computation | async-start | bytes 655360 | tf_op jit(solution)/shard_map/all_to_all | solution.py:77
  31.2 7.7 %copy-start.3 = (bf16[1536,128]{1,0:T(8,128)(2,1)S(1)}, bf16[1536,128]{1,0:T(8,128)(2,1)}, u32[]{:S(2)}) copy-start(bf16[1536,128]{1,0:T(8,128)(2,1)} %param.20) | copy-start | bytes 1179652
  33.4 14.6 %copy-start.4 = (bf16[128,1536]{1,0:T(8,128)(2,1)S(1)}, bf16[128,1536]{1,0:T(8,128)(2,1)}, u32[]{:S(2)}) copy-start(bf16[128,1536]{1,0:T(8,128)(2,1)} %param.21) | copy-start | bytes 1179652
  33.4 13.5 %all-to-all-start.1 = ((bf16[32,8,528]{2,1,0:T(8,128)(2,1)}), bf16[32,8,528]{2,1,0:T(8,128)(2,1)S(1)}, u32[]{:S(2)}, u32[]{:S(2)}) async-start(bf16[32,8,528]{2,1,0:T(8,128)(2,1)} %pad_maximum_fusion), calls=%async_computation.1 | async-start | bytes 655360 | tf_op jit(solution)/shard_map/all_to_all | solution.py:152
  39.1 31.2 %copy-start.5 = (f32[1536]{0:T(1024)S(1)}, f32[1536]{0:T(1024)}, u32[]{:S(2)}) copy-start(f32[1536]{0:T(1024)} %param.22) | copy-start | bytes 18436
  47.8 22.5 %copy-start.1 = (bf16[1536,576]{0,1:T(8,128)(2,1)S(1)}, bf16[1536,576]{0,1:T(8,128)(2,1)}, u32[]{:S(2)}) copy-start(bf16[1536,576]{0,1:T(8,128)(2,1)} %param.23) | copy-start | bytes 5308420
  48.2 4.7 %collective-permute-start = (bf16[32,1536]{1,0:T(8,128)(2,1)S(1)}, bf16[32,1536]{1,0:T(8,128)(2,1)S(1)}, u32[]{:S(2)}, u32[]{:S(2)}) collective-permute-start(bf16[32,1536]{1,0:T(8,128)(2,1)S(1)} %convolution_convert_fusion.1), channel_id=1, source_target_pairs={{0,1},{1,0},{2,3},{3,2},{4,5},{5,4},{6,7},{7,6},{8,12},{9,13},{10,... | collective-permute-start | bytes 294920 | tf_op jit(solution)/shard_map/ppermute | solution.py:29
  52.9 8.6 %collective-permute-start.1 = (bf16[32,1536]{1,0:T(8,128)(2,1)S(1)}, bf16[32,1536]{1,0:T(8,128)(2,1)S(1)}, u32[]{:S(2)}, u32[]{:S(2)}) collective-permute-start(bf16[32,1536]{1,0:T(8,128)(2,1)S(1)} %add.216), channel_id=1, source_target_pairs={{0,2},{1,3},{2,0},{3,1},{4,6},{5,7},{6,4},{7,5},{8,10},{9,11},{10,... | collective-permute-start | bytes 294920 | tf_op jit(solution)/shard_map/ppermute | solution.py:29
  61.5 8.6 %collective-permute-start.2 = (bf16[32,1536]{1,0:T(8,128)(2,1)S(1)}, bf16[32,1536]{1,0:T(8,128)(2,1)S(1)}, u32[]{:S(2)}, u32[]{:S(2)}) collective-permute-start(bf16[32,1536]{1,0:T(8,128)(2,1)S(1)} %add.217), channel_id=1, source_target_pairs={{0,4},{1,5},{2,6},{3,7},{4,0},{5,1},{6,2},{7,3},{8,9},{9,8},{10,11... | collective-permute-start | bytes 294920 | tf_op jit(solution)/shard_map/ppermute | solution.py:29
  73.5 5.3 %collective-permute-start.3 = (bf16[32,1536]{1,0:T(8,128)(2,1)S(1)}, bf16[32,1536]{1,0:T(8,128)(2,1)S(1)}, u32[]{:S(2)}, u32[]{:S(2)}) collective-permute-start(bf16[32,1536]{1,0:T(8,128)(2,1)S(1)} %convolution_convert_fusion), channel_id=1, source_target_pairs={{0,1},{1,0},{2,3},{3,2},{4,5},{5,4},{6,7},{7,6},{8,12},{9,13},{10,... | collective-permute-start | bytes 294920 | tf_op jit(solution)/shard_map/ppermute | solution.py:29
  78.8 6.8 %collective-permute-start.4 = (bf16[32,1536]{1,0:T(8,128)(2,1)S(1)}, bf16[32,1536]{1,0:T(8,128)(2,1)S(1)}, u32[]{:S(2)}, u32[]{:S(2)}) collective-permute-start(bf16[32,1536]{1,0:T(8,128)(2,1)S(1)} %add.224), channel_id=1, source_target_pairs={{0,2},{1,3},{2,0},{3,1},{4,6},{5,7},{6,4},{7,5},{8,10},{9,11},{10,... | collective-permute-start | bytes 294920 | tf_op jit(solution)/shard_map/ppermute | solution.py:29
  85.7 9.3 %collective-permute-start.5 = (bf16[32,1536]{1,0:T(8,128)(2,1)S(1)}, bf16[32,1536]{1,0:T(8,128)(2,1)S(1)}, u32[]{:S(2)}, u32[]{:S(2)}) collective-permute-start(bf16[32,1536]{1,0:T(8,128)(2,1)S(1)} %add.225), channel_id=1, source_target_pairs={{0,4},{1,5},{2,6},{3,7},{4,0},{5,1},{6,2},{7,3},{8,9},{9,8},{10,11... | collective-permute-start | bytes 294920 | tf_op jit(solution)/shard_map/ppermute | solution.py:29

commit v10 on v9

--- a/solution.py
+++ b/solution.py
@@ -14,19 +14,13 @@
     return values * lax.rsqrt(jnp.mean(values * values, axis=-1, keepdims=True) + epsilon) * gain
 
 
-def staggered_sum(values, req_size, tp_size):
-    steps = []
+def tree_sum(values, axis, size):
     step = 1
-    while step < tp_size:
-        steps.append(step)
+    while step < size // 2:
+        values = values + lax.ppermute(values, axis, [(i, i ^ step) for i in range(size)])
         step *= 2
-    for round_index in range(len(steps)):
-        pairs = []
-        for q in range(req_size):
-            order = steps if q % 2 == 0 else steps[::-1]
-            for t in range(tp_size):
-                pairs.append((q * tp_size + t, q * tp_size + (t ^ order[round_index])))
-        values = values + lax.ppermute(values, ("req", "tp"), pairs)
+    if size > 1:
+        values = values + lax.ppermute(values, axis, [(i, size - 1 - i) for i in range(size)])
     return values
 
 
@@ -194,7 +188,7 @@
             .reshape(req_dev * steps, heads_dev * head_dim)
         )
         projected = jnp.dot(attended, out_weight, preferred_element_type=jnp.float32)
-        attn_total = staggered_sum(projected.astype(jnp.bfloat16), req_size, tp_size).astype(jnp.float32)
+        attn_total = tree_sum(projected.astype(jnp.bfloat16), "tp", tp_size).astype(jnp.float32)
         residual = (token_rows.astype(jnp.float32) + attn_total).astype(jnp.bfloat16)
         mlp_in = rms_norm(residual.astype(jnp.float32), mlp_gain).astype(jnp.bfloat16)
         gate = jnp.dot(mlp_in, gate_weight, preferred_element_type=jnp.float32)
@@ -203,7 +197,7 @@
         mlp_part = jnp.dot(hidden, down_weight, preferred_element_type=jnp.float32).astype(
             jnp.bfloat16
         )
-        mlp_total = staggered_sum(mlp_part, req_size, tp_size).astype(jnp.float32)
+        mlp_total = tree_sum(mlp_part, "tp", tp_size).astype(jnp.float32)
         layer_out = (residual.astype(jnp.float32) + mlp_total).astype(jnp.bfloat16)
         return layer_out.reshape(req_dev, steps, width)
 

time: 97.2 us -> 94.8 us (0.975)
  starting transfers between devices: 34.1 us -> 25.4 us
  waiting for transfers between devices: 37.6 us -> 44.2 us
    ppermute x6, starting transfers between devices: 21.3 us -> 12.7 us  [the longest x2 7.08 us: tree_sum(): lax.ppermute(values, axis, [(i, size - 1 - i) for i in range(size)])]
    ppermute x6, waiting for transfers between devices: 22 us -> 28.6 us  [the longest x4 19.9 us: tree_sum(): lax.ppermute(values, axis, [(i, i ^ step) for i in range(size)])]
where the time goes in v10:
time: 94.8 us; the launch traced here: 93.6 us
  waiting for transfers between devices  44.2 us (47%)
  starting transfers between devices  25.4 us (27%)
  matrix products  11.1 us (12%)
  other arithmetic  6.76 us (7%)
  local copies, waits for them, and re-layouts  5.83 us (6%)
    ppermute x4, waiting for transfers between devices, tree_sum(): lax.ppermute(values, axis, [(i, i ^ step) for i in range(size)])  19.9 us
    ppermute x2, waiting for transfers between devices, tree_sum(): lax.ppermute(values, axis, [(i, size - 1 - i) for i in range(size)])  8.78 us
    all_to_all x1, waiting for transfers between devices, body(): lax.all_to_all(send, 'req', 0, 0, tiled=True).reshape(req_size, req_dev, -1)  7.79 us
    all_to_all x1, waiting for transfers between devices, body(): lax.all_to_all(jnp.broadcast_to(packed[None], (req_size,) + packed.shape)...  7.74 us
    all_to_all x1, starting transfers between devices, body(): lax.all_to_all(jnp.broadcast_to(packed[None], (req_size,) + packed.shape)...  7.62 us
    ppermute x2, starting transfers between devices, tree_sum(): lax.ppermute(values, axis, [(i, size - 1 - i) for i in range(size)])  7.08 us
    ppermute x4, starting transfers between devices, tree_sum(): lax.ppermute(values, axis, [(i, i ^ step) for i in range(size)])  5.59 us
    all_to_all x1, starting transfers between devices, body(): lax.all_to_all(send, 'req', 0, 0, tiled=True).reshape(req_size, req_dev, -1)  5.11 us
  transfers between devices with their start and end apart: 8, of which 8 were waited for; matrix products, arithmetic and copies ran while one was open for 1% of the time, Pallas kernels for 0%

profile of v10, /device:TPU:2, one launch (start us, length us, event | category | flops | bytes accessed | tf_op | source)
XLA Modules:
  0.0 93.6 jit_solution(865603104763036102)
XLA Ops:
  0.0 1.2 %multiply_reduce_fusion = f32[8,4]{1,0:T(8,128)S(1)} fusion(bf16[8,4,1536]{2,1,0:T(4,128)(2,1)} %param.13), kind=kLoop, calls=%fused_computation.39 | loop fusion | flops 147424 | bytes 98432 | tf_op jit(solution)/shard_map/reduce_sum | solution.py:14
  1.2 0.9 reshape.470
  2.1 0.7 fusion.53
  3.0 0.7 fusion.48
  3.7 0.8 multiply_convert_fusion
  4.5 1.2 %fusion.16 = bf16[32,128]{1,0:T(8,128)(2,1)S(1)} fusion(bf16[32,1536]{1,0:T(8,128)(2,1)S(1)} %multiply_convert_fusion, bf16[1536,128]{1,0:T(8,128)(2,1)} %param.18), kind=kOutput, calls=%fused_computation.19 | convolution fusion | flops 12591104 | bytes 499712 | tf_op jit(solution)/shard_map/dot_general | solution.py:54
  5.8 0.7 broadcast_in_dim.131
  6.6 7.6 %all-to-all-start = ((bf16[32,8,532]{2,1,0:T(8,128)(2,1)}), bf16[32,8,532]{2,1,0:T(8,128)(2,1)S(1)}, u32[]{:S(2)}, u32[]{:S(2)}) async-start(bf16[32,8,532]{2,1,0:T(8,128)(2,1)} %broadcast_in_dim.131), calls=%async_computation | async-start | bytes 655360 | tf_op jit(solution)/shard_map/all_to_all | solution.py:71
  14.7 7.7 %all-to-all-done = bf16[32,8,532]{2,1,0:T(8,128)(2,1)S(1)} async-done(((bf16[32,8,532]{2,1,0:T(8,128)(2,1)}), bf16[32,8,532]{2,1,0:T(8,128)(2,1)S(1)}, u32[]{:S(2)}, u32[]{:S(2)}) %all-to-all-start) | async-done | bytes 272416 | tf_op jit(solution)/shard_map/all_to_all | solution.py:71
  23.3 0.3 fusion.18
  24.2 0.7 gather_fusion
  24.8 3.1 %fusion.65 = (f32[72,4]{1,0:T(8,128)S(1)}, f32[72,4,128]{2,1,0:T(4,128)S(1)}) fusion(bf16[72,4,128]{2,1,0:T(4,128)(2,1)S(1)} %gather_fusion, bf16[72,2,128,128]{3,2,1,0:T(8,128)(2,1)} %param.16, s32[72,4]{1,0:T(8,128)S(1)} %add_add_fusion, s32[72,128]{1,0:T(8,128)S(1)} %iota_add_fusion, pred[72,128]{1,0:T(8,128)(4,1)S(1)} %broadcast_compare_fusion.1), kind=kOutput, calls=%fused_computation.129 | convolution fusion | flops 9584352 | bytes 2628864 | tf_op jit(solution)/shard_map/pqd,pkd->pqk/dot_general | solution.py:101
  28.4 0.3 fusion.56
  28.7 2.5 %fusion.9 = f32[72,4,128]{2,1,0:T(4,128)S(1)} fusion(bf16[72,2,128,128]{3,2,1,0:T(8,128)(2,1)} %param.16, f32[72,4]{1,0:T(8,128)S(1)} %get-tuple-element.14, f32[72,4,128]{2,1,0:T(4,128)S(1)} %get-tuple-element.28, f32[72,4]{1,0:T(8,128)S(1)} %get-tuple-element.27, s32[72,4]{1,0:T(8,128)S(1)} %add_add_fusion, s32[72,128]{1,0:T(8,128)S(1)} %iota_add_fusion, ...), kind=kOutput, calls=%fused_computation.11 | convolution fusion | flops 9658368 | bytes 2703744 | tf_op jit(solution)/shard_map/pqk,pkd->pqd/dot_general | solution.py:108
  31.9 0.5 convolution_convert_fusion.2
  32.6 0.8 pad_maximum_fusion
  33.4 5.1 %all-to-all-start.1 = ((bf16[32,8,528]{2,1,0:T(8,128)(2,1)}), bf16[32,8,528]{2,1,0:T(8,128)(2,1)S(1)}, u32[]{:S(2)}, u32[]{:S(2)}) async-start(bf16[32,8,528]{2,1,0:T(8,128)(2,1)} %pad_maximum_fusion), calls=%async_computation.1 | async-start | bytes 655360 | tf_op jit(solution)/shard_map/all_to_all | solution.py:146
  39.1 7.8 %all-to-all-done.1 = bf16[32,8,528]{2,1,0:T(8,128)(2,1)S(1)} async-done(((bf16[32,8,528]{2,1,0:T(8,128)(2,1)}), bf16[32,8,528]{2,1,0:T(8,128)(2,1)S(1)}, u32[]{:S(2)}, u32[]{:S(2)}) %all-to-all-start.1) | async-done | bytes 270368 | tf_op jit(solution)/shard_map/all_to_all | solution.py:146
  47.3 0.3 copy.115
  48.2 2.0 %collective-permute-start = (bf16[32,1536]{1,0:T(8,128)(2,1)S(1)}, bf16[32,1536]{1,0:T(8,128)(2,1)S(1)}, u32[]{:S(2)}, u32[]{:S(2)}) collective-permute-start(bf16[32,1536]{1,0:T(8,128)(2,1)S(1)} %convolution_convert_fusion.1), channel_id=1, source_target_pairs={{0,1},{1,0},{2,3},{3,2},{4,5},{5,4},{6,7},{7,6},{8,9},{9,8},{10,11... | collective-permute-start | bytes 294920 | tf_op jit(solution)/shard_map/ppermute | solution.py:20
  50.2 3.5 %collective-permute-done = bf16[32,1536]{1,0:T(8,128)(2,1)S(1)} collective-permute-done((bf16[32,1536]{1,0:T(8,128)(2,1)S(1)}, bf16[32,1536]{1,0:T(8,128)(2,1)S(1)}, u32[]{:S(2)}, u32[]{:S(2)}) %collective-permute-start) | collective-permute-done | bytes 98336 | tf_op jit(solution)/shard_map/ppermute | solution.py:20
  53.7 3.4 %collective-permute-start.1 = (bf16[32,1536]{1,0:T(8,128)(2,1)S(1)}, bf16[32,1536]{1,0:T(8,128)(2,1)S(1)}, u32[]{:S(2)}, u32[]{:S(2)}) collective-permute-start(bf16[32,1536]{1,0:T(8,128)(2,1)S(1)} %add.216), channel_id=1, source_target_pairs={{0,2},{1,3},{2,0},{3,1},{4,6},{5,7},{6,4},{7,5},{8,10},{9,11},{10,... | collective-permute-start | bytes 294920 | tf_op jit(solution)/shard_map/ppermute | solution.py:20
  57.0 4.9 %collective-permute-done.1 = bf16[32,1536]{1,0:T(8,128)(2,1)S(1)} collective-permute-done((bf16[32,1536]{1,0:T(8,128)(2,1)S(1)}, bf16[32,1536]{1,0:T(8,128)(2,1)S(1)}, u32[]{:S(2)}, u32[]{:S(2)}) %collective-permute-start.1) | collective-permute-done | bytes 98336 | tf_op jit(solution)/shard_map/ppermute | solution.py:20
  62.0 5.0 %collective-permute-start.2 = (bf16[32,1536]{1,0:T(8,128)(2,1)S(1)}, bf16[32,1536]{1,0:T(8,128)(2,1)S(1)}, u32[]{:S(2)}, u32[]{:S(2)}) collective-permute-start(bf16[32,1536]{1,0:T(8,128)(2,1)S(1)} %add.217), channel_id=1, source_target_pairs={{0,7},{1,6},{2,5},{3,4},{4,3},{5,2},{6,1},{7,0},{8,15},{9,14},{10,... | collective-permute-start | bytes 294920 | tf_op jit(solution)/shard_map/ppermute | solution.py:23
  66.9 4.2 %collective-permute-done.2 = bf16[32,1536]{1,0:T(8,128)(2,1)S(1)} collective-permute-done((bf16[32,1536]{1,0:T(8,128)(2,1)S(1)}, bf16[32,1536]{1,0:T(8,128)(2,1)S(1)}, u32[]{:S(2)}, u32[]{:S(2)}) %collective-permute-start.2) | collective-permute-done | bytes 98336 | tf_op jit(solution)/shard_map/ppermute | solution.py:23
  71.3 0.6 fusion.42
  71.9 2.5 %convolution_convert_fusion = bf16[32,1536]{1,0:T(8,128)(2,1)S(1)} fusion(bf16[576,1536]{1,0:T(8,128)(2,1)S(1)} %copy-done, bf16[1536,576]{0,1:T(8,128)(2,1)} %param.24, f32[32,576]{1,0:T(8,128)S(1)} %fusion.42, bf16[32,1536]{1,0:T(8,128)(2,1)S(1)} %get-tuple-element.8, f32[1536]{0:T(1024)S(1)} %copy-done.5, f32[32]{0:T(128)S(1)} %add_rsqrt_fusion.1), kind=kOutput, calls=%fused_computation.7 | convolution fusion | flops 113676288 | bytes 3815552 | tf_op jit(solution)/shard_map/dot_general | solution.py:197
  74.5 4.7 %collective-permute-done.3 = bf16[32,1536]{1,0:T(8,128)(2,1)S(1)} collective-permute-done((bf16[32,1536]{1,0:T(8,128)(2,1)S(1)}, bf16[32,1536]{1,0:T(8,128)(2,1)S(1)}, u32[]{:S(2)}, u32[]{:S(2)}) %collective-permute-start.3) | collective-permute-done | bytes 98336 | tf_op jit(solution)/shard_map/ppermute | solution.py:20
  79.4 6.8 %collective-permute-done.4 = bf16[32,1536]{1,0:T(8,128)(2,1)S(1)} collective-permute-done((bf16[32,1536]{1,0:T(8,128)(2,1)S(1)}, bf16[32,1536]{1,0:T(8,128)(2,1)S(1)}, u32[]{:S(2)}, u32[]{:S(2)}) %collective-permute-start.4) | collective-permute-done | bytes 98336 | tf_op jit(solution)/shard_map/ppermute | solution.py:20
  86.2 2.1 %collective-permute-start.5 = (bf16[32,1536]{1,0:T(8,128)(2,1)S(1)}, bf16[32,1536]{1,0:T(8,128)(2,1)S(1)}, u32[]{:S(2)}, u32[]{:S(2)}) collective-permute-start(bf16[32,1536]{1,0:T(8,128)(2,1)S(1)} %add.225), channel_id=1, source_target_pairs={{0,7},{1,6},{2,5},{3,4},{4,3},{5,2},{6,1},{7,0},{8,15},{9,14},{10,... | collective-permute-start | bytes 294920 | tf_op jit(solution)/shard_map/ppermute | solution.py:23
  88.4 4.6 %collective-permute-done.5 = bf16[32,1536]{1,0:T(8,128)(2,1)S(1)} collective-permute-done((bf16[32,1536]{1,0:T(8,128)(2,1)S(1)}, bf16[32,1536]{1,0:T(8,128)(2,1)S(1)}, u32[]{:S(2)}, u32[]{:S(2)}) %collective-permute-start.5) | collective-permute-done | bytes 98336 | tf_op jit(solution)/shard_map/ppermute | solution.py:23
  93.0 0.7 reshape.469
  (76 shorter events, 5.6 us)
Async XLA Ops:
  0.0 71.9 %copy-start = (bf16[576,1536]{1,0:T(8,128)(2,1)S(1)}, bf16[576,1536]{1,0:T(8,128)(2,1)}, u32[]{:S(2)}) copy-start(bf16[576,1536]{1,0:T(8,128)(2,1)} %param.25) | copy-start | bytes 5308420
  0.0 14.2 %copy-start.2 = (bf16[1536,128]{1,0:T(8,128)(2,1)S(1)}, bf16[1536,128]{1,0:T(8,128)(2,1)}, u32[]{:S(2)}) copy-start(bf16[1536,128]{1,0:T(8,128)(2,1)} %param.19) | copy-start | bytes 1179652
  6.6 15.9 %all-to-all-start = ((bf16[32,8,532]{2,1,0:T(8,128)(2,1)}), bf16[32,8,532]{2,1,0:T(8,128)(2,1)S(1)}, u32[]{:S(2)}, u32[]{:S(2)}) async-start(bf16[32,8,532]{2,1,0:T(8,128)(2,1)} %broadcast_in_dim.131), calls=%async_computation | async-start | bytes 655360 | tf_op jit(solution)/shard_map/all_to_all | solution.py:71
  31.2 7.7 %copy-start.3 = (bf16[1536,128]{1,0:T(8,128)(2,1)S(1)}, bf16[1536,128]{1,0:T(8,128)(2,1)}, u32[]{:S(2)}) copy-start(bf16[1536,128]{1,0:T(8,128)(2,1)} %param.20) | copy-start | bytes 1179652
  33.4 14.6 %copy-start.4 = (bf16[128,1536]{1,0:T(8,128)(2,1)S(1)}, bf16[128,1536]{1,0:T(8,128)(2,1)}, u32[]{:S(2)}) copy-start(bf16[128,1536]{1,0:T(8,128)(2,1)} %param.21) | copy-start | bytes 1179652
  33.4 13.5 %all-to-all-start.1 = ((bf16[32,8,528]{2,1,0:T(8,128)(2,1)}), bf16[32,8,528]{2,1,0:T(8,128)(2,1)S(1)}, u32[]{:S(2)}, u32[]{:S(2)}) async-start(bf16[32,8,528]{2,1,0:T(8,128)(2,1)} %pad_maximum_fusion), calls=%async_computation.1 | async-start | bytes 655360 | tf_op jit(solution)/shard_map/all_to_all | solution.py:146
  39.1 32.2 %copy-start.5 = (f32[1536]{0:T(1024)S(1)}, f32[1536]{0:T(1024)}, u32[]{:S(2)}) copy-start(f32[1536]{0:T(1024)} %param.22) | copy-start | bytes 18436
  47.8 23.5 %copy-start.1 = (bf16[1536,576]{0,1:T(8,128)(2,1)S(1)}, bf16[1536,576]{0,1:T(8,128)(2,1)}, u32[]{:S(2)}) copy-start(bf16[1536,576]{0,1:T(8,128)(2,1)} %param.23) | copy-start | bytes 5308420
  48.2 5.5 %collective-permute-start = (bf16[32,1536]{1,0:T(8,128)(2,1)S(1)}, bf16[32,1536]{1,0:T(8,128)(2,1)S(1)}, u32[]{:S(2)}, u32[]{:S(2)}) collective-permute-start(bf16[32,1536]{1,0:T(8,128)(2,1)S(1)} %convolution_convert_fusion.1), channel_id=1, source_target_pairs={{0,1},{1,0},{2,3},{3,2},{4,5},{5,4},{6,7},{7,6},{8,9},{9,8},{10,11... | collective-permute-start | bytes 294920 | tf_op jit(solution)/shard_map/ppermute | solution.py:20
  53.7 8.3 %collective-permute-start.1 = (bf16[32,1536]{1,0:T(8,128)(2,1)S(1)}, bf16[32,1536]{1,0:T(8,128)(2,1)S(1)}, u32[]{:S(2)}, u32[]{:S(2)}) collective-permute-start(bf16[32,1536]{1,0:T(8,128)(2,1)S(1)} %add.216), channel_id=1, source_target_pairs={{0,2},{1,3},{2,0},{3,1},{4,6},{5,7},{6,4},{7,5},{8,10},{9,11},{10,... | collective-permute-start | bytes 294920 | tf_op jit(solution)/shard_map/ppermute | solution.py:20
  62.0 9.2 %collective-permute-start.2 = (bf16[32,1536]{1,0:T(8,128)(2,1)S(1)}, bf16[32,1536]{1,0:T(8,128)(2,1)S(1)}, u32[]{:S(2)}, u32[]{:S(2)}) collective-permute-start(bf16[32,1536]{1,0:T(8,128)(2,1)S(1)} %add.217), channel_id=1, source_target_pairs={{0,7},{1,6},{2,5},{3,4},{4,3},{5,2},{6,1},{7,0},{8,15},{9,14},{10,... | collective-permute-start | bytes 294920 | tf_op jit(solution)/shard_map/ppermute | solution.py:23
  74.5 4.8 %collective-permute-start.3 = (bf16[32,1536]{1,0:T(8,128)(2,1)S(1)}, bf16[32,1536]{1,0:T(8,128)(2,1)S(1)}, u32[]{:S(2)}, u32[]{:S(2)}) collective-permute-start(bf16[32,1536]{1,0:T(8,128)(2,1)S(1)} %convolution_convert_fusion), channel_id=1, source_target_pairs={{0,1},{1,0},{2,3},{3,2},{4,5},{5,4},{6,7},{7,6},{8,9},{9,8},{10,11... | collective-permute-start | bytes 294920 | tf_op jit(solution)/shard_map/ppermute | solution.py:20
  79.3 7.0 %collective-permute-start.4 = (bf16[32,1536]{1,0:T(8,128)(2,1)S(1)}, bf16[32,1536]{1,0:T(8,128)(2,1)S(1)}, u32[]{:S(2)}, u32[]{:S(2)}) collective-permute-start(bf16[32,1536]{1,0:T(8,128)(2,1)S(1)} %add.224), channel_id=1, source_target_pairs={{0,2},{1,3},{2,0},{3,1},{4,6},{5,7},{6,4},{7,5},{8,10},{9,11},{10,... | collective-permute-start | bytes 294920 | tf_op jit(solution)/shard_map/ppermute | solution.py:20
  86.2 6.7 %collective-permute-start.5 = (bf16[32,1536]{1,0:T(8,128)(2,1)S(1)}, bf16[32,1536]{1,0:T(8,128)(2,1)S(1)}, u32[]{:S(2)}, u32[]{:S(2)}) collective-permute-start(bf16[32,1536]{1,0:T(8,128)(2,1)S(1)} %add.225), channel_id=1, source_target_pairs={{0,7},{1,6},{2,5},{3,4},{4,3},{5,2},{6,1},{7,0},{8,15},{9,14},{10,... | collective-permute-start | bytes 294920 | tf_op jit(solution)/shard_map/ppermute | solution.py:23

commit v11 on v10

--- a/solution.py
+++ b/solution.py
@@ -14,8 +14,8 @@
     return values * lax.rsqrt(jnp.mean(values * values, axis=-1, keepdims=True) + epsilon) * gain
 
 
-def tree_sum(values, axis, size):
-    step = 1
+def tree_sum(values, axis, size, first_step=1):
+    step = first_step
     while step < size // 2:
         values = values + lax.ppermute(values, axis, [(i, i ^ step) for i in range(size)])
         step *= 2
@@ -49,6 +49,7 @@
         requests = req_dev * req_size
         qwidth = steps * heads_dev * head_dim
         token_rows = tokens.reshape(req_dev * steps, width)
+        partner_weight = lax.ppermute(out_weight, "tp", [(i, i ^ 1) for i in range(tp_size)])
         normed = rms_norm(token_rows.astype(jnp.float32), norm_gain).astype(jnp.bfloat16)
         queries = (
             jnp.dot(normed, query_weight, preferred_element_type=jnp.float32) * head_dim ** (-0.5)
@@ -187,8 +188,20 @@
             .astype(jnp.bfloat16)
             .reshape(req_dev * steps, heads_dev * head_dim)
         )
-        projected = jnp.dot(attended, out_weight, preferred_element_type=jnp.float32)
-        attn_total = tree_sum(projected.astype(jnp.bfloat16), "tp", tp_size).astype(jnp.float32)
+        pair = [(i, i ^ 1) for i in range(tp_size)]
+        other_head = lax.ppermute(attended, "tp", pair)
+        lower = lax.axis_index("tp") % 2 == 0
+        pair_heads = jnp.concatenate(
+            [jnp.where(lower, attended, other_head), jnp.where(lower, other_head, attended)], axis=1
+        )
+        pair_weight = jnp.concatenate(
+            [jnp.where(lower, out_weight, partner_weight), jnp.where(lower, partner_weight, out_weight)],
+            axis=0,
+        )
+        projected = jnp.dot(pair_heads, pair_weight, preferred_element_type=jnp.float32)
+        attn_total = tree_sum(
+            projected.astype(jnp.bfloat16), "tp", tp_size, first_step=2
+        ).astype(jnp.float32)
         residual = (token_rows.astype(jnp.float32) + attn_total).astype(jnp.bfloat16)
         mlp_in = rms_norm(residual.astype(jnp.float32), mlp_gain).astype(jnp.bfloat16)
         gate = jnp.dot(mlp_in, gate_weight, preferred_element_type=jnp.float32)

time: 94.8 us -> 93.9 us (level)
  waiting for transfers between devices: 44.2 us -> 36.2 us
  other arithmetic: 6.76 us -> 9.93 us
  starting transfers between devices: 25.4 us -> 27.9 us
  local copies, waits for them, and re-layouts: 5.83 us -> 7.74 us
    ppermute x0 -> x2, starting transfers between devices: none -> 4 us  [the longest x1 2 us: body(): lax.ppermute(out_weight, 'tp', [(i, i ^ 1) for i in range(tp_size)])]
    ppermute x4 -> x3, waiting for transfers between devices: 19.9 us -> 15.9 us  [tree_sum(): lax.ppermute(values, axis, [(i, i ^ step) for i in range(size)])]
    all_to_all x1, waiting for transfers between devices: 7.74 us -> 5.14 us  [body(): lax.all_to_all(jnp.broadcast_to(packed[None], (req_size,) + packed.shape)...]
    ppermute x4 -> x3, starting transfers between devices: 5.59 us -> 3.8 us  [tree_sum(): lax.ppermute(values, axis, [(i, i ^ step) for i in range(size)])]
    all_to_all x1, waiting for transfers between devices: 7.79 us -> 6.45 us  [body(): lax.all_to_all(send, 'req', 0, 0, tiled=True).reshape(req_size, req_dev, -1)]
    another operation x4, local copies, waits for them, and re-layouts: 0.67 us -> 1.9 us
    select_n x0 -> x2, other arithmetic: none -> 1.06 us  [the longest x1 1.05 us: body(): jnp.where(lower, out_weight, partner_weight)]
  transfers between devices with their start and end apart: 8 -> 9, of which waited for: 8 -> 8; matrix products, arithmetic and copies ran while one was open for 1% -> 19% of each run, Pallas kernels for 0% -> 0%
where the time goes in v11:
time: 93.9 us; the launch traced here: 93.3 us
  waiting for transfers between devices  36.2 us (39%)
  starting transfers between devices  27.9 us (30%)
  matrix products  11.1 us (12%)
  other arithmetic  9.93 us (11%)
  local copies, waits for them, and re-layouts  7.74 us (8%)
    ppermute x3, waiting for transfers between devices, tree_sum(): lax.ppermute(values, axis, [(i, i ^ step) for i in range(size)])  15.9 us
    ppermute x2, waiting for transfers between devices, tree_sum(): lax.ppermute(values, axis, [(i, size - 1 - i) for i in range(size)])  8.06 us
    all_to_all x1, starting transfers between devices, body(): lax.all_to_all(jnp.broadcast_to(packed[None], (req_size,) + packed.shape)...  7.62 us
    ppermute x2, starting transfers between devices, tree_sum(): lax.ppermute(values, axis, [(i, size - 1 - i) for i in range(size)])  7.48 us
    all_to_all x1, waiting for transfers between devices, body(): lax.all_to_all(send, 'req', 0, 0, tiled=True).reshape(req_size, req_dev, -1)  6.45 us
    all_to_all x1, waiting for transfers between devices, body(): lax.all_to_all(jnp.broadcast_to(packed[None], (req_size,) + packed.shape)...  5.14 us
    all_to_all x1, starting transfers between devices, body(): lax.all_to_all(send, 'req', 0, 0, tiled=True).reshape(req_size, req_dev, -1)  4.98 us
    ppermute x3, starting transfers between devices, tree_sum(): lax.ppermute(values, axis, [(i, i ^ step) for i in range(size)])  3.8 us
  transfers between devices with their start and end apart: 9, of which 8 were waited for; matrix products, arithmetic and copies ran while one was open for 19% of the time, Pallas kernels for 0%

profile of v11, /device:TPU:2, one launch (start us, length us, event | category | flops | bytes accessed | tf_op | source)
XLA Modules:
  0.0 93.3 jit_solution(2271541989356566323)
XLA Ops:
  0.0 1.2 %multiply_reduce_fusion = f32[8,4]{1,0:T(8,128)S(1)} fusion(bf16[8,4,1536]{2,1,0:T(4,128)(2,1)} %param.13), kind=kLoop, calls=%fused_computation.44 | loop fusion | flops 147424 | bytes 98432 | tf_op jit(solution)/shard_map/reduce_sum | solution.py:14
  1.2 0.9 reshape.470
  3.0 0.7 fusion.54
  3.8 0.8 multiply_convert_fusion
  4.5 1.2 %fusion.16 = bf16[32,128]{1,0:T(8,128)(2,1)S(1)} fusion(bf16[32,1536]{1,0:T(8,128)(2,1)S(1)} %multiply_convert_fusion, bf16[1536,128]{1,0:T(8,128)(2,1)} %param.18), kind=kOutput, calls=%fused_computation.19 | convolution fusion | flops 12591104 | bytes 499712 | tf_op jit(solution)/shard_map/dot_general | solution.py:55
  5.9 0.7 broadcast_in_dim.131
  6.6 7.6 %all-to-all-start = ((bf16[32,8,532]{2,1,0:T(8,128)(2,1)}), bf16[32,8,532]{2,1,0:T(8,128)(2,1)S(1)}, u32[]{:S(2)}, u32[]{:S(2)}) async-start(bf16[32,8,532]{2,1,0:T(8,128)(2,1)} %broadcast_in_dim.131), calls=%async_computation | async-start | bytes 655360 | tf_op jit(solution)/shard_map/all_to_all | solution.py:72
  14.2 2.0 %collective-permute-start.1 = (bf16[128,1536]{1,0:T(8,128)(2,1)S(1)}, bf16[128,1536]{1,0:T(8,128)(2,1)}, u32[]{:S(2)}, u32[]{:S(2)}) collective-permute-start(bf16[128,1536]{1,0:T(8,128)(2,1)S(1)} %copy-done.4), channel_id=1, source_target_pairs={{0,1},{1,0},{2,3},{3,2},{4,5},{5,4},{6,7},{7,6},{8,9},{9,8},{10,11... | collective-permute-start | bytes 1179656 | tf_op jit(solution)/shard_map/ppermute | solution.py:52
  16.7 0.7 select_reduce_fusion.2
  17.4 5.1 %all-to-all-done = bf16[32,8,532]{2,1,0:T(8,128)(2,1)S(1)} async-done(((bf16[32,8,532]{2,1,0:T(8,128)(2,1)}), bf16[32,8,532]{2,1,0:T(8,128)(2,1)S(1)}, u32[]{:S(2)}, u32[]{:S(2)}) %all-to-all-start) | async-done | bytes 272416 | tf_op jit(solution)/shard_map/all_to_all | solution.py:72
  24.9 3.1 %fusion.72 = (f32[72,4]{1,0:T(8,128)S(1)}, f32[72,4,128]{2,1,0:T(4,128)S(1)}) fusion(bf16[72,4,128]{2,1,0:T(4,128)(2,1)S(1)} %gather_fusion, bf16[72,2,128,128]{3,2,1,0:T(8,128)(2,1)} %param.16, s32[72,4]{1,0:T(8,128)S(1)} %add_add_fusion, s32[72,128]{1,0:T(8,128)S(1)} %iota_add_fusion, pred[72,128]{1,0:T(8,128)(4,1)S(1)} %broadcast_compare_fusion.1), kind=kOutput, calls=%fused_computation.140 | convolution fusion | flops 9584352 | bytes 2628864 | tf_op jit(solution)/shard_map/pqd,pkd->pqk/dot_general | solution.py:102
  28.8 2.5 %fusion.9 = f32[72,4,128]{2,1,0:T(4,128)S(1)} fusion(bf16[72,2,128,128]{3,2,1,0:T(8,128)(2,1)} %param.16, f32[72,4]{1,0:T(8,128)S(1)} %get-tuple-element.14, f32[72,4,128]{2,1,0:T(4,128)S(1)} %get-tuple-element.32, f32[72,4]{1,0:T(8,128)S(1)} %get-tuple-element.31, s32[72,4]{1,0:T(8,128)S(1)} %add_add_fusion, s32[72,128]{1,0:T(8,128)S(1)} %iota_add_fusion, ...), kind=kOutput, calls=%fused_computation.11 | convolution fusion | flops 9658368 | bytes 2703744 | tf_op jit(solution)/shard_map/pqk,pkd->pqd/dot_general | solution.py:109
  31.6 0.8 copy.112
  32.4 0.8 copy.111
  33.8 1.7 %pad_maximum_fusion = bf16[32,8,528]{2,1,0:T(8,128)(2,1)} fusion(bf16[32,8,4]{2,1,0:T(8,128)(2,1)} %copy.112, bf16[32,8,4]{2,1,0:T(8,128)(2,1)} %copy.111, bf16[32,8,4]{2,1,0:T(8,128)(2,1)S(1)} %copy.110, bf16[32,8,516]{2,1,0:T(8,128)(2,1)S(1)} %bitcast.65), kind=kLoop, calls=%fused_computation.33 | loop fusion | flops 1081344 | bytes 540672 | tf_op jit(solution)/shard_map/concatenate | solution.py:144
  35.5 5.0 %all-to-all-start.1 = ((bf16[32,8,528]{2,1,0:T(8,128)(2,1)}), bf16[32,8,528]{2,1,0:T(8,128)(2,1)S(1)}, u32[]{:S(2)}, u32[]{:S(2)}) async-start(bf16[32,8,528]{2,1,0:T(8,128)(2,1)} %pad_maximum_fusion), calls=%async_computation.1 | async-start | bytes 655360 | tf_op jit(solution)/shard_map/all_to_all | solution.py:147
  40.5 0.8 fusion.51
  41.3 0.8 copy.114
  42.4 6.5 %all-to-all-done.1 = bf16[32,8,528]{2,1,0:T(8,128)(2,1)S(1)} async-done(((bf16[32,8,528]{2,1,0:T(8,128)(2,1)}), bf16[32,8,528]{2,1,0:T(8,128)(2,1)S(1)}, u32[]{:S(2)}, u32[]{:S(2)}) %all-to-all-start.1) | async-done | bytes 270368 | tf_op jit(solution)/shard_map/all_to_all | solution.py:147
  49.9 2.0 %collective-permute-start = (bf16[32,128]{1,0:T(8,128)(2,1)S(1)}, bf16[32,128]{1,0:T(8,128)(2,1)S(1)}, u32[]{:S(2)}, u32[]{:S(2)}) collective-permute-start(bf16[32,128]{1,0:T(8,128)(2,1)S(1)} %bitcast.72), channel_id=1, source_target_pairs={{0,1},{1,0},{2,3},{3,2},{4,5},{5,4},{6,7},{7,6},{8,9},{9,8},{10,11... | collective-permute-start | bytes 24584 | tf_op jit(solution)/shard_map/ppermute | solution.py:192
  51.9 1.1 %broadcast_select_fusion.1 = (bf16[128,1536]{1,0:T(8,128)(2,1)S(1)}, bf16[128,1536]{1,0:T(8,128)(2,1)S(1)}) fusion(bf16[128,1536]{1,0:T(8,128)(2,1)S(1)} %copy-done.4, bf16[128,1536]{1,0:T(8,128)(2,1)} %collective-permute-done.1, pred[]{:T(512)S(6)} %eq.60), kind=kLoop, calls=%fused_computation.32 | loop fusion | flops 393216 | bytes 1572865 | tf_op jit(solution)/shard_map/jit(_where)/select_n | solution.py:198
  53.0 0.7 collective-permute-done
  53.9 3.3 %collective-permute-start.2 = (bf16[32,1536]{1,0:T(8,128)(2,1)S(1)}, bf16[32,1536]{1,0:T(8,128)(2,1)S(1)}, u32[]{:S(2)}, u32[]{:S(2)}) collective-permute-start(bf16[32,1536]{1,0:T(8,128)(2,1)S(1)} %convolution_convert_fusion.1), channel_id=1, source_target_pairs={{0,2},{1,3},{2,0},{3,1},{4,6},{5,7},{6,4},{7,5},{8,10},{9,11},{10,... | collective-permute-start | bytes 294920 | tf_op jit(solution)/shard_map/ppermute | solution.py:20
  57.3 4.7 %collective-permute-done.2 = bf16[32,1536]{1,0:T(8,128)(2,1)S(1)} collective-permute-done((bf16[32,1536]{1,0:T(8,128)(2,1)S(1)}, bf16[32,1536]{1,0:T(8,128)(2,1)S(1)}, u32[]{:S(2)}, u32[]{:S(2)}) %collective-permute-start.2) | collective-permute-done | bytes 98336 | tf_op jit(solution)/shard_map/ppermute | solution.py:20
  62.0 5.0 %collective-permute-start.3 = (bf16[32,1536]{1,0:T(8,128)(2,1)S(1)}, bf16[32,1536]{1,0:T(8,128)(2,1)S(1)}, u32[]{:S(2)}, u32[]{:S(2)}) collective-permute-start(bf16[32,1536]{1,0:T(8,128)(2,1)S(1)} %add.218), channel_id=1, source_target_pairs={{0,7},{1,6},{2,5},{3,4},{4,3},{5,2},{6,1},{7,0},{8,15},{9,14},{10,... | collective-permute-start | bytes 294920 | tf_op jit(solution)/shard_map/ppermute | solution.py:23
  67.0 3.9 %collective-permute-done.3 = bf16[32,1536]{1,0:T(8,128)(2,1)S(1)} collective-permute-done((bf16[32,1536]{1,0:T(8,128)(2,1)S(1)}, bf16[32,1536]{1,0:T(8,128)(2,1)S(1)}, u32[]{:S(2)}, u32[]{:S(2)}) %collective-permute-start.3) | collective-permute-done | bytes 98336 | tf_op jit(solution)/shard_map/ppermute | solution.py:23
  71.7 2.5 %convolution_convert_fusion = bf16[32,1536]{1,0:T(8,128)(2,1)S(1)} fusion(bf16[576,1536]{1,0:T(8,128)(2,1)S(1)} %copy-done, bf16[1536,576]{0,1:T(8,128)(2,1)} %param.24, f32[32,576]{1,0:T(8,128)S(1)} %fusion.45, bf16[32,1536]{1,0:T(8,128)(2,1)S(1)} %get-tuple-element.8, f32[1536]{0:T(1024)S(1)} %copy-done.5, f32[32]{0:T(128)S(1)} %add_rsqrt_fusion.1), kind=kOutput, calls=%fused_computation.7 | convolution fusion | flops 113676288 | bytes 3815552 | tf_op jit(solution)/shard_map/dot_general | solution.py:210
  74.3 4.7 %collective-permute-done.4 = bf16[32,1536]{1,0:T(8,128)(2,1)S(1)} collective-permute-done((bf16[32,1536]{1,0:T(8,128)(2,1)S(1)}, bf16[32,1536]{1,0:T(8,128)(2,1)S(1)}, u32[]{:S(2)}, u32[]{:S(2)}) %collective-permute-start.4) | collective-permute-done | bytes 98336 | tf_op jit(solution)/shard_map/ppermute | solution.py:20
  79.4 6.5 %collective-permute-done.5 = bf16[32,1536]{1,0:T(8,128)(2,1)S(1)} collective-permute-done((bf16[32,1536]{1,0:T(8,128)(2,1)S(1)}, bf16[32,1536]{1,0:T(8,128)(2,1)S(1)}, u32[]{:S(2)}, u32[]{:S(2)}) %collective-permute-start.5) | collective-permute-done | bytes 98336 | tf_op jit(solution)/shard_map/ppermute | solution.py:20
  85.9 2.4 %collective-permute-start.6 = (bf16[32,1536]{1,0:T(8,128)(2,1)S(1)}, bf16[32,1536]{1,0:T(8,128)(2,1)S(1)}, u32[]{:S(2)}, u32[]{:S(2)}) collective-permute-start(bf16[32,1536]{1,0:T(8,128)(2,1)S(1)} %add.226), channel_id=1, source_target_pairs={{0,7},{1,6},{2,5},{3,4},{4,3},{5,2},{6,1},{7,0},{8,15},{9,14},{10,... | collective-permute-start | bytes 294920 | tf_op jit(solution)/shard_map/ppermute | solution.py:23
  88.3 4.2 %collective-permute-done.6 = bf16[32,1536]{1,0:T(8,128)(2,1)S(1)} collective-permute-done((bf16[32,1536]{1,0:T(8,128)(2,1)S(1)}, bf16[32,1536]{1,0:T(8,128)(2,1)S(1)}, u32[]{:S(2)}, u32[]{:S(2)}) %collective-permute-start.6) | collective-permute-done | bytes 98336 | tf_op jit(solution)/shard_map/ppermute | solution.py:23
  92.6 0.7 reshape.469
  (81 shorter events, 8.5 us)
Async XLA Ops:
  0.0 71.7 %copy-start = (bf16[576,1536]{1,0:T(8,128)(2,1)S(1)}, bf16[576,1536]{1,0:T(8,128)(2,1)}, u32[]{:S(2)}) copy-start(bf16[576,1536]{1,0:T(8,128)(2,1)} %param.25) | copy-start | bytes 5308420
  0.0 14.2 %copy-start.4 = (bf16[128,1536]{1,0:T(8,128)(2,1)S(1)}, bf16[128,1536]{1,0:T(8,128)(2,1)}, u32[]{:S(2)}) copy-start(bf16[128,1536]{1,0:T(8,128)(2,1)} %param.21) | copy-start | bytes 1179652
  0.0 16.2 %copy-start.2 = (bf16[1536,128]{1,0:T(8,128)(2,1)S(1)}, bf16[1536,128]{1,0:T(8,128)(2,1)}, u32[]{:S(2)}) copy-start(bf16[1536,128]{1,0:T(8,128)(2,1)} %param.19) | copy-start | bytes 1179652
  6.6 15.9 %all-to-all-start = ((bf16[32,8,532]{2,1,0:T(8,128)(2,1)}), bf16[32,8,532]{2,1,0:T(8,128)(2,1)S(1)}, u32[]{:S(2)}, u32[]{:S(2)}) async-start(bf16[32,8,532]{2,1,0:T(8,128)(2,1)} %broadcast_in_dim.131), calls=%async_computation | async-start | bytes 655360 | tf_op jit(solution)/shard_map/all_to_all | solution.py:72
  14.2 37.7 %collective-permute-start.1 = (bf16[128,1536]{1,0:T(8,128)(2,1)S(1)}, bf16[128,1536]{1,0:T(8,128)(2,1)}, u32[]{:S(2)}, u32[]{:S(2)}) collective-permute-start(bf16[128,1536]{1,0:T(8,128)(2,1)S(1)} %copy-done.4), channel_id=1, source_target_pairs={{0,1},{1,0},{2,3},{3,2},{4,5},{5,4},{6,7},{7,6},{8,9},{9,8},{10,11... | collective-permute-start | bytes 1179656 | tf_op jit(solution)/shard_map/ppermute | solution.py:52
  16.6 6.5 %copy-start.6 = (pred[4,4]{1,0:T(4,128)(4,1)}, pred[4,4]{1,0:T(4,128)(4,1)S(1)}, u32[]{:S(2)}) copy-start(pred[4,4]{1,0:T(4,128)(4,1)S(1)} %iota_compare_fusion.1) | copy-start | bytes 52
  31.2 11.0 %copy-start.3 = (bf16[1536,128]{1,0:T(8,128)(2,1)S(1)}, bf16[1536,128]{1,0:T(8,128)(2,1)}, u32[]{:S(2)}) copy-start(bf16[1536,128]{1,0:T(8,128)(2,1)} %param.20) | copy-start | bytes 1179652
  35.5 13.4 %all-to-all-start.1 = ((bf16[32,8,528]{2,1,0:T(8,128)(2,1)}), bf16[32,8,528]{2,1,0:T(8,128)(2,1)S(1)}, u32[]{:S(2)}, u32[]{:S(2)}) async-start(bf16[32,8,528]{2,1,0:T(8,128)(2,1)} %pad_maximum_fusion), calls=%async_computation.1 | async-start | bytes 655360 | tf_op jit(solution)/shard_map/all_to_all | solution.py:147
  49.9 21.1 %copy-start.1 = (bf16[1536,576]{0,1:T(8,128)(2,1)S(1)}, bf16[1536,576]{0,1:T(8,128)(2,1)}, u32[]{:S(2)}) copy-start(bf16[1536,576]{0,1:T(8,128)(2,1)} %param.23) | copy-start | bytes 5308420
  49.9 21.1 %copy-start.5 = (f32[1536]{0:T(1024)S(1)}, f32[1536]{0:T(1024)}, u32[]{:S(2)}) copy-start(f32[1536]{0:T(1024)} %param.22) | copy-start | bytes 18436
  49.9 3.7 %collective-permute-start = (bf16[32,128]{1,0:T(8,128)(2,1)S(1)}, bf16[32,128]{1,0:T(8,128)(2,1)S(1)}, u32[]{:S(2)}, u32[]{:S(2)}) collective-permute-start(bf16[32,128]{1,0:T(8,128)(2,1)S(1)} %bitcast.72), channel_id=1, source_target_pairs={{0,1},{1,0},{2,3},{3,2},{4,5},{5,4},{6,7},{7,6},{8,9},{9,8},{10,11... | collective-permute-start | bytes 24584 | tf_op jit(solution)/shard_map/ppermute | solution.py:192
  53.9 8.0 %collective-permute-start.2 = (bf16[32,1536]{1,0:T(8,128)(2,1)S(1)}, bf16[32,1536]{1,0:T(8,128)(2,1)S(1)}, u32[]{:S(2)}, u32[]{:S(2)}) collective-permute-start(bf16[32,1536]{1,0:T(8,128)(2,1)S(1)} %convolution_convert_fusion.1), channel_id=1, source_target_pairs={{0,2},{1,3},{2,0},{3,1},{4,6},{5,7},{6,4},{7,5},{8,10},{9,11},{10,... | collective-permute-start | bytes 294920 | tf_op jit(solution)/shard_map/ppermute | solution.py:20
  62.0 8.9 %collective-permute-start.3 = (bf16[32,1536]{1,0:T(8,128)(2,1)S(1)}, bf16[32,1536]{1,0:T(8,128)(2,1)S(1)}, u32[]{:S(2)}, u32[]{:S(2)}) collective-permute-start(bf16[32,1536]{1,0:T(8,128)(2,1)S(1)} %add.218), channel_id=1, source_target_pairs={{0,7},{1,6},{2,5},{3,4},{4,3},{5,2},{6,1},{7,0},{8,15},{9,14},{10,... | collective-permute-start | bytes 294920 | tf_op jit(solution)/shard_map/ppermute | solution.py:23
  74.2 4.7 %collective-permute-start.4 = (bf16[32,1536]{1,0:T(8,128)(2,1)S(1)}, bf16[32,1536]{1,0:T(8,128)(2,1)S(1)}, u32[]{:S(2)}, u32[]{:S(2)}) collective-permute-start(bf16[32,1536]{1,0:T(8,128)(2,1)S(1)} %convolution_convert_fusion), channel_id=1, source_target_pairs={{0,1},{1,0},{2,3},{3,2},{4,5},{5,4},{6,7},{7,6},{8,9},{9,8},{10,11... | collective-permute-start | bytes 294920 | tf_op jit(solution)/shard_map/ppermute | solution.py:20
  79.0 6.9 %collective-permute-start.5 = (bf16[32,1536]{1,0:T(8,128)(2,1)S(1)}, bf16[32,1536]{1,0:T(8,128)(2,1)S(1)}, u32[]{:S(2)}, u32[]{:S(2)}) collective-permute-start(bf16[32,1536]{1,0:T(8,128)(2,1)S(1)} %add.225), channel_id=1, source_target_pairs={{0,2},{1,3},{2,0},{3,1},{4,6},{5,7},{6,4},{7,5},{8,10},{9,11},{10,... | collective-permute-start | bytes 294920 | tf_op jit(solution)/shard_map/ppermute | solution.py:20
  85.9 6.6 %collective-permute-start.6 = (bf16[32,1536]{1,0:T(8,128)(2,1)S(1)}, bf16[32,1536]{1,0:T(8,128)(2,1)S(1)}, u32[]{:S(2)}, u32[]{:S(2)}) collective-permute-start(bf16[32,1536]{1,0:T(8,128)(2,1)S(1)} %add.226), channel_id=1, source_target_pairs={{0,7},{1,6},{2,5},{3,4},{4,3},{5,2},{6,1},{7,0},{8,15},{9,14},{10,... | collective-permute-start | bytes 294920 | tf_op jit(solution)/shard_map/ppermute | solution.py:23

commit v12 on v11

--- a/solution.py
+++ b/solution.py
@@ -190,15 +190,9 @@
         )
         pair = [(i, i ^ 1) for i in range(tp_size)]
         other_head = lax.ppermute(attended, "tp", pair)
-        lower = lax.axis_index("tp") % 2 == 0
-        pair_heads = jnp.concatenate(
-            [jnp.where(lower, attended, other_head), jnp.where(lower, other_head, attended)], axis=1
-        )
-        pair_weight = jnp.concatenate(
-            [jnp.where(lower, out_weight, partner_weight), jnp.where(lower, partner_weight, out_weight)],
-            axis=0,
-        )
-        projected = jnp.dot(pair_heads, pair_weight, preferred_element_type=jnp.float32)
+        projected = jnp.dot(attended, out_weight, preferred_element_type=jnp.float32) + jnp.dot(
+            other_head, partner_weight, preferred_element_type=jnp.float32
+        )
         attn_total = tree_sum(
             projected.astype(jnp.bfloat16), "tp", tp_size, first_step=2
         ).astype(jnp.float32)

time: 93.9 us -> 94.8 us (level)
  other arithmetic: 9.93 us -> 7.61 us
  waiting for transfers between devices: 36.2 us -> 38.4 us
  matrix products: 11.1 us -> 12.3 us
    all_to_all x1, waiting for transfers between devices: 6.45 us -> 7.81 us  [body(): lax.all_to_all(send, 'req', 0, 0, tiled=True).reshape(req_size, req_dev, -1)]
    dot_general x1 -> x2, matrix products: 0.22 us -> 1.35 us  [the longest x1 1.18 us: body(): jnp.dot(other_head, partner_weight, preferred_element_type=jnp.float32)]
    select_n x2 -> x0, other arithmetic: 1.06 us -> none  [the longest x1 1.05 us: body(): jnp.where(lower, out_weight, partner_weight)]
  transfers between devices with their start and end apart: 9 -> 9, of which waited for: 8 -> 8; matrix products, arithmetic and copies ran while one was open for 19% -> 16% of each run, Pallas kernels for 0% -> 0%
where the time goes in v12:
time: 94.8 us; the launch traced here: 94 us
  waiting for transfers between devices  38.4 us (41%)
  starting transfers between devices  28.3 us (30%)
  matrix products  12.3 us (13%)
  other arithmetic  7.61 us (8%)
  local copies, waits for them, and re-layouts  7.06 us (7%)
    ppermute x3, waiting for transfers between devices, tree_sum(): lax.ppermute(values, axis, [(i, i ^ step) for i in range(size)])  15.7 us
    all_to_all x1, waiting for transfers between devices, body(): lax.all_to_all(send, 'req', 0, 0, tiled=True).reshape(req_size, req_dev, -1)  7.81 us
    ppermute x2, starting transfers between devices, tree_sum(): lax.ppermute(values, axis, [(i, size - 1 - i) for i in range(size)])  7.76 us
    all_to_all x1, starting transfers between devices, body(): lax.all_to_all(jnp.broadcast_to(packed[None], (req_size,) + packed.shape)...  7.62 us
    ppermute x2, waiting for transfers between devices, tree_sum(): lax.ppermute(values, axis, [(i, size - 1 - i) for i in range(size)])  7.59 us
    all_to_all x1, waiting for transfers between devices, body(): lax.all_to_all(jnp.broadcast_to(packed[None], (req_size,) + packed.shape)...  5.73 us
    all_to_all x1, starting transfers between devices, body(): lax.all_to_all(send, 'req', 0, 0, tiled=True).reshape(req_size, req_dev, -1)  4.98 us
    ppermute x3, starting transfers between devices, tree_sum(): lax.ppermute(values, axis, [(i, i ^ step) for i in range(size)])  3.93 us
  transfers between devices with their start and end apart: 9, of which 8 were waited for; matrix products, arithmetic and copies ran while one was open for 16% of the time, Pallas kernels for 0%

profile of v12, /device:TPU:2, one launch (start us, length us, event | category | flops | bytes accessed | tf_op | source)
XLA Modules:
  0.0 94.0 jit_solution(4471593784372458106)
XLA Ops:
  0.0 1.2 %multiply_reduce_fusion = f32[8,4]{1,0:T(8,128)S(1)} fusion(bf16[8,4,1536]{2,1,0:T(4,128)(2,1)} %param.13), kind=kLoop, calls=%fused_computation.40 | loop fusion | flops 147424 | bytes 98432 | tf_op jit(solution)/shard_map/reduce_sum | solution.py:14
  1.2 0.9 reshape.470
  2.1 0.7 fusion.54
  3.0 0.7 fusion.49
  3.8 0.8 multiply_convert_fusion
  4.5 1.2 %fusion.17 = bf16[32,128]{1,0:T(8,128)(2,1)S(1)} fusion(bf16[32,1536]{1,0:T(8,128)(2,1)S(1)} %multiply_convert_fusion, bf16[1536,128]{1,0:T(8,128)(2,1)} %param.18), kind=kOutput, calls=%fused_computation.20 | convolution fusion | flops 12591104 | bytes 499712 | tf_op jit(solution)/shard_map/dot_general | solution.py:55
  5.9 0.7 broadcast_in_dim.131
  6.6 7.6 %all-to-all-start = ((bf16[32,8,532]{2,1,0:T(8,128)(2,1)}), bf16[32,8,532]{2,1,0:T(8,128)(2,1)S(1)}, u32[]{:S(2)}, u32[]{:S(2)}) async-start(bf16[32,8,532]{2,1,0:T(8,128)(2,1)} %broadcast_in_dim.131), calls=%async_computation | async-start | bytes 655360 | tf_op jit(solution)/shard_map/all_to_all | solution.py:72
  14.2 2.0 %collective-permute-start.1 = (bf16[128,1536]{1,0:T(8,128)(2,1)S(1)}, bf16[128,1536]{1,0:T(8,128)(2,1)}, u32[]{:S(2)}, u32[]{:S(2)}) collective-permute-start(bf16[128,1536]{1,0:T(8,128)(2,1)S(1)} %copy-done.2), channel_id=1, source_target_pairs={{0,1},{1,0},{2,3},{3,2},{4,5},{5,4},{6,7},{7,6},{8,9},{9,8},{10,11... | collective-permute-start | bytes 1179656 | tf_op jit(solution)/shard_map/ppermute | solution.py:52
  16.8 5.7 %all-to-all-done = bf16[32,8,532]{2,1,0:T(8,128)(2,1)S(1)} async-done(((bf16[32,8,532]{2,1,0:T(8,128)(2,1)}), bf16[32,8,532]{2,1,0:T(8,128)(2,1)S(1)}, u32[]{:S(2)}, u32[]{:S(2)}) %all-to-all-start) | async-done | bytes 272416 | tf_op jit(solution)/shard_map/all_to_all | solution.py:72
  24.2 0.7 gather_fusion
  24.9 3.1 %fusion.66 = (f32[72,4]{1,0:T(8,128)S(1)}, f32[72,4,128]{2,1,0:T(4,128)S(1)}) fusion(bf16[72,4,128]{2,1,0:T(4,128)(2,1)S(1)} %gather_fusion, bf16[72,2,128,128]{3,2,1,0:T(8,128)(2,1)} %param.16, s32[72,4]{1,0:T(8,128)S(1)} %add_add_fusion, s32[72,128]{1,0:T(8,128)S(1)} %iota_add_fusion, pred[72,128]{1,0:T(8,128)(4,1)S(1)} %broadcast_compare_fusion.1), kind=kOutput, calls=%fused_computation.130 | convolution fusion | flops 9584352 | bytes 2628864 | tf_op jit(solution)/shard_map/pqd,pkd->pqk/dot_general | solution.py:102
  28.8 2.5 %fusion.10 = f32[72,4,128]{2,1,0:T(4,128)S(1)} fusion(bf16[72,2,128,128]{3,2,1,0:T(8,128)(2,1)} %param.16, f32[72,4]{1,0:T(8,128)S(1)} %get-tuple-element.14, f32[72,4,128]{2,1,0:T(4,128)S(1)} %get-tuple-element.28, f32[72,4]{1,0:T(8,128)S(1)} %get-tuple-element.27, s32[72,4]{1,0:T(8,128)S(1)} %add_add_fusion, s32[72,128]{1,0:T(8,128)S(1)} %iota_add_fusion, ...), kind=kOutput, calls=%fused_computation.12 | convolution fusion | flops 9658368 | bytes 2703744 | tf_op jit(solution)/shard_map/pqk,pkd->pqd/dot_general | solution.py:109
  31.6 0.8 copy.112
  32.4 0.8 copy.111
  33.8 1.7 %pad_maximum_fusion = bf16[32,8,528]{2,1,0:T(8,128)(2,1)} fusion(bf16[32,8,4]{2,1,0:T(8,128)(2,1)} %copy.112, bf16[32,8,4]{2,1,0:T(8,128)(2,1)} %copy.111, bf16[32,8,4]{2,1,0:T(8,128)(2,1)S(1)} %copy.110, bf16[32,8,516]{2,1,0:T(8,128)(2,1)S(1)} %bitcast.69), kind=kLoop, calls=%fused_computation.29 | loop fusion | flops 1081344 | bytes 540672 | tf_op jit(solution)/shard_map/concatenate | solution.py:144
  35.5 5.0 %all-to-all-start.1 = ((bf16[32,8,528]{2,1,0:T(8,128)(2,1)}), bf16[32,8,528]{2,1,0:T(8,128)(2,1)S(1)}, u32[]{:S(2)}, u32[]{:S(2)}) async-start(bf16[32,8,528]{2,1,0:T(8,128)(2,1)} %pad_maximum_fusion), calls=%async_computation.1 | async-start | bytes 655360 | tf_op jit(solution)/shard_map/all_to_all | solution.py:147
  41.1 7.8 %all-to-all-done.1 = bf16[32,8,528]{2,1,0:T(8,128)(2,1)S(1)} async-done(((bf16[32,8,528]{2,1,0:T(8,128)(2,1)}), bf16[32,8,528]{2,1,0:T(8,128)(2,1)S(1)}, u32[]{:S(2)}, u32[]{:S(2)}) %all-to-all-start.1) | async-done | bytes 270368 | tf_op jit(solution)/shard_map/all_to_all | solution.py:147
  49.9 2.0 %collective-permute-start = (bf16[32,128]{1,0:T(8,128)(2,1)S(1)}, bf16[32,128]{1,0:T(8,128)(2,1)S(1)}, u32[]{:S(2)}, u32[]{:S(2)}) collective-permute-start(bf16[32,128]{1,0:T(8,128)(2,1)S(1)} %bitcast.76), channel_id=1, source_target_pairs={{0,1},{1,0},{2,3},{3,2},{4,5},{5,4},{6,7},{7,6},{8,9},{9,8},{10,11... | collective-permute-start | bytes 24584 | tf_op jit(solution)/shard_map/ppermute | solution.py:192
  52.1 1.5 %collective-permute-done = bf16[32,128]{1,0:T(8,128)(2,1)S(1)} collective-permute-done((bf16[32,128]{1,0:T(8,128)(2,1)S(1)}, bf16[32,128]{1,0:T(8,128)(2,1)S(1)}, u32[]{:S(2)}, u32[]{:S(2)}) %collective-permute-start) | collective-permute-done | bytes 8224 | tf_op jit(solution)/shard_map/ppermute | solution.py:192
  53.7 1.2 %fusion.6 = bf16[32,1536]{1,0:T(8,128)(2,1)S(1)} fusion(f32[32,1536]{1,0:T(8,128)S(1)} %fusion.68, bf16[32,128]{1,0:T(8,128)(2,1)S(1)} %collective-permute-done, bf16[128,1536]{1,0:T(8,128)(2,1)} %collective-permute-done.1), kind=kOutput, calls=%fused_computation.8 | convolution fusion | flops 12681216 | bytes 696320 | tf_op jit(solution)/shard_map/dot_general | solution.py:193
  54.9 3.4 %collective-permute-start.2 = (bf16[32,1536]{1,0:T(8,128)(2,1)S(1)}, bf16[32,1536]{1,0:T(8,128)(2,1)S(1)}, u32[]{:S(2)}, u32[]{:S(2)}) collective-permute-start(bf16[32,1536]{1,0:T(8,128)(2,1)S(1)} %fusion.6), channel_id=1, source_target_pairs={{0,2},{1,3},{2,0},{3,1},{4,6},{5,7},{6,4},{7,5},{8,10},{9,11},{10,... | collective-permute-start | bytes 294920 | tf_op jit(solution)/shard_map/ppermute | solution.py:20
  58.2 4.7 %collective-permute-done.2 = bf16[32,1536]{1,0:T(8,128)(2,1)S(1)} collective-permute-done((bf16[32,1536]{1,0:T(8,128)(2,1)S(1)}, bf16[32,1536]{1,0:T(8,128)(2,1)S(1)}, u32[]{:S(2)}, u32[]{:S(2)}) %collective-permute-start.2) | collective-permute-done | bytes 98336 | tf_op jit(solution)/shard_map/ppermute | solution.py:20
  62.9 5.1 %collective-permute-start.3 = (bf16[32,1536]{1,0:T(8,128)(2,1)S(1)}, bf16[32,1536]{1,0:T(8,128)(2,1)S(1)}, u32[]{:S(2)}, u32[]{:S(2)}) collective-permute-start(bf16[32,1536]{1,0:T(8,128)(2,1)S(1)} %add.217), channel_id=1, source_target_pairs={{0,7},{1,6},{2,5},{3,4},{4,3},{5,2},{6,1},{7,0},{8,15},{9,14},{10,... | collective-permute-start | bytes 294920 | tf_op jit(solution)/shard_map/ppermute | solution.py:23
  68.0 3.8 %collective-permute-done.3 = bf16[32,1536]{1,0:T(8,128)(2,1)S(1)} collective-permute-done((bf16[32,1536]{1,0:T(8,128)(2,1)S(1)}, bf16[32,1536]{1,0:T(8,128)(2,1)S(1)}, u32[]{:S(2)}, u32[]{:S(2)}) %collective-permute-start.3) | collective-permute-done | bytes 98336 | tf_op jit(solution)/shard_map/ppermute | solution.py:23
  72.0 0.6 fusion.43
  72.6 2.5 %convolution_convert_fusion = bf16[32,1536]{1,0:T(8,128)(2,1)S(1)} fusion(bf16[576,1536]{1,0:T(8,128)(2,1)S(1)} %copy-done, bf16[1536,576]{0,1:T(8,128)(2,1)} %param.24, f32[32,576]{1,0:T(8,128)S(1)} %fusion.43, bf16[32,1536]{1,0:T(8,128)(2,1)S(1)} %get-tuple-element.8, f32[1536]{0:T(1024)S(1)} %copy-done.5, f32[32]{0:T(128)S(1)} %add_rsqrt_fusion.1), kind=kOutput, calls=%fused_computation.9 | convolution fusion | flops 113676288 | bytes 3815552 | tf_op jit(solution)/shard_map/dot_general | solution.py:204
  75.2 4.6 %collective-permute-done.4 = bf16[32,1536]{1,0:T(8,128)(2,1)S(1)} collective-permute-done((bf16[32,1536]{1,0:T(8,128)(2,1)S(1)}, bf16[32,1536]{1,0:T(8,128)(2,1)S(1)}, u32[]{:S(2)}, u32[]{:S(2)}) %collective-permute-start.4) | collective-permute-done | bytes 98336 | tf_op jit(solution)/shard_map/ppermute | solution.py:20
  80.4 6.3 %collective-permute-done.5 = bf16[32,1536]{1,0:T(8,128)(2,1)S(1)} collective-permute-done((bf16[32,1536]{1,0:T(8,128)(2,1)S(1)}, bf16[32,1536]{1,0:T(8,128)(2,1)S(1)}, u32[]{:S(2)}, u32[]{:S(2)}) %collective-permute-start.5) | collective-permute-done | bytes 98336 | tf_op jit(solution)/shard_map/ppermute | solution.py:20
  86.7 2.7 %collective-permute-start.6 = (bf16[32,1536]{1,0:T(8,128)(2,1)S(1)}, bf16[32,1536]{1,0:T(8,128)(2,1)S(1)}, u32[]{:S(2)}, u32[]{:S(2)}) collective-permute-start(bf16[32,1536]{1,0:T(8,128)(2,1)S(1)} %add.225), channel_id=1, source_target_pairs={{0,7},{1,6},{2,5},{3,4},{4,3},{5,2},{6,1},{7,0},{8,15},{9,14},{10,... | collective-permute-start | bytes 294920 | tf_op jit(solution)/shard_map/ppermute | solution.py:23
  89.4 3.8 %collective-permute-done.6 = bf16[32,1536]{1,0:T(8,128)(2,1)S(1)} collective-permute-done((bf16[32,1536]{1,0:T(8,128)(2,1)S(1)}, bf16[32,1536]{1,0:T(8,128)(2,1)S(1)}, u32[]{:S(2)}, u32[]{:S(2)}) %collective-permute-start.6) | collective-permute-done | bytes 98336 | tf_op jit(solution)/shard_map/ppermute | solution.py:23
  93.3 0.7 reshape.469
  (78 shorter events, 6.9 us)
Async XLA Ops:
  0.0 72.6 %copy-start = (bf16[576,1536]{1,0:T(8,128)(2,1)S(1)}, bf16[576,1536]{1,0:T(8,128)(2,1)}, u32[]{:S(2)}) copy-start(bf16[576,1536]{1,0:T(8,128)(2,1)} %param.25) | copy-start | bytes 5308420
  0.0 14.2 %copy-start.2 = (bf16[128,1536]{1,0:T(8,128)(2,1)S(1)}, bf16[128,1536]{1,0:T(8,128)(2,1)}, u32[]{:S(2)}) copy-start(bf16[128,1536]{1,0:T(8,128)(2,1)} %param.21) | copy-start | bytes 1179652
  0.0 16.2 %copy-start.3 = (bf16[1536,128]{1,0:T(8,128)(2,1)S(1)}, bf16[1536,128]{1,0:T(8,128)(2,1)}, u32[]{:S(2)}) copy-start(bf16[1536,128]{1,0:T(8,128)(2,1)} %param.19) | copy-start | bytes 1179652
  6.6 15.9 %all-to-all-start = ((bf16[32,8,532]{2,1,0:T(8,128)(2,1)}), bf16[32,8,532]{2,1,0:T(8,128)(2,1)S(1)}, u32[]{:S(2)}, u32[]{:S(2)}) async-start(bf16[32,8,532]{2,1,0:T(8,128)(2,1)} %broadcast_in_dim.131), calls=%async_computation | async-start | bytes 655360 | tf_op jit(solution)/shard_map/all_to_all | solution.py:72
  14.2 37.9 %collective-permute-start.1 = (bf16[128,1536]{1,0:T(8,128)(2,1)S(1)}, bf16[128,1536]{1,0:T(8,128)(2,1)}, u32[]{:S(2)}, u32[]{:S(2)}) collective-permute-start(bf16[128,1536]{1,0:T(8,128)(2,1)S(1)} %copy-done.2), channel_id=1, source_target_pairs={{0,1},{1,0},{2,3},{3,2},{4,5},{5,4},{6,7},{7,6},{8,9},{9,8},{10,11... | collective-permute-start | bytes 1179656 | tf_op jit(solution)/shard_map/ppermute | solution.py:52
  31.2 9.7 %copy-start.4 = (bf16[1536,128]{1,0:T(8,128)(2,1)S(1)}, bf16[1536,128]{1,0:T(8,128)(2,1)}, u32[]{:S(2)}) copy-start(bf16[1536,128]{1,0:T(8,128)(2,1)} %param.20) | copy-start | bytes 1179652
  35.5 13.4 %all-to-all-start.1 = ((bf16[32,8,528]{2,1,0:T(8,128)(2,1)}), bf16[32,8,528]{2,1,0:T(8,128)(2,1)S(1)}, u32[]{:S(2)}, u32[]{:S(2)}) async-start(bf16[32,8,528]{2,1,0:T(8,128)(2,1)} %pad_maximum_fusion), calls=%async_computation.1 | async-start | bytes 655360 | tf_op jit(solution)/shard_map/all_to_all | solution.py:147
  49.1 22.8 %copy-start.5 = (f32[1536]{0:T(1024)S(1)}, f32[1536]{0:T(1024)}, u32[]{:S(2)}) copy-start(f32[1536]{0:T(1024)} %param.22) | copy-start | bytes 18436
  49.8 22.2 %copy-start.1 = (bf16[1536,576]{0,1:T(8,128)(2,1)S(1)}, bf16[1536,576]{0,1:T(8,128)(2,1)}, u32[]{:S(2)}) copy-start(bf16[1536,576]{0,1:T(8,128)(2,1)} %param.23) | copy-start | bytes 5308420
  49.9 3.7 %collective-permute-start = (bf16[32,128]{1,0:T(8,128)(2,1)S(1)}, bf16[32,128]{1,0:T(8,128)(2,1)S(1)}, u32[]{:S(2)}, u32[]{:S(2)}) collective-permute-start(bf16[32,128]{1,0:T(8,128)(2,1)S(1)} %bitcast.76), channel_id=1, source_target_pairs={{0,1},{1,0},{2,3},{3,2},{4,5},{5,4},{6,7},{7,6},{8,9},{9,8},{10,11... | collective-permute-start | bytes 24584 | tf_op jit(solution)/shard_map/ppermute | solution.py:192
  54.9 8.1 %collective-permute-start.2 = (bf16[32,1536]{1,0:T(8,128)(2,1)S(1)}, bf16[32,1536]{1,0:T(8,128)(2,1)S(1)}, u32[]{:S(2)}, u32[]{:S(2)}) collective-permute-start(bf16[32,1536]{1,0:T(8,128)(2,1)S(1)} %fusion.6), channel_id=1, source_target_pairs={{0,2},{1,3},{2,0},{3,1},{4,6},{5,7},{6,4},{7,5},{8,10},{9,11},{10,... | collective-permute-start | bytes 294920 | tf_op jit(solution)/shard_map/ppermute | solution.py:20
  62.9 8.8 %collective-permute-start.3 = (bf16[32,1536]{1,0:T(8,128)(2,1)S(1)}, bf16[32,1536]{1,0:T(8,128)(2,1)S(1)}, u32[]{:S(2)}, u32[]{:S(2)}) collective-permute-start(bf16[32,1536]{1,0:T(8,128)(2,1)S(1)} %add.217), channel_id=1, source_target_pairs={{0,7},{1,6},{2,5},{3,4},{4,3},{5,2},{6,1},{7,0},{8,15},{9,14},{10,... | collective-permute-start | bytes 294920 | tf_op jit(solution)/shard_map/ppermute | solution.py:23
  75.1 4.7 %collective-permute-start.4 = (bf16[32,1536]{1,0:T(8,128)(2,1)S(1)}, bf16[32,1536]{1,0:T(8,128)(2,1)S(1)}, u32[]{:S(2)}, u32[]{:S(2)}) collective-permute-start(bf16[32,1536]{1,0:T(8,128)(2,1)S(1)} %convolution_convert_fusion), channel_id=1, source_target_pairs={{0,1},{1,0},{2,3},{3,2},{4,5},{5,4},{6,7},{7,6},{8,9},{9,8},{10,11... | collective-permute-start | bytes 294920 | tf_op jit(solution)/shard_map/ppermute | solution.py:20
  79.8 6.9 %collective-permute-start.5 = (bf16[32,1536]{1,0:T(8,128)(2,1)S(1)}, bf16[32,1536]{1,0:T(8,128)(2,1)S(1)}, u32[]{:S(2)}, u32[]{:S(2)}) collective-permute-start(bf16[32,1536]{1,0:T(8,128)(2,1)S(1)} %add.224), channel_id=1, source_target_pairs={{0,2},{1,3},{2,0},{3,1},{4,6},{5,7},{6,4},{7,5},{8,10},{9,11},{10,... | collective-permute-start | bytes 294920 | tf_op jit(solution)/shard_map/ppermute | solution.py:20
  86.7 6.5 %collective-permute-start.6 = (bf16[32,1536]{1,0:T(8,128)(2,1)S(1)}, bf16[32,1536]{1,0:T(8,128)(2,1)S(1)}, u32[]{:S(2)}, u32[]{:S(2)}) collective-permute-start(bf16[32,1536]{1,0:T(8,128)(2,1)S(1)} %add.225), channel_id=1, source_target_pairs={{0,7},{1,6},{2,5},{3,4},{4,3},{5,2},{6,1},{7,0},{8,15},{9,14},{10,... | collective-permute-start | bytes 294920 | tf_op jit(solution)/shard_map/ppermute | solution.py:23

commit v13 on v12

--- a/solution.py
+++ b/solution.py
@@ -50,6 +50,12 @@
         qwidth = steps * heads_dev * head_dim
         token_rows = tokens.reshape(req_dev * steps, width)
         partner_weight = lax.ppermute(out_weight, "tp", [(i, i ^ 1) for i in range(tp_size)])
+        lower = lax.axis_index("tp") % 2 == 0
+        pair_weight = jnp.concatenate(
+            [jnp.where(lower, out_weight, partner_weight), jnp.where(lower, partner_weight, out_weight)],
+            axis=0,
+        )
+        far_weight = lax.ppermute(pair_weight, "tp", [(i, i ^ 2) for i in range(tp_size)])
         normed = rms_norm(token_rows.astype(jnp.float32), norm_gain).astype(jnp.bfloat16)
         queries = (
             jnp.dot(normed, query_weight, preferred_element_type=jnp.float32) * head_dim ** (-0.5)
@@ -189,12 +195,16 @@
             .reshape(req_dev * steps, heads_dev * head_dim)
         )
         pair = [(i, i ^ 1) for i in range(tp_size)]
+        quad = [(i, i ^ 2) for i in range(tp_size)]
         other_head = lax.ppermute(attended, "tp", pair)
-        projected = jnp.dot(attended, out_weight, preferred_element_type=jnp.float32) + jnp.dot(
-            other_head, partner_weight, preferred_element_type=jnp.float32
-        )
+        pair_heads = jnp.concatenate(
+            [jnp.where(lower, attended, other_head), jnp.where(lower, other_head, attended)], axis=1
+        )
+        projected = jnp.dot(pair_heads, pair_weight, preferred_element_type=jnp.float32)
+        far_heads = lax.ppermute(pair_heads, "tp", quad)
+        projected = projected + jnp.dot(far_heads, far_weight, preferred_element_type=jnp.float32)
         attn_total = tree_sum(
-            projected.astype(jnp.bfloat16), "tp", tp_size, first_step=2
+            projected.astype(jnp.bfloat16), "tp", tp_size, first_step=4
         ).astype(jnp.float32)
         residual = (token_rows.astype(jnp.float32) + attn_total).astype(jnp.bfloat16)
         mlp_in = rms_norm(residual.astype(jnp.float32), mlp_gain).astype(jnp.bfloat16)

time: 94.8 us -> 113 us (1.19)
  waiting for transfers between devices: 38.4 us -> 54.5 us
  starting transfers between devices: 28.3 us -> 30.6 us
  local copies, waits for them, and re-layouts: 7.06 us -> 5.85 us
    ppermute x0 -> x2, waiting for transfers between devices: none -> 15.3 us  [the longest x1 15.3 us: body(): far_heads = lax.ppermute(pair_heads, 'tp', quad)]
    ppermute x1, waiting for transfers between devices: 1.55 us -> 11.4 us  [body(): other_head = lax.ppermute(attended, 'tp', pair)]
    ppermute x0 -> x2, starting transfers between devices: none -> 6 us  [the longest x1 3.27 us: body(): lax.ppermute(pair_weight, 'tp', [(i, i ^ 2) for i in range(tp_size)])]
    all_to_all x1, waiting for transfers between devices: 7.81 us -> 3.1 us  [body(): lax.all_to_all(send, 'req', 0, 0, tiled=True).reshape(req_size, req_dev, -1)]
    ppermute x3 -> x2, waiting for transfers between devices: 15.7 us -> 11.6 us  [tree_sum(): lax.ppermute(values, axis, [(i, i ^ step) for i in range(size)])]
    ppermute x3 -> x2, starting transfers between devices: 3.93 us -> 0.13 us  [tree_sum(): lax.ppermute(values, axis, [(i, i ^ step) for i in range(size)])]
    another operation x4, local copies, waits for them, and re-layouts: 1.9 us -> 0.67 us
  transfers between devices with their start and end apart: 9 -> 10, of which waited for: 8 -> 8; matrix products, arithmetic and copies ran while one was open for 16% -> 13% of each run, Pallas kernels for 0% -> 0%
where the time goes in v13:
time: 113 us
  waiting for transfers between devices  54.5 us (48%)
  starting transfers between devices  30.6 us (27%)
  matrix products  12.5 us (11%)
  other arithmetic  8.73 us (8%)
  local copies, waits for them, and re-layouts  5.85 us (5%)
    ppermute x1, waiting for transfers between devices, body(): far_heads = lax.ppermute(pair_heads, 'tp', quad)  15.3 us
    ppermute x2, waiting for transfers between devices, tree_sum(): lax.ppermute(values, axis, [(i, i ^ step) for i in range(size)])  11.6 us
    ppermute x1, waiting for transfers between devices, body(): other_head = lax.ppermute(attended, 'tp', pair)  11.4 us
    ppermute x2, waiting for transfers between devices, tree_sum(): lax.ppermute(values, axis, [(i, size - 1 - i) for i in range(size)])  8 us
    ppermute x2, starting transfers between devices, tree_sum(): lax.ppermute(values, axis, [(i, size - 1 - i) for i in range(size)])  7.86 us
    all_to_all x1, starting transfers between devices, body(): lax.all_to_all(jnp.broadcast_to(packed[None], (req_size,) + packed.shape)...  7.62 us
    all_to_all x1, waiting for transfers between devices, body(): lax.all_to_all(jnp.broadcast_to(packed[None], (req_size,) + packed.shape)...  5.16 us
    all_to_all x1, starting transfers between devices, body(): lax.all_to_all(send, 'req', 0, 0, tiled=True).reshape(req_size, req_dev, -1)  4.98 us
  transfers between devices with their start and end apart: 10, of which 8 were waited for; matrix products, arithmetic and copies ran while one was open for 13% of the time, Pallas kernels for 0%

profile of v13, /device:TPU:2, one launch (start us, length us, event | category | flops | bytes accessed | tf_op | source)
XLA Modules:
  0.0 112.6 jit_solution(15176270487809130369)
XLA Ops:
  0.0 1.2 %multiply_reduce_fusion = f32[8,4]{1,0:T(8,128)S(1)} fusion(bf16[8,4,1536]{2,1,0:T(4,128)(2,1)} %param.13), kind=kLoop, calls=%fused_computation.43 | loop fusion | flops 147424 | bytes 98432 | tf_op jit(solution)/shard_map/reduce_sum | solution.py:14
  1.2 0.9 reshape.470
  2.1 0.7 fusion.54
  3.0 0.7 fusion.49
  3.8 0.8 multiply_convert_fusion
  4.5 1.2 %fusion.17 = bf16[32,128]{1,0:T(8,128)(2,1)S(1)} fusion(bf16[32,1536]{1,0:T(8,128)(2,1)S(1)} %multiply_convert_fusion, bf16[1536,128]{1,0:T(8,128)(2,1)} %param.18), kind=kOutput, calls=%fused_computation.20 | convolution fusion | flops 12591104 | bytes 499712 | tf_op jit(solution)/shard_map/dot_general | solution.py:61
  5.9 0.7 broadcast_in_dim.131
  6.6 7.6 %all-to-all-start = ((bf16[32,8,532]{2,1,0:T(8,128)(2,1)}), bf16[32,8,532]{2,1,0:T(8,128)(2,1)S(1)}, u32[]{:S(2)}, u32[]{:S(2)}) async-start(bf16[32,8,532]{2,1,0:T(8,128)(2,1)} %broadcast_in_dim.131), calls=%async_computation | async-start | bytes 655360 | tf_op jit(solution)/shard_map/all_to_all | solution.py:78
  14.2 2.0 %collective-permute-start.1 = (bf16[128,1536]{1,0:T(8,128)(2,1)}, bf16[128,1536]{1,0:T(8,128)(2,1)}, u32[]{:S(2)}, u32[]{:S(2)}) collective-permute-start(bf16[128,1536]{1,0:T(8,128)(2,1)} %param.21), channel_id=1, source_target_pairs={{0,1},{1,0},{2,3},{3,2},{4,5},{5,4},{6,7},{7,6},{8,9},{9,8},{10,11... | collective-permute-start | bytes 1179656 | tf_op jit(solution)/shard_map/ppermute | solution.py:52
  17.3 5.2 %all-to-all-done = bf16[32,8,532]{2,1,0:T(8,128)(2,1)S(1)} async-done(((bf16[32,8,532]{2,1,0:T(8,128)(2,1)}), bf16[32,8,532]{2,1,0:T(8,128)(2,1)S(1)}, u32[]{:S(2)}, u32[]{:S(2)}) %all-to-all-start) | async-done | bytes 272416 | tf_op jit(solution)/shard_map/all_to_all | solution.py:78
  24.2 0.7 gather_fusion
  24.9 3.1 %fusion.66 = (f32[72,4]{1,0:T(8,128)S(1)}, f32[72,4,128]{2,1,0:T(4,128)S(1)}) fusion(bf16[72,4,128]{2,1,0:T(4,128)(2,1)S(1)} %gather_fusion, bf16[72,2,128,128]{3,2,1,0:T(8,128)(2,1)} %param.16, s32[72,4]{1,0:T(8,128)S(1)} %add_add_fusion, s32[72,128]{1,0:T(8,128)S(1)} %iota_add_fusion, pred[72,128]{1,0:T(8,128)(4,1)S(1)} %broadcast_compare_fusion.1), kind=kOutput, calls=%fused_computation.136 | convolution fusion | flops 9584352 | bytes 2628864 | tf_op jit(solution)/shard_map/pqd,pkd->pqk/dot_general | solution.py:108
  28.8 2.5 %fusion.10 = f32[72,4,128]{2,1,0:T(4,128)S(1)} fusion(bf16[72,2,128,128]{3,2,1,0:T(8,128)(2,1)} %param.16, f32[72,4]{1,0:T(8,128)S(1)} %get-tuple-element.14, f32[72,4,128]{2,1,0:T(4,128)S(1)} %get-tuple-element.32, f32[72,4]{1,0:T(8,128)S(1)} %get-tuple-element.31, s32[72,4]{1,0:T(8,128)S(1)} %add_add_fusion, s32[72,128]{1,0:T(8,128)S(1)} %iota_add_fusion, ...), kind=kOutput, calls=%fused_computation.12 | convolution fusion | flops 9658368 | bytes 2703744 | tf_op jit(solution)/shard_map/pqk,pkd->pqd/dot_general | solution.py:115
  32.6 0.9 pad_maximum_fusion.1
  33.4 5.0 %all-to-all-start.1 = ((bf16[32,8,528]{2,1,0:T(8,128)(2,1)}), bf16[32,8,528]{2,1,0:T(8,128)(2,1)S(1)}, u32[]{:S(2)}, u32[]{:S(2)}) async-start(bf16[32,8,528]{2,1,0:T(8,128)(2,1)} %pad_maximum_fusion.1), calls=%async_computation.1 | async-start | bytes 655360 | tf_op jit(solution)/shard_map/all_to_all | solution.py:153
  38.5 1.1 broadcast_select_fusion.1
  39.5 0.9 pad_maximum_fusion
  40.4 3.3 %collective-permute-start.3 = (bf16[256,1536]{1,0:T(8,128)(2,1)}, bf16[256,1536]{1,0:T(8,128)(2,1)}, u32[]{:S(2)}, u32[]{:S(2)}) collective-permute-start(bf16[256,1536]{1,0:T(8,128)(2,1)} %pad_maximum_fusion), channel_id=1, source_target_pairs={{0,2},{1,3},{2,0},{3,1},{4,6},{5,7},{6,4},{7,5},{8,10},{9,11},{10,... | collective-permute-start | bytes 2359304 | tf_op jit(solution)/shard_map/ppermute | solution.py:58
  43.7 3.1 %all-to-all-done.1 = bf16[32,8,528]{2,1,0:T(8,128)(2,1)S(1)} async-done(((bf16[32,8,528]{2,1,0:T(8,128)(2,1)}), bf16[32,8,528]{2,1,0:T(8,128)(2,1)S(1)}, u32[]{:S(2)}, u32[]{:S(2)}) %all-to-all-start.1) | async-done | bytes 270368 | tf_op jit(solution)/shard_map/all_to_all | solution.py:153
  47.9 2.0 %collective-permute-start = (bf16[32,128]{1,0:T(8,128)(2,1)S(1)}, bf16[32,128]{1,0:T(8,128)(2,1)S(1)}, u32[]{:S(2)}, u32[]{:S(2)}) collective-permute-start(bf16[32,128]{1,0:T(8,128)(2,1)S(1)} %bitcast.74), channel_id=1, source_target_pairs={{0,1},{1,0},{2,3},{3,2},{4,5},{5,4},{6,7},{7,6},{8,9},{9,8},{10,11... | collective-permute-start | bytes 24584 | tf_op jit(solution)/shard_map/ppermute | solution.py:199
  49.9 11.4 %collective-permute-done = bf16[32,128]{1,0:T(8,128)(2,1)S(1)} collective-permute-done((bf16[32,128]{1,0:T(8,128)(2,1)S(1)}, bf16[32,128]{1,0:T(8,128)(2,1)S(1)}, u32[]{:S(2)}, u32[]{:S(2)}) %collective-permute-start) | collective-permute-done | bytes 8224 | tf_op jit(solution)/shard_map/ppermute | solution.py:199
  61.3 2.7 %collective-permute-start.2 = (bf16[32,256]{1,0:T(8,128)(2,1)S(1)}, bf16[32,256]{1,0:T(8,128)(2,1)S(1)}, u32[]{:S(2)}, u32[]{:S(2)}) collective-permute-start(bf16[32,256]{1,0:T(8,128)(2,1)S(1)} %pad_maximum_fusion.2), channel_id=1, source_target_pairs={{0,2},{1,3},{2,0},{3,1},{4,6},{5,7},{6,4},{7,5},{8,10},{9,11},{10,... | collective-permute-start | bytes 49160 | tf_op jit(solution)/shard_map/ppermute | solution.py:204
  64.0 15.3 %collective-permute-done.2 = bf16[32,256]{1,0:T(8,128)(2,1)S(1)} collective-permute-done((bf16[32,256]{1,0:T(8,128)(2,1)S(1)}, bf16[32,256]{1,0:T(8,128)(2,1)S(1)}, u32[]{:S(2)}, u32[]{:S(2)}) %collective-permute-start.2) | collective-permute-done | bytes 16416 | tf_op jit(solution)/shard_map/ppermute | solution.py:204
  79.3 1.4 %fusion.68 = f32[32,1536]{1,0:T(8,128)S(1)} fusion(bf16[32,256]{1,0:T(8,128)(2,1)S(1)} %collective-permute-done.2, bf16[256,1536]{1,0:T(8,128)(2,1)} %collective-permute-done.3), kind=kOutput, calls=%fused_computation.138 | convolution fusion | flops 25165824 | bytes 999424 | tf_op jit(solution)/shard_map/dot_general | solution.py:205
  80.9 5.3 %collective-permute-start.4 = (bf16[32,1536]{1,0:T(8,128)(2,1)S(1)}, bf16[32,1536]{1,0:T(8,128)(2,1)S(1)}, u32[]{:S(2)}, u32[]{:S(2)}) collective-permute-start(bf16[32,1536]{1,0:T(8,128)(2,1)S(1)} %fusion.6), channel_id=1, source_target_pairs={{0,7},{1,6},{2,5},{3,4},{4,3},{5,2},{6,1},{7,0},{8,15},{9,14},{10,... | collective-permute-start | bytes 294920 | tf_op jit(solution)/shard_map/ppermute | solution.py:23
  86.2 3.9 %collective-permute-done.4 = bf16[32,1536]{1,0:T(8,128)(2,1)S(1)} collective-permute-done((bf16[32,1536]{1,0:T(8,128)(2,1)S(1)}, bf16[32,1536]{1,0:T(8,128)(2,1)S(1)}, u32[]{:S(2)}, u32[]{:S(2)}) %collective-permute-start.4) | collective-permute-done | bytes 98336 | tf_op jit(solution)/shard_map/ppermute | solution.py:23
  90.9 2.5 %convolution_convert_fusion = bf16[32,1536]{1,0:T(8,128)(2,1)S(1)} fusion(bf16[576,1536]{1,0:T(8,128)(2,1)S(1)} %copy-done, bf16[1536,576]{0,1:T(8,128)(2,1)} %param.24, f32[32,576]{1,0:T(8,128)S(1)} %fusion.43, bf16[32,1536]{1,0:T(8,128)(2,1)S(1)} %get-tuple-element.8, f32[1536]{0:T(1024)S(1)} %copy-done.5, f32[32]{0:T(128)S(1)} %add_rsqrt_fusion.1), kind=kOutput, calls=%fused_computation.9 | convolution fusion | flops 113676288 | bytes 3815552 | tf_op jit(solution)/shard_map/dot_general | solution.py:214
  93.5 4.7 %collective-permute-done.5 = bf16[32,1536]{1,0:T(8,128)(2,1)S(1)} collective-permute-done((bf16[32,1536]{1,0:T(8,128)(2,1)S(1)}, bf16[32,1536]{1,0:T(8,128)(2,1)S(1)}, u32[]{:S(2)}, u32[]{:S(2)}) %collective-permute-start.5) | collective-permute-done | bytes 98336 | tf_op jit(solution)/shard_map/ppermute | solution.py:20
  98.3 6.9 %collective-permute-done.6 = bf16[32,1536]{1,0:T(8,128)(2,1)S(1)} collective-permute-done((bf16[32,1536]{1,0:T(8,128)(2,1)S(1)}, bf16[32,1536]{1,0:T(8,128)(2,1)S(1)}, u32[]{:S(2)}, u32[]{:S(2)}) %collective-permute-start.6) | collective-permute-done | bytes 98336 | tf_op jit(solution)/shard_map/ppermute | solution.py:20
  105.2 2.6 %collective-permute-start.7 = (bf16[32,1536]{1,0:T(8,128)(2,1)S(1)}, bf16[32,1536]{1,0:T(8,128)(2,1)S(1)}, u32[]{:S(2)}, u32[]{:S(2)}) collective-permute-start(bf16[32,1536]{1,0:T(8,128)(2,1)S(1)} %add.226), channel_id=1, source_target_pairs={{0,7},{1,6},{2,5},{3,4},{4,3},{5,2},{6,1},{7,0},{8,15},{9,14},{10,... | collective-permute-start | bytes 294920 | tf_op jit(solution)/shard_map/ppermute | solution.py:23
  107.7 4.1 %collective-permute-done.7 = bf16[32,1536]{1,0:T(8,128)(2,1)S(1)} collective-permute-done((bf16[32,1536]{1,0:T(8,128)(2,1)S(1)}, bf16[32,1536]{1,0:T(8,128)(2,1)S(1)}, u32[]{:S(2)}, u32[]{:S(2)}) %collective-permute-start.7) | collective-permute-done | bytes 98336 | tf_op jit(solution)/shard_map/ppermute | solution.py:23
  111.9 0.7 reshape.469
  (83 shorter events, 7.5 us)
Async XLA Ops:
  0.0 90.9 %copy-start = (bf16[576,1536]{1,0:T(8,128)(2,1)S(1)}, bf16[576,1536]{1,0:T(8,128)(2,1)}, u32[]{:S(2)}) copy-start(bf16[576,1536]{1,0:T(8,128)(2,1)} %param.25) | copy-start | bytes 5308420
  0.0 16.2 %copy-start.2 = (bf16[1536,128]{1,0:T(8,128)(2,1)S(1)}, bf16[1536,128]{1,0:T(8,128)(2,1)}, u32[]{:S(2)}) copy-start(bf16[1536,128]{1,0:T(8,128)(2,1)} %param.19) | copy-start | bytes 1179652
  0.0 17.2 %copy-start.3 = (bf16[1536,128]{1,0:T(8,128)(2,1)S(1)}, bf16[1536,128]{1,0:T(8,128)(2,1)}, u32[]{:S(2)}) copy-start(bf16[1536,128]{1,0:T(8,128)(2,1)} %param.20) | copy-start | bytes 1179652
  6.6 15.9 %all-to-all-start = ((bf16[32,8,532]{2,1,0:T(8,128)(2,1)}), bf16[32,8,532]{2,1,0:T(8,128)(2,1)S(1)}, u32[]{:S(2)}, u32[]{:S(2)}) async-start(bf16[32,8,532]{2,1,0:T(8,128)(2,1)} %broadcast_in_dim.131), calls=%async_computation | async-start | bytes 655360 | tf_op jit(solution)/shard_map/all_to_all | solution.py:78
  14.2 24.2 %collective-permute-start.1 = (bf16[128,1536]{1,0:T(8,128)(2,1)}, bf16[128,1536]{1,0:T(8,128)(2,1)}, u32[]{:S(2)}, u32[]{:S(2)}) collective-permute-start(bf16[128,1536]{1,0:T(8,128)(2,1)} %param.21), channel_id=1, source_target_pairs={{0,1},{1,0},{2,3},{3,2},{4,5},{5,4},{6,7},{7,6},{8,9},{9,8},{10,11... | collective-permute-start | bytes 1179656 | tf_op jit(solution)/shard_map/ppermute | solution.py:52
  31.2 7.2 %copy-start.4 = (bf16[128,1536]{1,0:T(8,128)(2,1)S(1)}, bf16[128,1536]{1,0:T(8,128)(2,1)}, u32[]{:S(2)}) copy-start(bf16[128,1536]{1,0:T(8,128)(2,1)} %param.21) | copy-start | bytes 1179652
  33.4 13.4 %all-to-all-start.1 = ((bf16[32,8,528]{2,1,0:T(8,128)(2,1)}), bf16[32,8,528]{2,1,0:T(8,128)(2,1)S(1)}, u32[]{:S(2)}, u32[]{:S(2)}) async-start(bf16[32,8,528]{2,1,0:T(8,128)(2,1)} %pad_maximum_fusion.1), calls=%async_computation.1 | async-start | bytes 655360 | tf_op jit(solution)/shard_map/all_to_all | solution.py:153
  40.4 38.9 %collective-permute-start.3 = (bf16[256,1536]{1,0:T(8,128)(2,1)}, bf16[256,1536]{1,0:T(8,128)(2,1)}, u32[]{:S(2)}, u32[]{:S(2)}) collective-permute-start(bf16[256,1536]{1,0:T(8,128)(2,1)} %pad_maximum_fusion), channel_id=1, source_target_pairs={{0,2},{1,3},{2,0},{3,1},{4,6},{5,7},{6,4},{7,5},{8,10},{9,11},{10,... | collective-permute-start | bytes 2359304 | tf_op jit(solution)/shard_map/ppermute | solution.py:58
  47.2 43.0 %copy-start.5 = (f32[1536]{0:T(1024)S(1)}, f32[1536]{0:T(1024)}, u32[]{:S(2)}) copy-start(f32[1536]{0:T(1024)} %param.22) | copy-start | bytes 18436
  47.7 42.6 %copy-start.1 = (bf16[1536,576]{0,1:T(8,128)(2,1)S(1)}, bf16[1536,576]{0,1:T(8,128)(2,1)}, u32[]{:S(2)}) copy-start(bf16[1536,576]{0,1:T(8,128)(2,1)} %param.23) | copy-start | bytes 5308420
  47.9 13.4 %collective-permute-start = (bf16[32,128]{1,0:T(8,128)(2,1)S(1)}, bf16[32,128]{1,0:T(8,128)(2,1)S(1)}, u32[]{:S(2)}, u32[]{:S(2)}) collective-permute-start(bf16[32,128]{1,0:T(8,128)(2,1)S(1)} %bitcast.74), channel_id=1, source_target_pairs={{0,1},{1,0},{2,3},{3,2},{4,5},{5,4},{6,7},{7,6},{8,9},{9,8},{10,11... | collective-permute-start | bytes 24584 | tf_op jit(solution)/shard_map/ppermute | solution.py:199
  61.3 18.0 %collective-permute-start.2 = (bf16[32,256]{1,0:T(8,128)(2,1)S(1)}, bf16[32,256]{1,0:T(8,128)(2,1)S(1)}, u32[]{:S(2)}, u32[]{:S(2)}) collective-permute-start(bf16[32,256]{1,0:T(8,128)(2,1)S(1)} %pad_maximum_fusion.2), channel_id=1, source_target_pairs={{0,2},{1,3},{2,0},{3,1},{4,6},{5,7},{6,4},{7,5},{8,10},{9,11},{10,... | collective-permute-start | bytes 49160 | tf_op jit(solution)/shard_map/ppermute | solution.py:204
  80.9 9.2 %collective-permute-start.4 = (bf16[32,1536]{1,0:T(8,128)(2,1)S(1)}, bf16[32,1536]{1,0:T(8,128)(2,1)S(1)}, u32[]{:S(2)}, u32[]{:S(2)}) collective-permute-start(bf16[32,1536]{1,0:T(8,128)(2,1)S(1)} %fusion.6), channel_id=1, source_target_pairs={{0,7},{1,6},{2,5},{3,4},{4,3},{5,2},{6,1},{7,0},{8,15},{9,14},{10,... | collective-permute-start | bytes 294920 | tf_op jit(solution)/shard_map/ppermute | solution.py:23
  93.4 4.8 %collective-permute-start.5 = (bf16[32,1536]{1,0:T(8,128)(2,1)S(1)}, bf16[32,1536]{1,0:T(8,128)(2,1)S(1)}, u32[]{:S(2)}, u32[]{:S(2)}) collective-permute-start(bf16[32,1536]{1,0:T(8,128)(2,1)S(1)} %convolution_convert_fusion), channel_id=1, source_target_pairs={{0,1},{1,0},{2,3},{3,2},{4,5},{5,4},{6,7},{7,6},{8,9},{9,8},{10,11... | collective-permute-start | bytes 294920 | tf_op jit(solution)/shard_map/ppermute | solution.py:20
  98.2 7.0 %collective-permute-start.6 = (bf16[32,1536]{1,0:T(8,128)(2,1)S(1)}, bf16[32,1536]{1,0:T(8,128)(2,1)S(1)}, u32[]{:S(2)}, u32[]{:S(2)}) collective-permute-start(bf16[32,1536]{1,0:T(8,128)(2,1)S(1)} %add.225), channel_id=1, source_target_pairs={{0,2},{1,3},{2,0},{3,1},{4,6},{5,7},{6,4},{7,5},{8,10},{9,11},{10,... | collective-permute-start | bytes 294920 | tf_op jit(solution)/shard_map/ppermute | solution.py:20
  105.2 6.7 %collective-permute-start.7 = (bf16[32,1536]{1,0:T(8,128)(2,1)S(1)}, bf16[32,1536]{1,0:T(8,128)(2,1)S(1)}, u32[]{:S(2)}, u32[]{:S(2)}) collective-permute-start(bf16[32,1536]{1,0:T(8,128)(2,1)S(1)} %add.226), channel_id=1, source_target_pairs={{0,7},{1,6},{2,5},{3,4},{4,3},{5,2},{6,1},{7,0},{8,15},{9,14},{10,... | collective-permute-start | bytes 294920 | tf_op jit(solution)/shard_map/ppermute | solution.py:23

commit v14 on v12

--- a/solution.py
+++ b/solution.py
@@ -50,6 +50,8 @@
         qwidth = steps * heads_dev * head_dim
         token_rows = tokens.reshape(req_dev * steps, width)
         partner_weight = lax.ppermute(out_weight, "tp", [(i, i ^ 1) for i in range(tp_size)])
+        far_weight = lax.ppermute(out_weight, "tp", [(i, i ^ 2) for i in range(tp_size)])
+        far_partner_weight = lax.ppermute(out_weight, "tp", [(i, i ^ 3) for i in range(tp_size)])
         normed = rms_norm(token_rows.astype(jnp.float32), norm_gain).astype(jnp.bfloat16)
         queries = (
             jnp.dot(normed, query_weight, preferred_element_type=jnp.float32) * head_dim ** (-0.5)
@@ -193,8 +195,16 @@
         projected = jnp.dot(attended, out_weight, preferred_element_type=jnp.float32) + jnp.dot(
             other_head, partner_weight, preferred_element_type=jnp.float32
         )
+        far = lax.ppermute(
+            jnp.concatenate([attended, other_head], axis=1), "tp", [(i, i ^ 2) for i in range(tp_size)]
+        )
+        far_width = attended.shape[1]
+        projected = projected + (
+            jnp.dot(far[:, :far_width], far_weight, preferred_element_type=jnp.float32)
+            + jnp.dot(far[:, far_width:], far_partner_weight, preferred_element_type=jnp.float32)
+        )
         attn_total = tree_sum(
-            projected.astype(jnp.bfloat16), "tp", tp_size, first_step=2
+            projected.astype(jnp.bfloat16), "tp", tp_size, first_step=4
         ).astype(jnp.float32)
         residual = (token_rows.astype(jnp.float32) + attn_total).astype(jnp.bfloat16)
         mlp_in = rms_norm(residual.astype(jnp.float32), mlp_gain).astype(jnp.bfloat16)

time: 94.8 us -> 95.1 us (level)
  the two profiles are of different devices: /device:TPU:2 before, /device:TPU:32 now
where the time goes in v14:
time: 95.1 us; the launch traced here: 94.5 us
  waiting for transfers between devices  36 us (38%)
  starting transfers between devices  31.1 us (33%)
  matrix products  14.6 us (15%)
  other arithmetic  6.56 us (7%)
  local copies, waits for them, and re-layouts  5.83 us (6%)
    ppermute x2, starting transfers between devices, tree_sum(): lax.ppermute(values, axis, [(i, size - 1 - i) for i in range(size)])  11.2 us
    ppermute x2, waiting for transfers between devices, tree_sum(): lax.ppermute(values, axis, [(i, i ^ step) for i in range(size)])  10.2 us
    all_to_all x1, waiting for transfers between devices, body(): lax.all_to_all(jnp.broadcast_to(packed[None], (req_size,) + packed.shape)...  8.95 us
    all_to_all x1, waiting for transfers between devices, body(): lax.all_to_all(send, 'req', 0, 0, tiled=True).reshape(req_size, req_dev, -1)  7.93 us
    all_to_all x1, starting transfers between devices, body(): lax.all_to_all(jnp.broadcast_to(packed[None], (req_size,) + packed.shape)...  7.32 us
    ppermute x2, waiting for transfers between devices, tree_sum(): lax.ppermute(values, axis, [(i, size - 1 - i) for i in range(size)])  5.19 us
    all_to_all x1, starting transfers between devices, body(): lax.all_to_all(send, 'req', 0, 0, tiled=True).reshape(req_size, req_dev, -1)  4.01 us
    dot_general x1, matrix products, body(): jnp.einsum('pqd,pkd->pqk', page_queries, kv_pages[:, 0], preferred_elemen...  3.08 us
  transfers between devices with their start and end apart: 11, of which 8 were waited for; matrix products, arithmetic and copies ran while one was open for 24% of the time, Pallas kernels for 0%

profile of v14, /device:TPU:32, one launch (start us, length us, event | category | flops | bytes accessed | tf_op | source)
XLA Modules:
  0.0 94.5 jit_solution(3907006609925556243)
XLA Ops:
  0.0 1.8 %collective-permute-start.1 = (bf16[128,1536]{1,0:T(8,128)(2,1)}, bf16[128,1536]{1,0:T(8,128)(2,1)}, u32[]{:S(2)}, u32[]{:S(2)}) collective-permute-start(bf16[128,1536]{1,0:T(8,128)(2,1)} %param.21), channel_id=1, source_target_pairs={{0,1},{1,0},{2,3},{3,2},{4,5},{5,4},{6,7},{7,6},{8,9},{9,8},{10,11... | collective-permute-start | bytes 1179656 | tf_op jit(solution)/shard_map/ppermute | solution.py:52
  1.8 2.0 %collective-permute-start.4 = (bf16[128,1536]{1,0:T(8,128)(2,1)}, bf16[128,1536]{1,0:T(8,128)(2,1)}, u32[]{:S(2)}, u32[]{:S(2)}) collective-permute-start(bf16[128,1536]{1,0:T(8,128)(2,1)} %param.21), channel_id=1, source_target_pairs={{0,3},{1,2},{2,1},{3,0},{4,7},{5,6},{6,5},{7,4},{8,11},{9,10},{10,... | collective-permute-start | bytes 1179656 | tf_op jit(solution)/shard_map/ppermute | solution.py:54
  4.4 1.0 %multiply_reduce_fusion = f32[8,4]{1,0:T(8,128)S(1)} fusion(bf16[8,4,1536]{2,1,0:T(4,128)(2,1)} %param.13), kind=kLoop, calls=%fused_computation.42 | loop fusion | flops 147424 | bytes 98432 | tf_op jit(solution)/shard_map/reduce_sum | solution.py:14
  5.4 0.9 reshape.470
  6.3 0.7 fusion.58
  7.3 0.7 fusion.53
  8.0 0.8 multiply_convert_fusion
  8.8 1.2 %fusion.18 = bf16[32,128]{1,0:T(8,128)(2,1)S(1)} fusion(bf16[32,1536]{1,0:T(8,128)(2,1)S(1)} %multiply_convert_fusion, bf16[1536,128]{1,0:T(8,128)(2,1)} %param.18), kind=kOutput, calls=%fused_computation.22 | convolution fusion | flops 12591104 | bytes 499712 | tf_op jit(solution)/shard_map/dot_general | solution.py:57
  10.1 0.7 broadcast_in_dim.131
  10.8 7.3 %all-to-all-start = ((bf16[32,8,532]{2,1,0:T(8,128)(2,1)}), bf16[32,8,532]{2,1,0:T(8,128)(2,1)S(1)}, u32[]{:S(2)}, u32[]{:S(2)}) async-start(bf16[32,8,532]{2,1,0:T(8,128)(2,1)} %broadcast_in_dim.131), calls=%async_computation | async-start | bytes 655360 | tf_op jit(solution)/shard_map/all_to_all | solution.py:74
  18.7 9.0 %all-to-all-done = bf16[32,8,532]{2,1,0:T(8,128)(2,1)S(1)} async-done(((bf16[32,8,532]{2,1,0:T(8,128)(2,1)}), bf16[32,8,532]{2,1,0:T(8,128)(2,1)S(1)}, u32[]{:S(2)}, u32[]{:S(2)}) %all-to-all-start) | async-done | bytes 272416 | tf_op jit(solution)/shard_map/all_to_all | solution.py:74
  30.0 3.1 %fusion.70 = (f32[72,4]{1,0:T(8,128)S(1)}, f32[72,4,128]{2,1,0:T(4,128)S(1)}) fusion(bf16[72,4,128]{2,1,0:T(4,128)(2,1)S(1)} %gather_fusion, bf16[72,2,128,128]{3,2,1,0:T(8,128)(2,1)} %param.16, s32[72,4]{1,0:T(8,128)S(1)} %add_add_fusion, s32[72,128]{1,0:T(8,128)S(1)} %iota_add_fusion, pred[72,128]{1,0:T(8,128)(4,1)S(1)} %broadcast_compare_fusion.1), kind=kOutput, calls=%fused_computation.136 | convolution fusion | flops 9584352 | bytes 2628864 | tf_op jit(solution)/shard_map/pqd,pkd->pqk/dot_general | solution.py:104
  33.9 2.5 %fusion.11 = f32[72,4,128]{2,1,0:T(4,128)S(1)} fusion(bf16[72,2,128,128]{3,2,1,0:T(8,128)(2,1)} %param.16, f32[72,4]{1,0:T(8,128)S(1)} %get-tuple-element.14, f32[72,4,128]{2,1,0:T(4,128)S(1)} %get-tuple-element.28, f32[72,4]{1,0:T(8,128)S(1)} %get-tuple-element.27, s32[72,4]{1,0:T(8,128)S(1)} %add_add_fusion, s32[72,128]{1,0:T(8,128)S(1)} %iota_add_fusion, ...), kind=kOutput, calls=%fused_computation.14 | convolution fusion | flops 9658368 | bytes 2703744 | tf_op jit(solution)/shard_map/pqk,pkd->pqd/dot_general | solution.py:111
  37.7 0.8 pad_maximum_fusion
  38.6 4.0 %all-to-all-start.1 = ((bf16[32,8,528]{2,1,0:T(8,128)(2,1)}), bf16[32,8,528]{2,1,0:T(8,128)(2,1)S(1)}, u32[]{:S(2)}, u32[]{:S(2)}) async-start(bf16[32,8,528]{2,1,0:T(8,128)(2,1)} %pad_maximum_fusion), calls=%async_computation.1 | async-start | bytes 655360 | tf_op jit(solution)/shard_map/all_to_all | solution.py:149
  43.0 1.2 %convolution_convert_fusion.2 = bf16[32,128]{1,0:T(8,128)(2,1)S(1)} fusion(bf16[32,1536]{1,0:T(8,128)(2,1)S(1)} %multiply_convert_fusion, bf16[1536,128]{1,0:T(8,128)(2,1)} %param.20), kind=kOutput, calls=%fused_computation.23 | convolution fusion | flops 12587008 | bytes 499712 | tf_op jit(solution)/shard_map/dot_general | solution.py:60
  44.1 7.9 %all-to-all-done.1 = bf16[32,8,528]{2,1,0:T(8,128)(2,1)S(1)} async-done(((bf16[32,8,528]{2,1,0:T(8,128)(2,1)}), bf16[32,8,528]{2,1,0:T(8,128)(2,1)S(1)}, u32[]{:S(2)}, u32[]{:S(2)}) %all-to-all-start.1) | async-done | bytes 270368 | tf_op jit(solution)/shard_map/all_to_all | solution.py:149
  53.1 1.0 %collective-permute-start = (bf16[32,128]{1,0:T(8,128)(2,1)S(1)}, bf16[32,128]{1,0:T(8,128)(2,1)S(1)}, u32[]{:S(2)}, u32[]{:S(2)}) collective-permute-start(bf16[32,128]{1,0:T(8,128)(2,1)S(1)} %bitcast.76), channel_id=1, source_target_pairs={{0,1},{1,0},{2,3},{3,2},{4,5},{5,4},{6,7},{7,6},{8,9},{9,8},{10,11... | collective-permute-start | bytes 24584 | tf_op jit(solution)/shard_map/ppermute | solution.py:194
  54.3 2.6 %collective-permute-done = bf16[32,128]{1,0:T(8,128)(2,1)S(1)} collective-permute-done((bf16[32,128]{1,0:T(8,128)(2,1)S(1)}, bf16[32,128]{1,0:T(8,128)(2,1)S(1)}, u32[]{:S(2)}, u32[]{:S(2)}) %collective-permute-start) | collective-permute-done | bytes 8224 | tf_op jit(solution)/shard_map/ppermute | solution.py:194
  56.9 2.4 %collective-permute-start.2 = (bf16[32,256]{1,0:T(8,128)(2,1)S(1)}, bf16[32,256]{1,0:T(8,128)(2,1)S(1)}, u32[]{:S(2)}, u32[]{:S(2)}) collective-permute-start(bf16[32,256]{1,0:T(8,128)(2,1)S(1)} %pad_maximum_fusion.1), channel_id=1, source_target_pairs={{0,2},{1,3},{2,0},{3,1},{4,6},{5,7},{6,4},{7,5},{8,10},{9,11},{10,... | collective-permute-start | bytes 49160 | tf_op jit(solution)/shard_map/ppermute | solution.py:198
  59.2 1.2 %convolution_add_fusion.1 = f32[32,1536]{1,0:T(8,128)S(1)} fusion(f32[32,1536]{1,0:T(8,128)S(1)} %fusion.72, bf16[32,128]{1,0:T(8,128)(2,1)S(1)} %collective-permute-done, bf16[128,1536]{1,0:T(8,128)(2,1)} %collective-permute-done.1), kind=kOutput, calls=%fused_computation.9 | convolution fusion | flops 12632064 | bytes 794624 | tf_op jit(solution)/shard_map/dot_general | solution.py:195
  60.4 1.1 %collective-permute-done.2 = bf16[32,256]{1,0:T(8,128)(2,1)S(1)} collective-permute-done((bf16[32,256]{1,0:T(8,128)(2,1)S(1)}, bf16[32,256]{1,0:T(8,128)(2,1)S(1)}, u32[]{:S(2)}, u32[]{:S(2)}) %collective-permute-start.2) | collective-permute-done | bytes 16416 | tf_op jit(solution)/shard_map/ppermute | solution.py:198
  61.5 1.2 %fusion.47 = f32[32,1536]{1,0:T(8,128)S(1)} fusion(bf16[128,1536]{1,0:T(8,128)(2,1)} %collective-permute-done.4, bf16[32,256]{1,0:T(8,128)(2,1)S(1)} %collective-permute-done.2), kind=kOutput, calls=%fused_computation.85 | convolution fusion | flops 12582912 | bytes 598016 | tf_op jit(solution)/shard_map/dot_general | solution.py:204
  62.9 5.9 %collective-permute-start.5 = (bf16[32,1536]{1,0:T(8,128)(2,1)S(1)}, bf16[32,1536]{1,0:T(8,128)(2,1)S(1)}, u32[]{:S(2)}, u32[]{:S(2)}) collective-permute-start(bf16[32,1536]{1,0:T(8,128)(2,1)S(1)} %fusion.7), channel_id=1, source_target_pairs={{0,7},{1,6},{2,5},{3,4},{4,3},{5,2},{6,1},{7,0},{8,15},{9,14},{10,... | collective-permute-start | bytes 294920 | tf_op jit(solution)/shard_map/ppermute | solution.py:23
  68.8 2.6 %collective-permute-done.5 = bf16[32,1536]{1,0:T(8,128)(2,1)S(1)} collective-permute-done((bf16[32,1536]{1,0:T(8,128)(2,1)S(1)}, bf16[32,1536]{1,0:T(8,128)(2,1)S(1)}, u32[]{:S(2)}, u32[]{:S(2)}) %collective-permute-start.5) | collective-permute-done | bytes 98336 | tf_op jit(solution)/shard_map/ppermute | solution.py:23
  72.2 2.5 %convolution_convert_fusion = bf16[32,1536]{1,0:T(8,128)(2,1)S(1)} fusion(bf16[576,1536]{1,0:T(8,128)(2,1)S(1)} %copy-done, bf16[1536,576]{0,1:T(8,128)(2,1)} %param.24, f32[32,576]{1,0:T(8,128)S(1)} %fusion.44, bf16[32,1536]{1,0:T(8,128)(2,1)S(1)} %get-tuple-element.8, f32[1536]{0:T(1024)S(1)} %copy-done.4, f32[32]{0:T(128)S(1)} %add_rsqrt_fusion.1), kind=kOutput, calls=%fused_computation.11 | convolution fusion | flops 113676288 | bytes 3815552 | tf_op jit(solution)/shard_map/dot_general | solution.py:214
  74.8 5.5 %collective-permute-done.6 = bf16[32,1536]{1,0:T(8,128)(2,1)S(1)} collective-permute-done((bf16[32,1536]{1,0:T(8,128)(2,1)S(1)}, bf16[32,1536]{1,0:T(8,128)(2,1)S(1)}, u32[]{:S(2)}, u32[]{:S(2)}) %collective-permute-start.6) | collective-permute-done | bytes 98336 | tf_op jit(solution)/shard_map/ppermute | solution.py:20
  80.3 0.8 collective-permute-start.7
  81.1 4.8 %collective-permute-done.7 = bf16[32,1536]{1,0:T(8,128)(2,1)S(1)} collective-permute-done((bf16[32,1536]{1,0:T(8,128)(2,1)S(1)}, bf16[32,1536]{1,0:T(8,128)(2,1)S(1)}, u32[]{:S(2)}, u32[]{:S(2)}) %collective-permute-start.7) | collective-permute-done | bytes 98336 | tf_op jit(solution)/shard_map/ppermute | solution.py:20
  85.9 5.2 %collective-permute-start.8 = (bf16[32,1536]{1,0:T(8,128)(2,1)S(1)}, bf16[32,1536]{1,0:T(8,128)(2,1)S(1)}, u32[]{:S(2)}, u32[]{:S(2)}) collective-permute-start(bf16[32,1536]{1,0:T(8,128)(2,1)S(1)} %add.229), channel_id=1, source_target_pairs={{0,7},{1,6},{2,5},{3,4},{4,3},{5,2},{6,1},{7,0},{8,15},{9,14},{10,... | collective-permute-start | bytes 294920 | tf_op jit(solution)/shard_map/ppermute | solution.py:23
  91.2 2.6 %collective-permute-done.8 = bf16[32,1536]{1,0:T(8,128)(2,1)S(1)} collective-permute-done((bf16[32,1536]{1,0:T(8,128)(2,1)S(1)}, bf16[32,1536]{1,0:T(8,128)(2,1)S(1)}, u32[]{:S(2)}, u32[]{:S(2)}) %collective-permute-start.8) | collective-permute-done | bytes 98336 | tf_op jit(solution)/shard_map/ppermute | solution.py:23
  93.8 0.7 reshape.469
  (82 shorter events, 8.5 us)
Async XLA Ops:
  0.0 72.2 %copy-start = (bf16[576,1536]{1,0:T(8,128)(2,1)S(1)}, bf16[576,1536]{1,0:T(8,128)(2,1)}, u32[]{:S(2)}) copy-start(bf16[576,1536]{1,0:T(8,128)(2,1)} %param.25) | copy-start | bytes 5308420
  0.0 18.1 %copy-start.3 = (bf16[1536,128]{1,0:T(8,128)(2,1)S(1)}, bf16[1536,128]{1,0:T(8,128)(2,1)}, u32[]{:S(2)}) copy-start(bf16[1536,128]{1,0:T(8,128)(2,1)} %param.19) | copy-start | bytes 1179652
  0.0 59.2 %collective-permute-start.1 = (bf16[128,1536]{1,0:T(8,128)(2,1)}, bf16[128,1536]{1,0:T(8,128)(2,1)}, u32[]{:S(2)}, u32[]{:S(2)}) collective-permute-start(bf16[128,1536]{1,0:T(8,128)(2,1)} %param.21), channel_id=1, source_target_pairs={{0,1},{1,0},{2,3},{3,2},{4,5},{5,4},{6,7},{7,6},{8,9},{9,8},{10,11... | collective-permute-start | bytes 1179656 | tf_op jit(solution)/shard_map/ppermute | solution.py:52
  1.8 58.6 %collective-permute-start.4 = (bf16[128,1536]{1,0:T(8,128)(2,1)}, bf16[128,1536]{1,0:T(8,128)(2,1)}, u32[]{:S(2)}, u32[]{:S(2)}) collective-permute-start(bf16[128,1536]{1,0:T(8,128)(2,1)} %param.21), channel_id=1, source_target_pairs={{0,3},{1,2},{2,1},{3,0},{4,7},{5,6},{6,5},{7,4},{8,11},{9,10},{10,... | collective-permute-start | bytes 1179656 | tf_op jit(solution)/shard_map/ppermute | solution.py:54
  3.8 58.8 %collective-permute-start.3 = (bf16[128,1536]{1,0:T(8,128)(2,1)}, bf16[128,1536]{1,0:T(8,128)(2,1)S(1)}, u32[]{:S(2)}, u32[]{:S(2)}) collective-permute-start(bf16[128,1536]{1,0:T(8,128)(2,1)} %param.21), channel_id=1, source_target_pairs={{0,2},{1,3},{2,0},{3,1},{4,6},{5,7},{6,4},{7,5},{8,10},{9,11},{10,... | collective-permute-start | bytes 1179656 | tf_op jit(solution)/shard_map/ppermute | solution.py:53
  10.8 16.8 %all-to-all-start = ((bf16[32,8,532]{2,1,0:T(8,128)(2,1)}), bf16[32,8,532]{2,1,0:T(8,128)(2,1)S(1)}, u32[]{:S(2)}, u32[]{:S(2)}) async-start(bf16[32,8,532]{2,1,0:T(8,128)(2,1)} %broadcast_in_dim.131), calls=%async_computation | async-start | bytes 655360 | tf_op jit(solution)/shard_map/all_to_all | solution.py:74
  38.6 15.6 %copy-start.2 = (bf16[128,1536]{1,0:T(8,128)(2,1)S(1)}, bf16[128,1536]{1,0:T(8,128)(2,1)}, u32[]{:S(2)}) copy-start(bf16[128,1536]{1,0:T(8,128)(2,1)} %param.21) | copy-start | bytes 1179652
  38.6 13.5 %all-to-all-start.1 = ((bf16[32,8,528]{2,1,0:T(8,128)(2,1)}), bf16[32,8,528]{2,1,0:T(8,128)(2,1)S(1)}, u32[]{:S(2)}, u32[]{:S(2)}) async-start(bf16[32,8,528]{2,1,0:T(8,128)(2,1)} %pad_maximum_fusion), calls=%async_computation.1 | async-start | bytes 655360 | tf_op jit(solution)/shard_map/all_to_all | solution.py:149
  53.0 18.6 %copy-start.1 = (bf16[1536,576]{0,1:T(8,128)(2,1)S(1)}, bf16[1536,576]{0,1:T(8,128)(2,1)}, u32[]{:S(2)}) copy-start(bf16[1536,576]{0,1:T(8,128)(2,1)} %param.23) | copy-start | bytes 5308420
  53.0 18.6 %copy-start.4 = (f32[1536]{0:T(1024)S(1)}, f32[1536]{0:T(1024)}, u32[]{:S(2)}) copy-start(f32[1536]{0:T(1024)} %param.22) | copy-start | bytes 18436
  53.1 3.7 %collective-permute-start = (bf16[32,128]{1,0:T(8,128)(2,1)S(1)}, bf16[32,128]{1,0:T(8,128)(2,1)S(1)}, u32[]{:S(2)}, u32[]{:S(2)}) collective-permute-start(bf16[32,128]{1,0:T(8,128)(2,1)S(1)} %bitcast.76), channel_id=1, source_target_pairs={{0,1},{1,0},{2,3},{3,2},{4,5},{5,4},{6,7},{7,6},{8,9},{9,8},{10,11... | collective-permute-start | bytes 24584 | tf_op jit(solution)/shard_map/ppermute | solution.py:194
  56.9 4.6 %collective-permute-start.2 = (bf16[32,256]{1,0:T(8,128)(2,1)S(1)}, bf16[32,256]{1,0:T(8,128)(2,1)S(1)}, u32[]{:S(2)}, u32[]{:S(2)}) collective-permute-start(bf16[32,256]{1,0:T(8,128)(2,1)S(1)} %pad_maximum_fusion.1), channel_id=1, source_target_pairs={{0,2},{1,3},{2,0},{3,1},{4,6},{5,7},{6,4},{7,5},{8,10},{9,11},{10,... | collective-permute-start | bytes 49160 | tf_op jit(solution)/shard_map/ppermute | solution.py:198
  62.9 8.5 %collective-permute-start.5 = (bf16[32,1536]{1,0:T(8,128)(2,1)S(1)}, bf16[32,1536]{1,0:T(8,128)(2,1)S(1)}, u32[]{:S(2)}, u32[]{:S(2)}) collective-permute-start(bf16[32,1536]{1,0:T(8,128)(2,1)S(1)} %fusion.7), channel_id=1, source_target_pairs={{0,7},{1,6},{2,5},{3,4},{4,3},{5,2},{6,1},{7,0},{8,15},{9,14},{10,... | collective-permute-start | bytes 294920 | tf_op jit(solution)/shard_map/ppermute | solution.py:23
  74.7 5.5 %collective-permute-start.6 = (bf16[32,1536]{1,0:T(8,128)(2,1)S(1)}, bf16[32,1536]{1,0:T(8,128)(2,1)S(1)}, u32[]{:S(2)}, u32[]{:S(2)}) collective-permute-start(bf16[32,1536]{1,0:T(8,128)(2,1)S(1)} %convolution_convert_fusion), channel_id=1, source_target_pairs={{0,1},{1,0},{2,3},{3,2},{4,5},{5,4},{6,7},{7,6},{8,9},{9,8},{10,11... | collective-permute-start | bytes 294920 | tf_op jit(solution)/shard_map/ppermute | solution.py:20
  80.3 5.6 %collective-permute-start.7 = (bf16[32,1536]{1,0:T(8,128)(2,1)S(1)}, bf16[32,1536]{1,0:T(8,128)(2,1)S(1)}, u32[]{:S(2)}, u32[]{:S(2)}) collective-permute-start(bf16[32,1536]{1,0:T(8,128)(2,1)S(1)} %add.228), channel_id=1, source_target_pairs={{0,2},{1,3},{2,0},{3,1},{4,6},{5,7},{6,4},{7,5},{8,10},{9,11},{10,... | collective-permute-start | bytes 294920 | tf_op jit(solution)/shard_map/ppermute | solution.py:20
  85.9 7.8 %collective-permute-start.8 = (bf16[32,1536]{1,0:T(8,128)(2,1)S(1)}, bf16[32,1536]{1,0:T(8,128)(2,1)S(1)}, u32[]{:S(2)}, u32[]{:S(2)}) collective-permute-start(bf16[32,1536]{1,0:T(8,128)(2,1)S(1)} %add.229), channel_id=1, source_target_pairs={{0,7},{1,6},{2,5},{3,4},{4,3},{5,2},{6,1},{7,0},{8,15},{9,14},{10,... | collective-permute-start | bytes 294920 | tf_op jit(solution)/shard_map/ppermute | solution.py:23

commit v15 on v11

--- a/solution.py
+++ b/solution.py
@@ -50,6 +50,7 @@
         qwidth = steps * heads_dev * head_dim
         token_rows = tokens.reshape(req_dev * steps, width)
         partner_weight = lax.ppermute(out_weight, "tp", [(i, i ^ 1) for i in range(tp_size)])
+        partner_down = lax.ppermute(down_weight, "tp", [(i, i ^ 1) for i in range(tp_size)])
         normed = rms_norm(token_rows.astype(jnp.float32), norm_gain).astype(jnp.bfloat16)
         queries = (
             jnp.dot(normed, query_weight, preferred_element_type=jnp.float32) * head_dim ** (-0.5)
@@ -207,10 +208,12 @@
         gate = jnp.dot(mlp_in, gate_weight, preferred_element_type=jnp.float32)
         upward = jnp.dot(mlp_in, up_weight, preferred_element_type=jnp.float32)
         hidden = (jax.nn.gelu(gate, approximate=True) * upward).astype(jnp.bfloat16)
-        mlp_part = jnp.dot(hidden, down_weight, preferred_element_type=jnp.float32).astype(
-            jnp.bfloat16
-        )
-        mlp_total = tree_sum(mlp_part, "tp", tp_size).astype(jnp.float32)
+        other_hidden = lax.ppermute(hidden, "tp", [(i, i ^ 1) for i in range(tp_size)])
+        mlp_part = (
+            jnp.dot(hidden, down_weight, preferred_element_type=jnp.float32)
+            + jnp.dot(other_hidden, partner_down, preferred_element_type=jnp.float32)
+        ).astype(jnp.bfloat16)
+        mlp_total = tree_sum(mlp_part, "tp", tp_size, first_step=2).astype(jnp.float32)
         layer_out = (residual.astype(jnp.float32) + mlp_total).astype(jnp.bfloat16)
         return layer_out.reshape(req_dev, steps, width)
 

time: 93.9 us -> 103 us (1.097)
  waiting for transfers between devices: 36.2 us -> 43.9 us
    ppermute x1, waiting for transfers between devices: 0.68 us -> 10.8 us  [body(): other_head = lax.ppermute(attended, 'tp', pair)]
    ppermute x3 -> x2, waiting for transfers between devices: 15.9 us -> 10.7 us  [tree_sum(): lax.ppermute(values, axis, [(i, i ^ step) for i in range(size)])]
    ppermute x0 -> x2, waiting for transfers between devices: none -> 3.5 us  [the longest x1 3.5 us: body(): lax.ppermute(hidden, 'tp', [(i, i ^ 1) for i in range(tp_size)])]
    dot_general x0 -> x2, matrix products: none -> 2.55 us  [the longest x1 1.89 us: body(): jnp.dot(other_hidden, partner_down, preferred_element_type=jnp.float32)]
    dot_general x1, matrix products: 2.52 us -> 0.4 us  [body(): jnp.dot(hidden, down_weight, preferred_element_type=jnp.float32)]
    ppermute x3 -> x2, starting transfers between devices: 3.8 us -> 3.49 us  [tree_sum(): lax.ppermute(values, axis, [(i, i ^ step) for i in range(size)])]
  transfers between devices with their start and end apart: 9 -> 10, of which waited for: 8 -> 8; matrix products, arithmetic and copies ran while one was open for 19% -> 20% of each run, Pallas kernels for 0% -> 0%
where the time goes in v15:
time: 103 us; the launch traced here: 102 us
  waiting for transfers between devices  43.9 us (43%)
  starting transfers between devices  28.5 us (28%)
  matrix products  11.6 us (11%)
  other arithmetic  9.9 us (10%)
  local copies, waits for them, and re-layouts  7.84 us (8%)
    ppermute x1, waiting for transfers between devices, body(): other_head = lax.ppermute(attended, 'tp', pair)  10.8 us
    ppermute x2, waiting for transfers between devices, tree_sum(): lax.ppermute(values, axis, [(i, i ^ step) for i in range(size)])  10.7 us
    ppermute x2, starting transfers between devices, tree_sum(): lax.ppermute(values, axis, [(i, size - 1 - i) for i in range(size)])  8.2 us
    all_to_all x1, starting transfers between devices, body(): lax.all_to_all(jnp.broadcast_to(packed[None], (req_size,) + packed.shape)...  7.62 us
    ppermute x2, waiting for transfers between devices, tree_sum(): lax.ppermute(values, axis, [(i, size - 1 - i) for i in range(size)])  7.41 us
    all_to_all x1, waiting for transfers between devices, body(): lax.all_to_all(send, 'req', 0, 0, tiled=True).reshape(req_size, req_dev, -1)  6.46 us
    all_to_all x1, waiting for transfers between devices, body(): lax.all_to_all(jnp.broadcast_to(packed[None], (req_size,) + packed.shape)...  5.03 us
    all_to_all x1, starting transfers between devices, body(): lax.all_to_all(send, 'req', 0, 0, tiled=True).reshape(req_size, req_dev, -1)  4.99 us
  transfers between devices with their start and end apart: 10, of which 8 were waited for; matrix products, arithmetic and copies ran while one was open for 20% of the time, Pallas kernels for 0%

profile of v15, /device:TPU:2, one launch (start us, length us, event | category | flops | bytes accessed | tf_op | source)
XLA Modules:
  0.0 102.0 jit_solution(3660759446779759201)
XLA Ops:
  0.0 1.2 %multiply_reduce_fusion = f32[8,4]{1,0:T(8,128)S(1)} fusion(bf16[8,4,1536]{2,1,0:T(4,128)(2,1)} %param.13), kind=kLoop, calls=%fused_computation.45 | loop fusion | flops 147424 | bytes 98432 | tf_op jit(solution)/shard_map/reduce_sum | solution.py:14
  1.2 0.9 reshape.470
  2.1 0.7 fusion.54
  3.0 0.7 fusion.49
  3.8 0.8 multiply_convert_fusion
  4.5 1.2 %fusion.17 = bf16[32,128]{1,0:T(8,128)(2,1)S(1)} fusion(bf16[32,1536]{1,0:T(8,128)(2,1)S(1)} %multiply_convert_fusion, bf16[1536,128]{1,0:T(8,128)(2,1)} %param.18), kind=kOutput, calls=%fused_computation.20 | convolution fusion | flops 12591104 | bytes 499712 | tf_op jit(solution)/shard_map/dot_general | solution.py:56
  5.9 0.7 broadcast_in_dim.131
  6.6 7.6 %all-to-all-start = ((bf16[32,8,532]{2,1,0:T(8,128)(2,1)}), bf16[32,8,532]{2,1,0:T(8,128)(2,1)S(1)}, u32[]{:S(2)}, u32[]{:S(2)}) async-start(bf16[32,8,532]{2,1,0:T(8,128)(2,1)} %broadcast_in_dim.131), calls=%async_computation | async-start | bytes 655360 | tf_op jit(solution)/shard_map/all_to_all | solution.py:73
  14.2 2.0 %collective-permute-start.1 = (bf16[128,1536]{1,0:T(8,128)(2,1)S(1)}, bf16[128,1536]{1,0:T(8,128)(2,1)}, u32[]{:S(2)}, u32[]{:S(2)}) collective-permute-start(bf16[128,1536]{1,0:T(8,128)(2,1)S(1)} %copy-done.5), channel_id=1, source_target_pairs={{0,1},{1,0},{2,3},{3,2},{4,5},{5,4},{6,7},{7,6},{8,9},{9,8},{10,11... | collective-permute-start | bytes 1179656 | tf_op jit(solution)/shard_map/ppermute | solution.py:52
  16.8 0.7 select_reduce_fusion.2
  17.5 5.0 %all-to-all-done = bf16[32,8,532]{2,1,0:T(8,128)(2,1)S(1)} async-done(((bf16[32,8,532]{2,1,0:T(8,128)(2,1)}), bf16[32,8,532]{2,1,0:T(8,128)(2,1)S(1)}, u32[]{:S(2)}, u32[]{:S(2)}) %all-to-all-start) | async-done | bytes 272416 | tf_op jit(solution)/shard_map/all_to_all | solution.py:73
  24.9 3.1 %fusion.63 = (f32[72,4]{1,0:T(8,128)S(1)}, f32[72,4,128]{2,1,0:T(4,128)S(1)}) fusion(bf16[72,4,128]{2,1,0:T(4,128)(2,1)S(1)} %gather_fusion, bf16[72,2,128,128]{3,2,1,0:T(8,128)(2,1)} %param.16, s32[72,4]{1,0:T(8,128)S(1)} %add_add_fusion, s32[72,128]{1,0:T(8,128)S(1)} %iota_add_fusion, pred[72,128]{1,0:T(8,128)(4,1)S(1)} %broadcast_compare_fusion.1), kind=kOutput, calls=%fused_computation.133 | convolution fusion | flops 9584352 | bytes 2628864 | tf_op jit(solution)/shard_map/pqd,pkd->pqk/dot_general | solution.py:103
  28.8 2.5 %fusion.10 = f32[72,4,128]{2,1,0:T(4,128)S(1)} fusion(bf16[72,2,128,128]{3,2,1,0:T(8,128)(2,1)} %param.16, f32[72,4]{1,0:T(8,128)S(1)} %get-tuple-element.14, f32[72,4,128]{2,1,0:T(4,128)S(1)} %get-tuple-element.32, f32[72,4]{1,0:T(8,128)S(1)} %get-tuple-element.31, s32[72,4]{1,0:T(8,128)S(1)} %add_add_fusion, s32[72,128]{1,0:T(8,128)S(1)} %iota_add_fusion, ...), kind=kOutput, calls=%fused_computation.12 | convolution fusion | flops 9658368 | bytes 2703744 | tf_op jit(solution)/shard_map/pqk,pkd->pqd/dot_general | solution.py:110
  31.6 0.8 copy.112
  32.4 0.8 copy.111
  33.8 1.7 %pad_maximum_fusion = bf16[32,8,528]{2,1,0:T(8,128)(2,1)} fusion(bf16[32,8,4]{2,1,0:T(8,128)(2,1)} %copy.112, bf16[32,8,4]{2,1,0:T(8,128)(2,1)} %copy.111, bf16[32,8,4]{2,1,0:T(8,128)(2,1)S(1)} %copy.110, bf16[32,8,516]{2,1,0:T(8,128)(2,1)S(1)} %bitcast.68), kind=kLoop, calls=%fused_computation.34 | loop fusion | flops 1081344 | bytes 540672 | tf_op jit(solution)/shard_map/concatenate | solution.py:145
  35.5 5.0 %all-to-all-start.1 = ((bf16[32,8,528]{2,1,0:T(8,128)(2,1)}), bf16[32,8,528]{2,1,0:T(8,128)(2,1)S(1)}, u32[]{:S(2)}, u32[]{:S(2)}) async-start(bf16[32,8,528]{2,1,0:T(8,128)(2,1)} %pad_maximum_fusion), calls=%async_computation.1 | async-start | bytes 655360 | tf_op jit(solution)/shard_map/all_to_all | solution.py:148
  40.5 0.8 fusion.46
  41.3 0.8 copy.114
  42.4 6.5 %all-to-all-done.1 = bf16[32,8,528]{2,1,0:T(8,128)(2,1)S(1)} async-done(((bf16[32,8,528]{2,1,0:T(8,128)(2,1)}), bf16[32,8,528]{2,1,0:T(8,128)(2,1)S(1)}, u32[]{:S(2)}, u32[]{:S(2)}) %all-to-all-start.1) | async-done | bytes 270368 | tf_op jit(solution)/shard_map/all_to_all | solution.py:148
  49.9 2.0 %collective-permute-start = (bf16[32,128]{1,0:T(8,128)(2,1)S(1)}, bf16[32,128]{1,0:T(8,128)(2,1)S(1)}, u32[]{:S(2)}, u32[]{:S(2)}) collective-permute-start(bf16[32,128]{1,0:T(8,128)(2,1)S(1)} %bitcast.75), channel_id=1, source_target_pairs={{0,1},{1,0},{2,3},{3,2},{4,5},{5,4},{6,7},{7,6},{8,9},{9,8},{10,11... | collective-permute-start | bytes 24584 | tf_op jit(solution)/shard_map/ppermute | solution.py:193
  51.9 1.1 %broadcast_select_fusion.1 = (bf16[128,1536]{1,0:T(8,128)(2,1)S(1)}, bf16[128,1536]{1,0:T(8,128)(2,1)S(1)}) fusion(bf16[128,1536]{1,0:T(8,128)(2,1)S(1)} %copy-done.5, bf16[128,1536]{1,0:T(8,128)(2,1)} %collective-permute-done.1, pred[]{:T(512)S(6)} %eq.60), kind=kLoop, calls=%fused_computation.33 | loop fusion | flops 393216 | bytes 1572865 | tf_op jit(solution)/shard_map/jit(_where)/select_n | solution.py:199
  53.0 10.8 %collective-permute-done = bf16[32,128]{1,0:T(8,128)(2,1)S(1)} collective-permute-done((bf16[32,128]{1,0:T(8,128)(2,1)S(1)}, bf16[32,128]{1,0:T(8,128)(2,1)S(1)}, u32[]{:S(2)}, u32[]{:S(2)}) %collective-permute-start) | collective-permute-done | bytes 8224 | tf_op jit(solution)/shard_map/ppermute | solution.py:193
  64.0 3.3 %collective-permute-start.2 = (bf16[32,1536]{1,0:T(8,128)(2,1)S(1)}, bf16[32,1536]{1,0:T(8,128)(2,1)S(1)}, u32[]{:S(2)}, u32[]{:S(2)}) collective-permute-start(bf16[32,1536]{1,0:T(8,128)(2,1)S(1)} %convolution_convert_fusion), channel_id=1, source_target_pairs={{0,2},{1,3},{2,0},{3,1},{4,6},{5,7},{6,4},{7,5},{8,10},{9,11},{10,... | collective-permute-start | bytes 294920 | tf_op jit(solution)/shard_map/ppermute | solution.py:20
  67.3 4.6 %collective-permute-done.2 = bf16[32,1536]{1,0:T(8,128)(2,1)S(1)} collective-permute-done((bf16[32,1536]{1,0:T(8,128)(2,1)S(1)}, bf16[32,1536]{1,0:T(8,128)(2,1)S(1)}, u32[]{:S(2)}, u32[]{:S(2)}) %collective-permute-start.2) | collective-permute-done | bytes 98336 | tf_op jit(solution)/shard_map/ppermute | solution.py:20
  72.0 5.0 %collective-permute-start.3 = (bf16[32,1536]{1,0:T(8,128)(2,1)S(1)}, bf16[32,1536]{1,0:T(8,128)(2,1)S(1)}, u32[]{:S(2)}, u32[]{:S(2)}) collective-permute-start(bf16[32,1536]{1,0:T(8,128)(2,1)S(1)} %add.218), channel_id=1, source_target_pairs={{0,7},{1,6},{2,5},{3,4},{4,3},{5,2},{6,1},{7,0},{8,15},{9,14},{10,... | collective-permute-start | bytes 294920 | tf_op jit(solution)/shard_map/ppermute | solution.py:23
  76.9 3.9 %collective-permute-done.3 = bf16[32,1536]{1,0:T(8,128)(2,1)S(1)} collective-permute-done((bf16[32,1536]{1,0:T(8,128)(2,1)S(1)}, bf16[32,1536]{1,0:T(8,128)(2,1)S(1)}, u32[]{:S(2)}, u32[]{:S(2)}) %collective-permute-start.3) | collective-permute-done | bytes 98336 | tf_op jit(solution)/shard_map/ppermute | solution.py:23
  82.9 3.5 %collective-permute-done.4 = bf16[32,576]{1,0:T(8,128)(2,1)S(1)} collective-permute-done((bf16[32,576]{1,0:T(8,128)(2,1)S(1)}, bf16[32,576]{1,0:T(8,128)(2,1)S(1)}, u32[]{:S(2)}, u32[]{:S(2)}) %collective-permute-start.4) | collective-permute-done | bytes 36896 | tf_op jit(solution)/shard_map/ppermute | solution.py:211
  86.4 1.9 %fusion.6 = bf16[32,1536]{1,0:T(8,128)(2,1)S(1)} fusion(f32[32,1536]{1,0:T(8,128)S(1)} %fusion.65, bf16[32,576]{1,0:T(8,128)(2,1)S(1)} %collective-permute-done.4, bf16[576,1536]{1,0:T(8,128)(2,1)} %collective-permute-done.5), kind=kOutput, calls=%fused_computation.8 | convolution fusion | flops 56721408 | bytes 2101248 | tf_op jit(solution)/shard_map/dot_general | solution.py:214
  88.4 6.1 %collective-permute-done.6 = bf16[32,1536]{1,0:T(8,128)(2,1)S(1)} collective-permute-done((bf16[32,1536]{1,0:T(8,128)(2,1)S(1)}, bf16[32,1536]{1,0:T(8,128)(2,1)S(1)}, u32[]{:S(2)}, u32[]{:S(2)}) %collective-permute-start.6) | collective-permute-done | bytes 98336 | tf_op jit(solution)/shard_map/ppermute | solution.py:20
  94.6 3.3 %collective-permute-start.7 = (bf16[32,1536]{1,0:T(8,128)(2,1)S(1)}, bf16[32,1536]{1,0:T(8,128)(2,1)S(1)}, u32[]{:S(2)}, u32[]{:S(2)}) collective-permute-start(bf16[32,1536]{1,0:T(8,128)(2,1)S(1)} %add.226), channel_id=1, source_target_pairs={{0,7},{1,6},{2,5},{3,4},{4,3},{5,2},{6,1},{7,0},{8,15},{9,14},{10,... | collective-permute-start | bytes 294920 | tf_op jit(solution)/shard_map/ppermute | solution.py:23
  97.9 3.5 %collective-permute-done.7 = bf16[32,1536]{1,0:T(8,128)(2,1)S(1)} collective-permute-done((bf16[32,1536]{1,0:T(8,128)(2,1)S(1)}, bf16[32,1536]{1,0:T(8,128)(2,1)S(1)}, u32[]{:S(2)}, u32[]{:S(2)}) %collective-permute-start.7) | collective-permute-done | bytes 98336 | tf_op jit(solution)/shard_map/ppermute | solution.py:23
  (86 shorter events, 9.5 us)
Async XLA Ops:
  0.0 81.0 %copy-start = (bf16[1536,576]{0,1:T(8,128)(2,1)S(1)}, bf16[1536,576]{0,1:T(8,128)(2,1)}, u32[]{:S(2)}) copy-start(bf16[1536,576]{0,1:T(8,128)(2,1)} %param.23) | copy-start | bytes 5308420
  0.0 14.2 %copy-start.5 = (bf16[128,1536]{1,0:T(8,128)(2,1)S(1)}, bf16[128,1536]{1,0:T(8,128)(2,1)}, u32[]{:S(2)}) copy-start(bf16[128,1536]{1,0:T(8,128)(2,1)} %param.21) | copy-start | bytes 1179652
  0.0 16.3 %copy-start.3 = (bf16[1536,128]{1,0:T(8,128)(2,1)S(1)}, bf16[1536,128]{1,0:T(8,128)(2,1)}, u32[]{:S(2)}) copy-start(bf16[1536,128]{1,0:T(8,128)(2,1)} %param.19) | copy-start | bytes 1179652
  6.6 15.9 %all-to-all-start = ((bf16[32,8,532]{2,1,0:T(8,128)(2,1)}), bf16[32,8,532]{2,1,0:T(8,128)(2,1)S(1)}, u32[]{:S(2)}, u32[]{:S(2)}) async-start(bf16[32,8,532]{2,1,0:T(8,128)(2,1)} %broadcast_in_dim.131), calls=%async_computation | async-start | bytes 655360 | tf_op jit(solution)/shard_map/all_to_all | solution.py:73
  14.2 37.7 %collective-permute-start.1 = (bf16[128,1536]{1,0:T(8,128)(2,1)S(1)}, bf16[128,1536]{1,0:T(8,128)(2,1)}, u32[]{:S(2)}, u32[]{:S(2)}) collective-permute-start(bf16[128,1536]{1,0:T(8,128)(2,1)S(1)} %copy-done.5), channel_id=1, source_target_pairs={{0,1},{1,0},{2,3},{3,2},{4,5},{5,4},{6,7},{7,6},{8,9},{9,8},{10,11... | collective-permute-start | bytes 1179656 | tf_op jit(solution)/shard_map/ppermute | solution.py:52
  16.2 70.2 %collective-permute-start.5 = (bf16[576,1536]{1,0:T(8,128)(2,1)}, bf16[576,1536]{1,0:T(8,128)(2,1)}, u32[]{:S(2)}, u32[]{:S(2)}) collective-permute-start(bf16[576,1536]{1,0:T(8,128)(2,1)} %param.25), channel_id=1, source_target_pairs={{0,1},{1,0},{2,3},{3,2},{4,5},{5,4},{6,7},{7,6},{8,9},{9,8},{10,11... | collective-permute-start | bytes 5308424 | tf_op jit(solution)/shard_map/ppermute | solution.py:53
  16.7 6.4 %copy-start.7 = (pred[4,4]{1,0:T(4,128)(4,1)}, pred[4,4]{1,0:T(4,128)(4,1)S(1)}, u32[]{:S(2)}) copy-start(pred[4,4]{1,0:T(4,128)(4,1)S(1)} %iota_compare_fusion.1) | copy-start | bytes 52
  31.2 11.0 %copy-start.4 = (bf16[1536,128]{1,0:T(8,128)(2,1)S(1)}, bf16[1536,128]{1,0:T(8,128)(2,1)}, u32[]{:S(2)}) copy-start(bf16[1536,128]{1,0:T(8,128)(2,1)} %param.20) | copy-start | bytes 1179652
  35.5 13.4 %all-to-all-start.1 = ((bf16[32,8,528]{2,1,0:T(8,128)(2,1)}), bf16[32,8,528]{2,1,0:T(8,128)(2,1)S(1)}, u32[]{:S(2)}, u32[]{:S(2)}) async-start(bf16[32,8,528]{2,1,0:T(8,128)(2,1)} %pad_maximum_fusion), calls=%async_computation.1 | async-start | bytes 655360 | tf_op jit(solution)/shard_map/all_to_all | solution.py:148
  49.9 31.1 %copy-start.6 = (f32[1536]{0:T(1024)S(1)}, f32[1536]{0:T(1024)}, u32[]{:S(2)}) copy-start(f32[1536]{0:T(1024)} %param.22) | copy-start | bytes 18436
  49.9 13.8 %collective-permute-start = (bf16[32,128]{1,0:T(8,128)(2,1)S(1)}, bf16[32,128]{1,0:T(8,128)(2,1)S(1)}, u32[]{:S(2)}, u32[]{:S(2)}) collective-permute-start(bf16[32,128]{1,0:T(8,128)(2,1)S(1)} %bitcast.75), channel_id=1, source_target_pairs={{0,1},{1,0},{2,3},{3,2},{4,5},{5,4},{6,7},{7,6},{8,9},{9,8},{10,11... | collective-permute-start | bytes 24584 | tf_op jit(solution)/shard_map/ppermute | solution.py:193
  63.8 17.9 %copy-start.1 = (bf16[1536,576]{0,1:T(8,128)(2,1)S(1)}, bf16[1536,576]{0,1:T(8,128)(2,1)}, u32[]{:S(2)}) copy-start(bf16[1536,576]{0,1:T(8,128)(2,1)} %param.24) | copy-start | bytes 5308420
  64.0 7.9 %collective-permute-start.2 = (bf16[32,1536]{1,0:T(8,128)(2,1)S(1)}, bf16[32,1536]{1,0:T(8,128)(2,1)S(1)}, u32[]{:S(2)}, u32[]{:S(2)}) collective-permute-start(bf16[32,1536]{1,0:T(8,128)(2,1)S(1)} %convolution_convert_fusion), channel_id=1, source_target_pairs={{0,2},{1,3},{2,0},{3,1},{4,6},{5,7},{6,4},{7,5},{8,10},{9,11},{10,... | collective-permute-start | bytes 294920 | tf_op jit(solution)/shard_map/ppermute | solution.py:20
  72.0 8.9 %collective-permute-start.3 = (bf16[32,1536]{1,0:T(8,128)(2,1)S(1)}, bf16[32,1536]{1,0:T(8,128)(2,1)S(1)}, u32[]{:S(2)}, u32[]{:S(2)}) collective-permute-start(bf16[32,1536]{1,0:T(8,128)(2,1)S(1)} %add.218), channel_id=1, source_target_pairs={{0,7},{1,6},{2,5},{3,4},{4,3},{5,2},{6,1},{7,0},{8,15},{9,14},{10,... | collective-permute-start | bytes 294920 | tf_op jit(solution)/shard_map/ppermute | solution.py:23
  81.0 1.5 %copy-start.2 = (bf16[576,1536]{1,0:T(8,128)(2,1)S(1)}, bf16[576,1536]{1,0:T(8,128)(2,1)}, u32[]{:S(2)}) copy-start(bf16[576,1536]{1,0:T(8,128)(2,1)} %param.25) | copy-start | bytes 5308420
  82.3 4.1 %collective-permute-start.4 = (bf16[32,576]{1,0:T(8,128)(2,1)S(1)}, bf16[32,576]{1,0:T(8,128)(2,1)S(1)}, u32[]{:S(2)}, u32[]{:S(2)}) collective-permute-start(bf16[32,576]{1,0:T(8,128)(2,1)S(1)} %fusion.13), channel_id=1, source_target_pairs={{0,1},{1,0},{2,3},{3,2},{4,5},{5,4},{6,7},{7,6},{8,9},{9,8},{10,11... | collective-permute-start | bytes 110600 | tf_op jit(solution)/shard_map/ppermute | solution.py:211
  88.3 6.3 %collective-permute-start.6 = (bf16[32,1536]{1,0:T(8,128)(2,1)S(1)}, bf16[32,1536]{1,0:T(8,128)(2,1)S(1)}, u32[]{:S(2)}, u32[]{:S(2)}) collective-permute-start(bf16[32,1536]{1,0:T(8,128)(2,1)S(1)} %fusion.6), channel_id=1, source_target_pairs={{0,2},{1,3},{2,0},{3,1},{4,6},{5,7},{6,4},{7,5},{8,10},{9,11},{10,... | collective-permute-start | bytes 294920 | tf_op jit(solution)/shard_map/ppermute | solution.py:20
  94.6 6.7 %collective-permute-start.7 = (bf16[32,1536]{1,0:T(8,128)(2,1)S(1)}, bf16[32,1536]{1,0:T(8,128)(2,1)S(1)}, u32[]{:S(2)}, u32[]{:S(2)}) collective-permute-start(bf16[32,1536]{1,0:T(8,128)(2,1)S(1)} %add.226), channel_id=1, source_target_pairs={{0,7},{1,6},{2,5},{3,4},{4,3},{5,2},{6,1},{7,0},{8,15},{9,14},{10,... | collective-permute-start | bytes 294920 | tf_op jit(solution)/shard_map/ppermute | solution.py:23

commit v16 on v11

--- a/solution.py
+++ b/solution.py
@@ -17,7 +17,7 @@
 def tree_sum(values, axis, size, first_step=1):
     step = first_step
     while step < size // 2:
-        values = values + lax.ppermute(values, axis, [(i, i ^ step) for i in range(size)])
+        values = values + lax.ppermute(values, axis, [(i, i ^ (2 * step - 1)) for i in range(size)])
         step *= 2
     if size > 1:
         values = values + lax.ppermute(values, axis, [(i, size - 1 - i) for i in range(size)])

time: 93.9 us -> 93.8 us (level)
  waiting for transfers between devices: 36.2 us -> 31.5 us
  starting transfers between devices: 27.9 us -> 32.4 us
    ppermute x3, waiting for transfers between devices: 15.9 us -> 11.9 us  [tree_sum(): lax.ppermute(values, axis, [(i, i ^ 2 * step - 1) for i in range(size)])]
    ppermute x3, starting transfers between devices: 3.8 us -> 7.64 us  [tree_sum(): lax.ppermute(values, axis, [(i, i ^ 2 * step - 1) for i in range(size)])]
where the time goes in v16:
time: 93.8 us; the launch traced here: 93.1 us
  starting transfers between devices  32.4 us (35%)
  waiting for transfers between devices  31.5 us (34%)
  matrix products  11.1 us (12%)
  other arithmetic  9.93 us (11%)
  local copies, waits for them, and re-layouts  7.74 us (8%)
    ppermute x3, waiting for transfers between devices, tree_sum(): lax.ppermute(values, axis, [(i, i ^ 2 * step - 1) for i in range(size)])  11.9 us
    ppermute x2, starting transfers between devices, tree_sum(): lax.ppermute(values, axis, [(i, size - 1 - i) for i in range(size)])  8.19 us
    ppermute x3, starting transfers between devices, tree_sum(): lax.ppermute(values, axis, [(i, i ^ 2 * step - 1) for i in range(size)])  7.64 us
    all_to_all x1, starting transfers between devices, body(): lax.all_to_all(jnp.broadcast_to(packed[None], (req_size,) + packed.shape)...  7.62 us
    ppermute x2, waiting for transfers between devices, tree_sum(): lax.ppermute(values, axis, [(i, size - 1 - i) for i in range(size)])  7.39 us
    all_to_all x1, waiting for transfers between devices, body(): lax.all_to_all(send, 'req', 0, 0, tiled=True).reshape(req_size, req_dev, -1)  6.45 us
    all_to_all x1, waiting for transfers between devices, body(): lax.all_to_all(jnp.broadcast_to(packed[None], (req_size,) + packed.shape)...  5.14 us
    all_to_all x1, starting transfers between devices, body(): lax.all_to_all(send, 'req', 0, 0, tiled=True).reshape(req_size, req_dev, -1)  4.98 us
  transfers between devices with their start and end apart: 9, of which 8 were waited for; matrix products, arithmetic and copies ran while one was open for 19% of the time, Pallas kernels for 0%

profile of v16, /device:TPU:2, one launch (start us, length us, event | category | flops | bytes accessed | tf_op | source)
XLA Modules:
  0.0 93.1 jit_solution(8585215443234414084)
XLA Ops:
  0.0 1.2 %multiply_reduce_fusion = f32[8,4]{1,0:T(8,128)S(1)} fusion(bf16[8,4,1536]{2,1,0:T(4,128)(2,1)} %param.13), kind=kLoop, calls=%fused_computation.44 | loop fusion | flops 147424 | bytes 98432 | tf_op jit(solution)/shard_map/reduce_sum | solution.py:14
  1.2 0.9 reshape.470
  3.0 0.7 fusion.54
  3.8 0.8 multiply_convert_fusion
  4.5 1.2 %fusion.16 = bf16[32,128]{1,0:T(8,128)(2,1)S(1)} fusion(bf16[32,1536]{1,0:T(8,128)(2,1)S(1)} %multiply_convert_fusion, bf16[1536,128]{1,0:T(8,128)(2,1)} %param.18), kind=kOutput, calls=%fused_computation.19 | convolution fusion | flops 12591104 | bytes 499712 | tf_op jit(solution)/shard_map/dot_general | solution.py:55
  5.9 0.7 broadcast_in_dim.131
  6.6 7.6 %all-to-all-start = ((bf16[32,8,532]{2,1,0:T(8,128)(2,1)}), bf16[32,8,532]{2,1,0:T(8,128)(2,1)S(1)}, u32[]{:S(2)}, u32[]{:S(2)}) async-start(bf16[32,8,532]{2,1,0:T(8,128)(2,1)} %broadcast_in_dim.131), calls=%async_computation | async-start | bytes 655360 | tf_op jit(solution)/shard_map/all_to_all | solution.py:72
  14.2 2.0 %collective-permute-start.1 = (bf16[128,1536]{1,0:T(8,128)(2,1)S(1)}, bf16[128,1536]{1,0:T(8,128)(2,1)}, u32[]{:S(2)}, u32[]{:S(2)}) collective-permute-start(bf16[128,1536]{1,0:T(8,128)(2,1)S(1)} %copy-done.4), channel_id=1, source_target_pairs={{0,1},{1,0},{2,3},{3,2},{4,5},{5,4},{6,7},{7,6},{8,9},{9,8},{10,11... | collective-permute-start | bytes 1179656 | tf_op jit(solution)/shard_map/ppermute | solution.py:52
  17.4 5.1 %all-to-all-done = bf16[32,8,532]{2,1,0:T(8,128)(2,1)S(1)} async-done(((bf16[32,8,532]{2,1,0:T(8,128)(2,1)}), bf16[32,8,532]{2,1,0:T(8,128)(2,1)S(1)}, u32[]{:S(2)}, u32[]{:S(2)}) %all-to-all-start) | async-done | bytes 272416 | tf_op jit(solution)/shard_map/all_to_all | solution.py:72
  24.9 3.1 %fusion.72 = (f32[72,4]{1,0:T(8,128)S(1)}, f32[72,4,128]{2,1,0:T(4,128)S(1)}) fusion(bf16[72,4,128]{2,1,0:T(4,128)(2,1)S(1)} %gather_fusion, bf16[72,2,128,128]{3,2,1,0:T(8,128)(2,1)} %param.16, s32[72,4]{1,0:T(8,128)S(1)} %add_add_fusion, s32[72,128]{1,0:T(8,128)S(1)} %iota_add_fusion, pred[72,128]{1,0:T(8,128)(4,1)S(1)} %broadcast_compare_fusion.1), kind=kOutput, calls=%fused_computation.140 | convolution fusion | flops 9584352 | bytes 2628864 | tf_op jit(solution)/shard_map/pqd,pkd->pqk/dot_general | solution.py:102
  28.8 2.5 %fusion.9 = f32[72,4,128]{2,1,0:T(4,128)S(1)} fusion(bf16[72,2,128,128]{3,2,1,0:T(8,128)(2,1)} %param.16, f32[72,4]{1,0:T(8,128)S(1)} %get-tuple-element.14, f32[72,4,128]{2,1,0:T(4,128)S(1)} %get-tuple-element.32, f32[72,4]{1,0:T(8,128)S(1)} %get-tuple-element.31, s32[72,4]{1,0:T(8,128)S(1)} %add_add_fusion, s32[72,128]{1,0:T(8,128)S(1)} %iota_add_fusion, ...), kind=kOutput, calls=%fused_computation.11 | convolution fusion | flops 9658368 | bytes 2703744 | tf_op jit(solution)/shard_map/pqk,pkd->pqd/dot_general | solution.py:109
  31.6 0.8 copy.112
  32.4 0.8 copy.111
  33.8 1.7 %pad_maximum_fusion = bf16[32,8,528]{2,1,0:T(8,128)(2,1)} fusion(bf16[32,8,4]{2,1,0:T(8,128)(2,1)} %copy.112, bf16[32,8,4]{2,1,0:T(8,128)(2,1)} %copy.111, bf16[32,8,4]{2,1,0:T(8,128)(2,1)S(1)} %copy.110, bf16[32,8,516]{2,1,0:T(8,128)(2,1)S(1)} %bitcast.65), kind=kLoop, calls=%fused_computation.33 | loop fusion | flops 1081344 | bytes 540672 | tf_op jit(solution)/shard_map/concatenate | solution.py:144
  35.5 5.0 %all-to-all-start.1 = ((bf16[32,8,528]{2,1,0:T(8,128)(2,1)}), bf16[32,8,528]{2,1,0:T(8,128)(2,1)S(1)}, u32[]{:S(2)}, u32[]{:S(2)}) async-start(bf16[32,8,528]{2,1,0:T(8,128)(2,1)} %pad_maximum_fusion), calls=%async_computation.1 | async-start | bytes 655360 | tf_op jit(solution)/shard_map/all_to_all | solution.py:147
  40.5 0.8 fusion.51
  41.3 0.8 copy.114
  42.4 6.5 %all-to-all-done.1 = bf16[32,8,528]{2,1,0:T(8,128)(2,1)S(1)} async-done(((bf16[32,8,528]{2,1,0:T(8,128)(2,1)}), bf16[32,8,528]{2,1,0:T(8,128)(2,1)S(1)}, u32[]{:S(2)}, u32[]{:S(2)}) %all-to-all-start.1) | async-done | bytes 270368 | tf_op jit(solution)/shard_map/all_to_all | solution.py:147
  49.9 2.0 %collective-permute-start = (bf16[32,128]{1,0:T(8,128)(2,1)S(1)}, bf16[32,128]{1,0:T(8,128)(2,1)S(1)}, u32[]{:S(2)}, u32[]{:S(2)}) collective-permute-start(bf16[32,128]{1,0:T(8,128)(2,1)S(1)} %bitcast.72), channel_id=1, source_target_pairs={{0,1},{1,0},{2,3},{3,2},{4,5},{5,4},{6,7},{7,6},{8,9},{9,8},{10,11... | collective-permute-start | bytes 24584 | tf_op jit(solution)/shard_map/ppermute | solution.py:192
  51.9 1.1 %broadcast_select_fusion.1 = (bf16[128,1536]{1,0:T(8,128)(2,1)S(1)}, bf16[128,1536]{1,0:T(8,128)(2,1)S(1)}) fusion(bf16[128,1536]{1,0:T(8,128)(2,1)S(1)} %copy-done.4, bf16[128,1536]{1,0:T(8,128)(2,1)} %collective-permute-done.1, pred[]{:T(512)S(6)} %eq.60), kind=kLoop, calls=%fused_computation.32 | loop fusion | flops 393216 | bytes 1572865 | tf_op jit(solution)/shard_map/jit(_where)/select_n | solution.py:198
  53.0 0.7 collective-permute-done
  53.9 4.7 %collective-permute-start.2 = (bf16[32,1536]{1,0:T(8,128)(2,1)S(1)}, bf16[32,1536]{1,0:T(8,128)(2,1)S(1)}, u32[]{:S(2)}, u32[]{:S(2)}) collective-permute-start(bf16[32,1536]{1,0:T(8,128)(2,1)S(1)} %convolution_convert_fusion.1), channel_id=1, source_target_pairs={{0,3},{1,2},{2,1},{3,0},{4,7},{5,6},{6,5},{7,4},{8,11},{9,10},{10,... | collective-permute-start | bytes 294920 | tf_op jit(solution)/shard_map/ppermute | solution.py:20
  58.6 2.6 %collective-permute-done.2 = bf16[32,1536]{1,0:T(8,128)(2,1)S(1)} collective-permute-done((bf16[32,1536]{1,0:T(8,128)(2,1)S(1)}, bf16[32,1536]{1,0:T(8,128)(2,1)S(1)}, u32[]{:S(2)}, u32[]{:S(2)}) %collective-permute-start.2) | collective-permute-done | bytes 98336 | tf_op jit(solution)/shard_map/ppermute | solution.py:20
  61.2 5.2 %collective-permute-start.3 = (bf16[32,1536]{1,0:T(8,128)(2,1)S(1)}, bf16[32,1536]{1,0:T(8,128)(2,1)S(1)}, u32[]{:S(2)}, u32[]{:S(2)}) collective-permute-start(bf16[32,1536]{1,0:T(8,128)(2,1)S(1)} %add.218), channel_id=1, source_target_pairs={{0,7},{1,6},{2,5},{3,4},{4,3},{5,2},{6,1},{7,0},{8,15},{9,14},{10,... | collective-permute-start | bytes 294920 | tf_op jit(solution)/shard_map/ppermute | solution.py:23
  66.5 3.6 %collective-permute-done.3 = bf16[32,1536]{1,0:T(8,128)(2,1)S(1)} collective-permute-done((bf16[32,1536]{1,0:T(8,128)(2,1)S(1)}, bf16[32,1536]{1,0:T(8,128)(2,1)S(1)}, u32[]{:S(2)}, u32[]{:S(2)}) %collective-permute-start.3) | collective-permute-done | bytes 98336 | tf_op jit(solution)/shard_map/ppermute | solution.py:23
  70.9 2.5 %convolution_convert_fusion = bf16[32,1536]{1,0:T(8,128)(2,1)S(1)} fusion(bf16[576,1536]{1,0:T(8,128)(2,1)S(1)} %copy-done, bf16[1536,576]{0,1:T(8,128)(2,1)} %param.24, f32[32,576]{1,0:T(8,128)S(1)} %fusion.45, bf16[32,1536]{1,0:T(8,128)(2,1)S(1)} %get-tuple-element.8, f32[1536]{0:T(1024)S(1)} %copy-done.5, f32[32]{0:T(128)S(1)} %add_rsqrt_fusion.1), kind=kOutput, calls=%fused_computation.7 | convolution fusion | flops 113676288 | bytes 3815552 | tf_op jit(solution)/shard_map/dot_general | solution.py:210
  73.4 1.0 %collective-permute-start.4 = (bf16[32,1536]{1,0:T(8,128)(2,1)S(1)}, bf16[32,1536]{1,0:T(8,128)(2,1)S(1)}, u32[]{:S(2)}, u32[]{:S(2)}) collective-permute-start(bf16[32,1536]{1,0:T(8,128)(2,1)S(1)} %convolution_convert_fusion), channel_id=1, source_target_pairs={{0,1},{1,0},{2,3},{3,2},{4,5},{5,4},{6,7},{7,6},{8,9},{9,8},{10,11... | collective-permute-start | bytes 294920 | tf_op jit(solution)/shard_map/ppermute | solution.py:20
  74.4 3.7 %collective-permute-done.4 = bf16[32,1536]{1,0:T(8,128)(2,1)S(1)} collective-permute-done((bf16[32,1536]{1,0:T(8,128)(2,1)S(1)}, bf16[32,1536]{1,0:T(8,128)(2,1)S(1)}, u32[]{:S(2)}, u32[]{:S(2)}) %collective-permute-start.4) | collective-permute-done | bytes 98336 | tf_op jit(solution)/shard_map/ppermute | solution.py:20
  78.1 2.0 %collective-permute-start.5 = (bf16[32,1536]{1,0:T(8,128)(2,1)S(1)}, bf16[32,1536]{1,0:T(8,128)(2,1)S(1)}, u32[]{:S(2)}, u32[]{:S(2)}) collective-permute-start(bf16[32,1536]{1,0:T(8,128)(2,1)S(1)} %add.225), channel_id=1, source_target_pairs={{0,3},{1,2},{2,1},{3,0},{4,7},{5,6},{6,5},{7,4},{8,11},{9,10},{10,... | collective-permute-start | bytes 294920 | tf_op jit(solution)/shard_map/ppermute | solution.py:20
  80.1 5.6 %collective-permute-done.5 = bf16[32,1536]{1,0:T(8,128)(2,1)S(1)} collective-permute-done((bf16[32,1536]{1,0:T(8,128)(2,1)S(1)}, bf16[32,1536]{1,0:T(8,128)(2,1)S(1)}, u32[]{:S(2)}, u32[]{:S(2)}) %collective-permute-start.5) | collective-permute-done | bytes 98336 | tf_op jit(solution)/shard_map/ppermute | solution.py:20
  85.7 3.0 %collective-permute-start.6 = (bf16[32,1536]{1,0:T(8,128)(2,1)S(1)}, bf16[32,1536]{1,0:T(8,128)(2,1)S(1)}, u32[]{:S(2)}, u32[]{:S(2)}) collective-permute-start(bf16[32,1536]{1,0:T(8,128)(2,1)S(1)} %add.226), channel_id=1, source_target_pairs={{0,7},{1,6},{2,5},{3,4},{4,3},{5,2},{6,1},{7,0},{8,15},{9,14},{10,... | collective-permute-start | bytes 294920 | tf_op jit(solution)/shard_map/ppermute | solution.py:23
  88.7 3.7 %collective-permute-done.6 = bf16[32,1536]{1,0:T(8,128)(2,1)S(1)} collective-permute-done((bf16[32,1536]{1,0:T(8,128)(2,1)S(1)}, bf16[32,1536]{1,0:T(8,128)(2,1)S(1)}, u32[]{:S(2)}, u32[]{:S(2)}) %collective-permute-start.6) | collective-permute-done | bytes 98336 | tf_op jit(solution)/shard_map/ppermute | solution.py:23
  (81 shorter events, 9.4 us)
Async XLA Ops:
  0.0 70.9 %copy-start = (bf16[576,1536]{1,0:T(8,128)(2,1)S(1)}, bf16[576,1536]{1,0:T(8,128)(2,1)}, u32[]{:S(2)}) copy-start(bf16[576,1536]{1,0:T(8,128)(2,1)} %param.25) | copy-start | bytes 5308420
  0.0 14.2 %copy-start.4 = (bf16[128,1536]{1,0:T(8,128)(2,1)S(1)}, bf16[128,1536]{1,0:T(8,128)(2,1)}, u32[]{:S(2)}) copy-start(bf16[128,1536]{1,0:T(8,128)(2,1)} %param.21) | copy-start | bytes 1179652
  0.0 16.2 %copy-start.2 = (bf16[1536,128]{1,0:T(8,128)(2,1)S(1)}, bf16[1536,128]{1,0:T(8,128)(2,1)}, u32[]{:S(2)}) copy-start(bf16[1536,128]{1,0:T(8,128)(2,1)} %param.19) | copy-start | bytes 1179652
  6.6 15.9 %all-to-all-start = ((bf16[32,8,532]{2,1,0:T(8,128)(2,1)}), bf16[32,8,532]{2,1,0:T(8,128)(2,1)S(1)}, u32[]{:S(2)}, u32[]{:S(2)}) async-start(bf16[32,8,532]{2,1,0:T(8,128)(2,1)} %broadcast_in_dim.131), calls=%async_computation | async-start | bytes 655360 | tf_op jit(solution)/shard_map/all_to_all | solution.py:72
  14.2 37.7 %collective-permute-start.1 = (bf16[128,1536]{1,0:T(8,128)(2,1)S(1)}, bf16[128,1536]{1,0:T(8,128)(2,1)}, u32[]{:S(2)}, u32[]{:S(2)}) collective-permute-start(bf16[128,1536]{1,0:T(8,128)(2,1)S(1)} %copy-done.4), channel_id=1, source_target_pairs={{0,1},{1,0},{2,3},{3,2},{4,5},{5,4},{6,7},{7,6},{8,9},{9,8},{10,11... | collective-permute-start | bytes 1179656 | tf_op jit(solution)/shard_map/ppermute | solution.py:52
  16.6 6.5 %copy-start.6 = (pred[4,4]{1,0:T(4,128)(4,1)}, pred[4,4]{1,0:T(4,128)(4,1)S(1)}, u32[]{:S(2)}) copy-start(pred[4,4]{1,0:T(4,128)(4,1)S(1)} %iota_compare_fusion.1) | copy-start | bytes 52
  31.2 11.0 %copy-start.3 = (bf16[1536,128]{1,0:T(8,128)(2,1)S(1)}, bf16[1536,128]{1,0:T(8,128)(2,1)}, u32[]{:S(2)}) copy-start(bf16[1536,128]{1,0:T(8,128)(2,1)} %param.20) | copy-start | bytes 1179652
  35.5 13.4 %all-to-all-start.1 = ((bf16[32,8,528]{2,1,0:T(8,128)(2,1)}), bf16[32,8,528]{2,1,0:T(8,128)(2,1)S(1)}, u32[]{:S(2)}, u32[]{:S(2)}) async-start(bf16[32,8,528]{2,1,0:T(8,128)(2,1)} %pad_maximum_fusion), calls=%async_computation.1 | async-start | bytes 655360 | tf_op jit(solution)/shard_map/all_to_all | solution.py:147
  49.9 20.4 %copy-start.1 = (bf16[1536,576]{0,1:T(8,128)(2,1)S(1)}, bf16[1536,576]{0,1:T(8,128)(2,1)}, u32[]{:S(2)}) copy-start(bf16[1536,576]{0,1:T(8,128)(2,1)} %param.23) | copy-start | bytes 5308420
  49.9 20.4 %copy-start.5 = (f32[1536]{0:T(1024)S(1)}, f32[1536]{0:T(1024)}, u32[]{:S(2)}) copy-start(f32[1536]{0:T(1024)} %param.22) | copy-start | bytes 18436
  49.9 3.7 %collective-permute-start = (bf16[32,128]{1,0:T(8,128)(2,1)S(1)}, bf16[32,128]{1,0:T(8,128)(2,1)S(1)}, u32[]{:S(2)}, u32[]{:S(2)}) collective-permute-start(bf16[32,128]{1,0:T(8,128)(2,1)S(1)} %bitcast.72), channel_id=1, source_target_pairs={{0,1},{1,0},{2,3},{3,2},{4,5},{5,4},{6,7},{7,6},{8,9},{9,8},{10,11... | collective-permute-start | bytes 24584 | tf_op jit(solution)/shard_map/ppermute | solution.py:192
  53.9 7.3 %collective-permute-start.2 = (bf16[32,1536]{1,0:T(8,128)(2,1)S(1)}, bf16[32,1536]{1,0:T(8,128)(2,1)S(1)}, u32[]{:S(2)}, u32[]{:S(2)}) collective-permute-start(bf16[32,1536]{1,0:T(8,128)(2,1)S(1)} %convolution_convert_fusion.1), channel_id=1, source_target_pairs={{0,3},{1,2},{2,1},{3,0},{4,7},{5,6},{6,5},{7,4},{8,11},{9,10},{10,... | collective-permute-start | bytes 294920 | tf_op jit(solution)/shard_map/ppermute | solution.py:20
  61.2 8.9 %collective-permute-start.3 = (bf16[32,1536]{1,0:T(8,128)(2,1)S(1)}, bf16[32,1536]{1,0:T(8,128)(2,1)S(1)}, u32[]{:S(2)}, u32[]{:S(2)}) collective-permute-start(bf16[32,1536]{1,0:T(8,128)(2,1)S(1)} %add.218), channel_id=1, source_target_pairs={{0,7},{1,6},{2,5},{3,4},{4,3},{5,2},{6,1},{7,0},{8,15},{9,14},{10,... | collective-permute-start | bytes 294920 | tf_op jit(solution)/shard_map/ppermute | solution.py:23
  73.4 4.7 %collective-permute-start.4 = (bf16[32,1536]{1,0:T(8,128)(2,1)S(1)}, bf16[32,1536]{1,0:T(8,128)(2,1)S(1)}, u32[]{:S(2)}, u32[]{:S(2)}) collective-permute-start(bf16[32,1536]{1,0:T(8,128)(2,1)S(1)} %convolution_convert_fusion), channel_id=1, source_target_pairs={{0,1},{1,0},{2,3},{3,2},{4,5},{5,4},{6,7},{7,6},{8,9},{9,8},{10,11... | collective-permute-start | bytes 294920 | tf_op jit(solution)/shard_map/ppermute | solution.py:20
  78.1 7.6 %collective-permute-start.5 = (bf16[32,1536]{1,0:T(8,128)(2,1)S(1)}, bf16[32,1536]{1,0:T(8,128)(2,1)S(1)}, u32[]{:S(2)}, u32[]{:S(2)}) collective-permute-start(bf16[32,1536]{1,0:T(8,128)(2,1)S(1)} %add.225), channel_id=1, source_target_pairs={{0,3},{1,2},{2,1},{3,0},{4,7},{5,6},{6,5},{7,4},{8,11},{9,10},{10,... | collective-permute-start | bytes 294920 | tf_op jit(solution)/shard_map/ppermute | solution.py:20
  85.7 6.7 %collective-permute-start.6 = (bf16[32,1536]{1,0:T(8,128)(2,1)S(1)}, bf16[32,1536]{1,0:T(8,128)(2,1)S(1)}, u32[]{:S(2)}, u32[]{:S(2)}) collective-permute-start(bf16[32,1536]{1,0:T(8,128)(2,1)S(1)} %add.226), channel_id=1, source_target_pairs={{0,7},{1,6},{2,5},{3,4},{4,3},{5,2},{6,1},{7,0},{8,15},{9,14},{10,... | collective-permute-start | bytes 294920 | tf_op jit(solution)/shard_map/ppermute | solution.py:23

commit v17 on v16

--- a/solution.py
+++ b/solution.py
@@ -133,7 +133,7 @@
         sent = jnp.dot(
             member.astype(jnp.float32),
             scaled,
-            precision=lax.Precision.HIGHEST,
+            precision=lax.Precision.HIGH,
             preferred_element_type=jnp.float32,
         )
         flat_max = local_max.reshape(requests, nsh)

time: 93.8 us -> 93.7 us (level)
  no operation moved by 1% of the time
where the time goes in v17:
time: 93.7 us; the launch traced here: 93.1 us
  starting transfers between devices  32.4 us (35%)
  waiting for transfers between devices  31.5 us (34%)
  matrix products  11.1 us (12%)
  other arithmetic  9.93 us (11%)
  local copies, waits for them, and re-layouts  7.74 us (8%)
    ppermute x3, waiting for transfers between devices, tree_sum(): lax.ppermute(values, axis, [(i, i ^ 2 * step - 1) for i in range(size)])  11.9 us
    ppermute x2, starting transfers between devices, tree_sum(): lax.ppermute(values, axis, [(i, size - 1 - i) for i in range(size)])  8.19 us
    ppermute x3, starting transfers between devices, tree_sum(): lax.ppermute(values, axis, [(i, i ^ 2 * step - 1) for i in range(size)])  7.64 us
    all_to_all x1, starting transfers between devices, body(): lax.all_to_all(jnp.broadcast_to(packed[None], (req_size,) + packed.shape)...  7.62 us
    ppermute x2, waiting for transfers between devices, tree_sum(): lax.ppermute(values, axis, [(i, size - 1 - i) for i in range(size)])  7.39 us
    all_to_all x1, waiting for transfers between devices, body(): lax.all_to_all(send, 'req', 0, 0, tiled=True).reshape(req_size, req_dev, -1)  6.45 us
    all_to_all x1, waiting for transfers between devices, body(): lax.all_to_all(jnp.broadcast_to(packed[None], (req_size,) + packed.shape)...  5.14 us
    all_to_all x1, starting transfers between devices, body(): lax.all_to_all(send, 'req', 0, 0, tiled=True).reshape(req_size, req_dev, -1)  4.98 us
  transfers between devices with their start and end apart: 9, of which 8 were waited for; matrix products, arithmetic and copies ran while one was open for 19% of the time, Pallas kernels for 0%

profile of v17, /device:TPU:2, one launch (start us, length us, event | category | flops | bytes accessed | tf_op | source)
XLA Modules:
  0.0 93.1 jit_solution(10237771021395991052)
XLA Ops:
  0.0 1.2 %multiply_reduce_fusion = f32[8,4]{1,0:T(8,128)S(1)} fusion(bf16[8,4,1536]{2,1,0:T(4,128)(2,1)} %param.13), kind=kLoop, calls=%fused_computation.44 | loop fusion | flops 147424 | bytes 98432 | tf_op jit(solution)/shard_map/reduce_sum | solution.py:14
  1.2 0.9 reshape.470
  3.0 0.7 fusion.54
  3.8 0.8 multiply_convert_fusion
  4.5 1.2 %fusion.16 = bf16[32,128]{1,0:T(8,128)(2,1)S(1)} fusion(bf16[32,1536]{1,0:T(8,128)(2,1)S(1)} %multiply_convert_fusion, bf16[1536,128]{1,0:T(8,128)(2,1)} %param.18), kind=kOutput, calls=%fused_computation.19 | convolution fusion | flops 12591104 | bytes 499712 | tf_op jit(solution)/shard_map/dot_general | solution.py:55
  5.9 0.7 broadcast_in_dim.131
  6.6 7.6 %all-to-all-start = ((bf16[32,8,532]{2,1,0:T(8,128)(2,1)}), bf16[32,8,532]{2,1,0:T(8,128)(2,1)S(1)}, u32[]{:S(2)}, u32[]{:S(2)}) async-start(bf16[32,8,532]{2,1,0:T(8,128)(2,1)} %broadcast_in_dim.131), calls=%async_computation | async-start | bytes 655360 | tf_op jit(solution)/shard_map/all_to_all | solution.py:72
  14.2 2.0 %collective-permute-start.1 = (bf16[128,1536]{1,0:T(8,128)(2,1)S(1)}, bf16[128,1536]{1,0:T(8,128)(2,1)}, u32[]{:S(2)}, u32[]{:S(2)}) collective-permute-start(bf16[128,1536]{1,0:T(8,128)(2,1)S(1)} %copy-done.4), channel_id=1, source_target_pairs={{0,1},{1,0},{2,3},{3,2},{4,5},{5,4},{6,7},{7,6},{8,9},{9,8},{10,11... | collective-permute-start | bytes 1179656 | tf_op jit(solution)/shard_map/ppermute | solution.py:52
  16.7 0.7 select_reduce_fusion.2
  17.4 5.1 %all-to-all-done = bf16[32,8,532]{2,1,0:T(8,128)(2,1)S(1)} async-done(((bf16[32,8,532]{2,1,0:T(8,128)(2,1)}), bf16[32,8,532]{2,1,0:T(8,128)(2,1)S(1)}, u32[]{:S(2)}, u32[]{:S(2)}) %all-to-all-start) | async-done | bytes 272416 | tf_op jit(solution)/shard_map/all_to_all | solution.py:72
  24.9 3.1 %fusion.72 = (f32[72,4]{1,0:T(8,128)S(1)}, f32[72,4,128]{2,1,0:T(4,128)S(1)}) fusion(bf16[72,4,128]{2,1,0:T(4,128)(2,1)S(1)} %gather_fusion, bf16[72,2,128,128]{3,2,1,0:T(8,128)(2,1)} %param.16, s32[72,4]{1,0:T(8,128)S(1)} %add_add_fusion, s32[72,128]{1,0:T(8,128)S(1)} %iota_add_fusion, pred[72,128]{1,0:T(8,128)(4,1)S(1)} %broadcast_compare_fusion.1), kind=kOutput, calls=%fused_computation.140 | convolution fusion | flops 9584352 | bytes 2628864 | tf_op jit(solution)/shard_map/pqd,pkd->pqk/dot_general | solution.py:102
  28.8 2.5 %fusion.9 = f32[72,4,128]{2,1,0:T(4,128)S(1)} fusion(bf16[72,2,128,128]{3,2,1,0:T(8,128)(2,1)} %param.16, f32[72,4]{1,0:T(8,128)S(1)} %get-tuple-element.14, f32[72,4,128]{2,1,0:T(4,128)S(1)} %get-tuple-element.32, f32[72,4]{1,0:T(8,128)S(1)} %get-tuple-element.31, s32[72,4]{1,0:T(8,128)S(1)} %add_add_fusion, s32[72,128]{1,0:T(8,128)S(1)} %iota_add_fusion, ...), kind=kOutput, calls=%fused_computation.11 | convolution fusion | flops 9658368 | bytes 2703744 | tf_op jit(solution)/shard_map/pqk,pkd->pqd/dot_general | solution.py:109
  31.6 0.8 copy.112
  32.4 0.8 copy.111
  33.7 1.7 %pad_maximum_fusion = bf16[32,8,528]{2,1,0:T(8,128)(2,1)} fusion(bf16[32,8,4]{2,1,0:T(8,128)(2,1)} %copy.112, bf16[32,8,4]{2,1,0:T(8,128)(2,1)} %copy.111, bf16[32,8,4]{2,1,0:T(8,128)(2,1)S(1)} %copy.110, bf16[32,8,516]{2,1,0:T(8,128)(2,1)S(1)} %bitcast.65), kind=kLoop, calls=%fused_computation.33 | loop fusion | flops 1081344 | bytes 540672 | tf_op jit(solution)/shard_map/concatenate | solution.py:144
  35.4 5.0 %all-to-all-start.1 = ((bf16[32,8,528]{2,1,0:T(8,128)(2,1)}), bf16[32,8,528]{2,1,0:T(8,128)(2,1)S(1)}, u32[]{:S(2)}, u32[]{:S(2)}) async-start(bf16[32,8,528]{2,1,0:T(8,128)(2,1)} %pad_maximum_fusion), calls=%async_computation.1 | async-start | bytes 655360 | tf_op jit(solution)/shard_map/all_to_all | solution.py:147
  40.4 0.8 fusion.51
  41.2 0.8 copy.114
  42.4 6.5 %all-to-all-done.1 = bf16[32,8,528]{2,1,0:T(8,128)(2,1)S(1)} async-done(((bf16[32,8,528]{2,1,0:T(8,128)(2,1)}), bf16[32,8,528]{2,1,0:T(8,128)(2,1)S(1)}, u32[]{:S(2)}, u32[]{:S(2)}) %all-to-all-start.1) | async-done | bytes 270368 | tf_op jit(solution)/shard_map/all_to_all | solution.py:147
  49.9 2.0 %collective-permute-start = (bf16[32,128]{1,0:T(8,128)(2,1)S(1)}, bf16[32,128]{1,0:T(8,128)(2,1)S(1)}, u32[]{:S(2)}, u32[]{:S(2)}) collective-permute-start(bf16[32,128]{1,0:T(8,128)(2,1)S(1)} %bitcast.72), channel_id=1, source_target_pairs={{0,1},{1,0},{2,3},{3,2},{4,5},{5,4},{6,7},{7,6},{8,9},{9,8},{10,11... | collective-permute-start | bytes 24584 | tf_op jit(solution)/shard_map/ppermute | solution.py:192
  51.9 1.1 %broadcast_select_fusion.1 = (bf16[128,1536]{1,0:T(8,128)(2,1)S(1)}, bf16[128,1536]{1,0:T(8,128)(2,1)S(1)}) fusion(bf16[128,1536]{1,0:T(8,128)(2,1)S(1)} %copy-done.4, bf16[128,1536]{1,0:T(8,128)(2,1)} %collective-permute-done.1, pred[]{:T(512)S(6)} %eq.60), kind=kLoop, calls=%fused_computation.32 | loop fusion | flops 393216 | bytes 1572865 | tf_op jit(solution)/shard_map/jit(_where)/select_n | solution.py:198
  53.8 4.7 %collective-permute-start.2 = (bf16[32,1536]{1,0:T(8,128)(2,1)S(1)}, bf16[32,1536]{1,0:T(8,128)(2,1)S(1)}, u32[]{:S(2)}, u32[]{:S(2)}) collective-permute-start(bf16[32,1536]{1,0:T(8,128)(2,1)S(1)} %convolution_convert_fusion.1), channel_id=1, source_target_pairs={{0,3},{1,2},{2,1},{3,0},{4,7},{5,6},{6,5},{7,4},{8,11},{9,10},{10,... | collective-permute-start | bytes 294920 | tf_op jit(solution)/shard_map/ppermute | solution.py:20
  58.5 2.6 %collective-permute-done.2 = bf16[32,1536]{1,0:T(8,128)(2,1)S(1)} collective-permute-done((bf16[32,1536]{1,0:T(8,128)(2,1)S(1)}, bf16[32,1536]{1,0:T(8,128)(2,1)S(1)}, u32[]{:S(2)}, u32[]{:S(2)}) %collective-permute-start.2) | collective-permute-done | bytes 98336 | tf_op jit(solution)/shard_map/ppermute | solution.py:20
  61.2 5.2 %collective-permute-start.3 = (bf16[32,1536]{1,0:T(8,128)(2,1)S(1)}, bf16[32,1536]{1,0:T(8,128)(2,1)S(1)}, u32[]{:S(2)}, u32[]{:S(2)}) collective-permute-start(bf16[32,1536]{1,0:T(8,128)(2,1)S(1)} %add.218), channel_id=1, source_target_pairs={{0,7},{1,6},{2,5},{3,4},{4,3},{5,2},{6,1},{7,0},{8,15},{9,14},{10,... | collective-permute-start | bytes 294920 | tf_op jit(solution)/shard_map/ppermute | solution.py:23
  66.4 3.6 %collective-permute-done.3 = bf16[32,1536]{1,0:T(8,128)(2,1)S(1)} collective-permute-done((bf16[32,1536]{1,0:T(8,128)(2,1)S(1)}, bf16[32,1536]{1,0:T(8,128)(2,1)S(1)}, u32[]{:S(2)}, u32[]{:S(2)}) %collective-permute-start.3) | collective-permute-done | bytes 98336 | tf_op jit(solution)/shard_map/ppermute | solution.py:23
  70.8 2.5 %convolution_convert_fusion = bf16[32,1536]{1,0:T(8,128)(2,1)S(1)} fusion(bf16[576,1536]{1,0:T(8,128)(2,1)S(1)} %copy-done, bf16[1536,576]{0,1:T(8,128)(2,1)} %param.24, f32[32,576]{1,0:T(8,128)S(1)} %fusion.45, bf16[32,1536]{1,0:T(8,128)(2,1)S(1)} %get-tuple-element.8, f32[1536]{0:T(1024)S(1)} %copy-done.5, f32[32]{0:T(128)S(1)} %add_rsqrt_fusion.1), kind=kOutput, calls=%fused_computation.7 | convolution fusion | flops 113676288 | bytes 3815552 | tf_op jit(solution)/shard_map/dot_general | solution.py:210
  73.4 1.0 %collective-permute-start.4 = (bf16[32,1536]{1,0:T(8,128)(2,1)S(1)}, bf16[32,1536]{1,0:T(8,128)(2,1)S(1)}, u32[]{:S(2)}, u32[]{:S(2)}) collective-permute-start(bf16[32,1536]{1,0:T(8,128)(2,1)S(1)} %convolution_convert_fusion), channel_id=1, source_target_pairs={{0,1},{1,0},{2,3},{3,2},{4,5},{5,4},{6,7},{7,6},{8,9},{9,8},{10,11... | collective-permute-start | bytes 294920 | tf_op jit(solution)/shard_map/ppermute | solution.py:20
  74.3 3.7 %collective-permute-done.4 = bf16[32,1536]{1,0:T(8,128)(2,1)S(1)} collective-permute-done((bf16[32,1536]{1,0:T(8,128)(2,1)S(1)}, bf16[32,1536]{1,0:T(8,128)(2,1)S(1)}, u32[]{:S(2)}, u32[]{:S(2)}) %collective-permute-start.4) | collective-permute-done | bytes 98336 | tf_op jit(solution)/shard_map/ppermute | solution.py:20
  78.1 2.0 %collective-permute-start.5 = (bf16[32,1536]{1,0:T(8,128)(2,1)S(1)}, bf16[32,1536]{1,0:T(8,128)(2,1)S(1)}, u32[]{:S(2)}, u32[]{:S(2)}) collective-permute-start(bf16[32,1536]{1,0:T(8,128)(2,1)S(1)} %add.225), channel_id=1, source_target_pairs={{0,3},{1,2},{2,1},{3,0},{4,7},{5,6},{6,5},{7,4},{8,11},{9,10},{10,... | collective-permute-start | bytes 294920 | tf_op jit(solution)/shard_map/ppermute | solution.py:20
  80.0 5.6 %collective-permute-done.5 = bf16[32,1536]{1,0:T(8,128)(2,1)S(1)} collective-permute-done((bf16[32,1536]{1,0:T(8,128)(2,1)S(1)}, bf16[32,1536]{1,0:T(8,128)(2,1)S(1)}, u32[]{:S(2)}, u32[]{:S(2)}) %collective-permute-start.5) | collective-permute-done | bytes 98336 | tf_op jit(solution)/shard_map/ppermute | solution.py:20
  85.6 3.0 %collective-permute-start.6 = (bf16[32,1536]{1,0:T(8,128)(2,1)S(1)}, bf16[32,1536]{1,0:T(8,128)(2,1)S(1)}, u32[]{:S(2)}, u32[]{:S(2)}) collective-permute-start(bf16[32,1536]{1,0:T(8,128)(2,1)S(1)} %add.226), channel_id=1, source_target_pairs={{0,7},{1,6},{2,5},{3,4},{4,3},{5,2},{6,1},{7,0},{8,15},{9,14},{10,... | collective-permute-start | bytes 294920 | tf_op jit(solution)/shard_map/ppermute | solution.py:23
  88.6 3.7 %collective-permute-done.6 = bf16[32,1536]{1,0:T(8,128)(2,1)S(1)} collective-permute-done((bf16[32,1536]{1,0:T(8,128)(2,1)S(1)}, bf16[32,1536]{1,0:T(8,128)(2,1)S(1)}, u32[]{:S(2)}, u32[]{:S(2)}) %collective-permute-start.6) | collective-permute-done | bytes 98336 | tf_op jit(solution)/shard_map/ppermute | solution.py:23
  (81 shorter events, 9.3 us)
Async XLA Ops:
  0.0 70.8 %copy-start = (bf16[576,1536]{1,0:T(8,128)(2,1)S(1)}, bf16[576,1536]{1,0:T(8,128)(2,1)}, u32[]{:S(2)}) copy-start(bf16[576,1536]{1,0:T(8,128)(2,1)} %param.25) | copy-start | bytes 5308420
  0.0 14.2 %copy-start.4 = (bf16[128,1536]{1,0:T(8,128)(2,1)S(1)}, bf16[128,1536]{1,0:T(8,128)(2,1)}, u32[]{:S(2)}) copy-start(bf16[128,1536]{1,0:T(8,128)(2,1)} %param.21) | copy-start | bytes 1179652
  0.0 16.2 %copy-start.2 = (bf16[1536,128]{1,0:T(8,128)(2,1)S(1)}, bf16[1536,128]{1,0:T(8,128)(2,1)}, u32[]{:S(2)}) copy-start(bf16[1536,128]{1,0:T(8,128)(2,1)} %param.19) | copy-start | bytes 1179652
  6.6 15.9 %all-to-all-start = ((bf16[32,8,532]{2,1,0:T(8,128)(2,1)}), bf16[32,8,532]{2,1,0:T(8,128)(2,1)S(1)}, u32[]{:S(2)}, u32[]{:S(2)}) async-start(bf16[32,8,532]{2,1,0:T(8,128)(2,1)} %broadcast_in_dim.131), calls=%async_computation | async-start | bytes 655360 | tf_op jit(solution)/shard_map/all_to_all | solution.py:72
  14.2 37.6 %collective-permute-start.1 = (bf16[128,1536]{1,0:T(8,128)(2,1)S(1)}, bf16[128,1536]{1,0:T(8,128)(2,1)}, u32[]{:S(2)}, u32[]{:S(2)}) collective-permute-start(bf16[128,1536]{1,0:T(8,128)(2,1)S(1)} %copy-done.4), channel_id=1, source_target_pairs={{0,1},{1,0},{2,3},{3,2},{4,5},{5,4},{6,7},{7,6},{8,9},{9,8},{10,11... | collective-permute-start | bytes 1179656 | tf_op jit(solution)/shard_map/ppermute | solution.py:52
  16.6 6.5 %copy-start.6 = (pred[4,4]{1,0:T(4,128)(4,1)}, pred[4,4]{1,0:T(4,128)(4,1)S(1)}, u32[]{:S(2)}) copy-start(pred[4,4]{1,0:T(4,128)(4,1)S(1)} %iota_compare_fusion.1) | copy-start | bytes 52
  31.2 10.9 %copy-start.3 = (bf16[1536,128]{1,0:T(8,128)(2,1)S(1)}, bf16[1536,128]{1,0:T(8,128)(2,1)}, u32[]{:S(2)}) copy-start(bf16[1536,128]{1,0:T(8,128)(2,1)} %param.20) | copy-start | bytes 1179652
  35.4 13.4 %all-to-all-start.1 = ((bf16[32,8,528]{2,1,0:T(8,128)(2,1)}), bf16[32,8,528]{2,1,0:T(8,128)(2,1)S(1)}, u32[]{:S(2)}, u32[]{:S(2)}) async-start(bf16[32,8,528]{2,1,0:T(8,128)(2,1)} %pad_maximum_fusion), calls=%async_computation.1 | async-start | bytes 655360 | tf_op jit(solution)/shard_map/all_to_all | solution.py:147
  49.8 20.4 %copy-start.1 = (bf16[1536,576]{0,1:T(8,128)(2,1)S(1)}, bf16[1536,576]{0,1:T(8,128)(2,1)}, u32[]{:S(2)}) copy-start(bf16[1536,576]{0,1:T(8,128)(2,1)} %param.23) | copy-start | bytes 5308420
  49.9 20.4 %copy-start.5 = (f32[1536]{0:T(1024)S(1)}, f32[1536]{0:T(1024)}, u32[]{:S(2)}) copy-start(f32[1536]{0:T(1024)} %param.22) | copy-start | bytes 18436
  49.9 3.7 %collective-permute-start = (bf16[32,128]{1,0:T(8,128)(2,1)S(1)}, bf16[32,128]{1,0:T(8,128)(2,1)S(1)}, u32[]{:S(2)}, u32[]{:S(2)}) collective-permute-start(bf16[32,128]{1,0:T(8,128)(2,1)S(1)} %bitcast.72), channel_id=1, source_target_pairs={{0,1},{1,0},{2,3},{3,2},{4,5},{5,4},{6,7},{7,6},{8,9},{9,8},{10,11... | collective-permute-start | bytes 24584 | tf_op jit(solution)/shard_map/ppermute | solution.py:192
  53.8 7.3 %collective-permute-start.2 = (bf16[32,1536]{1,0:T(8,128)(2,1)S(1)}, bf16[32,1536]{1,0:T(8,128)(2,1)S(1)}, u32[]{:S(2)}, u32[]{:S(2)}) collective-permute-start(bf16[32,1536]{1,0:T(8,128)(2,1)S(1)} %convolution_convert_fusion.1), channel_id=1, source_target_pairs={{0,3},{1,2},{2,1},{3,0},{4,7},{5,6},{6,5},{7,4},{8,11},{9,10},{10,... | collective-permute-start | bytes 294920 | tf_op jit(solution)/shard_map/ppermute | solution.py:20
  61.2 8.9 %collective-permute-start.3 = (bf16[32,1536]{1,0:T(8,128)(2,1)S(1)}, bf16[32,1536]{1,0:T(8,128)(2,1)S(1)}, u32[]{:S(2)}, u32[]{:S(2)}) collective-permute-start(bf16[32,1536]{1,0:T(8,128)(2,1)S(1)} %add.218), channel_id=1, source_target_pairs={{0,7},{1,6},{2,5},{3,4},{4,3},{5,2},{6,1},{7,0},{8,15},{9,14},{10,... | collective-permute-start | bytes 294920 | tf_op jit(solution)/shard_map/ppermute | solution.py:23
  73.4 4.7 %collective-permute-start.4 = (bf16[32,1536]{1,0:T(8,128)(2,1)S(1)}, bf16[32,1536]{1,0:T(8,128)(2,1)S(1)}, u32[]{:S(2)}, u32[]{:S(2)}) collective-permute-start(bf16[32,1536]{1,0:T(8,128)(2,1)S(1)} %convolution_convert_fusion), channel_id=1, source_target_pairs={{0,1},{1,0},{2,3},{3,2},{4,5},{5,4},{6,7},{7,6},{8,9},{9,8},{10,11... | collective-permute-start | bytes 294920 | tf_op jit(solution)/shard_map/ppermute | solution.py:20
  78.1 7.6 %collective-permute-start.5 = (bf16[32,1536]{1,0:T(8,128)(2,1)S(1)}, bf16[32,1536]{1,0:T(8,128)(2,1)S(1)}, u32[]{:S(2)}, u32[]{:S(2)}) collective-permute-start(bf16[32,1536]{1,0:T(8,128)(2,1)S(1)} %add.225), channel_id=1, source_target_pairs={{0,3},{1,2},{2,1},{3,0},{4,7},{5,6},{6,5},{7,4},{8,11},{9,10},{10,... | collective-permute-start | bytes 294920 | tf_op jit(solution)/shard_map/ppermute | solution.py:20
  85.6 6.7 %collective-permute-start.6 = (bf16[32,1536]{1,0:T(8,128)(2,1)S(1)}, bf16[32,1536]{1,0:T(8,128)(2,1)S(1)}, u32[]{:S(2)}, u32[]{:S(2)}) collective-permute-start(bf16[32,1536]{1,0:T(8,128)(2,1)S(1)} %add.226), channel_id=1, source_target_pairs={{0,7},{1,6},{2,5},{3,4},{4,3},{5,2},{6,1},{7,0},{8,15},{9,14},{10,... | collective-permute-start | bytes 294920 | tf_op jit(solution)/shard_map/ppermute | solution.py:23
